TPU v7x, 512 devices: a whole 4x4x16 slice. The times are simulated.
512 devices in a mesh: ctx: 64 (over z, x_lo, core), tp: 8 (over y, x_hi).
Axes of the slice: x: 4 (x_hi: 2, x_lo: 2; x = x_hi * 2 + x_lo), y: 4, z: 16, core: 2. Of those that a mesh axis runs over, the one named last changes fastest.
Arguments:
- queries: bfloat16 [8192, 4096], P('ctx', 'tp'), may hold values from -5 to 5
- keys: bfloat16 [8192, 1024], P('ctx', 'tp'), may hold values from -5 to 5
- values: bfloat16 [8192, 1024], P('ctx', 'tp'), may hold values from -6 to 6
- docs: int32 [8192], P('ctx'), may hold values from 0 to 11, never falling along the last dimension, each value on 1 to 4224 neighbouring positions
- out_weight: bfloat16 [4096, 4096], P('tp'), may hold values from -0.09375 to 0.09375
Outputs:
- mixed: bfloat16 [8192, 4096], P('ctx', 'tp')
All inputs are finite; a program needn't handle non-finite values.
Results may differ from a plain program's by a relative error of at most 0.014.
Values may be sent and summed in bfloat16 or wider, within the bound.
No kernel may reach another device: no remote copies, remote signals or barrier semaphores. Data moves between devices by JAX's collectives and lax.ppermute only.
A program may use at most 64 MiB of HBM per device.

v0:
```python
import math

import jax
import jax.numpy as jnp
from jax import lax
from jax.sharding import PartitionSpec as P

HEAD_DIM = 128


neg_large = -1e30


def attend(state, query_half, query_pos, query_doc, key_part, value_part, key_pos, key_doc):
    peak, total, accum = state
    scores = jnp.einsum("igkd,jgd->gkij", query_half, key_part, preferred_element_type=jnp.float32)
    scores = scores * (1.0 / math.sqrt(key_part.shape[-1]))
    allowed = (key_pos[None, :] <= query_pos[:, None]) & (key_doc[None, :] == query_doc[:, None])
    block_peak = jnp.max(jnp.where(allowed, scores, neg_large), axis=-1)
    new_peak = jnp.maximum(peak, block_peak)
    rescale = jnp.exp(peak - new_peak)
    weights = jnp.where(allowed, jnp.exp(scores - new_peak[..., None]), 0.0)
    total = total * rescale + jnp.sum(weights, axis=-1)
    update = jnp.einsum(
        "gkij,jgd->gkid",
        weights.astype(jnp.bfloat16),
        value_part,
        preferred_element_type=jnp.float32,
    )
    accum = accum * rescale[..., None] + update
    return (new_peak, total, accum)


def visit(state, query_half, query_pos, query_doc, key_part, value_part, key_pos, key_doc):
    needed = jnp.min(key_pos) <= jnp.max(query_pos)

    def compute(current):
        return attend(
            current, query_half, query_pos, query_doc, key_part, value_part, key_pos, key_doc
        )

    def unchanged(current):
        return current

    return lax.cond(needed, compute, unchanged, state)


def finish(state):
    peak, total, accum = state
    summed = accum / total[..., None]
    kv_count, group_size, row_count, head_dim = summed.shape
    summed = jnp.transpose(summed, (2, 0, 1, 3)).reshape(
        row_count, kv_count * group_size * head_dim
    )
    return summed.astype(jnp.bfloat16)


def shards(queries, keys, values, docs, out_weight):
    row_count = queries.shape[0]
    half_rows = row_count // 2
    head_dim = HEAD_DIM
    kv_local = keys.shape[1] // head_dim
    group_size = queries.shape[1] // keys.shape[1]
    my_index = lax.axis_index("ctx")
    all_docs = lax.all_gather(docs, "ctx", axis=0, tiled=True)
    offsets = jnp.arange(half_rows, dtype=jnp.int32)
    shard_offsets = jnp.arange(row_count, dtype=jnp.int32)
    lower_queries = queries[:half_rows]
    upper_queries = queries[half_rows:]
    low_positions = my_index * row_count + offsets
    high_positions = my_index * row_count + half_rows + offsets
    low_docs = jnp.take(all_docs, low_positions)
    high_docs = jnp.take(all_docs, high_positions)
    query_low = lower_queries.reshape(half_rows, kv_local, group_size, head_dim)
    query_high = upper_queries.reshape(half_rows, kv_local, group_size, head_dim)
    empty = (
        jnp.full((kv_local, group_size, half_rows), neg_large, jnp.float32),
        jnp.zeros((kv_local, group_size, half_rows), jnp.float32),
        jnp.zeros((kv_local, group_size, half_rows, head_dim), jnp.float32),
    )
    carry = (empty, empty)
    key_piece = lax.all_gather(keys, "ctx", axis=0, tiled=True)
    value_piece = lax.all_gather(values, "ctx", axis=0, tiled=True)
    shard_count = key_piece.shape[0] // row_count
    shaped_keys = key_piece.reshape(shard_count, row_count, kv_local, head_dim)
    shaped_values = value_piece.reshape(shard_count, row_count, kv_local, head_dim)
    shard_numbers = jnp.arange(shard_count, dtype=jnp.int32)

    def one_shard(states, inputs):
        key_part, value_part, shard_number = inputs
        key_pos = shard_number * row_count + shard_offsets
        key_doc = jnp.take(all_docs, key_pos)
        state_low, state_high = states
        state_low = visit(
            state_low, query_low, low_positions, low_docs, key_part, value_part, key_pos, key_doc
        )
        state_high = visit(
            state_high,
            query_high,
            high_positions,
            high_docs,
            key_part,
            value_part,
            key_pos,
            key_doc,
        )
        return ((state_low, state_high), None)

    carry, unused = lax.scan(one_shard, carry, (shaped_keys, shaped_values, shard_numbers))
    attention = jnp.concatenate([finish(carry[0]), finish(carry[1])], axis=0)
    partial_terms = jnp.dot(attention, out_weight, preferred_element_type=jnp.float32)
    mixed = lax.psum_scatter(
        partial_terms.astype(jnp.bfloat16), "tp", scatter_dimension=1, tiled=True
    )
    return mixed


def solution(mesh):
    placed = (P("ctx", "tp"), P("ctx", "tp"), P("ctx", "tp"), P("ctx"), P("tp", None))
    return jax.shard_map(
        shards, mesh=mesh, in_specs=placed, out_specs=P("ctx", "tp"), check_vma=False
    )
```

profile of v0, /device:TPU:24, one launch (start us, length us, event | category | flops | bytes accessed | tf_op | source)
XLA Modules:
  0.0 863.2 jit_solution(10624895469857638994)
XLA Ops:
  8.1 69.5 %all-gather = s32[64,1,128]{2,1,0:T(1,128)S(1)} all-gather(s32[1,1,128]{2,1,0:T(1,128)} %bitcast.123), channel_id=1, replica_groups=mesh['ctx'=64,'tp'=8] {'ctx'}, dimensions={0}, use_global_device_ids=true | all-gather | bytes 33280 | tf_op jit(solution)/shard_map/all_gather | solution.py:65
  80.8 55.0 %all-gather.4.cloned.1.call-done = bf16[8192,128]{1,0:T(8,128)(2,1)} async-done(((bf16[128,128]{1,0:T(8,128)(2,1)}), bf16[8192,128]{1,0:T(8,128)(2,1)}) %all-gather.4.cloned.1.call-update) | async-done | bytes 2097168 | tf_op jit(solution)/shard_map/all_gather | solution.py:82
  135.8 120.7 %all-gather.6.cloned.1.call-done = bf16[8192,128]{1,0:T(8,128)(2,1)} async-done(((bf16[128,128]{1,0:T(8,128)(2,1)}), bf16[8192,128]{1,0:T(8,128)(2,1)}) %all-gather.6.cloned.1.call-update) | async-done | bytes 2097168 | tf_op jit(solution)/shard_map/all_gather | solution.py:83
  256.5 410.4 %while.22 = (s32[]{:T(128)}, f32[1,4,64]{2,1,0:T(4,128)S(1)}, f32[1,4,64]{2,1,0:T(4,128)S(1)}, f32[1,4,64,128]{3,2,1,0:T(8,128)S(1)}, f32[1,4,64]{2,1,0:T(4,128)...) while((s32[]{:T(128)}, f32[1,4,64]{2,1,0:T(4,128)S(1)}, ...), condition=%wide.region_12.14_spmd.clone, body=%wide.region_2.13_spmd.clone.sunk | while | flops 34328964 | bytes 1815597 | solution.py:109
  257.8 1.1 gather_fusion
  265.9 1.1 gather_fusion
  272.3 1.1 gather_fusion
  278.7 1.1 gather_fusion
  285.0 1.1 gather_fusion
  291.4 1.1 gather_fusion
  297.8 1.1 gather_fusion
  304.2 1.1 gather_fusion
  310.6 1.1 gather_fusion
  317.0 1.1 gather_fusion
  323.4 1.1 gather_fusion
  329.7 1.1 gather_fusion
  336.1 1.1 gather_fusion
  342.5 1.1 gather_fusion
  348.9 1.1 gather_fusion
  419.1 1.1 gather_fusion
  540.5 1.1 gather_fusion
  661.8 1.1 gather_fusion
  667.3 3.9 convolution_convert_fusion
  671.3 185.4 %reduce-scatter.2.cloned.1.call-done = bf16[128,512]{1,0:T(8,128)(2,1)} async-done(((bf16[128,4096]{1,0:T(8,128)(2,1)}), bf16[128,512]{1,0:T(8,128)(2,1)}) %reduce-scatter.2.cloned.1.call-update) | async-done | bytes 131088 | tf_op jit(solution)/shard_map/reduce_scatter | solution.py:112
  (734 shorter events, 195.0 us)
Async XLA Ops:
  6.5 129.2 %all-gather.4.cloned.1.call-start = ((), (), s32[]{:S(2)}) async-start(), calls=%async_computation.1 | async-start | bytes 2129920 | tf_op jit(solution)/shard_map/all_gather | solution.py:82
  7.3 249.2 %all-gather.6.cloned.1.call-start = ((), (), s32[]{:S(2)}) async-start(), calls=%async_computation.2 | async-start | bytes 2129920 | tf_op jit(solution)/shard_map/all_gather | solution.py:83
  8.0 848.7 %reduce-scatter.2.cloned.1.call-start = ((), (), s32[]{:S(2)}) async-start(), calls=%async_computation.3 | async-start | bytes 1179648 | tf_op jit(solution)/shard_map/reduce_scatter | solution.py:112
Sparse Core Ops, SparseCore 0:
  9.5 126.2 all-gather.3
  137.9 118.4 all-gather.5
  671.4 185.2 reduce-scatter.1
where the time goes:
time: 871 us; the launch traced here: 863 us
  waiting for transfers between devices  363 us (42%)
  loops' own time  203 us (23%)
  local copies, waits for them, and re-layouts  165 us (19%)
  blocking collectives  69.5 us (8%)
  other arithmetic  45.1 us (5%)
  between operations  13.2 us (2%)
    another operation x1, loops' own time, shards(): lax.scan(one_shard, carry, (shaped_keys, shaped_values, shard_numbers))  201 us
    reduce_scatter x1, waiting for transfers between devices, shards(): lax.psum_scatter(partial_terms.astype(jnp.bfloat16), 'tp', scatter_dimens...  185 us
    all_gather x1, waiting for transfers between devices, shards(): value_piece = lax.all_gather(values, 'ctx', axis=0, tiled=True)  121 us
    gather x64, local copies, waits for them, and re-layouts, one_shard(): key_doc = jnp.take(all_docs, key_pos)  73.5 us
    all_gather x1, blocking collectives, shards(): all_docs = lax.all_gather(docs, 'ctx', axis=0, tiled=True)  69.5 us
    all_gather x1, waiting for transfers between devices, shards(): key_piece = lax.all_gather(keys, 'ctx', axis=0, tiled=True)  55 us
    squeeze x64, local copies, waits for them, and re-layouts, shards(): lax.scan(one_shard, carry, (shaped_keys, shaped_values, shard_numbers))  50.4 us
    reduce_min x64, other arithmetic, visit(): needed = jnp.min(key_pos) <= jnp.max(query_pos)  42.4 us
  transfers between devices with their start and end apart: 3, of which 3 were waited for; matrix products, arithmetic and copies ran while one was open for 0% of the time, Pallas kernels for 0%

commit v1 on v0

v1 whole, which is shorter than its diff:
```python
import math

import jax
import jax.numpy as jnp
from jax import lax
from jax.sharding import PartitionSpec as P

HEAD_DIM = 128
MAX_DOC = 4224
PLANE = 4
neg_large = -1e30


def shards(queries, keys, values, docs, out_weight):
    rows = queries.shape[0]
    head_dim = HEAD_DIM
    group_size = queries.shape[1] // keys.shape[1]
    ctx = lax.psum(1, "ctx")
    tp = lax.psum(1, "tp")
    my_index = lax.axis_index("ctx")
    my_tp = lax.axis_index("tp")
    plane = my_index // PLANE
    slot = my_index % PLANE

    shards_back = -(-(MAX_DOC - 1) // rows)
    hops = min(-(-(shards_back + PLANE - 1) // PLANE), ctx // PLANE - 1)

    kv = jnp.concatenate([keys, values], axis=1)
    plane_kv = [kv]
    plane_docs = [docs]
    for offset in range(1, PLANE):
        perm = [(s, s ^ offset) for s in range(ctx)]
        plane_kv.append(lax.ppermute(kv, "ctx", perm))
        plane_docs.append(lax.ppermute(docs, "ctx", perm))
    block_kv = jnp.stack(plane_kv)
    block_docs = jnp.stack(plane_docs)

    forward = [(s, s + PLANE) for s in range(ctx - PLANE)]
    all_kv = [block_kv]
    all_docs = [block_docs]
    for hop in range(hops):
        block_kv = lax.ppermute(block_kv, "ctx", forward)
        block_docs = lax.ppermute(block_docs, "ctx", forward)
        all_kv.append(block_kv)
        all_docs.append(block_docs)
    all_kv = jnp.stack(all_kv)
    all_docs = jnp.stack(all_docs)
    count = all_kv.shape[0] * PLANE * rows

    hop_ids = jnp.arange(hops + 1, dtype=jnp.int32)[:, None, None]
    offsets = jnp.arange(PLANE, dtype=jnp.int32)[None, :, None]
    tokens = jnp.arange(rows, dtype=jnp.int32)[None, None, :]
    key_shard = PLANE * (plane - hop_ids) + (slot ^ offsets)
    key_pos = (key_shard * rows + tokens).reshape(count)
    key_doc = all_docs.reshape(count)
    key_part = all_kv[..., :head_dim].reshape(count, head_dim)
    value_part = all_kv[..., head_dim:].reshape(count, head_dim)

    query_pos = my_index * rows + jnp.arange(rows, dtype=jnp.int32)
    query = queries.reshape(rows, group_size, head_dim)
    scores = jnp.einsum("ihd,jd->hij", query, key_part, preferred_element_type=jnp.float32)
    scores = scores * (1.0 / math.sqrt(head_dim))
    allowed = (
        (key_pos[None, :] <= query_pos[:, None])
        & (key_pos[None, :] >= 0)
        & (key_doc[None, :] == docs[:, None])
    )
    peak = jnp.max(jnp.where(allowed, scores, neg_large), axis=-1)
    weight = jnp.where(allowed, jnp.exp(scores - peak[..., None]), 0.0)
    total = jnp.sum(weight, axis=-1)
    summed = jnp.einsum(
        "hij,jd->hid", weight.astype(jnp.bfloat16), value_part, preferred_element_type=jnp.float32
    )
    summed = summed / total[..., None]
    attention = jnp.transpose(summed, (1, 0, 2)).reshape(rows, group_size * head_dim)
    attention = attention.astype(jnp.bfloat16)

    partial_terms = jnp.dot(attention, out_weight, preferred_element_type=jnp.float32)
    width = partial_terms.shape[1] // tp
    chunks = jnp.transpose(partial_terms.reshape(rows, tp, width), (1, 0, 2))
    mixed = lax.dynamic_index_in_dim(chunks, my_tp, 0, keepdims=False)
    sent = chunks.astype(jnp.bfloat16)
    for shift in range(1, tp):
        piece = lax.dynamic_index_in_dim(sent, (my_tp + shift) % tp, 0, keepdims=False)
        perm = [(t, (t + shift) % tp) for t in range(tp)]
        mixed = mixed + lax.ppermute(piece, "tp", perm).astype(jnp.float32)
    return mixed.astype(jnp.bfloat16)


def solution(mesh):
    placed = (P("ctx", "tp"), P("ctx", "tp"), P("ctx", "tp"), P("ctx"), P("tp", None))
    return jax.shard_map(
        shards, mesh=mesh, in_specs=placed, out_specs=P("ctx", "tp"), check_vma=False
    )
```

time: 871 us -> 206 us (0.24)
  the two profiles are of different devices: /device:TPU:24 before, /device:TPU:128 now
where the time goes in v1:
time: 206 us; the launch traced here: 205 us
  starting transfers between devices  96.7 us (47%)
  waiting for transfers between devices  67 us (33%)
  other arithmetic  20.8 us (10%)
  matrix products  10.5 us (5%)
  local copies, waits for them, and re-layouts  9.1 us (4%)
    ppermute x9, waiting for transfers between devices, shards(): block_kv = lax.ppermute(block_kv, 'ctx', forward)  42 us
    ppermute x9, starting transfers between devices, shards(): block_docs = lax.ppermute(block_docs, 'ctx', forward)  27.7 us
    ppermute x7, starting transfers between devices, shards(): mixed = mixed + lax.ppermute(piece, 'tp', perm).astype(jnp.float32)  27.4 us
    ppermute x9, starting transfers between devices, shards(): block_kv = lax.ppermute(block_kv, 'ctx', forward)  26.1 us
    ppermute x9, waiting for transfers between devices, shards(): block_docs = lax.ppermute(block_docs, 'ctx', forward)  17.8 us
    sub x1, other arithmetic, shards(): weight = jnp.where(allowed, jnp.exp(scores - peak[..., None]), 0.0)  14.7 us
    ppermute x3, starting transfers between devices, shards(): plane_docs.append(lax.ppermute(docs, 'ctx', perm))  7.73 us
    ppermute x3, starting transfers between devices, shards(): plane_kv.append(lax.ppermute(kv, 'ctx', perm))  7.71 us
  transfers between devices with their start and end apart: 31, of which 15 were waited for; matrix products, arithmetic and copies ran while one was open for 5% of the time, Pallas kernels for 0%

profile of v1, /device:TPU:128, one launch (start us, length us, event | category | flops | bytes accessed | tf_op | source)
XLA Modules:
  0.0 204.8 jit_solution(2920145263253011575)
XLA Ops:
  15.0 6.5 %copy.15 = bf16[4096,512]{1,0:T(8,128)(2,1)} copy(bf16[4096,512]{0,1:T(8,128)(2,1)} %bitcast.127) | data formatting | bytes 8388608 | tf_op jit(solution)/shard_map/dot_general | solution.py:78
  23.9 3.8 %collective-permute-start.3 = (s32[4,128]{1,0:T(4,128)S(1)}, s32[4,128]{1,0:T(4,128)S(1)}, u32[]{:S(2)}, u32[]{:S(2)}) collective-permute-start(s32[4,128]{1,0:T(4,128)S(1)} %pad_add_fusion), channel_id=1, source_target_pairs={{0,32},{8,40},{16,48},{24,56},{32,64},{40,72},{48,80},{56,88},{64,... | collective-permute-start | bytes 6152 | tf_op jit(solution)/shard_map/ppermute | solution.py:43
  33.2 4.1 %collective-permute-done.4 = s32[4,128]{1,0:T(4,128)S(1)} collective-permute-done((s32[4,128]{1,0:T(4,128)S(1)}, s32[4,128]{1,0:T(4,128)S(1)}, u32[]{:S(2)}, u32[]{:S(2)}) %collective-permute-start.4) | collective-permute-done | bytes 2080 | tf_op jit(solution)/shard_map/ppermute | solution.py:43
  39.3 3.8 %collective-permute-start.15 = (bf16[4,128,256]{2,1,0:T(8,128)(2,1)S(1)}, bf16[4,128,256]{2,1,0:T(8,128)(2,1)S(1)}, u32[]{:S(2)}, u32[]{:S(2)}) collective-permute-start(bf16[4,128,256]{2,1,0:T(8,128)(2,1)S(1)} %pad_maximum_fusion), channel_id=1, source_target_pairs={{0,32},{8,40},{16,48},{24,56},{32,64},{40,72},{48,80},{56,88},{64,... | collective-permute-start | bytes 786440 | tf_op jit(solution)/shard_map/ppermute | solution.py:42
  44.0 4.5 %collective-permute-start.6 = (s32[4,128]{1,0:T(4,128)S(1)}, s32[4,128]{1,0:T(4,128)S(1)}, u32[]{:S(2)}, u32[]{:S(2)}) collective-permute-start(s32[4,128]{1,0:T(4,128)S(1)} %collective-permute-done.5), channel_id=1, source_target_pairs={{0,32},{8,40},{16,48},{24,56},{32,64},{40,72},{48,80},{56,88},{64,... | collective-permute-start | bytes 6152 | tf_op jit(solution)/shard_map/ppermute | solution.py:43
  50.7 4.5 %collective-permute-start.7 = (s32[4,128]{1,0:T(4,128)S(1)}, s32[4,128]{1,0:T(4,128)S(1)}, u32[]{:S(2)}, u32[]{:S(2)}) collective-permute-start(s32[4,128]{1,0:T(4,128)S(1)} %collective-permute-done.6), channel_id=1, source_target_pairs={{0,32},{8,40},{16,48},{24,56},{32,64},{40,72},{48,80},{56,88},{64,... | collective-permute-start | bytes 6152 | tf_op jit(solution)/shard_map/ppermute | solution.py:43
  55.2 4.2 %collective-permute-start.16 = (bf16[4,128,256]{2,1,0:T(8,128)(2,1)S(1)}, bf16[4,128,256]{2,1,0:T(8,128)(2,1)S(1)}, u32[]{:S(2)}, u32[]{:S(2)}) collective-permute-start(bf16[4,128,256]{2,1,0:T(8,128)(2,1)S(1)} %collective-permute-done.15), channel_id=1, source_target_pairs={{0,32},{8,40},{16,48},{24,56},{32,64},{40,72},{48,80},{56,88},{64,... | collective-permute-start | bytes 786440 | tf_op jit(solution)/shard_map/ppermute | solution.py:42
  62.2 3.9 %collective-permute-done.8 = s32[4,128]{1,0:T(4,128)S(1)} collective-permute-done((s32[4,128]{1,0:T(4,128)S(1)}, s32[4,128]{1,0:T(4,128)S(1)}, u32[]{:S(2)}, u32[]{:S(2)}) %collective-permute-start.8) | collective-permute-done | bytes 2080 | tf_op jit(solution)/shard_map/ppermute | solution.py:43
  68.6 4.2 %collective-permute-start.17 = (bf16[4,128,256]{2,1,0:T(8,128)(2,1)S(1)}, bf16[4,128,256]{2,1,0:T(8,128)(2,1)S(1)}, u32[]{:S(2)}, u32[]{:S(2)}) collective-permute-start(bf16[4,128,256]{2,1,0:T(8,128)(2,1)S(1)} %collective-permute-done.16), channel_id=1, source_target_pairs={{0,32},{8,40},{16,48},{24,56},{32,64},{40,72},{48,80},{56,88},{64,... | collective-permute-start | bytes 786440 | tf_op jit(solution)/shard_map/ppermute | solution.py:42
  75.6 3.9 %collective-permute-done.10 = s32[4,128]{1,0:T(4,128)S(1)} collective-permute-done((s32[4,128]{1,0:T(4,128)S(1)}, s32[4,128]{1,0:T(4,128)S(1)}, u32[]{:S(2)}, u32[]{:S(2)}) %collective-permute-start.10) | collective-permute-done | bytes 2080 | tf_op jit(solution)/shard_map/ppermute | solution.py:43
  81.9 4.2 %collective-permute-start.18 = (bf16[4,128,256]{2,1,0:T(8,128)(2,1)S(1)}, bf16[4,128,256]{2,1,0:T(8,128)(2,1)S(1)}, u32[]{:S(2)}, u32[]{:S(2)}) collective-permute-start(bf16[4,128,256]{2,1,0:T(8,128)(2,1)S(1)} %collective-permute-done.17), channel_id=1, source_target_pairs={{0,32},{8,40},{16,48},{24,56},{32,64},{40,72},{48,80},{56,88},{64,... | collective-permute-start | bytes 786440 | tf_op jit(solution)/shard_map/ppermute | solution.py:42
  86.2 7.2 %collective-permute-done.18 = bf16[4,128,256]{2,1,0:T(8,128)(2,1)S(1)} collective-permute-done((bf16[4,128,256]{2,1,0:T(8,128)(2,1)S(1)}, bf16[4,128,256]{2,1,0:T(8,128)(2,1)S(1)}, u32[]{:S(2)}, u32[]{:S(2)}) %collective-permute-start.18) | collective-permute-done | bytes 262176 | tf_op jit(solution)/shard_map/ppermute | solution.py:42
  95.3 4.0 %compare_and_fusion = pred[128,5120]{0,1:T(8,128)(4,1)S(1)} fusion(s32[128]{0:T(128)S(1)} %copy-done.2, s32[128]{0:T(128)S(1)} %iota_add_fusion.1, s32[5120]{0:T(1024)S(1)} %bitcast.140, s32[5120]{0:T(1024)S(1)} %bitcast.138, pred[5120]{0:T(1024)(128)(4,1)S(1)} %broadcast_compare_fusion), kind=kLoop, calls=%fused_computation.12 | loop fusion | flops 2621440 | bytes 702464 | tf_op jit(solution)/shard_map/and | solution.py:64
  99.4 4.7 %collective-permute-done.19 = bf16[4,128,256]{2,1,0:T(8,128)(2,1)S(1)} collective-permute-done((bf16[4,128,256]{2,1,0:T(8,128)(2,1)S(1)}, bf16[4,128,256]{2,1,0:T(8,128)(2,1)S(1)}, u32[]{:S(2)}, u32[]{:S(2)}) %collective-permute-start.19) | collective-permute-done | bytes 262176 | tf_op jit(solution)/shard_map/ppermute | solution.py:42
  106.0 7.8 %collective-permute-done.20 = bf16[4,128,256]{2,1,0:T(8,128)(2,1)S(1)} collective-permute-done((bf16[4,128,256]{2,1,0:T(8,128)(2,1)S(1)}, bf16[4,128,256]{2,1,0:T(8,128)(2,1)S(1)}, u32[]{:S(2)}, u32[]{:S(2)}) %collective-permute-start.20) | collective-permute-done | bytes 262176 | tf_op jit(solution)/shard_map/ppermute | solution.py:42
  115.8 7.5 %collective-permute-done.21 = bf16[4,128,256]{2,1,0:T(8,128)(2,1)S(1)} collective-permute-done((bf16[4,128,256]{2,1,0:T(8,128)(2,1)S(1)}, bf16[4,128,256]{2,1,0:T(8,128)(2,1)S(1)}, u32[]{:S(2)}, u32[]{:S(2)}) %collective-permute-start.21) | collective-permute-done | bytes 262176 | tf_op jit(solution)/shard_map/ppermute | solution.py:42
  125.2 7.5 %collective-permute-done.22 = bf16[4,128,256]{2,1,0:T(8,128)(2,1)S(1)} collective-permute-done((bf16[4,128,256]{2,1,0:T(8,128)(2,1)S(1)}, bf16[4,128,256]{2,1,0:T(8,128)(2,1)S(1)}, u32[]{:S(2)}, u32[]{:S(2)}) %collective-permute-start.22) | collective-permute-done | bytes 262176 | tf_op jit(solution)/shard_map/ppermute | solution.py:42
  134.9 7.3 %collective-permute-done.23 = bf16[4,128,256]{2,1,0:T(8,128)(2,1)S(1)} collective-permute-done((bf16[4,128,256]{2,1,0:T(8,128)(2,1)S(1)}, bf16[4,128,256]{2,1,0:T(8,128)(2,1)S(1)}, u32[]{:S(2)}, u32[]{:S(2)}) %collective-permute-start.23) | collective-permute-done | bytes 262176 | tf_op jit(solution)/shard_map/ppermute | solution.py:42
  142.7 5.5 %fusion.26 = f32[5120,128,4]{1,0,2:T(8,128)} fusion(bf16[5120,128,1]{1,0,2:T(8,128)(2,1)S(1)} %bitcast.126, bf16[128,512]{1,0:T(8,128)(2,1)S(1)} %copy-done), kind=kOutput, calls=%fused_computation.35 | convolution fusion | flops 671088640 | bytes 11927552 | tf_op jit(solution)/shard_map/ihd,jd->hij/dot_general | solution.py:61
  148.2 14.7 %fusion.32 = (f32[4,128]{1,0:T(4,128)S(1)}, bf16[4,128,5120]{1,2,0:T(8,128)(2,1)}) fusion(f32[5120,128,4]{1,0,2:T(8,128)} %fusion.26, pred[128,5120]{0,1:T(8,128)(4,1)S(1)} %compare_and_fusion), kind=kOutput, calls=%fused_computation.67 | output fusion | flops 18355200 | bytes 16386048 | tf_op jit(solution)/shard_map/sub | solution.py:69
  168.3 7.4 %collective-permute-start.30 = (bf16[128,512]{1,0:T(8,128)(2,1)S(1)}, bf16[128,512]{1,0:T(8,128)(2,1)S(1)}, u32[]{:S(2)}, u32[]{:S(2)}) collective-permute-start(bf16[128,512]{1,0:T(8,128)(2,1)S(1)} %get-tuple-element.8), channel_id=1, source_target_pairs={{0,7},{1,0},{2,1},{3,2},{4,3},{5,4},{6,5},{7,6},{8,15},{9,8},{10,9... | collective-permute-start | bytes 393224 | tf_op jit(solution)/shard_map/ppermute | solution.py:86
  180.7 4.8 %collective-permute-start.27 = (bf16[128,512]{1,0:T(8,128)(2,1)S(1)}, bf16[128,512]{1,0:T(8,128)(2,1)S(1)}, u32[]{:S(2)}, u32[]{:S(2)}) collective-permute-start(bf16[128,512]{1,0:T(8,128)(2,1)S(1)} %get-tuple-element.11), channel_id=1, source_target_pairs={{0,4},{1,5},{2,6},{3,7},{4,0},{5,1},{6,2},{7,3},{8,12},{9,13},{10,... | collective-permute-start | bytes 393224 | tf_op jit(solution)/shard_map/ppermute | solution.py:86
  188.6 3.8 %collective-permute-start.25 = (bf16[128,512]{1,0:T(8,128)(2,1)S(1)}, bf16[128,512]{1,0:T(8,128)(2,1)}, u32[]{:S(2)}, u32[]{:S(2)}) collective-permute-start(bf16[128,512]{1,0:T(8,128)(2,1)S(1)} %get-tuple-element.13), channel_id=1, source_target_pairs={{0,2},{1,3},{2,4},{3,5},{4,6},{5,7},{6,0},{7,1},{8,10},{9,11},{10,... | collective-permute-start | bytes 393224 | tf_op jit(solution)/shard_map/ppermute | solution.py:86
  198.1 4.9 %collective-permute-done.24 = bf16[128,512]{1,0:T(8,128)(2,1)} collective-permute-done((bf16[128,512]{1,0:T(8,128)(2,1)S(1)}, bf16[128,512]{1,0:T(8,128)(2,1)}, u32[]{:S(2)}, u32[]{:S(2)}) %collective-permute-start.24) | collective-permute-done | bytes 131104 | tf_op jit(solution)/shard_map/ppermute | solution.py:86
  (83 shorter events, 69.4 us)
Async XLA Ops:
  1.6 37.6 %collective-permute-start.14 = (bf16[128,256]{1,0:T(8,128)(2,1)S(1)}, bf16[128,256]{1,0:T(8,128)(2,1)S(1)}, u32[]{:S(2)}, u32[]{:S(2)}) collective-permute-start(bf16[128,256]{1,0:T(8,128)(2,1)S(1)} %constant_dynamic-update-slice_fusion), channel_id=1, source_target_pairs={{0,24},{8,16},{16,8},{24,0},{32,56},{40,48},{48,40},{56,32},{64,88... | collective-permute-start | bytes 196616 | tf_op jit(solution)/shard_map/ppermute | solution.py:33
  4.4 34.8 %collective-permute-start.13 = (bf16[128,256]{1,0:T(8,128)(2,1)S(1)}, bf16[128,256]{1,0:T(8,128)(2,1)S(1)}, u32[]{:S(2)}, u32[]{:S(2)}) collective-permute-start(bf16[128,256]{1,0:T(8,128)(2,1)S(1)} %constant_dynamic-update-slice_fusion), channel_id=1, source_target_pairs={{0,16},{8,24},{16,0},{24,8},{32,48},{40,56},{48,32},{56,40},{64,80... | collective-permute-start | bytes 196616 | tf_op jit(solution)/shard_map/ppermute | solution.py:33
  6.9 14.6 %collective-permute-start.2 = (s32[128]{0:T(128)}, s32[128]{0:T(128)S(1)}, u32[]{:S(2)}, u32[]{:S(2)}) collective-permute-start(s32[128]{0:T(128)} %param.8), channel_id=1, source_target_pairs={{0,24},{8,16},{16,8},{24,0},{32,56},{40,48},{48,40},{56,32},{64,88... | collective-permute-start | bytes 1544 | tf_op jit(solution)/shard_map/ppermute | solution.py:34
  10.3 13.6 %collective-permute-start.1 = (s32[128]{0:T(128)}, s32[128]{0:T(128)S(1)}, u32[]{:S(2)}, u32[]{:S(2)}) collective-permute-start(s32[128]{0:T(128)} %param.8), channel_id=1, source_target_pairs={{0,16},{8,24},{16,0},{24,8},{32,48},{40,56},{48,32},{56,40},{64,80... | collective-permute-start | bytes 1544 | tf_op jit(solution)/shard_map/ppermute | solution.py:34
  12.7 11.2 %collective-permute-start = (s32[128]{0:T(128)}, s32[128]{0:T(128)S(1)}, u32[]{:S(2)}, u32[]{:S(2)}) collective-permute-start(s32[128]{0:T(128)} %param.8), channel_id=1, source_target_pairs={{0,8},{8,0},{16,24},{24,16},{32,40},{40,32},{48,56},{56,48},{64,72... | collective-permute-start | bytes 1544 | tf_op jit(solution)/shard_map/ppermute | solution.py:34
  21.5 17.8 %collective-permute-start.12 = (bf16[128,256]{1,0:T(8,128)(2,1)S(1)}, bf16[128,256]{1,0:T(8,128)(2,1)S(1)}, u32[]{:S(2)}, u32[]{:S(2)}) collective-permute-start(bf16[128,256]{1,0:T(8,128)(2,1)S(1)} %constant_dynamic-update-slice_fusion), channel_id=1, source_target_pairs={{0,8},{8,0},{16,24},{24,16},{32,40},{40,32},{48,56},{56,48},{64,72... | collective-permute-start | bytes 196616 | tf_op jit(solution)/shard_map/ppermute | solution.py:33
  37.3 6.7 %collective-permute-start.5 = (s32[4,128]{1,0:T(4,128)S(1)}, s32[4,128]{1,0:T(4,128)S(1)}, u32[]{:S(2)}, u32[]{:S(2)}) collective-permute-start(s32[4,128]{1,0:T(4,128)S(1)} %collective-permute-done.4), channel_id=1, source_target_pairs={{0,32},{8,40},{16,48},{24,56},{32,64},{40,72},{48,80},{56,88},{64,... | collective-permute-start | bytes 6152 | tf_op jit(solution)/shard_map/ppermute | solution.py:43
  39.3 15.9 %collective-permute-start.15 = (bf16[4,128,256]{2,1,0:T(8,128)(2,1)S(1)}, bf16[4,128,256]{2,1,0:T(8,128)(2,1)S(1)}, u32[]{:S(2)}, u32[]{:S(2)}) collective-permute-start(bf16[4,128,256]{2,1,0:T(8,128)(2,1)S(1)} %pad_maximum_fusion), channel_id=1, source_target_pairs={{0,32},{8,40},{16,48},{24,56},{32,64},{40,72},{48,80},{56,88},{64,... | collective-permute-start | bytes 786440 | tf_op jit(solution)/shard_map/ppermute | solution.py:42
  50.7 8.7 %collective-permute-start.7 = (s32[4,128]{1,0:T(4,128)S(1)}, s32[4,128]{1,0:T(4,128)S(1)}, u32[]{:S(2)}, u32[]{:S(2)}) collective-permute-start(s32[4,128]{1,0:T(4,128)S(1)} %collective-permute-done.6), channel_id=1, source_target_pairs={{0,32},{8,40},{16,48},{24,56},{32,64},{40,72},{48,80},{56,88},{64,... | collective-permute-start | bytes 6152 | tf_op jit(solution)/shard_map/ppermute | solution.py:43
  55.2 13.3 %collective-permute-start.16 = (bf16[4,128,256]{2,1,0:T(8,128)(2,1)S(1)}, bf16[4,128,256]{2,1,0:T(8,128)(2,1)S(1)}, u32[]{:S(2)}, u32[]{:S(2)}) collective-permute-start(bf16[4,128,256]{2,1,0:T(8,128)(2,1)S(1)} %collective-permute-done.15), channel_id=1, source_target_pairs={{0,32},{8,40},{16,48},{24,56},{32,64},{40,72},{48,80},{56,88},{64,... | collective-permute-start | bytes 786440 | tf_op jit(solution)/shard_map/ppermute | solution.py:42
  68.6 13.3 %collective-permute-start.17 = (bf16[4,128,256]{2,1,0:T(8,128)(2,1)S(1)}, bf16[4,128,256]{2,1,0:T(8,128)(2,1)S(1)}, u32[]{:S(2)}, u32[]{:S(2)}) collective-permute-start(bf16[4,128,256]{2,1,0:T(8,128)(2,1)S(1)} %collective-permute-done.16), channel_id=1, source_target_pairs={{0,32},{8,40},{16,48},{24,56},{32,64},{40,72},{48,80},{56,88},{64,... | collective-permute-start | bytes 786440 | tf_op jit(solution)/shard_map/ppermute | solution.py:42
  81.9 11.5 %collective-permute-start.18 = (bf16[4,128,256]{2,1,0:T(8,128)(2,1)S(1)}, bf16[4,128,256]{2,1,0:T(8,128)(2,1)S(1)}, u32[]{:S(2)}, u32[]{:S(2)}) collective-permute-start(bf16[4,128,256]{2,1,0:T(8,128)(2,1)S(1)} %collective-permute-done.17), channel_id=1, source_target_pairs={{0,32},{8,40},{16,48},{24,56},{32,64},{40,72},{48,80},{56,88},{64,... | collective-permute-start | bytes 786440 | tf_op jit(solution)/shard_map/ppermute | solution.py:42
  93.4 10.7 %collective-permute-start.19 = (bf16[4,128,256]{2,1,0:T(8,128)(2,1)S(1)}, bf16[4,128,256]{2,1,0:T(8,128)(2,1)S(1)}, u32[]{:S(2)}, u32[]{:S(2)}) collective-permute-start(bf16[4,128,256]{2,1,0:T(8,128)(2,1)S(1)} %collective-permute-done.18), channel_id=1, source_target_pairs={{0,32},{8,40},{16,48},{24,56},{32,64},{40,72},{48,80},{56,88},{64,... | collective-permute-start | bytes 786440 | tf_op jit(solution)/shard_map/ppermute | solution.py:42
  104.1 9.7 %collective-permute-start.20 = (bf16[4,128,256]{2,1,0:T(8,128)(2,1)S(1)}, bf16[4,128,256]{2,1,0:T(8,128)(2,1)S(1)}, u32[]{:S(2)}, u32[]{:S(2)}) collective-permute-start(bf16[4,128,256]{2,1,0:T(8,128)(2,1)S(1)} %collective-permute-done.19), channel_id=1, source_target_pairs={{0,32},{8,40},{16,48},{24,56},{32,64},{40,72},{48,80},{56,88},{64,... | collective-permute-start | bytes 786440 | tf_op jit(solution)/shard_map/ppermute | solution.py:42
  113.8 9.5 %collective-permute-start.21 = (bf16[4,128,256]{2,1,0:T(8,128)(2,1)S(1)}, bf16[4,128,256]{2,1,0:T(8,128)(2,1)S(1)}, u32[]{:S(2)}, u32[]{:S(2)}) collective-permute-start(bf16[4,128,256]{2,1,0:T(8,128)(2,1)S(1)} %collective-permute-done.20), channel_id=1, source_target_pairs={{0,32},{8,40},{16,48},{24,56},{32,64},{40,72},{48,80},{56,88},{64,... | collective-permute-start | bytes 786440 | tf_op jit(solution)/shard_map/ppermute | solution.py:42
  123.3 9.5 %collective-permute-start.22 = (bf16[4,128,256]{2,1,0:T(8,128)(2,1)S(1)}, bf16[4,128,256]{2,1,0:T(8,128)(2,1)S(1)}, u32[]{:S(2)}, u32[]{:S(2)}) collective-permute-start(bf16[4,128,256]{2,1,0:T(8,128)(2,1)S(1)} %collective-permute-done.21), channel_id=1, source_target_pairs={{0,32},{8,40},{16,48},{24,56},{32,64},{40,72},{48,80},{56,88},{64,... | collective-permute-start | bytes 786440 | tf_op jit(solution)/shard_map/ppermute | solution.py:42
  132.7 9.5 %collective-permute-start.23 = (bf16[4,128,256]{2,1,0:T(8,128)(2,1)S(1)}, bf16[4,128,256]{2,1,0:T(8,128)(2,1)S(1)}, u32[]{:S(2)}, u32[]{:S(2)}) collective-permute-start(bf16[4,128,256]{2,1,0:T(8,128)(2,1)S(1)} %collective-permute-done.22), channel_id=1, source_target_pairs={{0,32},{8,40},{16,48},{24,56},{32,64},{40,72},{48,80},{56,88},{64,... | collective-permute-start | bytes 786440 | tf_op jit(solution)/shard_map/ppermute | solution.py:42
  168.3 20.3 %collective-permute-start.30 = (bf16[128,512]{1,0:T(8,128)(2,1)S(1)}, bf16[128,512]{1,0:T(8,128)(2,1)S(1)}, u32[]{:S(2)}, u32[]{:S(2)}) collective-permute-start(bf16[128,512]{1,0:T(8,128)(2,1)S(1)} %get-tuple-element.8), channel_id=1, source_target_pairs={{0,7},{1,0},{2,1},{3,2},{4,3},{5,4},{6,5},{7,6},{8,15},{9,8},{10,9... | collective-permute-start | bytes 393224 | tf_op jit(solution)/shard_map/ppermute | solution.py:86
  175.8 16.7 %collective-permute-start.29 = (bf16[128,512]{1,0:T(8,128)(2,1)S(1)}, bf16[128,512]{1,0:T(8,128)(2,1)S(1)}, u32[]{:S(2)}, u32[]{:S(2)}) collective-permute-start(bf16[128,512]{1,0:T(8,128)(2,1)S(1)} %get-tuple-element.9), channel_id=1, source_target_pairs={{0,6},{1,7},{2,0},{3,1},{4,2},{5,3},{6,4},{7,5},{8,14},{9,15},{10,... | collective-permute-start | bytes 393224 | tf_op jit(solution)/shard_map/ppermute | solution.py:86
  178.4 17.4 %collective-permute-start.28 = (bf16[128,512]{1,0:T(8,128)(2,1)S(1)}, bf16[128,512]{1,0:T(8,128)(2,1)S(1)}, u32[]{:S(2)}, u32[]{:S(2)}) collective-permute-start(bf16[128,512]{1,0:T(8,128)(2,1)S(1)} %get-tuple-element.10), channel_id=1, source_target_pairs={{0,5},{1,6},{2,7},{3,0},{4,1},{5,2},{6,3},{7,4},{8,13},{9,14},{10,... | collective-permute-start | bytes 393224 | tf_op jit(solution)/shard_map/ppermute | solution.py:86
  180.7 15.2 %collective-permute-start.27 = (bf16[128,512]{1,0:T(8,128)(2,1)S(1)}, bf16[128,512]{1,0:T(8,128)(2,1)S(1)}, u32[]{:S(2)}, u32[]{:S(2)}) collective-permute-start(bf16[128,512]{1,0:T(8,128)(2,1)S(1)} %get-tuple-element.11), channel_id=1, source_target_pairs={{0,4},{1,5},{2,6},{3,7},{4,0},{5,1},{6,2},{7,3},{8,12},{9,13},{10,... | collective-permute-start | bytes 393224 | tf_op jit(solution)/shard_map/ppermute | solution.py:86
  185.5 10.8 %collective-permute-start.26 = (bf16[128,512]{1,0:T(8,128)(2,1)S(1)}, bf16[128,512]{1,0:T(8,128)(2,1)S(1)}, u32[]{:S(2)}, u32[]{:S(2)}) collective-permute-start(bf16[128,512]{1,0:T(8,128)(2,1)S(1)} %get-tuple-element.12), channel_id=1, source_target_pairs={{0,3},{1,4},{2,5},{3,6},{4,7},{5,0},{6,1},{7,2},{8,11},{9,12},{10,... | collective-permute-start | bytes 393224 | tf_op jit(solution)/shard_map/ppermute | solution.py:86
  188.6 9.5 %collective-permute-start.25 = (bf16[128,512]{1,0:T(8,128)(2,1)S(1)}, bf16[128,512]{1,0:T(8,128)(2,1)}, u32[]{:S(2)}, u32[]{:S(2)}) collective-permute-start(bf16[128,512]{1,0:T(8,128)(2,1)S(1)} %get-tuple-element.13), channel_id=1, source_target_pairs={{0,2},{1,3},{2,4},{3,5},{4,6},{5,7},{6,0},{7,1},{8,10},{9,11},{10,... | collective-permute-start | bytes 393224 | tf_op jit(solution)/shard_map/ppermute | solution.py:86
  192.5 10.6 %collective-permute-start.24 = (bf16[128,512]{1,0:T(8,128)(2,1)S(1)}, bf16[128,512]{1,0:T(8,128)(2,1)}, u32[]{:S(2)}, u32[]{:S(2)}) collective-permute-start(bf16[128,512]{1,0:T(8,128)(2,1)S(1)} %get-tuple-element.7), channel_id=1, source_target_pairs={{0,1},{1,2},{2,3},{3,4},{4,5},{5,6},{6,7},{7,0},{8,9},{9,10},{10,1... | collective-permute-start | bytes 393224 | tf_op jit(solution)/shard_map/ppermute | solution.py:86
  (10 other events, 202.1 us)

commit v2 on v1

v2 whole, which is shorter than its diff:
```python
import math

import jax
import jax.numpy as jnp
from jax import lax
from jax.experimental import pallas as pl
from jax.experimental.pallas import tpu as pltpu
from jax.sharding import PartitionSpec as P

HEAD_DIM = 128
MAX_DOC = 4224
PLANE = 4
DOC_ROWS = 8
neg_large = -1e30


def attend_kernel(query_ref, block_ref, key_pos_ref, key_doc_ref, query_pos_ref,
                  query_doc_ref, weight_ref, out_ref):
    rows, width = query_ref.shape
    count, _, packed = block_ref.shape
    head_dim = packed // 2
    heads = width // head_dim
    tokens = count * rows
    key_part = block_ref[:, :rows, :head_dim].reshape(tokens, head_dim)
    value_part = block_ref[:, :rows, head_dim:].reshape(tokens, head_dim)
    key_pos = key_pos_ref[...]
    query_pos = query_pos_ref[...]
    allowed = (
        (key_pos <= query_pos) & (key_pos >= 0) & (key_doc_ref[...] == query_doc_ref[...])
    )
    scale = 1.0 / math.sqrt(head_dim)
    outputs = []
    for head in range(heads):
        query = query_ref[:, head * head_dim:(head + 1) * head_dim]
        scores = lax.dot_general(
            query, key_part, (((1,), (1,)), ((), ())), preferred_element_type=jnp.float32
        )
        scores = scores * scale
        peak = jnp.max(jnp.where(allowed, scores, neg_large), axis=1, keepdims=True)
        weight = jnp.where(allowed, jnp.exp(scores - peak), 0.0)
        total = jnp.sum(weight, axis=1, keepdims=True)
        summed = jnp.dot(
            weight.astype(jnp.bfloat16), value_part, preferred_element_type=jnp.float32
        )
        outputs.append((summed / total).astype(jnp.bfloat16))
    attention = jnp.concatenate(outputs, axis=1)
    partial_terms = jnp.dot(attention, weight_ref[...], preferred_element_type=jnp.float32)
    pieces, _, piece_width = out_ref.shape
    for piece in range(pieces):
        out_ref[piece] = partial_terms[:, piece * piece_width:(piece + 1) * piece_width].astype(
            out_ref.dtype
        )


def attend(query, blocks, key_pos, key_doc, query_pos, query_doc, out_weight, pieces):
    rows = query.shape[0]
    width = out_weight.shape[1]
    tokens = blocks.shape[0] * rows
    flops = 4 * rows * tokens * query.shape[1] + 2 * rows * query.shape[1] * width
    moved = blocks.size * 2 + out_weight.size * 2 + rows * width * 2
    vmem = pl.BlockSpec(memory_space=pltpu.VMEM)
    return pl.pallas_call(
        attend_kernel,
        out_shape=jax.ShapeDtypeStruct((pieces, rows, width // pieces), jnp.bfloat16),
        in_specs=[vmem] * 7,
        out_specs=vmem,
        cost_estimate=pl.CostEstimate(
            flops=flops, transcendentals=rows * tokens * query.shape[1] // HEAD_DIM,
            bytes_accessed=moved,
        ),
    )(query, blocks, key_pos, key_doc, query_pos, query_doc, out_weight)


def shards(queries, keys, values, docs, out_weight):
    rows = queries.shape[0]
    head_dim = HEAD_DIM
    ctx = lax.psum(1, "ctx")
    tp = lax.psum(1, "tp")
    my_index = lax.axis_index("ctx")
    my_tp = lax.axis_index("tp")
    plane = my_index // PLANE
    slot = my_index % PLANE

    shards_back = -(-(MAX_DOC - 1) // rows)
    hops = min(-(-(shards_back + PLANE - 1) // PLANE), ctx // PLANE - 1)

    doc_rows = jnp.zeros((DOC_ROWS, 2 * head_dim), jnp.bfloat16)
    doc_rows = doc_rows.at[0, :rows].set(docs.astype(jnp.bfloat16))
    block = jnp.concatenate([jnp.concatenate([keys, values], axis=1), doc_rows], axis=0)

    partner = lax.ppermute(block, "ctx", [(s, s ^ 2) for s in range(ctx)])
    pair = jnp.stack([block, partner])
    forward = [(s, s + PLANE) for s in range(ctx - PLANE)]
    collected = [pair]
    for hop in range(hops):
        pair = lax.ppermute(pair, "ctx", forward)
        collected.append(pair)
    mine = jnp.stack(collected)
    sibling = lax.ppermute(mine, "ctx", [(s, s ^ 1) for s in range(ctx)])
    blocks = jnp.stack([mine, sibling])
    count = blocks.shape[0] * blocks.shape[1] * blocks.shape[2]

    sib_ids = jnp.arange(2, dtype=jnp.int32)[:, None, None, None]
    hop_ids = jnp.arange(hops + 1, dtype=jnp.int32)[None, :, None, None]
    pair_ids = jnp.arange(2, dtype=jnp.int32)[None, None, :, None]
    tokens = jnp.arange(rows, dtype=jnp.int32)[None, None, None, :]
    key_shard = PLANE * (plane - hop_ids) + (slot ^ sib_ids ^ (2 * pair_ids))
    key_pos = (key_shard * rows + tokens).reshape(1, count * rows)
    blocks = blocks.reshape(count, rows + DOC_ROWS, 2 * head_dim)
    key_doc = blocks[:, rows, :rows].astype(jnp.int32).reshape(1, count * rows)

    query_pos = (my_index * rows + jnp.arange(rows, dtype=jnp.int32)).reshape(rows, 1)
    query_doc = docs.reshape(rows, 1)
    chunks = attend(queries, blocks, key_pos, key_doc, query_pos, query_doc, out_weight, tp)

    width = chunks.shape[-1]
    lanes = 2
    ring = tp // lanes
    my_lane = my_tp % lanes
    my_ring = my_tp // lanes
    chunks = chunks.reshape(ring, lanes, rows, width)
    keep = lax.dynamic_index_in_dim(chunks, my_lane, 1, keepdims=False)
    give = lax.dynamic_index_in_dim(chunks, 1 - my_lane, 1, keepdims=False)
    got = lax.ppermute(give, "tp", [(t, t ^ 1) for t in range(tp)])
    stage = keep.astype(jnp.float32) + got.astype(jnp.float32)
    mixed = lax.dynamic_index_in_dim(stage, my_ring, 0, keepdims=False)
    sent = stage.astype(jnp.bfloat16)
    for shift in range(1, ring):
        piece = lax.dynamic_index_in_dim(sent, (my_ring + shift) % ring, 0, keepdims=False)
        perm = [(t, (t + lanes * shift) % tp) for t in range(tp)]
        mixed = mixed + lax.ppermute(piece, "tp", perm).astype(jnp.float32)
    return mixed.astype(jnp.bfloat16)


def solution(mesh):
    placed = (P("ctx", "tp"), P("ctx", "tp"), P("ctx", "tp"), P("ctx"), P("tp", None))
    return jax.shard_map(
        shards, mesh=mesh, in_specs=placed, out_specs=P("ctx", "tp"), check_vma=False
    )
```

time: 206 us -> 141 us (0.68)
  the two profiles are of different devices: /device:TPU:128 before, /device:TPU:258 now
where the time goes in v2:
time: 141 us; the launch traced here: 140 us
  waiting for transfers between devices  80.7 us (57%)
  starting transfers between devices  37 us (26%)
  Pallas kernels  11.6 us (8%)
  other arithmetic  6.55 us (5%)
  local copies, waits for them, and re-layouts  4.04 us (3%)
    ppermute x9, waiting for transfers between devices, shards(): pair = lax.ppermute(pair, 'ctx', forward)  57.1 us
    ppermute x9, starting transfers between devices, shards(): pair = lax.ppermute(pair, 'ctx', forward)  18.2 us
    ppermute x1, waiting for transfers between devices, shards(): got = lax.ppermute(give, 'tp', [(t, t ^ 1) for t in range(tp)])  13.2 us
    pallas_call x1, Pallas kernels, attend(): pl.pallas_call(attend_kernel, out_shape=jax.ShapeDtypeStruct((pieces, row...  11.6 us
    ppermute x3, starting transfers between devices, shards(): mixed = mixed + lax.ppermute(piece, 'tp', perm).astype(jnp.float32)  10.3 us
    ppermute x3, waiting for transfers between devices, shards(): mixed = mixed + lax.ppermute(piece, 'tp', perm).astype(jnp.float32)  5.75 us
    ppermute x1, starting transfers between devices, shards(): got = lax.ppermute(give, 'tp', [(t, t ^ 1) for t in range(tp)])  4.05 us
    ppermute x1, waiting for transfers between devices, shards(): partner = lax.ppermute(block, 'ctx', [(s, s ^ 2) for s in range(ctx)])  3.75 us
  transfers between devices with their start and end apart: 15, of which 14 were waited for; matrix products, arithmetic and copies ran while one was open for 2% of the time, Pallas kernels for 0%

profile of v2, /device:TPU:258, one launch (start us, length us, event | category | flops | bytes accessed | tf_op | source)
XLA Modules:
  0.0 140.2 jit_solution(7514575519309126554)
XLA Ops:
  1.4 2.4 %collective-permute-start = (bf16[136,256]{1,0:T(8,128)(2,1)S(1)}, bf16[136,256]{1,0:T(8,128)(2,1)S(1)}, u32[]{:S(2)}, u32[]{:S(2)}) collective-permute-start(bf16[136,256]{1,0:T(8,128)(2,1)S(1)} %get-tuple-element.23), channel_id=1, source_target_pairs={{0,16},{8,24},{16,0},{24,8},{32,48},{40,56},{48,32},{56,40},{64,80... | collective-permute-start | bytes 208904 | tf_op jit(solution)/shard_map/ppermute | solution.py:91
  3.9 3.8 %collective-permute-done = bf16[136,256]{1,0:T(8,128)(2,1)S(1)} collective-permute-done((bf16[136,256]{1,0:T(8,128)(2,1)S(1)}, bf16[136,256]{1,0:T(8,128)(2,1)S(1)}, u32[]{:S(2)}, u32[]{:S(2)}) %collective-permute-start) | collective-permute-done | bytes 69664 | tf_op jit(solution)/shard_map/ppermute | solution.py:91
  7.7 2.9 %collective-permute-start.1 = (bf16[2,136,256]{2,1,0:T(8,128)(2,1)S(1)}, bf16[2,136,256]{2,1,0:T(8,128)(2,1)S(1)}, u32[]{:S(2)}, u32[]{:S(2)}) collective-permute-start(bf16[2,136,256]{2,1,0:T(8,128)(2,1)S(1)} %pad_maximum_fusion.1), channel_id=1, source_target_pairs={{0,32},{8,40},{16,48},{24,56},{32,64},{40,72},{48,80},{56,88},{64,... | collective-permute-start | bytes 417800 | tf_op jit(solution)/shard_map/ppermute | solution.py:96
  10.6 5.2 %collective-permute-done.1 = bf16[2,136,256]{2,1,0:T(8,128)(2,1)S(1)} collective-permute-done((bf16[2,136,256]{2,1,0:T(8,128)(2,1)S(1)}, bf16[2,136,256]{2,1,0:T(8,128)(2,1)S(1)}, u32[]{:S(2)}, u32[]{:S(2)}) %collective-permute-start.1) | collective-permute-done | bytes 139296 | tf_op jit(solution)/shard_map/ppermute | solution.py:96
  15.8 1.9 %collective-permute-start.2 = (bf16[2,136,256]{2,1,0:T(8,128)(2,1)S(1)}, bf16[2,136,256]{2,1,0:T(8,128)(2,1)S(1)}, u32[]{:S(2)}, u32[]{:S(2)}) collective-permute-start(bf16[2,136,256]{2,1,0:T(8,128)(2,1)S(1)} %collective-permute-done.1), channel_id=1, source_target_pairs={{0,32},{8,40},{16,48},{24,56},{32,64},{40,72},{48,80},{56,88},{64,... | collective-permute-start | bytes 417800 | tf_op jit(solution)/shard_map/ppermute | solution.py:96
  17.8 6.2 %collective-permute-done.2 = bf16[2,136,256]{2,1,0:T(8,128)(2,1)S(1)} collective-permute-done((bf16[2,136,256]{2,1,0:T(8,128)(2,1)S(1)}, bf16[2,136,256]{2,1,0:T(8,128)(2,1)S(1)}, u32[]{:S(2)}, u32[]{:S(2)}) %collective-permute-start.2) | collective-permute-done | bytes 139296 | tf_op jit(solution)/shard_map/ppermute | solution.py:96
  24.0 1.9 %collective-permute-start.3 = (bf16[2,136,256]{2,1,0:T(8,128)(2,1)S(1)}, bf16[2,136,256]{2,1,0:T(8,128)(2,1)S(1)}, u32[]{:S(2)}, u32[]{:S(2)}) collective-permute-start(bf16[2,136,256]{2,1,0:T(8,128)(2,1)S(1)} %collective-permute-done.2), channel_id=1, source_target_pairs={{0,32},{8,40},{16,48},{24,56},{32,64},{40,72},{48,80},{56,88},{64,... | collective-permute-start | bytes 417800 | tf_op jit(solution)/shard_map/ppermute | solution.py:96
  25.9 6.2 %collective-permute-done.3 = bf16[2,136,256]{2,1,0:T(8,128)(2,1)S(1)} collective-permute-done((bf16[2,136,256]{2,1,0:T(8,128)(2,1)S(1)}, bf16[2,136,256]{2,1,0:T(8,128)(2,1)S(1)}, u32[]{:S(2)}, u32[]{:S(2)}) %collective-permute-start.3) | collective-permute-done | bytes 139296 | tf_op jit(solution)/shard_map/ppermute | solution.py:96
  34.1 6.4 %collective-permute-done.4 = bf16[2,136,256]{2,1,0:T(8,128)(2,1)S(1)} collective-permute-done((bf16[2,136,256]{2,1,0:T(8,128)(2,1)S(1)}, bf16[2,136,256]{2,1,0:T(8,128)(2,1)S(1)}, u32[]{:S(2)}, u32[]{:S(2)}) %collective-permute-start.4) | collective-permute-done | bytes 139296 | tf_op jit(solution)/shard_map/ppermute | solution.py:96
  42.4 7.6 %collective-permute-done.5 = bf16[2,136,256]{2,1,0:T(8,128)(2,1)S(1)} collective-permute-done((bf16[2,136,256]{2,1,0:T(8,128)(2,1)S(1)}, bf16[2,136,256]{2,1,0:T(8,128)(2,1)S(1)}, u32[]{:S(2)}, u32[]{:S(2)}) %collective-permute-start.5) | collective-permute-done | bytes 139296 | tf_op jit(solution)/shard_map/ppermute | solution.py:96
  51.9 6.8 %collective-permute-done.6 = bf16[2,136,256]{2,1,0:T(8,128)(2,1)S(1)} collective-permute-done((bf16[2,136,256]{2,1,0:T(8,128)(2,1)S(1)}, bf16[2,136,256]{2,1,0:T(8,128)(2,1)S(1)}, u32[]{:S(2)}, u32[]{:S(2)}) %collective-permute-start.6) | collective-permute-done | bytes 139296 | tf_op jit(solution)/shard_map/ppermute | solution.py:96
  60.7 6.2 %collective-permute-done.7 = bf16[2,136,256]{2,1,0:T(8,128)(2,1)S(1)} collective-permute-done((bf16[2,136,256]{2,1,0:T(8,128)(2,1)S(1)}, bf16[2,136,256]{2,1,0:T(8,128)(2,1)S(1)}, u32[]{:S(2)}, u32[]{:S(2)}) %collective-permute-start.7) | collective-permute-done | bytes 139296 | tf_op jit(solution)/shard_map/ppermute | solution.py:96
  66.9 1.9 %collective-permute-start.8 = (bf16[2,136,256]{2,1,0:T(8,128)(2,1)S(1)}, bf16[2,136,256]{2,1,0:T(8,128)(2,1)S(1)}, u32[]{:S(2)}, u32[]{:S(2)}) collective-permute-start(bf16[2,136,256]{2,1,0:T(8,128)(2,1)S(1)} %collective-permute-done.7), channel_id=1, source_target_pairs={{0,32},{8,40},{16,48},{24,56},{32,64},{40,72},{48,80},{56,88},{64,... | collective-permute-start | bytes 417800 | tf_op jit(solution)/shard_map/ppermute | solution.py:96
  68.8 6.2 %collective-permute-done.8 = bf16[2,136,256]{2,1,0:T(8,128)(2,1)S(1)} collective-permute-done((bf16[2,136,256]{2,1,0:T(8,128)(2,1)S(1)}, bf16[2,136,256]{2,1,0:T(8,128)(2,1)S(1)}, u32[]{:S(2)}, u32[]{:S(2)}) %collective-permute-start.8) | collective-permute-done | bytes 139296 | tf_op jit(solution)/shard_map/ppermute | solution.py:96
  77.0 6.2 %collective-permute-done.9 = bf16[2,136,256]{2,1,0:T(8,128)(2,1)S(1)} collective-permute-done((bf16[2,136,256]{2,1,0:T(8,128)(2,1)S(1)}, bf16[2,136,256]{2,1,0:T(8,128)(2,1)S(1)}, u32[]{:S(2)}, u32[]{:S(2)}) %collective-permute-start.9) | collective-permute-done | bytes 139296 | tf_op jit(solution)/shard_map/ppermute | solution.py:96
  83.2 1.9 %collective-permute-start.10 = (bf16[10,2,136,256]{3,2,1,0:T(8,128)(2,1)S(1)}, bf16[10,2,136,256]{3,2,1,0:T(8,128)(2,1)S(1)}, u32[]{:S(2)}, u32[]{:S(2)}) collective-permute-start(bf16[10,2,136,256]{3,2,1,0:T(8,128)(2,1)S(1)} %bitcast_dynamic-update-slice_fusion), channel_id=1, source_target_pairs={{0,8},{8,0},{16,24},{24,16},{32,40},{40,32},{48,56},{56,48},{64,72... | collective-permute-start | bytes 4177928 | tf_op jit(solution)/shard_map/ppermute | solution.py:99
  89.4 2.0 %pad_maximum_fusion = bf16[2,10,2,136,256]{4,3,2,1,0:T(8,128)(2,1)S(1)} fusion(bf16[1,10,2,136,256]{4,3,2,1,0:T(8,128)(2,1)} %bitcast.61, bf16[1,10,2,136,256]{4,3,2,1,0:T(8,128)(2,1)} %bitcast.60), kind=kLoop, calls=%fused_computation | loop fusion | flops 1392640 | bytes 5570560 | tf_op jit(solution)/shard_map/stack | solution.py:100
  92.9 11.6 %shard_map.55 = bf16[8,128,512]{2,1,0:T(8,128)(2,1)} custom-call(bf16[128,512]{1,0:T(8,128)(2,1)} %query_ref.1, bf16[40,136,256]{2,1,0:T(8,128)(2,1)} %bitcast.57, s32[1,5120]{1,0:T(1,128)} %bitcast.64, s32[1,5120]{1,0:T(1,128)} %fusion.5.key_doc_ref, s32[128,1]{1,0:T(8,128)} %iota_add_fusion.query_pos_ref, s32[128,1]{1,0:T(8,128)} %copy.6.query_doc_ref, ...), custom_call_target="tpu_custom_call" | custom-call | flops 1879048192 | bytes 8028160 | tf_op jit(solution)/shard_map/pallas_call | solution.py:62
  105.7 4.1 %collective-permute-start.11 = (bf16[4,128,512]{2,1,0:T(8,128)(2,1)S(1)}, bf16[4,128,512]{2,1,0:T(8,128)(2,1)S(1)}, u32[]{:S(2)}, u32[]{:S(2)}) collective-permute-start(bf16[4,128,512]{2,1,0:T(8,128)(2,1)S(1)} %dynamic-slice_bitcast_fusion), channel_id=1, source_target_pairs={{0,1},{1,0},{2,3},{3,2},{4,5},{5,4},{6,7},{7,6},{8,9},{9,8},{10,11... | collective-permute-start | bytes 1572872 | tf_op jit(solution)/shard_map/ppermute | solution.py:124
  109.8 13.2 %collective-permute-done.11 = bf16[4,128,512]{2,1,0:T(8,128)(2,1)S(1)} collective-permute-done((bf16[4,128,512]{2,1,0:T(8,128)(2,1)S(1)}, bf16[4,128,512]{2,1,0:T(8,128)(2,1)S(1)}, u32[]{:S(2)}, u32[]{:S(2)}) %collective-permute-start.11) | collective-permute-done | bytes 524320 | tf_op jit(solution)/shard_map/ppermute | solution.py:124
  123.3 4.9 %collective-permute-start.14 = (bf16[128,512]{1,0:T(8,128)(2,1)S(1)}, bf16[128,512]{1,0:T(8,128)(2,1)S(1)}, u32[]{:S(2)}, u32[]{:S(2)}) collective-permute-start(bf16[128,512]{1,0:T(8,128)(2,1)S(1)} %get-tuple-element.20), channel_id=1, source_target_pairs={{0,6},{1,7},{2,0},{3,1},{4,2},{5,3},{6,4},{7,5},{8,14},{9,15},{10,... | collective-permute-start | bytes 393224 | tf_op jit(solution)/shard_map/ppermute | solution.py:131
  128.2 2.5 %collective-permute-start.13 = (bf16[128,512]{1,0:T(8,128)(2,1)S(1)}, bf16[128,512]{1,0:T(8,128)(2,1)S(1)}, u32[]{:S(2)}, u32[]{:S(2)}) collective-permute-start(bf16[128,512]{1,0:T(8,128)(2,1)S(1)} %get-tuple-element.21), channel_id=1, source_target_pairs={{0,4},{1,5},{2,6},{3,7},{4,0},{5,1},{6,2},{7,3},{8,12},{9,13},{10,... | collective-permute-start | bytes 393224 | tf_op jit(solution)/shard_map/ppermute | solution.py:131
  130.8 2.9 %collective-permute-start.12 = (bf16[128,512]{1,0:T(8,128)(2,1)S(1)}, bf16[128,512]{1,0:T(8,128)(2,1)S(1)}, u32[]{:S(2)}, u32[]{:S(2)}) collective-permute-start(bf16[128,512]{1,0:T(8,128)(2,1)S(1)} %get-tuple-element.19), channel_id=1, source_target_pairs={{0,2},{1,3},{2,4},{3,5},{4,6},{5,7},{6,0},{7,1},{8,10},{9,11},{10,... | collective-permute-start | bytes 393224 | tf_op jit(solution)/shard_map/ppermute | solution.py:131
  133.7 4.4 %collective-permute-done.13 = bf16[128,512]{1,0:T(8,128)(2,1)S(1)} collective-permute-done((bf16[128,512]{1,0:T(8,128)(2,1)S(1)}, bf16[128,512]{1,0:T(8,128)(2,1)S(1)}, u32[]{:S(2)}, u32[]{:S(2)}) %collective-permute-start.13) | collective-permute-done | bytes 131104 | tf_op jit(solution)/shard_map/ppermute | solution.py:131
  (43 shorter events, 20.3 us)
Async XLA Ops:
  1.4 6.2 %collective-permute-start = (bf16[136,256]{1,0:T(8,128)(2,1)S(1)}, bf16[136,256]{1,0:T(8,128)(2,1)S(1)}, u32[]{:S(2)}, u32[]{:S(2)}) collective-permute-start(bf16[136,256]{1,0:T(8,128)(2,1)S(1)} %get-tuple-element.23), channel_id=1, source_target_pairs={{0,16},{8,24},{16,0},{24,8},{32,48},{40,56},{48,32},{56,40},{64,80... | collective-permute-start | bytes 208904 | tf_op jit(solution)/shard_map/ppermute | solution.py:91
  7.7 77.5 %copy-start.4 = (s32[128]{0:T(128)S(1)}, s32[128]{0:T(128)}, u32[]{:S(2)}) copy-start(s32[128]{0:T(128)} %param.10) | copy-start | bytes 1540
  7.7 8.2 %collective-permute-start.1 = (bf16[2,136,256]{2,1,0:T(8,128)(2,1)S(1)}, bf16[2,136,256]{2,1,0:T(8,128)(2,1)S(1)}, u32[]{:S(2)}, u32[]{:S(2)}) collective-permute-start(bf16[2,136,256]{2,1,0:T(8,128)(2,1)S(1)} %pad_maximum_fusion.1), channel_id=1, source_target_pairs={{0,32},{8,40},{16,48},{24,56},{32,64},{40,72},{48,80},{56,88},{64,... | collective-permute-start | bytes 417800 | tf_op jit(solution)/shard_map/ppermute | solution.py:96
  15.8 8.1 %collective-permute-start.2 = (bf16[2,136,256]{2,1,0:T(8,128)(2,1)S(1)}, bf16[2,136,256]{2,1,0:T(8,128)(2,1)S(1)}, u32[]{:S(2)}, u32[]{:S(2)}) collective-permute-start(bf16[2,136,256]{2,1,0:T(8,128)(2,1)S(1)} %collective-permute-done.1), channel_id=1, source_target_pairs={{0,32},{8,40},{16,48},{24,56},{32,64},{40,72},{48,80},{56,88},{64,... | collective-permute-start | bytes 417800 | tf_op jit(solution)/shard_map/ppermute | solution.py:96
  24.0 8.1 %collective-permute-start.3 = (bf16[2,136,256]{2,1,0:T(8,128)(2,1)S(1)}, bf16[2,136,256]{2,1,0:T(8,128)(2,1)S(1)}, u32[]{:S(2)}, u32[]{:S(2)}) collective-permute-start(bf16[2,136,256]{2,1,0:T(8,128)(2,1)S(1)} %collective-permute-done.2), channel_id=1, source_target_pairs={{0,32},{8,40},{16,48},{24,56},{32,64},{40,72},{48,80},{56,88},{64,... | collective-permute-start | bytes 417800 | tf_op jit(solution)/shard_map/ppermute | solution.py:96
  32.1 8.3 %collective-permute-start.4 = (bf16[2,136,256]{2,1,0:T(8,128)(2,1)S(1)}, bf16[2,136,256]{2,1,0:T(8,128)(2,1)S(1)}, u32[]{:S(2)}, u32[]{:S(2)}) collective-permute-start(bf16[2,136,256]{2,1,0:T(8,128)(2,1)S(1)} %collective-permute-done.3), channel_id=1, source_target_pairs={{0,32},{8,40},{16,48},{24,56},{32,64},{40,72},{48,80},{56,88},{64,... | collective-permute-start | bytes 417800 | tf_op jit(solution)/shard_map/ppermute | solution.py:96
  40.5 9.5 %collective-permute-start.5 = (bf16[2,136,256]{2,1,0:T(8,128)(2,1)S(1)}, bf16[2,136,256]{2,1,0:T(8,128)(2,1)S(1)}, u32[]{:S(2)}, u32[]{:S(2)}) collective-permute-start(bf16[2,136,256]{2,1,0:T(8,128)(2,1)S(1)} %collective-permute-done.4), channel_id=1, source_target_pairs={{0,32},{8,40},{16,48},{24,56},{32,64},{40,72},{48,80},{56,88},{64,... | collective-permute-start | bytes 417800 | tf_op jit(solution)/shard_map/ppermute | solution.py:96
  50.0 8.8 %collective-permute-start.6 = (bf16[2,136,256]{2,1,0:T(8,128)(2,1)S(1)}, bf16[2,136,256]{2,1,0:T(8,128)(2,1)S(1)}, u32[]{:S(2)}, u32[]{:S(2)}) collective-permute-start(bf16[2,136,256]{2,1,0:T(8,128)(2,1)S(1)} %collective-permute-done.5), channel_id=1, source_target_pairs={{0,32},{8,40},{16,48},{24,56},{32,64},{40,72},{48,80},{56,88},{64,... | collective-permute-start | bytes 417800 | tf_op jit(solution)/shard_map/ppermute | solution.py:96
  58.8 8.1 %collective-permute-start.7 = (bf16[2,136,256]{2,1,0:T(8,128)(2,1)S(1)}, bf16[2,136,256]{2,1,0:T(8,128)(2,1)S(1)}, u32[]{:S(2)}, u32[]{:S(2)}) collective-permute-start(bf16[2,136,256]{2,1,0:T(8,128)(2,1)S(1)} %collective-permute-done.6), channel_id=1, source_target_pairs={{0,32},{8,40},{16,48},{24,56},{32,64},{40,72},{48,80},{56,88},{64,... | collective-permute-start | bytes 417800 | tf_op jit(solution)/shard_map/ppermute | solution.py:96
  66.9 8.1 %collective-permute-start.8 = (bf16[2,136,256]{2,1,0:T(8,128)(2,1)S(1)}, bf16[2,136,256]{2,1,0:T(8,128)(2,1)S(1)}, u32[]{:S(2)}, u32[]{:S(2)}) collective-permute-start(bf16[2,136,256]{2,1,0:T(8,128)(2,1)S(1)} %collective-permute-done.7), channel_id=1, source_target_pairs={{0,32},{8,40},{16,48},{24,56},{32,64},{40,72},{48,80},{56,88},{64,... | collective-permute-start | bytes 417800 | tf_op jit(solution)/shard_map/ppermute | solution.py:96
  75.1 8.1 %collective-permute-start.9 = (bf16[2,136,256]{2,1,0:T(8,128)(2,1)S(1)}, bf16[2,136,256]{2,1,0:T(8,128)(2,1)S(1)}, u32[]{:S(2)}, u32[]{:S(2)}) collective-permute-start(bf16[2,136,256]{2,1,0:T(8,128)(2,1)S(1)} %collective-permute-done.8), channel_id=1, source_target_pairs={{0,32},{8,40},{16,48},{24,56},{32,64},{40,72},{48,80},{56,88},{64,... | collective-permute-start | bytes 417800 | tf_op jit(solution)/shard_map/ppermute | solution.py:96
  83.2 5.1 %copy-start.2 = (bf16[10,2,136,256]{3,2,1,0:T(8,128)(2,1)}, bf16[10,2,136,256]{3,2,1,0:T(8,128)(2,1)S(1)}, u32[]{:S(2)}) copy-start(bf16[10,2,136,256]{3,2,1,0:T(8,128)(2,1)S(1)} %bitcast_dynamic-update-slice_fusion) | copy-start | bytes 4177924
  83.2 5.0 %collective-permute-start.10 = (bf16[10,2,136,256]{3,2,1,0:T(8,128)(2,1)S(1)}, bf16[10,2,136,256]{3,2,1,0:T(8,128)(2,1)S(1)}, u32[]{:S(2)}, u32[]{:S(2)}) collective-permute-start(bf16[10,2,136,256]{3,2,1,0:T(8,128)(2,1)S(1)} %bitcast_dynamic-update-slice_fusion), channel_id=1, source_target_pairs={{0,8},{8,0},{16,24},{24,16},{32,40},{40,32},{48,56},{56,48},{64,72... | collective-permute-start | bytes 4177928 | tf_op jit(solution)/shard_map/ppermute | solution.py:99
  88.3 1.1 copy-start.3
  91.4 1.6 %copy-start = (bf16[2,10,2,136,256]{4,3,2,1,0:T(8,128)(2,1)}, bf16[2,10,2,136,256]{4,3,2,1,0:T(8,128)(2,1)S(1)}, u32[]{:S(2)}) copy-start(bf16[2,10,2,136,256]{4,3,2,1,0:T(8,128)(2,1)S(1)} %pad_maximum_fusion) | copy-start | bytes 8355844
  104.5 18.6 %copy-start.1 = (bf16[8,128,512]{2,1,0:T(8,128)(2,1)S(1)}, bf16[8,128,512]{2,1,0:T(8,128)(2,1)}, u32[]{:S(2)}) copy-start(bf16[8,128,512]{2,1,0:T(8,128)(2,1)} %shard_map.55) | copy-start | bytes 3145732
  105.7 17.4 %collective-permute-start.11 = (bf16[4,128,512]{2,1,0:T(8,128)(2,1)S(1)}, bf16[4,128,512]{2,1,0:T(8,128)(2,1)S(1)}, u32[]{:S(2)}, u32[]{:S(2)}) collective-permute-start(bf16[4,128,512]{2,1,0:T(8,128)(2,1)S(1)} %dynamic-slice_bitcast_fusion), channel_id=1, source_target_pairs={{0,1},{1,0},{2,3},{3,2},{4,5},{5,4},{6,7},{7,6},{8,9},{9,8},{10,11... | collective-permute-start | bytes 1572872 | tf_op jit(solution)/shard_map/ppermute | solution.py:124
  123.3 10.4 %collective-permute-start.14 = (bf16[128,512]{1,0:T(8,128)(2,1)S(1)}, bf16[128,512]{1,0:T(8,128)(2,1)S(1)}, u32[]{:S(2)}, u32[]{:S(2)}) collective-permute-start(bf16[128,512]{1,0:T(8,128)(2,1)S(1)} %get-tuple-element.20), channel_id=1, source_target_pairs={{0,6},{1,7},{2,0},{3,1},{4,2},{5,3},{6,4},{7,5},{8,14},{9,15},{10,... | collective-permute-start | bytes 393224 | tf_op jit(solution)/shard_map/ppermute | solution.py:131
  128.2 9.9 %collective-permute-start.13 = (bf16[128,512]{1,0:T(8,128)(2,1)S(1)}, bf16[128,512]{1,0:T(8,128)(2,1)S(1)}, u32[]{:S(2)}, u32[]{:S(2)}) collective-permute-start(bf16[128,512]{1,0:T(8,128)(2,1)S(1)} %get-tuple-element.21), channel_id=1, source_target_pairs={{0,4},{1,5},{2,6},{3,7},{4,0},{5,1},{6,2},{7,3},{8,12},{9,13},{10,... | collective-permute-start | bytes 393224 | tf_op jit(solution)/shard_map/ppermute | solution.py:131
  130.8 8.7 %collective-permute-start.12 = (bf16[128,512]{1,0:T(8,128)(2,1)S(1)}, bf16[128,512]{1,0:T(8,128)(2,1)S(1)}, u32[]{:S(2)}, u32[]{:S(2)}) collective-permute-start(bf16[128,512]{1,0:T(8,128)(2,1)S(1)} %get-tuple-element.19), channel_id=1, source_target_pairs={{0,2},{1,3},{2,4},{3,5},{4,6},{5,7},{6,0},{7,1},{8,10},{9,11},{10,... | collective-permute-start | bytes 393224 | tf_op jit(solution)/shard_map/ppermute | solution.py:131

commit v3 on v2

v3 whole, which is shorter than its diff:
```python
import math

import jax
import jax.numpy as jnp
from jax import lax
from jax.experimental import pallas as pl
from jax.experimental.pallas import tpu as pltpu
from jax.sharding import PartitionSpec as P

HEAD_DIM = 128
MAX_DOC = 4224
PLANE = 4
DOC_ROWS = 8
neg_large = -1e30


def attend_kernel(*refs):
    query_ref = refs[0]
    block_refs = refs[1:-6]
    key_pos_ref, key_doc_ref, query_pos_ref, query_doc_ref, weight_ref, out_ref = refs[-6:]
    rows, width = query_ref.shape
    head_dim = block_refs[0].shape[-1] // 2
    heads = width // head_dim
    key_part = jnp.concatenate(
        [ref[:, :rows, :head_dim].reshape(ref.shape[0] * rows, head_dim) for ref in block_refs],
        axis=0,
    )
    value_part = jnp.concatenate(
        [ref[:, :rows, head_dim:].reshape(ref.shape[0] * rows, head_dim) for ref in block_refs],
        axis=0,
    )
    key_pos = key_pos_ref[...]
    query_pos = query_pos_ref[...]
    allowed = (
        (key_pos <= query_pos) & (key_pos >= 0) & (key_doc_ref[...] == query_doc_ref[...])
    )
    bias = jnp.where(allowed, 0.0, neg_large)
    scale = 1.0 / math.sqrt(head_dim)
    outputs = []
    for head in range(heads):
        query = query_ref[:, head * head_dim:(head + 1) * head_dim]
        scores = lax.dot_general(
            query, key_part, (((1,), (1,)), ((), ())), preferred_element_type=jnp.float32
        )
        scores = scores * scale + bias
        peak = jnp.max(scores, axis=1, keepdims=True)
        weight = jnp.exp(scores - peak)
        total = jnp.sum(weight, axis=1, keepdims=True)
        summed = jnp.dot(
            weight.astype(jnp.bfloat16), value_part, preferred_element_type=jnp.float32
        )
        outputs.append((summed / total).astype(jnp.bfloat16))
    attention = jnp.concatenate(outputs, axis=1)
    partial_terms = jnp.dot(attention, weight_ref[...], preferred_element_type=jnp.float32)
    pieces, _, piece_width = out_ref.shape
    for piece in range(pieces):
        out_ref[piece] = partial_terms[:, piece * piece_width:(piece + 1) * piece_width].astype(
            out_ref.dtype
        )


def attend(query, blocks, key_pos, key_doc, query_pos, query_doc, out_weight, pieces):
    rows = query.shape[0]
    width = out_weight.shape[1]
    tokens = key_pos.shape[1]
    flops = 4 * rows * tokens * query.shape[1] + 2 * rows * query.shape[1] * width
    moved = sum(b.size for b in blocks) * 2 + out_weight.size * 2 + rows * width * 2
    vmem = pl.BlockSpec(memory_space=pltpu.VMEM)
    return pl.pallas_call(
        attend_kernel,
        out_shape=jax.ShapeDtypeStruct((pieces, rows, width // pieces), jnp.bfloat16),
        in_specs=[vmem] * (6 + len(blocks)),
        out_specs=vmem,
        cost_estimate=pl.CostEstimate(
            flops=flops, transcendentals=rows * tokens * query.shape[1] // HEAD_DIM,
            bytes_accessed=moved,
        ),
    )(query, *blocks, key_pos, key_doc, query_pos, query_doc, out_weight)


def shards(queries, keys, values, docs, out_weight):
    rows = queries.shape[0]
    head_dim = HEAD_DIM
    ctx = lax.psum(1, "ctx")
    tp = lax.psum(1, "tp")
    my_index = lax.axis_index("ctx")
    my_tp = lax.axis_index("tp")
    plane = my_index // PLANE
    slot = my_index % PLANE

    shards_back = -(-(MAX_DOC - 1) // rows)
    hops = min(-(-(shards_back + PLANE - 1) // PLANE), ctx // PLANE - 1)

    doc_rows = jnp.zeros((DOC_ROWS, 2 * head_dim), jnp.bfloat16)
    doc_rows = doc_rows.at[0, :rows].set(docs.astype(jnp.bfloat16))
    block = jnp.concatenate([jnp.concatenate([keys, values], axis=1), doc_rows], axis=0)

    partner = lax.ppermute(block, "ctx", [(s, s ^ 2) for s in range(ctx)])
    pair = jnp.stack([block, partner])
    forward = [(s, s + PLANE) for s in range(ctx - PLANE)]
    collected = [pair]
    for hop in range(hops):
        pair = lax.ppermute(pair, "ctx", forward)
        collected.append(pair)
    early = (hops + 2) // 2
    swap = [(s, s ^ 1) for s in range(ctx)]
    blocks, key_pos, key_doc = [], [], []
    tokens = jnp.arange(rows, dtype=jnp.int32)[None, None, :]
    pair_ids = jnp.arange(2, dtype=jnp.int32)[None, :, None]
    for first, last in ((0, early), (early, hops + 1)):
        mine = jnp.stack(collected[first:last])
        sibling = lax.ppermute(mine, "ctx", swap)
        hop_ids = jnp.arange(first, last, dtype=jnp.int32)[:, None, None]
        for piece, flip in ((mine, 0), (sibling, 1)):
            key_shard = PLANE * (plane - hop_ids) + (slot ^ flip ^ (2 * pair_ids))
            key_pos.append((key_shard * rows + tokens).reshape(1, -1))
            piece = piece.reshape(-1, rows + DOC_ROWS, 2 * head_dim)
            key_doc.append(piece[:, rows, :rows].astype(jnp.int32).reshape(1, -1))
            blocks.append(piece)
    key_pos = jnp.concatenate(key_pos, axis=1)
    key_doc = jnp.concatenate(key_doc, axis=1)

    query_pos = (my_index * rows + jnp.arange(rows, dtype=jnp.int32)).reshape(rows, 1)
    query_doc = docs.reshape(rows, 1)
    chunks = attend(queries, blocks, key_pos, key_doc, query_pos, query_doc, out_weight, tp)

    received = lax.all_to_all(chunks, "tp", 0, 0, tiled=True)
    mixed = jnp.sum(received.astype(jnp.float32), axis=0)
    return mixed.astype(jnp.bfloat16)


def solution(mesh):
    placed = (P("ctx", "tp"), P("ctx", "tp"), P("ctx", "tp"), P("ctx"), P("tp", None))
    return jax.shard_map(
        shards, mesh=mesh, in_specs=placed, out_specs=P("ctx", "tp"), check_vma=False
    )
```

time: 141 us -> 125 us (0.89)
  the two profiles are of different devices: /device:TPU:258 before, /device:TPU:128 now
where the time goes in v3:
time: 125 us; the launch traced here: 124 us
  waiting for transfers between devices  56.4 us (45%)
  starting transfers between devices  27 us (22%)
  blocking collectives  24.4 us (20%)
  Pallas kernels  9.79 us (8%)
  other arithmetic  4.62 us (4%)
  local copies, waits for them, and re-layouts  1.69 us (1%)
    ppermute x9, waiting for transfers between devices, shards(): pair = lax.ppermute(pair, 'ctx', forward)  52.6 us
    all_to_all x1, blocking collectives, shards(): received = lax.all_to_all(chunks, 'tp', 0, 0, tiled=True)  24.4 us
    ppermute x9, starting transfers between devices, shards(): pair = lax.ppermute(pair, 'ctx', forward)  19.8 us
    pallas_call x1, Pallas kernels, attend(): pl.pallas_call(attend_kernel, out_shape=jax.ShapeDtypeStruct((pieces, row...  9.79 us
    ppermute x2, starting transfers between devices, shards(): sibling = lax.ppermute(mine, 'ctx', swap)  3.84 us
    ppermute x1, starting transfers between devices, shards(): partner = lax.ppermute(block, 'ctx', [(s, s ^ 2) for s in range(ctx)])  3.4 us
  transfers between devices with their start and end apart: 12, of which 11 were waited for; matrix products, arithmetic and copies ran while one was open for 3% of the time, Pallas kernels for 0%

profile of v3, /device:TPU:128, one launch (start us, length us, event | category | flops | bytes accessed | tf_op | source)
XLA Modules:
  0.0 124.2 jit_solution(13478790124777667899)
XLA Ops:
  1.4 3.4 %collective-permute-start = (bf16[136,256]{1,0:T(8,128)(2,1)S(1)}, bf16[136,256]{1,0:T(8,128)(2,1)S(1)}, u32[]{:S(2)}, u32[]{:S(2)}) collective-permute-start(bf16[136,256]{1,0:T(8,128)(2,1)S(1)} %get-tuple-element.18), channel_id=1, source_target_pairs={{0,16},{8,24},{16,0},{24,8},{32,48},{40,56},{48,32},{56,40},{64,80... | collective-permute-start | bytes 208904 | tf_op jit(solution)/shard_map/ppermute | solution.py:98
  7.7 3.8 %collective-permute-start.1 = (bf16[2,136,256]{2,1,0:T(8,128)(2,1)S(1)}, bf16[2,136,256]{2,1,0:T(8,128)(2,1)S(1)}, u32[]{:S(2)}, u32[]{:S(2)}) collective-permute-start(bf16[2,136,256]{2,1,0:T(8,128)(2,1)S(1)} %pad_maximum_fusion), channel_id=1, source_target_pairs={{0,32},{8,40},{16,48},{24,56},{32,64},{40,72},{48,80},{56,88},{64,... | collective-permute-start | bytes 417800 | tf_op jit(solution)/shard_map/ppermute | solution.py:103
  13.5 2.3 %collective-permute-done.1 = bf16[2,136,256]{2,1,0:T(8,128)(2,1)S(1)} collective-permute-done((bf16[2,136,256]{2,1,0:T(8,128)(2,1)S(1)}, bf16[2,136,256]{2,1,0:T(8,128)(2,1)S(1)}, u32[]{:S(2)}, u32[]{:S(2)}) %collective-permute-start.1) | collective-permute-done | bytes 139296 | tf_op jit(solution)/shard_map/ppermute | solution.py:103
  15.8 2.6 %collective-permute-start.2 = (bf16[2,136,256]{2,1,0:T(8,128)(2,1)S(1)}, bf16[2,136,256]{2,1,0:T(8,128)(2,1)S(1)}, u32[]{:S(2)}, u32[]{:S(2)}) collective-permute-start(bf16[2,136,256]{2,1,0:T(8,128)(2,1)S(1)} %collective-permute-done.1), channel_id=1, source_target_pairs={{0,32},{8,40},{16,48},{24,56},{32,64},{40,72},{48,80},{56,88},{64,... | collective-permute-start | bytes 417800 | tf_op jit(solution)/shard_map/ppermute | solution.py:103
  18.5 5.5 %collective-permute-done.2 = bf16[2,136,256]{2,1,0:T(8,128)(2,1)S(1)} collective-permute-done((bf16[2,136,256]{2,1,0:T(8,128)(2,1)S(1)}, bf16[2,136,256]{2,1,0:T(8,128)(2,1)S(1)}, u32[]{:S(2)}, u32[]{:S(2)}) %collective-permute-start.2) | collective-permute-done | bytes 139296 | tf_op jit(solution)/shard_map/ppermute | solution.py:103
  24.0 1.9 %collective-permute-start.3 = (bf16[2,136,256]{2,1,0:T(8,128)(2,1)S(1)}, bf16[2,136,256]{2,1,0:T(8,128)(2,1)S(1)}, u32[]{:S(2)}, u32[]{:S(2)}) collective-permute-start(bf16[2,136,256]{2,1,0:T(8,128)(2,1)S(1)} %collective-permute-done.2), channel_id=1, source_target_pairs={{0,32},{8,40},{16,48},{24,56},{32,64},{40,72},{48,80},{56,88},{64,... | collective-permute-start | bytes 417800 | tf_op jit(solution)/shard_map/ppermute | solution.py:103
  25.9 6.2 %collective-permute-done.3 = bf16[2,136,256]{2,1,0:T(8,128)(2,1)S(1)} collective-permute-done((bf16[2,136,256]{2,1,0:T(8,128)(2,1)S(1)}, bf16[2,136,256]{2,1,0:T(8,128)(2,1)S(1)}, u32[]{:S(2)}, u32[]{:S(2)}) %collective-permute-start.3) | collective-permute-done | bytes 139296 | tf_op jit(solution)/shard_map/ppermute | solution.py:103
  32.1 1.9 %collective-permute-start.4 = (bf16[2,136,256]{2,1,0:T(8,128)(2,1)S(1)}, bf16[2,136,256]{2,1,0:T(8,128)(2,1)S(1)}, u32[]{:S(2)}, u32[]{:S(2)}) collective-permute-start(bf16[2,136,256]{2,1,0:T(8,128)(2,1)S(1)} %collective-permute-done.3), channel_id=1, source_target_pairs={{0,32},{8,40},{16,48},{24,56},{32,64},{40,72},{48,80},{56,88},{64,... | collective-permute-start | bytes 417800 | tf_op jit(solution)/shard_map/ppermute | solution.py:103
  34.1 6.2 %collective-permute-done.4 = bf16[2,136,256]{2,1,0:T(8,128)(2,1)S(1)} collective-permute-done((bf16[2,136,256]{2,1,0:T(8,128)(2,1)S(1)}, bf16[2,136,256]{2,1,0:T(8,128)(2,1)S(1)}, u32[]{:S(2)}, u32[]{:S(2)}) %collective-permute-start.4) | collective-permute-done | bytes 139296 | tf_op jit(solution)/shard_map/ppermute | solution.py:103
  40.3 1.9 %collective-permute-start.5 = (bf16[5,2,136,256]{3,2,1,0:T(8,128)(2,1)S(1)}, bf16[5,2,136,256]{3,2,1,0:T(8,128)(2,1)S(1)}, u32[]{:S(2)}, u32[]{:S(2)}) collective-permute-start(bf16[5,2,136,256]{3,2,1,0:T(8,128)(2,1)S(1)} %bitcast_dynamic-update-slice_fusion.5), channel_id=1, source_target_pairs={{0,8},{8,0},{16,24},{24,16},{32,40},{40,32},{48,56},{56,48},{64,72... | collective-permute-start | bytes 2088968 | tf_op jit(solution)/shard_map/ppermute | solution.py:112
  42.2 1.9 %collective-permute-start.6 = (bf16[2,136,256]{2,1,0:T(8,128)(2,1)S(1)}, bf16[2,136,256]{2,1,0:T(8,128)(2,1)S(1)}, u32[]{:S(2)}, u32[]{:S(2)}) collective-permute-start(bf16[2,136,256]{2,1,0:T(8,128)(2,1)S(1)} %collective-permute-done.4), channel_id=1, source_target_pairs={{0,32},{8,40},{16,48},{24,56},{32,64},{40,72},{48,80},{56,88},{64,... | collective-permute-start | bytes 417800 | tf_op jit(solution)/shard_map/ppermute | solution.py:103
  44.2 7.2 %collective-permute-done.6 = bf16[2,136,256]{2,1,0:T(8,128)(2,1)S(1)} collective-permute-done((bf16[2,136,256]{2,1,0:T(8,128)(2,1)S(1)}, bf16[2,136,256]{2,1,0:T(8,128)(2,1)S(1)}, u32[]{:S(2)}, u32[]{:S(2)}) %collective-permute-start.6) | collective-permute-done | bytes 139296 | tf_op jit(solution)/shard_map/ppermute | solution.py:103
  51.4 1.9 %collective-permute-start.7 = (bf16[2,136,256]{2,1,0:T(8,128)(2,1)S(1)}, bf16[2,136,256]{2,1,0:T(8,128)(2,1)S(1)}, u32[]{:S(2)}, u32[]{:S(2)}) collective-permute-start(bf16[2,136,256]{2,1,0:T(8,128)(2,1)S(1)} %collective-permute-done.6), channel_id=1, source_target_pairs={{0,32},{8,40},{16,48},{24,56},{32,64},{40,72},{48,80},{56,88},{64,... | collective-permute-start | bytes 417800 | tf_op jit(solution)/shard_map/ppermute | solution.py:103
  53.3 6.4 %collective-permute-done.7 = bf16[2,136,256]{2,1,0:T(8,128)(2,1)S(1)} collective-permute-done((bf16[2,136,256]{2,1,0:T(8,128)(2,1)S(1)}, bf16[2,136,256]{2,1,0:T(8,128)(2,1)S(1)}, u32[]{:S(2)}, u32[]{:S(2)}) %collective-permute-start.7) | collective-permute-done | bytes 139296 | tf_op jit(solution)/shard_map/ppermute | solution.py:103
  59.8 1.9 %collective-permute-start.8 = (bf16[2,136,256]{2,1,0:T(8,128)(2,1)S(1)}, bf16[2,136,256]{2,1,0:T(8,128)(2,1)S(1)}, u32[]{:S(2)}, u32[]{:S(2)}) collective-permute-start(bf16[2,136,256]{2,1,0:T(8,128)(2,1)S(1)} %collective-permute-done.7), channel_id=1, source_target_pairs={{0,32},{8,40},{16,48},{24,56},{32,64},{40,72},{48,80},{56,88},{64,... | collective-permute-start | bytes 417800 | tf_op jit(solution)/shard_map/ppermute | solution.py:103
  61.7 6.2 %collective-permute-done.8 = bf16[2,136,256]{2,1,0:T(8,128)(2,1)S(1)} collective-permute-done((bf16[2,136,256]{2,1,0:T(8,128)(2,1)S(1)}, bf16[2,136,256]{2,1,0:T(8,128)(2,1)S(1)}, u32[]{:S(2)}, u32[]{:S(2)}) %collective-permute-start.8) | collective-permute-done | bytes 139296 | tf_op jit(solution)/shard_map/ppermute | solution.py:103
  67.9 1.9 %collective-permute-start.9 = (bf16[2,136,256]{2,1,0:T(8,128)(2,1)S(1)}, bf16[2,136,256]{2,1,0:T(8,128)(2,1)S(1)}, u32[]{:S(2)}, u32[]{:S(2)}) collective-permute-start(bf16[2,136,256]{2,1,0:T(8,128)(2,1)S(1)} %collective-permute-done.8), channel_id=1, source_target_pairs={{0,32},{8,40},{16,48},{24,56},{32,64},{40,72},{48,80},{56,88},{64,... | collective-permute-start | bytes 417800 | tf_op jit(solution)/shard_map/ppermute | solution.py:103
  69.9 6.2 %collective-permute-done.9 = bf16[2,136,256]{2,1,0:T(8,128)(2,1)S(1)} collective-permute-done((bf16[2,136,256]{2,1,0:T(8,128)(2,1)S(1)}, bf16[2,136,256]{2,1,0:T(8,128)(2,1)S(1)}, u32[]{:S(2)}, u32[]{:S(2)}) %collective-permute-start.9) | collective-permute-done | bytes 139296 | tf_op jit(solution)/shard_map/ppermute | solution.py:103
  76.1 1.9 %collective-permute-start.10 = (bf16[2,136,256]{2,1,0:T(8,128)(2,1)S(1)}, bf16[2,136,256]{2,1,0:T(8,128)(2,1)S(1)}, u32[]{:S(2)}, u32[]{:S(2)}) collective-permute-start(bf16[2,136,256]{2,1,0:T(8,128)(2,1)S(1)} %collective-permute-done.9), channel_id=1, source_target_pairs={{0,32},{8,40},{16,48},{24,56},{32,64},{40,72},{48,80},{56,88},{64,... | collective-permute-start | bytes 417800 | tf_op jit(solution)/shard_map/ppermute | solution.py:103
  78.0 6.2 %collective-permute-done.10 = bf16[2,136,256]{2,1,0:T(8,128)(2,1)S(1)} collective-permute-done((bf16[2,136,256]{2,1,0:T(8,128)(2,1)S(1)}, bf16[2,136,256]{2,1,0:T(8,128)(2,1)S(1)}, u32[]{:S(2)}, u32[]{:S(2)}) %collective-permute-start.10) | collective-permute-done | bytes 139296 | tf_op jit(solution)/shard_map/ppermute | solution.py:103
  84.3 1.9 %collective-permute-start.11 = (bf16[5,2,136,256]{3,2,1,0:T(8,128)(2,1)S(1)}, bf16[5,2,136,256]{3,2,1,0:T(8,128)(2,1)S(1)}, u32[]{:S(2)}, u32[]{:S(2)}) collective-permute-start(bf16[5,2,136,256]{3,2,1,0:T(8,128)(2,1)S(1)} %bitcast_dynamic-update-slice_fusion), channel_id=1, source_target_pairs={{0,8},{8,0},{16,24},{24,16},{32,40},{40,32},{48,56},{56,48},{64,72... | collective-permute-start | bytes 2088968 | tf_op jit(solution)/shard_map/ppermute | solution.py:112
  86.2 2.1 %collective-permute-done.11 = bf16[5,2,136,256]{3,2,1,0:T(8,128)(2,1)S(1)} collective-permute-done((bf16[5,2,136,256]{3,2,1,0:T(8,128)(2,1)S(1)}, bf16[5,2,136,256]{3,2,1,0:T(8,128)(2,1)S(1)}, u32[]{:S(2)}, u32[]{:S(2)}) %collective-permute-start.11) | collective-permute-done | bytes 696352 | tf_op jit(solution)/shard_map/ppermute | solution.py:112
  89.2 9.8 %shard_map.55 = bf16[8,128,512]{2,1,0:T(8,128)(2,1)} custom-call(bf16[128,512]{1,0:T(8,128)(2,1)} %refs_0_.1, bf16[10,136,256]{2,1,0:T(8,128)(2,1)} %bitcast.43, bf16[10,136,256]{2,1,0:T(8,128)(2,1)} %bitcast.47, bf16[10,136,256]{2,1,0:T(8,128)(2,1)} %bitcast.45, bf16[10,136,256]{2,1,0:T(8,128)(2,1)} %bitcast.49, s32[1,5120]{1,0:T(1,128)} %pad_add_fusion.refs_5_, ...), custom_call_target="tpu_custom_call" | custom-call | flops 1879048192 | bytes 8028160 | tf_op jit(solution)/shard_map/pallas_call | solution.py:69
  99.0 24.4 %all_to_all.5 = bf16[8,128,512]{2,1,0:T(8,128)(2,1)S(1)} all-to-all(bf16[8,128,512]{2,1,0:T(8,128)(2,1)} %shard_map.55), channel_id=1, replica_groups=mesh['ctx'=64,'tp'=8] {'tp'}, dimensions={0} | all-to-all | bytes 2097152 | tf_op jit(solution)/shard_map/all_to_all | solution.py:127
  (39 shorter events, 8.0 us)
Async XLA Ops:
  1.4 6.2 %collective-permute-start = (bf16[136,256]{1,0:T(8,128)(2,1)S(1)}, bf16[136,256]{1,0:T(8,128)(2,1)S(1)}, u32[]{:S(2)}, u32[]{:S(2)}) collective-permute-start(bf16[136,256]{1,0:T(8,128)(2,1)S(1)} %get-tuple-element.18), channel_id=1, source_target_pairs={{0,16},{8,24},{16,0},{24,8},{32,48},{40,56},{48,32},{56,40},{64,80... | collective-permute-start | bytes 208904 | tf_op jit(solution)/shard_map/ppermute | solution.py:98
  7.7 8.2 %collective-permute-start.1 = (bf16[2,136,256]{2,1,0:T(8,128)(2,1)S(1)}, bf16[2,136,256]{2,1,0:T(8,128)(2,1)S(1)}, u32[]{:S(2)}, u32[]{:S(2)}) collective-permute-start(bf16[2,136,256]{2,1,0:T(8,128)(2,1)S(1)} %pad_maximum_fusion), channel_id=1, source_target_pairs={{0,32},{8,40},{16,48},{24,56},{32,64},{40,72},{48,80},{56,88},{64,... | collective-permute-start | bytes 417800 | tf_op jit(solution)/shard_map/ppermute | solution.py:103
  15.8 8.1 %collective-permute-start.2 = (bf16[2,136,256]{2,1,0:T(8,128)(2,1)S(1)}, bf16[2,136,256]{2,1,0:T(8,128)(2,1)S(1)}, u32[]{:S(2)}, u32[]{:S(2)}) collective-permute-start(bf16[2,136,256]{2,1,0:T(8,128)(2,1)S(1)} %collective-permute-done.1), channel_id=1, source_target_pairs={{0,32},{8,40},{16,48},{24,56},{32,64},{40,72},{48,80},{56,88},{64,... | collective-permute-start | bytes 417800 | tf_op jit(solution)/shard_map/ppermute | solution.py:103
  24.0 8.1 %collective-permute-start.3 = (bf16[2,136,256]{2,1,0:T(8,128)(2,1)S(1)}, bf16[2,136,256]{2,1,0:T(8,128)(2,1)S(1)}, u32[]{:S(2)}, u32[]{:S(2)}) collective-permute-start(bf16[2,136,256]{2,1,0:T(8,128)(2,1)S(1)} %collective-permute-done.2), channel_id=1, source_target_pairs={{0,32},{8,40},{16,48},{24,56},{32,64},{40,72},{48,80},{56,88},{64,... | collective-permute-start | bytes 417800 | tf_op jit(solution)/shard_map/ppermute | solution.py:103
  32.1 8.1 %collective-permute-start.4 = (bf16[2,136,256]{2,1,0:T(8,128)(2,1)S(1)}, bf16[2,136,256]{2,1,0:T(8,128)(2,1)S(1)}, u32[]{:S(2)}, u32[]{:S(2)}) collective-permute-start(bf16[2,136,256]{2,1,0:T(8,128)(2,1)S(1)} %collective-permute-done.3), channel_id=1, source_target_pairs={{0,32},{8,40},{16,48},{24,56},{32,64},{40,72},{48,80},{56,88},{64,... | collective-permute-start | bytes 417800 | tf_op jit(solution)/shard_map/ppermute | solution.py:103
  40.3 48.7 %copy-start = (bf16[5,2,136,256]{3,2,1,0:T(8,128)(2,1)}, bf16[5,2,136,256]{3,2,1,0:T(8,128)(2,1)S(1)}, u32[]{:S(2)}) copy-start(bf16[5,2,136,256]{3,2,1,0:T(8,128)(2,1)S(1)} %bitcast_dynamic-update-slice_fusion.5) | copy-start | bytes 2088964
  40.3 45.9 %collective-permute-start.5 = (bf16[5,2,136,256]{3,2,1,0:T(8,128)(2,1)S(1)}, bf16[5,2,136,256]{3,2,1,0:T(8,128)(2,1)S(1)}, u32[]{:S(2)}, u32[]{:S(2)}) collective-permute-start(bf16[5,2,136,256]{3,2,1,0:T(8,128)(2,1)S(1)} %bitcast_dynamic-update-slice_fusion.5), channel_id=1, source_target_pairs={{0,8},{8,0},{16,24},{24,16},{32,40},{40,32},{48,56},{56,48},{64,72... | collective-permute-start | bytes 2088968 | tf_op jit(solution)/shard_map/ppermute | solution.py:112
  42.2 9.2 %collective-permute-start.6 = (bf16[2,136,256]{2,1,0:T(8,128)(2,1)S(1)}, bf16[2,136,256]{2,1,0:T(8,128)(2,1)S(1)}, u32[]{:S(2)}, u32[]{:S(2)}) collective-permute-start(bf16[2,136,256]{2,1,0:T(8,128)(2,1)S(1)} %collective-permute-done.4), channel_id=1, source_target_pairs={{0,32},{8,40},{16,48},{24,56},{32,64},{40,72},{48,80},{56,88},{64,... | collective-permute-start | bytes 417800 | tf_op jit(solution)/shard_map/ppermute | solution.py:103
  51.4 8.4 %collective-permute-start.7 = (bf16[2,136,256]{2,1,0:T(8,128)(2,1)S(1)}, bf16[2,136,256]{2,1,0:T(8,128)(2,1)S(1)}, u32[]{:S(2)}, u32[]{:S(2)}) collective-permute-start(bf16[2,136,256]{2,1,0:T(8,128)(2,1)S(1)} %collective-permute-done.6), channel_id=1, source_target_pairs={{0,32},{8,40},{16,48},{24,56},{32,64},{40,72},{48,80},{56,88},{64,... | collective-permute-start | bytes 417800 | tf_op jit(solution)/shard_map/ppermute | solution.py:103
  59.8 8.1 %collective-permute-start.8 = (bf16[2,136,256]{2,1,0:T(8,128)(2,1)S(1)}, bf16[2,136,256]{2,1,0:T(8,128)(2,1)S(1)}, u32[]{:S(2)}, u32[]{:S(2)}) collective-permute-start(bf16[2,136,256]{2,1,0:T(8,128)(2,1)S(1)} %collective-permute-done.7), channel_id=1, source_target_pairs={{0,32},{8,40},{16,48},{24,56},{32,64},{40,72},{48,80},{56,88},{64,... | collective-permute-start | bytes 417800 | tf_op jit(solution)/shard_map/ppermute | solution.py:103
  67.9 8.1 %collective-permute-start.9 = (bf16[2,136,256]{2,1,0:T(8,128)(2,1)S(1)}, bf16[2,136,256]{2,1,0:T(8,128)(2,1)S(1)}, u32[]{:S(2)}, u32[]{:S(2)}) collective-permute-start(bf16[2,136,256]{2,1,0:T(8,128)(2,1)S(1)} %collective-permute-done.8), channel_id=1, source_target_pairs={{0,32},{8,40},{16,48},{24,56},{32,64},{40,72},{48,80},{56,88},{64,... | collective-permute-start | bytes 417800 | tf_op jit(solution)/shard_map/ppermute | solution.py:103
  76.1 8.1 %collective-permute-start.10 = (bf16[2,136,256]{2,1,0:T(8,128)(2,1)S(1)}, bf16[2,136,256]{2,1,0:T(8,128)(2,1)S(1)}, u32[]{:S(2)}, u32[]{:S(2)}) collective-permute-start(bf16[2,136,256]{2,1,0:T(8,128)(2,1)S(1)} %collective-permute-done.9), channel_id=1, source_target_pairs={{0,32},{8,40},{16,48},{24,56},{32,64},{40,72},{48,80},{56,88},{64,... | collective-permute-start | bytes 417800 | tf_op jit(solution)/shard_map/ppermute | solution.py:103
  84.3 4.8 %copy-start.1 = (bf16[5,2,136,256]{3,2,1,0:T(8,128)(2,1)}, bf16[5,2,136,256]{3,2,1,0:T(8,128)(2,1)S(1)}, u32[]{:S(2)}) copy-start(bf16[5,2,136,256]{3,2,1,0:T(8,128)(2,1)S(1)} %bitcast_dynamic-update-slice_fusion) | copy-start | bytes 2088964
  84.3 4.1 %collective-permute-start.11 = (bf16[5,2,136,256]{3,2,1,0:T(8,128)(2,1)S(1)}, bf16[5,2,136,256]{3,2,1,0:T(8,128)(2,1)S(1)}, u32[]{:S(2)}, u32[]{:S(2)}) collective-permute-start(bf16[5,2,136,256]{3,2,1,0:T(8,128)(2,1)S(1)} %bitcast_dynamic-update-slice_fusion), channel_id=1, source_target_pairs={{0,8},{8,0},{16,24},{24,16},{32,40},{40,32},{48,56},{56,48},{64,72... | collective-permute-start | bytes 2088968 | tf_op jit(solution)/shard_map/ppermute | solution.py:112
  86.2 2.8 %copy-start.2 = (bf16[5,2,136,256]{3,2,1,0:T(8,128)(2,1)}, bf16[5,2,136,256]{3,2,1,0:T(8,128)(2,1)S(1)}, u32[]{:S(2)}) copy-start(bf16[5,2,136,256]{3,2,1,0:T(8,128)(2,1)S(1)} %collective-permute-done.5) | copy-start | bytes 2088964
  88.3 0.9 copy-start.3

commit v4 on v2

v4 whole, which is shorter than its diff:
```python
import math

import jax
import jax.numpy as jnp
from jax import lax
from jax.experimental import pallas as pl
from jax.experimental.pallas import tpu as pltpu
from jax.sharding import PartitionSpec as P

HEAD_DIM = 128
MAX_DOC = 4224
PLANE = 4
DOC_ROWS = 8
neg_large = -1e30


def partial_kernel(query_ref, block_ref, key_pos_ref, key_doc_ref, query_pos_ref,
                   query_doc_ref, out_ref, stats_ref):
    rows = query_pos_ref.shape[0]
    width = query_ref.shape[1]
    count, _, packed = block_ref.shape
    head_dim = packed // 2
    heads = width // head_dim
    tokens = count * rows
    key_part = block_ref[:, :rows, :head_dim].reshape(tokens, head_dim)
    value_part = block_ref[:, :rows, head_dim:].reshape(tokens, head_dim)
    allowed = (
        (key_pos_ref[...] <= query_pos_ref[...])
        & (key_pos_ref[...] >= 0)
        & (key_doc_ref[...] == query_doc_ref[...])
    )
    scale = 1.0 / math.sqrt(head_dim)
    for head in range(heads):
        query = query_ref[:rows, head * head_dim:(head + 1) * head_dim]
        scores = lax.dot_general(
            query, key_part, (((1,), (1,)), ((), ())), preferred_element_type=jnp.float32
        )
        scores = scores * scale
        peak = jnp.max(jnp.where(allowed, scores, neg_large), axis=1, keepdims=True)
        weight = jnp.where(allowed, jnp.exp(scores - peak), 0.0)
        total = jnp.sum(weight, axis=1, keepdims=True)
        summed = jnp.dot(
            weight.astype(jnp.bfloat16), value_part, preferred_element_type=jnp.float32
        )
        normed = jnp.where(total > 0.0, summed / jnp.maximum(total, 1e-30), 0.0)
        out_ref[:, head * head_dim:(head + 1) * head_dim] = normed.astype(out_ref.dtype)
        stats_ref[:, head:head + 1] = peak
        stats_ref[:, heads + head:heads + head + 1] = total


def partial(query, blocks, key_pos, key_doc, query_pos, query_doc, out_dtype):
    rows = query_pos.shape[0]
    width = query.shape[1]
    heads = width // HEAD_DIM
    tokens = key_pos.shape[1]
    vmem = pl.BlockSpec(memory_space=pltpu.VMEM)
    return pl.pallas_call(
        partial_kernel,
        out_shape=(
            jax.ShapeDtypeStruct((rows, width), out_dtype),
            jax.ShapeDtypeStruct((rows, 2 * heads), jnp.float32),
        ),
        in_specs=[vmem] * 6,
        out_specs=(vmem, vmem),
        cost_estimate=pl.CostEstimate(
            flops=4 * rows * tokens * width, transcendentals=rows * tokens * heads,
            bytes_accessed=blocks.size * 2 + query.size * 2 + rows * width * 4,
        ),
    )(query, blocks, key_pos, key_doc, query_pos, query_doc)


def merge_kernel(near_ref, near_stats_ref, far_ref, far_stats_ref, weight_ref, out_ref):
    rows, width = near_ref.shape
    heads = near_stats_ref.shape[1] // 2
    head_dim = width // heads
    outputs = []
    for head in range(heads):
        near_peak = near_stats_ref[:, head:head + 1]
        near_total = near_stats_ref[:, heads + head:heads + head + 1]
        far_peak = far_stats_ref[:, head:head + 1]
        far_total = far_stats_ref[:, heads + head:heads + head + 1]
        peak = jnp.maximum(near_peak, far_peak)
        near_share = near_total * jnp.exp(near_peak - peak)
        far_share = far_total * jnp.exp(far_peak - peak)
        columns = slice(head * head_dim, (head + 1) * head_dim)
        summed = (
            near_ref[:, columns].astype(jnp.float32) * near_share
            + far_ref[:, columns].astype(jnp.float32) * far_share
        )
        outputs.append((summed / (near_share + far_share)).astype(jnp.bfloat16))
    attention = jnp.concatenate(outputs, axis=1)
    partial_terms = jnp.dot(attention, weight_ref[...], preferred_element_type=jnp.float32)
    pieces, _, piece_width = out_ref.shape
    for piece in range(pieces):
        out_ref[piece] = partial_terms[:, piece * piece_width:(piece + 1) * piece_width].astype(
            out_ref.dtype
        )


def merge(near, near_stats, far, far_stats, out_weight, pieces):
    rows = near.shape[0]
    width = out_weight.shape[1]
    vmem = pl.BlockSpec(memory_space=pltpu.VMEM)
    return pl.pallas_call(
        merge_kernel,
        out_shape=jax.ShapeDtypeStruct((pieces, rows, width // pieces), jnp.bfloat16),
        in_specs=[vmem] * 5,
        out_specs=vmem,
        cost_estimate=pl.CostEstimate(
            flops=2 * rows * near.shape[1] * width, transcendentals=0,
            bytes_accessed=out_weight.size * 2 + rows * width * 2,
        ),
    )(near, near_stats, far, far_stats, out_weight)


def shards(queries, keys, values, docs, out_weight):
    rows = queries.shape[0]
    head_dim = HEAD_DIM
    ctx = lax.psum(1, "ctx")
    tp = lax.psum(1, "tp")
    my_index = lax.axis_index("ctx")
    plane = my_index // PLANE
    slot = my_index % PLANE
    planes = ctx // PLANE

    shards_back = -(-(MAX_DOC - 1) // rows)
    reach = min(-(-(shards_back + PLANE - 1) // PLANE), planes - 1)
    hops = reach // 2
    far = hops + 1

    doc_rows = jnp.zeros((DOC_ROWS, 2 * head_dim), jnp.bfloat16)
    doc_rows = doc_rows.at[0, :rows].set(docs.astype(jnp.bfloat16))
    block = jnp.concatenate([jnp.concatenate([keys, values], axis=1), doc_rows], axis=0)

    query_docs = jnp.zeros((DOC_ROWS, queries.shape[1]), jnp.bfloat16)
    query_docs = query_docs.at[0, :rows].set(docs.astype(jnp.bfloat16))
    packed_queries = jnp.concatenate([queries, query_docs], axis=0)
    back = [(s, s - PLANE * far) for s in range(PLANE * far, ctx)]
    visiting = lax.ppermute(packed_queries, "ctx", back)

    plane_blocks = [block]
    for offset in range(1, PLANE):
        plane_blocks.append(lax.ppermute(block, "ctx", [(s, s ^ offset) for s in range(ctx)]))
    current = jnp.stack(plane_blocks)
    forward = [(s, s + PLANE) for s in range(ctx - PLANE)]
    collected = [current]
    for hop in range(hops):
        current = lax.ppermute(current, "ctx", forward)
        collected.append(current)
    blocks = jnp.stack(collected)

    hop_ids = jnp.arange(hops + 1, dtype=jnp.int32)[:, None, None]
    offsets = jnp.arange(PLANE, dtype=jnp.int32)[None, :, None]
    tokens = jnp.arange(rows, dtype=jnp.int32)[None, None, :]
    key_shard = PLANE * (plane - hop_ids) + (slot ^ offsets)
    key_pos = (key_shard * rows + tokens).reshape(1, -1)
    blocks = blocks.reshape(-1, rows + DOC_ROWS, 2 * head_dim)
    key_doc = blocks[:, rows, :rows].astype(jnp.int32).reshape(1, -1)

    offsets_in_shard = jnp.arange(rows, dtype=jnp.int32).reshape(rows, 1)
    visit_pos = (my_index + PLANE * far) * rows + offsets_in_shard
    visit_doc = visiting[rows, :rows].astype(jnp.int32).reshape(rows, 1)
    visit_out, visit_stats = partial(
        visiting, blocks, key_pos, key_doc, visit_pos, visit_doc, jnp.bfloat16
    )
    ahead = [(s, s + PLANE * far) for s in range(ctx - PLANE * far)]
    far_out = lax.ppermute(visit_out, "ctx", ahead)
    far_stats = lax.ppermute(visit_stats, "ctx", ahead)

    query_pos = my_index * rows + offsets_in_shard
    near_out, near_stats = partial(
        queries, blocks, key_pos, key_doc, query_pos, docs.reshape(rows, 1), jnp.float32
    )
    has_far = plane >= far
    heads = near_stats.shape[1] // 2
    lane = jnp.arange(2 * heads, dtype=jnp.int32)[None, :]
    far_stats = jnp.where(has_far, far_stats, jnp.where(lane < heads, neg_large, 0.0))
    chunks = merge(near_out, near_stats, far_out, far_stats, out_weight, tp)

    received = lax.all_to_all(chunks, "tp", 0, 0, tiled=True)
    mixed = jnp.sum(received.astype(jnp.float32), axis=0)
    return mixed.astype(jnp.bfloat16)


def solution(mesh):
    placed = (P("ctx", "tp"), P("ctx", "tp"), P("ctx", "tp"), P("ctx"), P("tp", None))
    return jax.shard_map(
        shards, mesh=mesh, in_specs=placed, out_specs=P("ctx", "tp"), check_vma=False
    )
```

time: 141 us -> 116 us (0.82)
  the two profiles are of different devices: /device:TPU:258 before, /device:TPU:128 now
where the time goes in v4:
time: 116 us; the launch traced here: 115 us
  starting transfers between devices  38.4 us (33%)
  waiting for transfers between devices  27.5 us (24%)
  blocking collectives  23.3 us (20%)
  Pallas kernels  15.7 us (14%)
  other arithmetic  6.54 us (6%)
  local copies, waits for them, and re-layouts  3.32 us (3%)
    all_to_all x1, blocking collectives, shards(): received = lax.all_to_all(chunks, 'tp', 0, 0, tiled=True)  23.3 us
    ppermute x4, waiting for transfers between devices, shards(): current = lax.ppermute(current, 'ctx', forward)  21.8 us
    ppermute x4, starting transfers between devices, shards(): current = lax.ppermute(current, 'ctx', forward)  17.6 us
    pallas_call x2, Pallas kernels, partial(): pl.pallas_call(partial_kernel, out_shape=(jax.ShapeDtypeStruct((rows, wid...  11.2 us
    ppermute x3, starting transfers between devices, shards(): lax.ppermute(block, 'ctx', [(s, s ^ offset) for s in range(ctx)])  7.59 us
    ppermute x1, starting transfers between devices, shards(): far_out = lax.ppermute(visit_out, 'ctx', ahead)  6.77 us
    ppermute x1, waiting for transfers between devices, shards(): far_stats = lax.ppermute(visit_stats, 'ctx', ahead)  5.65 us
    ppermute x1, starting transfers between devices, shards(): far_stats = lax.ppermute(visit_stats, 'ctx', ahead)  5.19 us
  transfers between devices with their start and end apart: 10, of which 5 were waited for; matrix products, arithmetic and copies ran while one was open for 5% of the time, Pallas kernels for 5%

profile of v4, /device:TPU:128, one launch (start us, length us, event | category | flops | bytes accessed | tf_op | source)
XLA Modules:
  0.0 115.0 jit_solution(11793867288739974277)
XLA Ops:
  0.7 0.8 fusion.6
  1.4 2.8 %collective-permute-start.2 = (bf16[136,256]{1,0:T(8,128)(2,1)S(1)}, bf16[136,256]{1,0:T(8,128)(2,1)S(1)}, u32[]{:S(2)}, u32[]{:S(2)}) collective-permute-start(bf16[136,256]{1,0:T(8,128)(2,1)S(1)} %get-tuple-element.38), channel_id=1, source_target_pairs={{0,24},{8,16},{16,8},{24,0},{32,56},{40,48},{48,40},{56,32},{64,88... | collective-permute-start | bytes 208904 | tf_op jit(solution)/shard_map/ppermute | solution.py:143
  4.3 2.5 %collective-permute-start.1 = (bf16[136,256]{1,0:T(8,128)(2,1)S(1)}, bf16[136,256]{1,0:T(8,128)(2,1)S(1)}, u32[]{:S(2)}, u32[]{:S(2)}) collective-permute-start(bf16[136,256]{1,0:T(8,128)(2,1)S(1)} %get-tuple-element.38), channel_id=1, source_target_pairs={{0,16},{8,24},{16,0},{24,8},{32,48},{40,56},{48,32},{56,40},{64,80... | collective-permute-start | bytes 208904 | tf_op jit(solution)/shard_map/ppermute | solution.py:143
  6.8 2.3 %collective-permute-start = (bf16[136,256]{1,0:T(8,128)(2,1)S(1)}, bf16[136,256]{1,0:T(8,128)(2,1)S(1)}, u32[]{:S(2)}, u32[]{:S(2)}) collective-permute-start(bf16[136,256]{1,0:T(8,128)(2,1)S(1)} %get-tuple-element.38), channel_id=1, source_target_pairs={{0,8},{8,0},{16,24},{24,16},{32,40},{40,32},{48,56},{56,48},{64,72... | collective-permute-start | bytes 208904 | tf_op jit(solution)/shard_map/ppermute | solution.py:143
  9.1 0.9 fusion.1
  10.0 1.3 %collective-permute-start.7 = (bf16[136,512]{1,0:T(8,128)(2,1)S(1)}, bf16[136,512]{1,0:T(8,128)(2,1)S(1)}, u32[]{:S(2)}, u32[]{:S(2)}) collective-permute-start(bf16[136,512]{1,0:T(8,128)(2,1)S(1)} %fusion.1), channel_id=1, source_target_pairs={{160,0},{168,8},{176,16},{184,24},{192,32},{200,40},{208,48},{216,... | collective-permute-start | bytes 417800 | tf_op jit(solution)/shard_map/ppermute | solution.py:139
  11.5 8.1 %collective-permute-start.3 = (bf16[4,136,256]{2,1,0:T(8,128)(2,1)S(1)}, bf16[4,136,256]{2,1,0:T(8,128)(2,1)S(1)}, u32[]{:S(2)}, u32[]{:S(2)}) collective-permute-start(bf16[4,136,256]{2,1,0:T(8,128)(2,1)S(1)} %pad_maximum_fusion), channel_id=1, source_target_pairs={{0,32},{8,40},{16,48},{24,56},{32,64},{40,72},{48,80},{56,88},{64,... | collective-permute-start | bytes 835592 | tf_op jit(solution)/shard_map/ppermute | solution.py:148
  20.9 4.5 %collective-permute-done.3 = bf16[4,136,256]{2,1,0:T(8,128)(2,1)S(1)} collective-permute-done((bf16[4,136,256]{2,1,0:T(8,128)(2,1)S(1)}, bf16[4,136,256]{2,1,0:T(8,128)(2,1)S(1)}, u32[]{:S(2)}, u32[]{:S(2)}) %collective-permute-start.3) | collective-permute-done | bytes 278560 | tf_op jit(solution)/shard_map/ppermute | solution.py:148
  25.4 4.4 %collective-permute-start.4 = (bf16[4,136,256]{2,1,0:T(8,128)(2,1)S(1)}, bf16[4,136,256]{2,1,0:T(8,128)(2,1)S(1)}, u32[]{:S(2)}, u32[]{:S(2)}) collective-permute-start(bf16[4,136,256]{2,1,0:T(8,128)(2,1)S(1)} %collective-permute-done.3), channel_id=1, source_target_pairs={{0,32},{8,40},{16,48},{24,56},{32,64},{40,72},{48,80},{56,88},{64,... | collective-permute-start | bytes 835592 | tf_op jit(solution)/shard_map/ppermute | solution.py:148
  30.4 1.4 %copy.6.query_doc_ref = s32[128,1]{1,0:T(8,128)} copy(s32[128,1]{0,1:T(1,128)} %bitcast.41) | data formatting | bytes 1024 | tf_op jit(solution)/shard_map/reshape | solution.py:172
  31.8 4.1 %collective-permute-done.4 = bf16[4,136,256]{2,1,0:T(8,128)(2,1)S(1)} collective-permute-done((bf16[4,136,256]{2,1,0:T(8,128)(2,1)S(1)}, bf16[4,136,256]{2,1,0:T(8,128)(2,1)S(1)}, u32[]{:S(2)}, u32[]{:S(2)}) %collective-permute-start.4) | collective-permute-done | bytes 278560 | tf_op jit(solution)/shard_map/ppermute | solution.py:148
  35.9 3.2 %collective-permute-start.5 = (bf16[4,136,256]{2,1,0:T(8,128)(2,1)S(1)}, bf16[4,136,256]{2,1,0:T(8,128)(2,1)S(1)}, u32[]{:S(2)}, u32[]{:S(2)}) collective-permute-start(bf16[4,136,256]{2,1,0:T(8,128)(2,1)S(1)} %collective-permute-done.4), channel_id=1, source_target_pairs={{0,32},{8,40},{16,48},{24,56},{32,64},{40,72},{48,80},{56,88},{64,... | collective-permute-start | bytes 835592 | tf_op jit(solution)/shard_map/ppermute | solution.py:148
  39.1 0.7 copy.7.query_doc_ref
  39.8 5.7 %collective-permute-done.5 = bf16[4,136,256]{2,1,0:T(8,128)(2,1)S(1)} collective-permute-done((bf16[4,136,256]{2,1,0:T(8,128)(2,1)S(1)}, bf16[4,136,256]{2,1,0:T(8,128)(2,1)S(1)}, u32[]{:S(2)}, u32[]{:S(2)}) %collective-permute-start.5) | collective-permute-done | bytes 278560 | tf_op jit(solution)/shard_map/ppermute | solution.py:148
  45.5 2.0 %collective-permute-start.6 = (bf16[4,136,256]{2,1,0:T(8,128)(2,1)S(1)}, bf16[4,136,256]{2,1,0:T(8,128)(2,1)S(1)}, u32[]{:S(2)}, u32[]{:S(2)}) collective-permute-start(bf16[4,136,256]{2,1,0:T(8,128)(2,1)S(1)} %collective-permute-done.5), channel_id=1, source_target_pairs={{0,32},{8,40},{16,48},{24,56},{32,64},{40,72},{48,80},{56,88},{64,... | collective-permute-start | bytes 835592 | tf_op jit(solution)/shard_map/ppermute | solution.py:148
  47.5 7.6 %collective-permute-done.6 = bf16[4,136,256]{2,1,0:T(8,128)(2,1)S(1)} collective-permute-done((bf16[4,136,256]{2,1,0:T(8,128)(2,1)S(1)}, bf16[4,136,256]{2,1,0:T(8,128)(2,1)S(1)}, u32[]{:S(2)}, u32[]{:S(2)}) %collective-permute-start.6) | collective-permute-done | bytes 278560 | tf_op jit(solution)/shard_map/ppermute | solution.py:148
  56.3 5.6 %shard_map.56 = (bf16[128,512]{1,0:T(8,128)(2,1)}, f32[128,8]{1,0:T(8,128)}) custom-call(bf16[136,512]{1,0:T(8,128)(2,1)} %copy-done.2, bf16[20,136,256]{2,1,0:T(8,128)(2,1)} %bitcast.37, s32[1,2560]{1,0:T(1,128)} %bitcast.39, s32[1,2560]{1,0:T(1,128)} %fusion.4.key_doc_ref, s32[128,1]{1,0:T(8,128)} %iota_add_fusion.query_pos_ref, s32[128,1]{1,0:T(8,128)} %copy.7.query_doc_ref), custom_call_target="tpu_custom_call" | custom-call | flops 671088640 | bytes 1794048 | tf_op jit(solution)/shard_map/pallas_call | solution.py:57
  61.9 6.8 %collective-permute-start.8 = (bf16[128,512]{1,0:T(8,128)(2,1)}, bf16[128,512]{1,0:T(8,128)(2,1)S(1)}, u32[]{:S(2)}, u32[]{:S(2)}) collective-permute-start(bf16[128,512]{1,0:T(8,128)(2,1)} %get-tuple-element.35), channel_id=1, source_target_pairs={{0,160},{8,168},{16,176},{24,184},{32,192},{40,200},{48,208},{56,2... | collective-permute-start | bytes 393224 | tf_op jit(solution)/shard_map/ppermute | solution.py:167
  68.6 5.2 %collective-permute-start.9 = (f32[128,8]{1,0:T(8,128)}, f32[128,8]{1,0:T(8,128)S(1)}, u32[]{:S(2)}, u32[]{:S(2)}) collective-permute-start(f32[128,8]{1,0:T(8,128)} %get-tuple-element.36), channel_id=1, source_target_pairs={{0,160},{8,168},{16,176},{24,184},{32,192},{40,200},{48,208},{56,2... | collective-permute-start | bytes 12296 | tf_op jit(solution)/shard_map/ppermute | solution.py:168
  73.8 5.6 %shard_map.55 = (f32[128,512]{1,0:T(8,128)}, f32[128,8]{1,0:T(8,128)}) custom-call(bf16[128,512]{1,0:T(8,128)(2,1)} %query_ref.1, bf16[20,136,256]{2,1,0:T(8,128)(2,1)} %bitcast.38, s32[1,2560]{1,0:T(1,128)} %bitcast.40, s32[1,2560]{1,0:T(1,128)} %fusion.4.key_doc_ref, s32[128,1]{1,0:T(8,128)} %iota_add_fusion.1.query_pos_ref, s32[128,1]{1,0:T(8,128)} %copy.6.query_doc_ref), custom_call_target="tpu_custom_call" | custom-call | flops 671088640 | bytes 1785856 | tf_op jit(solution)/shard_map/pallas_call | solution.py:57
  79.5 5.7 %collective-permute-done.9 = f32[128,8]{1,0:T(8,128)S(1)} collective-permute-done((f32[128,8]{1,0:T(8,128)}, f32[128,8]{1,0:T(8,128)S(1)}, u32[]{:S(2)}, u32[]{:S(2)}) %collective-permute-start.9) | collective-permute-done | bytes 4128 | tf_op jit(solution)/shard_map/ppermute | solution.py:168
  86.4 4.5 %shard_map.57 = bf16[8,128,512]{2,1,0:T(8,128)(2,1)} custom-call(f32[128,512]{1,0:T(8,128)} %get-tuple-element.33.near_ref, f32[128,8]{1,0:T(8,128)} %get-tuple-element.34.near_stats_ref, bf16[128,512]{1,0:T(8,128)(2,1)} %copy-done, f32[128,8]{1,0:T(8,128)} %broadcast_select_fusion.far_stats_ref, bf16[512,4096]{1,0:T(8,128)(2,1)} %weight_ref.1), custom_call_target="tpu_custom_call" | custom-call | flops 536870912 | bytes 5242880 | tf_op jit(solution)/shard_map/pallas_call | solution.py:104
  90.9 23.3 %all_to_all.5 = bf16[8,128,512]{2,1,0:T(8,128)(2,1)S(1)} all-to-all(bf16[8,128,512]{2,1,0:T(8,128)(2,1)} %shard_map.57), channel_id=1, replica_groups=mesh['ctx'=64,'tp'=8] {'tp'}, dimensions={0} | all-to-all | bytes 2097152 | tf_op jit(solution)/shard_map/all_to_all | solution.py:180
  114.2 0.8 reduce_sum.12
  (28 shorter events, 5.2 us)
Async XLA Ops:
  1.4 10.0 %collective-permute-start.2 = (bf16[136,256]{1,0:T(8,128)(2,1)S(1)}, bf16[136,256]{1,0:T(8,128)(2,1)S(1)}, u32[]{:S(2)}, u32[]{:S(2)}) collective-permute-start(bf16[136,256]{1,0:T(8,128)(2,1)S(1)} %get-tuple-element.38), channel_id=1, source_target_pairs={{0,24},{8,16},{16,8},{24,0},{32,56},{40,48},{48,40},{56,32},{64,88... | collective-permute-start | bytes 208904 | tf_op jit(solution)/shard_map/ppermute | solution.py:143
  4.3 7.1 %collective-permute-start.1 = (bf16[136,256]{1,0:T(8,128)(2,1)S(1)}, bf16[136,256]{1,0:T(8,128)(2,1)S(1)}, u32[]{:S(2)}, u32[]{:S(2)}) collective-permute-start(bf16[136,256]{1,0:T(8,128)(2,1)S(1)} %get-tuple-element.38), channel_id=1, source_target_pairs={{0,16},{8,24},{16,0},{24,8},{32,48},{40,56},{48,32},{56,40},{64,80... | collective-permute-start | bytes 208904 | tf_op jit(solution)/shard_map/ppermute | solution.py:143
  6.8 4.6 %collective-permute-start = (bf16[136,256]{1,0:T(8,128)(2,1)S(1)}, bf16[136,256]{1,0:T(8,128)(2,1)S(1)}, u32[]{:S(2)}, u32[]{:S(2)}) collective-permute-start(bf16[136,256]{1,0:T(8,128)(2,1)S(1)} %get-tuple-element.38), channel_id=1, source_target_pairs={{0,8},{8,0},{16,24},{24,16},{32,40},{40,32},{48,56},{56,48},{64,72... | collective-permute-start | bytes 208904 | tf_op jit(solution)/shard_map/ppermute | solution.py:143
  10.0 29.1 %collective-permute-start.7 = (bf16[136,512]{1,0:T(8,128)(2,1)S(1)}, bf16[136,512]{1,0:T(8,128)(2,1)S(1)}, u32[]{:S(2)}, u32[]{:S(2)}) collective-permute-start(bf16[136,512]{1,0:T(8,128)(2,1)S(1)} %fusion.1), channel_id=1, source_target_pairs={{160,0},{168,8},{176,16},{184,24},{192,32},{200,40},{208,48},{216,... | collective-permute-start | bytes 417800 | tf_op jit(solution)/shard_map/ppermute | solution.py:139
  11.5 13.9 %collective-permute-start.3 = (bf16[4,136,256]{2,1,0:T(8,128)(2,1)S(1)}, bf16[4,136,256]{2,1,0:T(8,128)(2,1)S(1)}, u32[]{:S(2)}, u32[]{:S(2)}) collective-permute-start(bf16[4,136,256]{2,1,0:T(8,128)(2,1)S(1)} %pad_maximum_fusion), channel_id=1, source_target_pairs={{0,32},{8,40},{16,48},{24,56},{32,64},{40,72},{48,80},{56,88},{64,... | collective-permute-start | bytes 835592 | tf_op jit(solution)/shard_map/ppermute | solution.py:148
  25.4 10.5 %collective-permute-start.4 = (bf16[4,136,256]{2,1,0:T(8,128)(2,1)S(1)}, bf16[4,136,256]{2,1,0:T(8,128)(2,1)S(1)}, u32[]{:S(2)}, u32[]{:S(2)}) collective-permute-start(bf16[4,136,256]{2,1,0:T(8,128)(2,1)S(1)} %collective-permute-done.3), channel_id=1, source_target_pairs={{0,32},{8,40},{16,48},{24,56},{32,64},{40,72},{48,80},{56,88},{64,... | collective-permute-start | bytes 835592 | tf_op jit(solution)/shard_map/ppermute | solution.py:148
  35.9 9.6 %collective-permute-start.5 = (bf16[4,136,256]{2,1,0:T(8,128)(2,1)S(1)}, bf16[4,136,256]{2,1,0:T(8,128)(2,1)S(1)}, u32[]{:S(2)}, u32[]{:S(2)}) collective-permute-start(bf16[4,136,256]{2,1,0:T(8,128)(2,1)S(1)} %collective-permute-done.4), channel_id=1, source_target_pairs={{0,32},{8,40},{16,48},{24,56},{32,64},{40,72},{48,80},{56,88},{64,... | collective-permute-start | bytes 835592 | tf_op jit(solution)/shard_map/ppermute | solution.py:148
  39.1 16.8 %copy-start.2 = (bf16[136,512]{1,0:T(8,128)(2,1)}, bf16[136,512]{1,0:T(8,128)(2,1)S(1)}, u32[]{:S(2)}) copy-start(bf16[136,512]{1,0:T(8,128)(2,1)S(1)} %collective-permute-done.7.query_ref) | copy-start | bytes 417796
  45.5 9.6 %collective-permute-start.6 = (bf16[4,136,256]{2,1,0:T(8,128)(2,1)S(1)}, bf16[4,136,256]{2,1,0:T(8,128)(2,1)S(1)}, u32[]{:S(2)}, u32[]{:S(2)}) collective-permute-start(bf16[4,136,256]{2,1,0:T(8,128)(2,1)S(1)} %collective-permute-done.5), channel_id=1, source_target_pairs={{0,32},{8,40},{16,48},{24,56},{32,64},{40,72},{48,80},{56,88},{64,... | collective-permute-start | bytes 835592 | tf_op jit(solution)/shard_map/ppermute | solution.py:148
  55.2 1.1 copy-start.1
  61.9 23.9 %collective-permute-start.8 = (bf16[128,512]{1,0:T(8,128)(2,1)}, bf16[128,512]{1,0:T(8,128)(2,1)S(1)}, u32[]{:S(2)}, u32[]{:S(2)}) collective-permute-start(bf16[128,512]{1,0:T(8,128)(2,1)} %get-tuple-element.35), channel_id=1, source_target_pairs={{0,160},{8,168},{16,176},{24,184},{32,192},{40,200},{48,208},{56,2... | collective-permute-start | bytes 393224 | tf_op jit(solution)/shard_map/ppermute | solution.py:167
  68.6 16.5 %collective-permute-start.9 = (f32[128,8]{1,0:T(8,128)}, f32[128,8]{1,0:T(8,128)S(1)}, u32[]{:S(2)}, u32[]{:S(2)}) collective-permute-start(f32[128,8]{1,0:T(8,128)} %get-tuple-element.36), channel_id=1, source_target_pairs={{0,160},{8,168},{16,176},{24,184},{32,192},{40,200},{48,208},{56,2... | collective-permute-start | bytes 12296 | tf_op jit(solution)/shard_map/ppermute | solution.py:168
  85.7 0.7 copy-start

commit v5 on v4

v5 whole, which is shorter than its diff:
```python
import math

import jax
import jax.numpy as jnp
from jax import lax
from jax.experimental import pallas as pl
from jax.experimental.pallas import tpu as pltpu
from jax.sharding import PartitionSpec as P

HEAD_DIM = 128
MAX_DOC = 4224
PLANE = 4
DOC_ROWS = 8
neg_large = -1e30


def step_kernel(*refs):
    (own_ref, visit_ref, block_ref, key_pos_ref, key_doc_ref, own_pos_ref, own_doc_ref,
     visit_pos_ref, visit_doc_ref) = refs[:9]
    states_in = refs[9:15]
    states_out = refs[15:]
    rows = own_pos_ref.shape[0]
    width = own_ref.shape[1]
    count, _, packed = block_ref.shape
    head_dim = packed // 2
    heads = width // head_dim
    tokens = count * rows
    key_part = block_ref[:, :rows, :head_dim].reshape(tokens, head_dim)
    value_part = block_ref[:, :rows, head_dim:].reshape(tokens, head_dim)
    key_pos = key_pos_ref[...]
    key_doc = key_doc_ref[...]
    scale = 1.0 / math.sqrt(head_dim)
    sets = (
        (own_ref, own_pos_ref, own_doc_ref, states_in[0:3], states_out[0:3]),
        (visit_ref, visit_pos_ref, visit_doc_ref, states_in[3:6], states_out[3:6]),
    )
    for query_ref, pos_ref, doc_ref, (peak_in, total_in, acc_in), (peak_out, total_out,
                                                                  acc_out) in sets:
        allowed = (key_pos <= pos_ref[...]) & (key_pos >= 0) & (key_doc == doc_ref[...])
        for head in range(heads):
            columns = slice(head * head_dim, (head + 1) * head_dim)
            query = query_ref[:rows, columns]
            scores = lax.dot_general(
                query, key_part, (((1,), (1,)), ((), ())), preferred_element_type=jnp.float32
            )
            scores = scores * scale
            old_peak = peak_in[:, head:head + 1]
            block_peak = jnp.max(jnp.where(allowed, scores, neg_large), axis=1, keepdims=True)
            peak = jnp.maximum(old_peak, block_peak)
            rescale = jnp.exp(old_peak - peak)
            weight = jnp.where(allowed, jnp.exp(scores - peak), 0.0)
            total = total_in[:, head:head + 1] * rescale + jnp.sum(weight, axis=1, keepdims=True)
            update = jnp.dot(
                weight.astype(jnp.bfloat16), value_part, preferred_element_type=jnp.float32
            )
            acc_out[:, columns] = acc_in[:, columns] * rescale + update
            peak_out[:, head:head + 1] = peak
            total_out[:, head:head + 1] = total


def step(own, visiting, block, key_pos, key_doc, own_pos, own_doc, visit_pos, visit_doc,
         states):
    rows = own_pos.shape[0]
    width = own.shape[1]
    heads = width // HEAD_DIM
    tokens = key_pos.shape[1]
    vmem = pl.BlockSpec(memory_space=pltpu.VMEM)
    shapes = tuple(jax.ShapeDtypeStruct(x.shape, x.dtype) for x in states)
    return pl.pallas_call(
        step_kernel,
        out_shape=shapes,
        in_specs=[vmem] * (9 + len(states)),
        out_specs=tuple([vmem] * len(states)),
        input_output_aliases={9 + i: i for i in range(len(states))},
        cost_estimate=pl.CostEstimate(
            flops=8 * rows * tokens * width, transcendentals=2 * rows * tokens * heads,
            bytes_accessed=block.size * 2 + 4 * rows * width * 4,
        ),
    )(own, visiting, block, key_pos, key_doc, own_pos, own_doc, visit_pos, visit_doc, *states)


def merge_kernel(near_peak_ref, near_total_ref, near_ref, far_ref, far_stats_ref, weight_ref,
                 out_ref):
    rows, width = near_ref.shape
    heads = near_peak_ref.shape[1]
    head_dim = width // heads
    outputs = []
    for head in range(heads):
        near_peak = near_peak_ref[:, head:head + 1]
        near_total = near_total_ref[:, head:head + 1]
        far_peak = far_stats_ref[:, head:head + 1]
        far_total = far_stats_ref[:, heads + head:heads + head + 1]
        peak = jnp.maximum(near_peak, far_peak)
        near_scale = jnp.exp(near_peak - peak)
        near_share = near_total * near_scale
        far_share = far_total * jnp.exp(far_peak - peak)
        columns = slice(head * head_dim, (head + 1) * head_dim)
        summed = (
            near_ref[:, columns] * near_scale
            + far_ref[:, columns].astype(jnp.float32) * far_share
        )
        outputs.append((summed / (near_share + far_share)).astype(jnp.bfloat16))
    attention = jnp.concatenate(outputs, axis=1)
    partial_terms = jnp.dot(attention, weight_ref[...], preferred_element_type=jnp.float32)
    pieces, _, piece_width = out_ref.shape
    for piece in range(pieces):
        out_ref[piece] = partial_terms[:, piece * piece_width:(piece + 1) * piece_width].astype(
            out_ref.dtype
        )


def merge(near_peak, near_total, near, far, far_stats, out_weight, pieces):
    rows = near.shape[0]
    width = out_weight.shape[1]
    vmem = pl.BlockSpec(memory_space=pltpu.VMEM)
    return pl.pallas_call(
        merge_kernel,
        out_shape=jax.ShapeDtypeStruct((pieces, rows, width // pieces), jnp.bfloat16),
        in_specs=[vmem] * 6,
        out_specs=vmem,
        cost_estimate=pl.CostEstimate(
            flops=2 * rows * near.shape[1] * width, transcendentals=0,
            bytes_accessed=out_weight.size * 2 + rows * width * 2,
        ),
    )(near_peak, near_total, near, far, far_stats, out_weight)


def shards(queries, keys, values, docs, out_weight):
    rows = queries.shape[0]
    head_dim = HEAD_DIM
    ctx = lax.psum(1, "ctx")
    tp = lax.psum(1, "tp")
    my_index = lax.axis_index("ctx")
    plane = my_index // PLANE
    slot = my_index % PLANE
    planes = ctx // PLANE

    shards_back = -(-(MAX_DOC - 1) // rows)
    reach = min(-(-(shards_back + PLANE - 1) // PLANE), planes - 1)
    hops = reach // 2
    far = hops + 1

    doc_rows = jnp.zeros((DOC_ROWS, 2 * head_dim), jnp.bfloat16)
    doc_rows = doc_rows.at[0, :rows].set(docs.astype(jnp.bfloat16))
    block = jnp.concatenate([jnp.concatenate([keys, values], axis=1), doc_rows], axis=0)

    query_docs = jnp.zeros((DOC_ROWS, queries.shape[1]), jnp.bfloat16)
    query_docs = query_docs.at[0, :rows].set(docs.astype(jnp.bfloat16))
    packed_queries = jnp.concatenate([queries, query_docs], axis=0)
    back = [(s, s - PLANE * far) for s in range(PLANE * far, ctx)]
    visiting = lax.ppermute(packed_queries, "ctx", back)

    plane_blocks = [block]
    for offset in range(1, PLANE):
        plane_blocks.append(lax.ppermute(block, "ctx", [(s, s ^ offset) for s in range(ctx)]))
    current = jnp.stack(plane_blocks)
    offsets_in_shard = jnp.arange(rows, dtype=jnp.int32).reshape(rows, 1)
    visit_pos = (my_index + PLANE * far) * rows + offsets_in_shard
    visit_doc = visiting[rows, :rows].astype(jnp.int32).reshape(rows, 1)
    own_pos = my_index * rows + offsets_in_shard
    own_doc = docs.reshape(rows, 1)
    heads = queries.shape[1] // head_dim
    empty = (
        jnp.full((rows, heads), neg_large, jnp.float32),
        jnp.zeros((rows, heads), jnp.float32),
        jnp.zeros((rows, queries.shape[1]), jnp.float32),
    )
    states = empty + empty

    offsets = jnp.arange(PLANE, dtype=jnp.int32)[:, None]
    tokens = jnp.arange(rows, dtype=jnp.int32)[None, :]
    forward = [(s, s + PLANE) for s in range(ctx - PLANE)]
    for hop in range(hops + 1):
        if hop:
            current = lax.ppermute(current, "ctx", forward)
        key_shard = PLANE * (plane - hop) + (slot ^ offsets)
        key_pos = (key_shard * rows + tokens).reshape(1, -1)
        key_doc = current[:, rows, :rows].astype(jnp.int32).reshape(1, -1)
        states = step(
            queries, visiting, current, key_pos, key_doc, own_pos, own_doc, visit_pos,
            visit_doc, states,
        )

    near_peak, near_total, near_acc, visit_peak, visit_total, visit_acc = states
    visit_out = jnp.where(
        visit_total[:, :, None] > 0.0,
        visit_acc.reshape(rows, heads, head_dim)
        / jnp.maximum(visit_total, 1e-30)[:, :, None],
        0.0,
    ).reshape(rows, heads * head_dim).astype(jnp.bfloat16)
    visit_stats = jnp.concatenate([visit_peak, visit_total], axis=1)
    ahead = [(s, s + PLANE * far) for s in range(ctx - PLANE * far)]
    far_out = lax.ppermute(visit_out, "ctx", ahead)
    far_stats = lax.ppermute(visit_stats, "ctx", ahead)

    has_far = plane >= far
    lane = jnp.arange(2 * heads, dtype=jnp.int32)[None, :]
    far_stats = jnp.where(has_far, far_stats, jnp.where(lane < heads, neg_large, 0.0))
    chunks = merge(near_peak, near_total, near_acc, far_out, far_stats, out_weight, tp)

    received = lax.all_to_all(chunks, "tp", 0, 0, tiled=True)
    mixed = jnp.sum(received.astype(jnp.float32), axis=0)
    return mixed.astype(jnp.bfloat16)


def solution(mesh):
    placed = (P("ctx", "tp"), P("ctx", "tp"), P("ctx", "tp"), P("ctx"), P("tp", None))
    return jax.shard_map(
        shards, mesh=mesh, in_specs=placed, out_specs=P("ctx", "tp"), check_vma=False
    )
```

time: 116 us -> 140 us (1.21)
  the two profiles are of different devices: /device:TPU:128 before, /device:TPU:416 now
where the time goes in v5:
time: 140 us; the launch traced here: 139 us
  waiting for transfers between devices  34.3 us (24%)
  Pallas kernels  30.3 us (22%)
  starting transfers between devices  27.8 us (20%)
  blocking collectives  23.7 us (17%)
  other arithmetic  13.5 us (10%)
  local copies, waits for them, and re-layouts  9.1 us (6%)
    pallas_call x5, Pallas kernels, step(): pl.pallas_call(step_kernel, out_shape=shapes, in_specs=[vmem] * (9 + len(...  25.8 us
    all_to_all x1, blocking collectives, shards(): received = lax.all_to_all(chunks, 'tp', 0, 0, tiled=True)  23.7 us
    ppermute x1, waiting for transfers between devices, shards(): far_out = lax.ppermute(visit_out, 'ctx', ahead)  12 us
    ppermute x4, starting transfers between devices, shards(): current = lax.ppermute(current, 'ctx', forward)  11.7 us
    ppermute x4, waiting for transfers between devices, shards(): current = lax.ppermute(current, 'ctx', forward)  11.6 us
    ppermute x1, waiting for transfers between devices, shards(): far_stats = lax.ppermute(visit_stats, 'ctx', ahead)  10.8 us
    ppermute x3, starting transfers between devices, shards(): lax.ppermute(block, 'ctx', [(s, s ^ offset) for s in range(ctx)])  7.59 us
    ppermute x1, starting transfers between devices, shards(): visiting = lax.ppermute(packed_queries, 'ctx', back)  5.91 us
  transfers between devices with their start and end apart: 10, of which 4 were waited for; matrix products, arithmetic and copies ran while one was open for 11% of the time, Pallas kernels for 15%

profile of v5, /device:TPU:416, one launch (start us, length us, event | category | flops | bytes accessed | tf_op | source)
XLA Modules:
  0.0 139.0 jit_solution(17637596137546221584)
XLA Ops:
  1.4 1.9 %collective-permute-start.1 = (bf16[136,256]{1,0:T(8,128)(2,1)S(1)}, bf16[136,256]{1,0:T(8,128)(2,1)S(1)}, u32[]{:S(2)}, u32[]{:S(2)}) collective-permute-start(bf16[136,256]{1,0:T(8,128)(2,1)S(1)} %get-tuple-element.90), channel_id=1, source_target_pairs={{0,8},{8,0},{16,24},{24,16},{32,40},{40,32},{48,56},{56,48},{64,72... | collective-permute-start | bytes 208904 | tf_op jit(solution)/shard_map/ppermute | solution.py:155
  3.4 3.4 %collective-permute-start.2 = (bf16[136,256]{1,0:T(8,128)(2,1)S(1)}, bf16[136,256]{1,0:T(8,128)(2,1)S(1)}, u32[]{:S(2)}, u32[]{:S(2)}) collective-permute-start(bf16[136,256]{1,0:T(8,128)(2,1)S(1)} %get-tuple-element.90), channel_id=1, source_target_pairs={{0,16},{8,24},{16,0},{24,8},{32,48},{40,56},{48,32},{56,40},{64,80... | collective-permute-start | bytes 208904 | tf_op jit(solution)/shard_map/ppermute | solution.py:155
  6.8 2.3 %collective-permute-start.3 = (bf16[136,256]{1,0:T(8,128)(2,1)S(1)}, bf16[136,256]{1,0:T(8,128)(2,1)S(1)}, u32[]{:S(2)}, u32[]{:S(2)}) collective-permute-start(bf16[136,256]{1,0:T(8,128)(2,1)S(1)} %get-tuple-element.90), channel_id=1, source_target_pairs={{0,24},{8,16},{16,8},{24,0},{32,56},{40,48},{48,40},{56,32},{64,88... | collective-permute-start | bytes 208904 | tf_op jit(solution)/shard_map/ppermute | solution.py:155
  9.1 0.9 fusion.3
  10.0 5.9 %collective-permute-start = (bf16[136,512]{1,0:T(8,128)(2,1)S(1)}, bf16[136,512]{1,0:T(8,128)(2,1)S(1)}, u32[]{:S(2)}, u32[]{:S(2)}) collective-permute-start(bf16[136,512]{1,0:T(8,128)(2,1)S(1)} %fusion.3), channel_id=1, source_target_pairs={{160,0},{168,8},{176,16},{184,24},{192,32},{200,40},{208,48},{216,... | collective-permute-start | bytes 417800 | tf_op jit(solution)/shard_map/ppermute | solution.py:151
  19.3 2.9 %collective-permute-start.4 = (bf16[4,136,256]{2,1,0:T(8,128)(2,1)S(1)}, bf16[4,136,256]{2,1,0:T(8,128)(2,1)S(1)}, u32[]{:S(2)}, u32[]{:S(2)}) collective-permute-start(bf16[4,136,256]{2,1,0:T(8,128)(2,1)S(1)} %pad_maximum_fusion.refs_2_), channel_id=1, source_target_pairs={{0,32},{8,40},{16,48},{24,56},{32,64},{40,72},{48,80},{56,88},{64,... | collective-permute-start | bytes 835592 | tf_op jit(solution)/shard_map/ppermute | solution.py:175
  22.9 6.9 %collective-permute-done.4.refs_2_ = bf16[4,136,256]{2,1,0:T(8,128)(2,1)S(1)} collective-permute-done((bf16[4,136,256]{2,1,0:T(8,128)(2,1)S(1)}, bf16[4,136,256]{2,1,0:T(8,128)(2,1)S(1)}, u32[]{:S(2)}, u32[]{:S(2)}) %collective-permute-start.4) | collective-permute-done | bytes 278560 | tf_op jit(solution)/shard_map/ppermute | solution.py:175
  29.7 2.9 %collective-permute-start.5 = (bf16[4,136,256]{2,1,0:T(8,128)(2,1)S(1)}, bf16[4,136,256]{2,1,0:T(8,128)(2,1)S(1)}, u32[]{:S(2)}, u32[]{:S(2)}) collective-permute-start(bf16[4,136,256]{2,1,0:T(8,128)(2,1)S(1)} %collective-permute-done.4.refs_2_), channel_id=1, source_target_pairs={{0,32},{8,40},{16,48},{24,56},{32,64},{40,72},{48,80},{56,88},{64,... | collective-permute-start | bytes 835592 | tf_op jit(solution)/shard_map/ppermute | solution.py:175
  32.7 1.4 copy.69.refs_6_
  34.7 4.7 %collective-permute-done.5.refs_2_ = bf16[4,136,256]{2,1,0:T(8,128)(2,1)S(1)} collective-permute-done((bf16[4,136,256]{2,1,0:T(8,128)(2,1)S(1)}, bf16[4,136,256]{2,1,0:T(8,128)(2,1)S(1)}, u32[]{:S(2)}, u32[]{:S(2)}) %collective-permute-start.5) | collective-permute-done | bytes 278560 | tf_op jit(solution)/shard_map/ppermute | solution.py:175
  39.4 2.9 %collective-permute-start.6 = (bf16[4,136,256]{2,1,0:T(8,128)(2,1)S(1)}, bf16[4,136,256]{2,1,0:T(8,128)(2,1)S(1)}, u32[]{:S(2)}, u32[]{:S(2)}) collective-permute-start(bf16[4,136,256]{2,1,0:T(8,128)(2,1)S(1)} %collective-permute-done.5.refs_2_), channel_id=1, source_target_pairs={{0,32},{8,40},{16,48},{24,56},{32,64},{40,72},{48,80},{56,88},{64,... | collective-permute-start | bytes 835592 | tf_op jit(solution)/shard_map/ppermute | solution.py:175
  47.0 5.2 %shard_map.55 = (f32[128,4]{1,0:T(8,128)}, f32[128,4]{1,0:T(8,128)}, f32[128,512]{1,0:T(8,128)}, f32[128,4]{1,0:T(8,128)}, f32[128,4]{1,0:T(8,128)}, /*index=5*/f32[128,512]{1,0:T(8,128)}) custom-call(bf16[128,512]{1,0:T(8,128)(2,1)} %refs_0_.9, ...), custom_call_target="tpu_custom_call", output_to_operand_aliasing={{0}: (9, {}), {1}: (10, {}), {2}: (11, {}), {3}: (12, {}), ... | custom-call | flops 268435456 | bytes 1327104 | tf_op jit(solution)/shard_map/pallas_call | solution.py:69
  52.7 5.2 %shard_map.56 = (f32[128,4]{1,0:T(8,128)}, f32[128,4]{1,0:T(8,128)}, f32[128,512]{1,0:T(8,128)}, f32[128,4]{1,0:T(8,128)}, f32[128,4]{1,0:T(8,128)}, /*index=5*/f32[128,512]{1,0:T(8,128)}) custom-call(bf16[128,512]{1,0:T(8,128)(2,1)} %refs_0_.9, ...), custom_call_target="tpu_custom_call", output_to_operand_aliasing={{0}: (9, {}), {1}: (10, {}), {2}: (11, {}), {3}: (12, {}), ... | custom-call | flops 268435456 | bytes 1327104 | tf_op jit(solution)/shard_map/pallas_call | solution.py:69
  57.9 2.9 %collective-permute-start.7 = (bf16[4,136,256]{2,1,0:T(8,128)(2,1)S(1)}, bf16[4,136,256]{2,1,0:T(8,128)(2,1)S(1)}, u32[]{:S(2)}, u32[]{:S(2)}) collective-permute-start(bf16[4,136,256]{2,1,0:T(8,128)(2,1)S(1)} %collective-permute-done.6.refs_2_), channel_id=1, source_target_pairs={{0,32},{8,40},{16,48},{24,56},{32,64},{40,72},{48,80},{56,88},{64,... | collective-permute-start | bytes 835592 | tf_op jit(solution)/shard_map/ppermute | solution.py:175
  61.4 5.2 %shard_map.57 = (f32[128,4]{1,0:T(8,128)}, f32[128,4]{1,0:T(8,128)}, f32[128,512]{1,0:T(8,128)}, f32[128,4]{1,0:T(8,128)}, f32[128,4]{1,0:T(8,128)}, /*index=5*/f32[128,512]{1,0:T(8,128)}) custom-call(bf16[128,512]{1,0:T(8,128)(2,1)} %refs_0_.9, ...), custom_call_target="tpu_custom_call", output_to_operand_aliasing={{0}: (9, {}), {1}: (10, {}), {2}: (11, {}), {3}: (12, {}), ... | custom-call | flops 268435456 | bytes 1327104 | tf_op jit(solution)/shard_map/pallas_call | solution.py:69
  67.2 5.2 %shard_map.58 = (f32[128,4]{1,0:T(8,128)}, f32[128,4]{1,0:T(8,128)}, f32[128,512]{1,0:T(8,128)}, f32[128,4]{1,0:T(8,128)}, f32[128,4]{1,0:T(8,128)}, /*index=5*/f32[128,512]{1,0:T(8,128)}) custom-call(bf16[128,512]{1,0:T(8,128)(2,1)} %refs_0_.9, ...), custom_call_target="tpu_custom_call", output_to_operand_aliasing={{0}: (9, {}), {1}: (10, {}), {2}: (11, {}), {3}: (12, {}), ... | custom-call | flops 268435456 | bytes 1327104 | tf_op jit(solution)/shard_map/pallas_call | solution.py:69
  73.0 5.2 %shard_map.59 = (f32[128,4]{1,0:T(8,128)}, f32[128,4]{1,0:T(8,128)}, f32[128,512]{1,0:T(8,128)}, f32[128,4]{1,0:T(8,128)}, f32[128,4]{1,0:T(8,128)}, /*index=5*/f32[128,512]{1,0:T(8,128)}) custom-call(bf16[128,512]{1,0:T(8,128)(2,1)} %refs_0_.9, ...), custom_call_target="tpu_custom_call", output_to_operand_aliasing={{0}: (9, {}), {1}: (10, {}), {2}: (11, {}), {3}: (12, {}), ... | custom-call | flops 268435456 | bytes 1327104 | tf_op jit(solution)/shard_map/pallas_call | solution.py:69
  81.8 1.3 collective-permute-start.9
  83.6 1.0 fusion.2
  84.6 1.3 collective-permute-start.8
  85.9 10.8 %collective-permute-done.9 = f32[128,8]{1,0:T(8,128)S(1)} collective-permute-done((f32[128,8]{1,0:T(8,128)S(1)}, f32[128,8]{1,0:T(8,128)S(1)}, u32[]{:S(2)}, u32[]{:S(2)}) %collective-permute-start.9) | collective-permute-done | bytes 4128 | tf_op jit(solution)/shard_map/ppermute | solution.py:194
  97.3 12.0 %collective-permute-done.8.far_ref = bf16[128,512]{1,0:T(8,128)(2,1)S(1)} collective-permute-done((bf16[128,512]{1,0:T(8,128)(2,1)S(1)}, bf16[128,512]{1,0:T(8,128)(2,1)S(1)}, u32[]{:S(2)}, u32[]{:S(2)}) %collective-permute-start.8) | collective-permute-done | bytes 131104 | tf_op jit(solution)/shard_map/ppermute | solution.py:193
  109.9 4.5 %shard_map.60 = bf16[8,128,512]{2,1,0:T(8,128)(2,1)} custom-call(f32[128,4]{1,0:T(8,128)} %get-tuple-element.83.near_peak_ref, f32[128,4]{1,0:T(8,128)} %get-tuple-element.84.near_total_ref, f32[128,512]{1,0:T(8,128)} %get-tuple-element.85.near_ref, bf16[128,512]{1,0:T(8,128)(2,1)} %copy-done.6, f32[128,8]{1,0:T(8,128)} %broadcast_select_fusion.far_stats_ref, ...), custom_call_target="tpu_custom_call" | custom-call | flops 536870912 | bytes 5242880 | tf_op jit(solution)/shard_map/pallas_call | solution.py:116
  114.5 23.7 %all_to_all.5 = bf16[8,128,512]{2,1,0:T(8,128)(2,1)S(1)} all-to-all(bf16[8,128,512]{2,1,0:T(8,128)(2,1)} %shard_map.60), channel_id=1, replica_groups=mesh['ctx'=64,'tp'=8] {'tp'}, dimensions={0} | all-to-all | bytes 2097152 | tf_op jit(solution)/shard_map/all_to_all | solution.py:201
  (56 shorter events, 19.3 us)
Async XLA Ops:
  1.4 17.8 %collective-permute-start.1 = (bf16[136,256]{1,0:T(8,128)(2,1)S(1)}, bf16[136,256]{1,0:T(8,128)(2,1)S(1)}, u32[]{:S(2)}, u32[]{:S(2)}) collective-permute-start(bf16[136,256]{1,0:T(8,128)(2,1)S(1)} %get-tuple-element.90), channel_id=1, source_target_pairs={{0,8},{8,0},{16,24},{24,16},{32,40},{40,32},{48,56},{56,48},{64,72... | collective-permute-start | bytes 208904 | tf_op jit(solution)/shard_map/ppermute | solution.py:155
  3.4 15.8 %collective-permute-start.2 = (bf16[136,256]{1,0:T(8,128)(2,1)S(1)}, bf16[136,256]{1,0:T(8,128)(2,1)S(1)}, u32[]{:S(2)}, u32[]{:S(2)}) collective-permute-start(bf16[136,256]{1,0:T(8,128)(2,1)S(1)} %get-tuple-element.90), channel_id=1, source_target_pairs={{0,16},{8,24},{16,0},{24,8},{32,48},{40,56},{48,32},{56,40},{64,80... | collective-permute-start | bytes 208904 | tf_op jit(solution)/shard_map/ppermute | solution.py:155
  6.8 12.4 %collective-permute-start.3 = (bf16[136,256]{1,0:T(8,128)(2,1)S(1)}, bf16[136,256]{1,0:T(8,128)(2,1)S(1)}, u32[]{:S(2)}, u32[]{:S(2)}) collective-permute-start(bf16[136,256]{1,0:T(8,128)(2,1)S(1)} %get-tuple-element.90), channel_id=1, source_target_pairs={{0,24},{8,16},{16,8},{24,0},{32,56},{40,48},{48,40},{56,32},{64,88... | collective-permute-start | bytes 208904 | tf_op jit(solution)/shard_map/ppermute | solution.py:155
  10.0 32.3 %collective-permute-start = (bf16[136,512]{1,0:T(8,128)(2,1)S(1)}, bf16[136,512]{1,0:T(8,128)(2,1)S(1)}, u32[]{:S(2)}, u32[]{:S(2)}) collective-permute-start(bf16[136,512]{1,0:T(8,128)(2,1)S(1)} %fusion.3), channel_id=1, source_target_pairs={{160,0},{168,8},{176,16},{184,24},{192,32},{200,40},{208,48},{216,... | collective-permute-start | bytes 417800 | tf_op jit(solution)/shard_map/ppermute | solution.py:151
  19.3 27.7 %copy-start.1 = (bf16[4,136,256]{2,1,0:T(8,128)(2,1)}, bf16[4,136,256]{2,1,0:T(8,128)(2,1)S(1)}, u32[]{:S(2)}) copy-start(bf16[4,136,256]{2,1,0:T(8,128)(2,1)S(1)} %pad_maximum_fusion.refs_2_) | copy-start | bytes 835588
  19.3 10.5 %collective-permute-start.4 = (bf16[4,136,256]{2,1,0:T(8,128)(2,1)S(1)}, bf16[4,136,256]{2,1,0:T(8,128)(2,1)S(1)}, u32[]{:S(2)}, u32[]{:S(2)}) collective-permute-start(bf16[4,136,256]{2,1,0:T(8,128)(2,1)S(1)} %pad_maximum_fusion.refs_2_), channel_id=1, source_target_pairs={{0,32},{8,40},{16,48},{24,56},{32,64},{40,72},{48,80},{56,88},{64,... | collective-permute-start | bytes 835592 | tf_op jit(solution)/shard_map/ppermute | solution.py:175
  29.7 23.0 %copy-start.4 = (bf16[4,136,256]{2,1,0:T(8,128)(2,1)}, bf16[4,136,256]{2,1,0:T(8,128)(2,1)S(1)}, u32[]{:S(2)}) copy-start(bf16[4,136,256]{2,1,0:T(8,128)(2,1)S(1)} %collective-permute-done.4.refs_2_) | copy-start | bytes 835588
  29.7 9.6 %collective-permute-start.5 = (bf16[4,136,256]{2,1,0:T(8,128)(2,1)S(1)}, bf16[4,136,256]{2,1,0:T(8,128)(2,1)S(1)}, u32[]{:S(2)}, u32[]{:S(2)}) collective-permute-start(bf16[4,136,256]{2,1,0:T(8,128)(2,1)S(1)} %collective-permute-done.4.refs_2_), channel_id=1, source_target_pairs={{0,32},{8,40},{16,48},{24,56},{32,64},{40,72},{48,80},{56,88},{64,... | collective-permute-start | bytes 835592 | tf_op jit(solution)/shard_map/ppermute | solution.py:175
  39.4 22.1 %copy-start.3 = (bf16[4,136,256]{2,1,0:T(8,128)(2,1)}, bf16[4,136,256]{2,1,0:T(8,128)(2,1)S(1)}, u32[]{:S(2)}) copy-start(bf16[4,136,256]{2,1,0:T(8,128)(2,1)S(1)} %collective-permute-done.5.refs_2_) | copy-start | bytes 835588
  39.4 18.5 %collective-permute-start.6 = (bf16[4,136,256]{2,1,0:T(8,128)(2,1)S(1)}, bf16[4,136,256]{2,1,0:T(8,128)(2,1)S(1)}, u32[]{:S(2)}, u32[]{:S(2)}) collective-permute-start(bf16[4,136,256]{2,1,0:T(8,128)(2,1)S(1)} %collective-permute-done.5.refs_2_), channel_id=1, source_target_pairs={{0,32},{8,40},{16,48},{24,56},{32,64},{40,72},{48,80},{56,88},{64,... | collective-permute-start | bytes 835592 | tf_op jit(solution)/shard_map/ppermute | solution.py:175
  42.3 4.7 %copy-start = (bf16[136,512]{1,0:T(8,128)(2,1)}, bf16[136,512]{1,0:T(8,128)(2,1)S(1)}, u32[]{:S(2)}) copy-start(bf16[136,512]{1,0:T(8,128)(2,1)S(1)} %collective-permute-done.refs_1_) | copy-start | bytes 417796
  57.9 9.3 %copy-start.2 = (bf16[4,136,256]{2,1,0:T(8,128)(2,1)}, bf16[4,136,256]{2,1,0:T(8,128)(2,1)S(1)}, u32[]{:S(2)}) copy-start(bf16[4,136,256]{2,1,0:T(8,128)(2,1)S(1)} %collective-permute-done.6.refs_2_) | copy-start | bytes 835588
  57.9 14.4 %collective-permute-start.7 = (bf16[4,136,256]{2,1,0:T(8,128)(2,1)S(1)}, bf16[4,136,256]{2,1,0:T(8,128)(2,1)S(1)}, u32[]{:S(2)}, u32[]{:S(2)}) collective-permute-start(bf16[4,136,256]{2,1,0:T(8,128)(2,1)S(1)} %collective-permute-done.6.refs_2_), channel_id=1, source_target_pairs={{0,32},{8,40},{16,48},{24,56},{32,64},{40,72},{48,80},{56,88},{64,... | collective-permute-start | bytes 835592 | tf_op jit(solution)/shard_map/ppermute | solution.py:175
  72.3 0.7 copy-start.5
  81.8 14.8 %collective-permute-start.9 = (f32[128,8]{1,0:T(8,128)S(1)}, f32[128,8]{1,0:T(8,128)S(1)}, u32[]{:S(2)}, u32[]{:S(2)}) collective-permute-start(f32[128,8]{1,0:T(8,128)S(1)} %copy.73), channel_id=1, source_target_pairs={{0,160},{8,168},{16,176},{24,184},{32,192},{40,200},{48,208},{56,2... | collective-permute-start | bytes 12296 | tf_op jit(solution)/shard_map/ppermute | solution.py:194
  84.6 24.7 %collective-permute-start.8 = (bf16[128,512]{1,0:T(8,128)(2,1)S(1)}, bf16[128,512]{1,0:T(8,128)(2,1)S(1)}, u32[]{:S(2)}, u32[]{:S(2)}) collective-permute-start(bf16[128,512]{1,0:T(8,128)(2,1)S(1)} %fusion.2), channel_id=1, source_target_pairs={{0,160},{8,168},{16,176},{24,184},{32,192},{40,200},{48,208},{56,2... | collective-permute-start | bytes 393224 | tf_op jit(solution)/shard_map/ppermute | solution.py:193
  109.3 0.7 copy-start.6

commit v6 on v4

--- a/solution.py
+++ b/solution.py
@@ -163,9 +163,20 @@
     visit_out, visit_stats = partial(
         visiting, blocks, key_pos, key_doc, visit_pos, visit_doc, jnp.bfloat16
     )
+    stats_rows = visit_stats.T
+    parts = []
+    for part in range(3):
+        rounded = lax.reduce_precision(stats_rows, exponent_bits=8, mantissa_bits=7)
+        parts.append(rounded.astype(jnp.bfloat16))
+        stats_rows = stats_rows - rounded
+    parts = jnp.concatenate(parts, axis=0)
+    parts = jnp.pad(parts, ((0, 0), (0, visit_out.shape[1] - rows)))
     ahead = [(s, s + PLANE * far) for s in range(ctx - PLANE * far)]
-    far_out = lax.ppermute(visit_out, "ctx", ahead)
-    far_stats = lax.ppermute(visit_stats, "ctx", ahead)
+    got = lax.ppermute(jnp.concatenate([visit_out, parts], axis=0), "ctx", ahead)
+    far_out = got[:rows]
+    split = visit_stats.shape[1]
+    got_parts = got[rows:, :rows].astype(jnp.float32)
+    far_stats = (got_parts[:split] + got_parts[split:2 * split] + got_parts[2 * split:]).T
 
     query_pos = my_index * rows + offsets_in_shard
     near_out, near_stats = partial(

time: 116 us -> 125 us (1.078)
  waiting for transfers between devices: 27.5 us -> 39.1 us
  starting transfers between devices: 38.4 us -> 33.3 us
    ppermute x2 -> x1, waiting for transfers between devices: 5.65 us -> 17.3 us  [shards(): lax.ppermute(jnp.concatenate([visit_out, parts], axis=0), 'ctx', ahead)]
    ppermute x2 -> x1, starting transfers between devices: 12 us -> 6.78 us  [shards(): lax.ppermute(jnp.concatenate([visit_out, parts], axis=0), 'ctx', ahead)]
  transfers between devices with their start and end apart: 10 -> 9, of which waited for: 5 -> 5; matrix products, arithmetic and copies ran while one was open for 5% -> 4% of each run, Pallas kernels for 5% -> 5%
where the time goes in v6:
time: 125 us; the launch traced here: 124 us
  waiting for transfers between devices  39.1 us (31%)
  starting transfers between devices  33.3 us (27%)
  blocking collectives  23.6 us (19%)
  Pallas kernels  15.7 us (13%)
  other arithmetic  7.67 us (6%)
  local copies, waits for them, and re-layouts  4.44 us (4%)
    all_to_all x1, blocking collectives, shards(): received = lax.all_to_all(chunks, 'tp', 0, 0, tiled=True)  23.6 us
    ppermute x4, waiting for transfers between devices, shards(): current = lax.ppermute(current, 'ctx', forward)  21.8 us
    ppermute x4, starting transfers between devices, shards(): current = lax.ppermute(current, 'ctx', forward)  17.6 us
    ppermute x1, waiting for transfers between devices, shards(): lax.ppermute(jnp.concatenate([visit_out, parts], axis=0), 'ctx', ahead)  17.3 us
    pallas_call x2, Pallas kernels, partial(): pl.pallas_call(partial_kernel, out_shape=(jax.ShapeDtypeStruct((rows, wid...  11.2 us
    ppermute x3, starting transfers between devices, shards(): lax.ppermute(block, 'ctx', [(s, s ^ offset) for s in range(ctx)])  7.59 us
    ppermute x1, starting transfers between devices, shards(): lax.ppermute(jnp.concatenate([visit_out, parts], axis=0), 'ctx', ahead)  6.78 us
    pallas_call x1, Pallas kernels, merge(): pl.pallas_call(merge_kernel, out_shape=jax.ShapeDtypeStruct((pieces, rows...  4.47 us
  transfers between devices with their start and end apart: 9, of which 5 were waited for; matrix products, arithmetic and copies ran while one was open for 4% of the time, Pallas kernels for 5%

profile of v6, /device:TPU:128, one launch (start us, length us, event | category | flops | bytes accessed | tf_op | source)
XLA Modules:
  0.0 124.0 jit_solution(10937895178982415207)
XLA Ops:
  0.7 0.8 fusion.15
  1.4 2.8 %collective-permute-start.2 = (bf16[136,256]{1,0:T(8,128)(2,1)S(1)}, bf16[136,256]{1,0:T(8,128)(2,1)S(1)}, u32[]{:S(2)}, u32[]{:S(2)}) collective-permute-start(bf16[136,256]{1,0:T(8,128)(2,1)S(1)} %get-tuple-element.38), channel_id=1, source_target_pairs={{0,24},{8,16},{16,8},{24,0},{32,56},{40,48},{48,40},{56,32},{64,88... | collective-permute-start | bytes 208904 | tf_op jit(solution)/shard_map/ppermute | solution.py:143
  4.3 2.5 %collective-permute-start.1 = (bf16[136,256]{1,0:T(8,128)(2,1)S(1)}, bf16[136,256]{1,0:T(8,128)(2,1)S(1)}, u32[]{:S(2)}, u32[]{:S(2)}) collective-permute-start(bf16[136,256]{1,0:T(8,128)(2,1)S(1)} %get-tuple-element.38), channel_id=1, source_target_pairs={{0,16},{8,24},{16,0},{24,8},{32,48},{40,56},{48,32},{56,40},{64,80... | collective-permute-start | bytes 208904 | tf_op jit(solution)/shard_map/ppermute | solution.py:143
  6.8 2.3 %collective-permute-start = (bf16[136,256]{1,0:T(8,128)(2,1)S(1)}, bf16[136,256]{1,0:T(8,128)(2,1)S(1)}, u32[]{:S(2)}, u32[]{:S(2)}) collective-permute-start(bf16[136,256]{1,0:T(8,128)(2,1)S(1)} %get-tuple-element.38), channel_id=1, source_target_pairs={{0,8},{8,0},{16,24},{24,16},{32,40},{40,32},{48,56},{56,48},{64,72... | collective-permute-start | bytes 208904 | tf_op jit(solution)/shard_map/ppermute | solution.py:143
  9.1 0.9 fusion.4
  10.0 1.3 %collective-permute-start.7 = (bf16[136,512]{1,0:T(8,128)(2,1)S(1)}, bf16[136,512]{1,0:T(8,128)(2,1)S(1)}, u32[]{:S(2)}, u32[]{:S(2)}) collective-permute-start(bf16[136,512]{1,0:T(8,128)(2,1)S(1)} %fusion.4), channel_id=1, source_target_pairs={{160,0},{168,8},{176,16},{184,24},{192,32},{200,40},{208,48},{216,... | collective-permute-start | bytes 417800 | tf_op jit(solution)/shard_map/ppermute | solution.py:139
  11.4 8.1 %collective-permute-start.3 = (bf16[4,136,256]{2,1,0:T(8,128)(2,1)S(1)}, bf16[4,136,256]{2,1,0:T(8,128)(2,1)S(1)}, u32[]{:S(2)}, u32[]{:S(2)}) collective-permute-start(bf16[4,136,256]{2,1,0:T(8,128)(2,1)S(1)} %pad_maximum_fusion), channel_id=1, source_target_pairs={{0,32},{8,40},{16,48},{24,56},{32,64},{40,72},{48,80},{56,88},{64,... | collective-permute-start | bytes 835592 | tf_op jit(solution)/shard_map/ppermute | solution.py:148
  20.3 5.0 %collective-permute-done.3 = bf16[4,136,256]{2,1,0:T(8,128)(2,1)S(1)} collective-permute-done((bf16[4,136,256]{2,1,0:T(8,128)(2,1)S(1)}, bf16[4,136,256]{2,1,0:T(8,128)(2,1)S(1)}, u32[]{:S(2)}, u32[]{:S(2)}) %collective-permute-start.3) | collective-permute-done | bytes 278560 | tf_op jit(solution)/shard_map/ppermute | solution.py:148
  25.3 4.4 %collective-permute-start.4 = (bf16[4,136,256]{2,1,0:T(8,128)(2,1)S(1)}, bf16[4,136,256]{2,1,0:T(8,128)(2,1)S(1)}, u32[]{:S(2)}, u32[]{:S(2)}) collective-permute-start(bf16[4,136,256]{2,1,0:T(8,128)(2,1)S(1)} %collective-permute-done.3), channel_id=1, source_target_pairs={{0,32},{8,40},{16,48},{24,56},{32,64},{40,72},{48,80},{56,88},{64,... | collective-permute-start | bytes 835592 | tf_op jit(solution)/shard_map/ppermute | solution.py:148
  31.0 1.4 %copy.22.query_doc_ref = s32[128,1]{1,0:T(8,128)} copy(s32[128,1]{0,1:T(1,128)} %bitcast.50) | data formatting | bytes 1024 | tf_op jit(solution)/shard_map/reshape | solution.py:183
  32.4 3.4 %collective-permute-done.4 = bf16[4,136,256]{2,1,0:T(8,128)(2,1)S(1)} collective-permute-done((bf16[4,136,256]{2,1,0:T(8,128)(2,1)S(1)}, bf16[4,136,256]{2,1,0:T(8,128)(2,1)S(1)}, u32[]{:S(2)}, u32[]{:S(2)}) %collective-permute-start.4) | collective-permute-done | bytes 278560 | tf_op jit(solution)/shard_map/ppermute | solution.py:148
  35.8 3.2 %collective-permute-start.5 = (bf16[4,136,256]{2,1,0:T(8,128)(2,1)S(1)}, bf16[4,136,256]{2,1,0:T(8,128)(2,1)S(1)}, u32[]{:S(2)}, u32[]{:S(2)}) collective-permute-start(bf16[4,136,256]{2,1,0:T(8,128)(2,1)S(1)} %collective-permute-done.4), channel_id=1, source_target_pairs={{0,32},{8,40},{16,48},{24,56},{32,64},{40,72},{48,80},{56,88},{64,... | collective-permute-start | bytes 835592 | tf_op jit(solution)/shard_map/ppermute | solution.py:148
  39.8 5.7 %collective-permute-done.5 = bf16[4,136,256]{2,1,0:T(8,128)(2,1)S(1)} collective-permute-done((bf16[4,136,256]{2,1,0:T(8,128)(2,1)S(1)}, bf16[4,136,256]{2,1,0:T(8,128)(2,1)S(1)}, u32[]{:S(2)}, u32[]{:S(2)}) %collective-permute-start.5) | collective-permute-done | bytes 278560 | tf_op jit(solution)/shard_map/ppermute | solution.py:148
  45.5 2.0 %collective-permute-start.6 = (bf16[4,136,256]{2,1,0:T(8,128)(2,1)S(1)}, bf16[4,136,256]{2,1,0:T(8,128)(2,1)S(1)}, u32[]{:S(2)}, u32[]{:S(2)}) collective-permute-start(bf16[4,136,256]{2,1,0:T(8,128)(2,1)S(1)} %collective-permute-done.5), channel_id=1, source_target_pairs={{0,32},{8,40},{16,48},{24,56},{32,64},{40,72},{48,80},{56,88},{64,... | collective-permute-start | bytes 835592 | tf_op jit(solution)/shard_map/ppermute | solution.py:148
  47.5 7.6 %collective-permute-done.6 = bf16[4,136,256]{2,1,0:T(8,128)(2,1)S(1)} collective-permute-done((bf16[4,136,256]{2,1,0:T(8,128)(2,1)S(1)}, bf16[4,136,256]{2,1,0:T(8,128)(2,1)S(1)}, u32[]{:S(2)}, u32[]{:S(2)}) %collective-permute-start.6) | collective-permute-done | bytes 278560 | tf_op jit(solution)/shard_map/ppermute | solution.py:148
  56.2 5.6 %shard_map.56 = (bf16[128,512]{1,0:T(8,128)(2,1)}, f32[128,8]{1,0:T(8,128)}) custom-call(bf16[136,512]{1,0:T(8,128)(2,1)} %copy-done.1, bf16[20,136,256]{2,1,0:T(8,128)(2,1)} %bitcast.46, s32[1,2560]{1,0:T(1,128)} %bitcast.48, s32[1,2560]{1,0:T(1,128)} %fusion.13.key_doc_ref, s32[128,1]{1,0:T(8,128)} %iota_add_fusion.query_pos_ref, s32[128,1]{1,0:T(8,128)} %copy.23.query_doc_ref), custom_call_target="tpu_custom_call" | custom-call | flops 671088640 | bytes 1794048 | tf_op jit(solution)/shard_map/pallas_call | solution.py:57
  61.8 0.9 reduce-precision_convert_fusion.1
  62.7 1.0 copy.24
  63.9 6.8 %collective-permute-start.8 = (bf16[152,512]{0,1:T(8,128)(2,1)S(1)}, bf16[152,512]{0,1:T(8,128)(2,1)S(1)}, u32[]{:S(2)}, u32[]{:S(2)}) collective-permute-start(bf16[152,512]{0,1:T(8,128)(2,1)S(1)} %pad_maximum_fusion.1), channel_id=1, source_target_pairs={{0,160},{8,168},{16,176},{24,184},{32,192},{40,200},{48,208},{56,2... | collective-permute-start | bytes 466952 | tf_op jit(solution)/shard_map/ppermute | solution.py:175
  70.7 5.6 %shard_map.55 = (f32[128,512]{1,0:T(8,128)}, f32[128,8]{1,0:T(8,128)}) custom-call(bf16[128,512]{1,0:T(8,128)(2,1)} %query_ref.1, bf16[20,136,256]{2,1,0:T(8,128)(2,1)} %bitcast.47, s32[1,2560]{1,0:T(1,128)} %bitcast.49, s32[1,2560]{1,0:T(1,128)} %fusion.13.key_doc_ref, s32[128,1]{1,0:T(8,128)} %iota_add_fusion.1.query_pos_ref, s32[128,1]{1,0:T(8,128)} %copy.22.query_doc_ref), custom_call_target="tpu_custom_call" | custom-call | flops 671088640 | bytes 1785856 | tf_op jit(solution)/shard_map/pallas_call | solution.py:57
  76.3 17.3 %collective-permute-done.8 = bf16[152,512]{0,1:T(8,128)(2,1)S(1)} collective-permute-done((bf16[152,512]{0,1:T(8,128)(2,1)S(1)}, bf16[152,512]{0,1:T(8,128)(2,1)S(1)}, u32[]{:S(2)}, u32[]{:S(2)}) %collective-permute-start.8) | collective-permute-done | bytes 155680 | tf_op jit(solution)/shard_map/ppermute | solution.py:175
  95.1 4.5 %shard_map.57 = bf16[8,128,512]{2,1,0:T(8,128)(2,1)} custom-call(f32[128,512]{1,0:T(8,128)} %get-tuple-element.33.near_ref, f32[128,8]{1,0:T(8,128)} %get-tuple-element.34.near_stats_ref, bf16[128,512]{1,0:T(8,128)(2,1)} %copy.25.far_ref, f32[128,8]{1,0:T(8,128)} %fusion.12.far_stats_ref, bf16[512,4096]{1,0:T(8,128)(2,1)} %weight_ref.1), custom_call_target="tpu_custom_call" | custom-call | flops 536870912 | bytes 5242880 | tf_op jit(solution)/shard_map/pallas_call | solution.py:104
  99.6 23.6 %all_to_all.5 = bf16[8,128,512]{2,1,0:T(8,128)(2,1)S(1)} all-to-all(bf16[8,128,512]{2,1,0:T(8,128)(2,1)} %shard_map.57), channel_id=1, replica_groups=mesh['ctx'=64,'tp'=8] {'tp'}, dimensions={0} | all-to-all | bytes 2097152 | tf_op jit(solution)/shard_map/all_to_all | solution.py:191
  123.2 0.8 reduce_sum.12
  (31 shorter events, 6.3 us)
Async XLA Ops:
  1.4 9.9 %collective-permute-start.2 = (bf16[136,256]{1,0:T(8,128)(2,1)S(1)}, bf16[136,256]{1,0:T(8,128)(2,1)S(1)}, u32[]{:S(2)}, u32[]{:S(2)}) collective-permute-start(bf16[136,256]{1,0:T(8,128)(2,1)S(1)} %get-tuple-element.38), channel_id=1, source_target_pairs={{0,24},{8,16},{16,8},{24,0},{32,56},{40,48},{48,40},{56,32},{64,88... | collective-permute-start | bytes 208904 | tf_op jit(solution)/shard_map/ppermute | solution.py:143
  4.3 7.1 %collective-permute-start.1 = (bf16[136,256]{1,0:T(8,128)(2,1)S(1)}, bf16[136,256]{1,0:T(8,128)(2,1)S(1)}, u32[]{:S(2)}, u32[]{:S(2)}) collective-permute-start(bf16[136,256]{1,0:T(8,128)(2,1)S(1)} %get-tuple-element.38), channel_id=1, source_target_pairs={{0,16},{8,24},{16,0},{24,8},{32,48},{40,56},{48,32},{56,40},{64,80... | collective-permute-start | bytes 208904 | tf_op jit(solution)/shard_map/ppermute | solution.py:143
  6.8 4.6 %collective-permute-start = (bf16[136,256]{1,0:T(8,128)(2,1)S(1)}, bf16[136,256]{1,0:T(8,128)(2,1)S(1)}, u32[]{:S(2)}, u32[]{:S(2)}) collective-permute-start(bf16[136,256]{1,0:T(8,128)(2,1)S(1)} %get-tuple-element.38), channel_id=1, source_target_pairs={{0,8},{8,0},{16,24},{24,16},{32,40},{40,32},{48,56},{56,48},{64,72... | collective-permute-start | bytes 208904 | tf_op jit(solution)/shard_map/ppermute | solution.py:143
  10.0 29.0 %collective-permute-start.7 = (bf16[136,512]{1,0:T(8,128)(2,1)S(1)}, bf16[136,512]{1,0:T(8,128)(2,1)S(1)}, u32[]{:S(2)}, u32[]{:S(2)}) collective-permute-start(bf16[136,512]{1,0:T(8,128)(2,1)S(1)} %fusion.4), channel_id=1, source_target_pairs={{160,0},{168,8},{176,16},{184,24},{192,32},{200,40},{208,48},{216,... | collective-permute-start | bytes 417800 | tf_op jit(solution)/shard_map/ppermute | solution.py:139
  11.4 13.9 %collective-permute-start.3 = (bf16[4,136,256]{2,1,0:T(8,128)(2,1)S(1)}, bf16[4,136,256]{2,1,0:T(8,128)(2,1)S(1)}, u32[]{:S(2)}, u32[]{:S(2)}) collective-permute-start(bf16[4,136,256]{2,1,0:T(8,128)(2,1)S(1)} %pad_maximum_fusion), channel_id=1, source_target_pairs={{0,32},{8,40},{16,48},{24,56},{32,64},{40,72},{48,80},{56,88},{64,... | collective-permute-start | bytes 835592 | tf_op jit(solution)/shard_map/ppermute | solution.py:148
  25.3 10.5 %collective-permute-start.4 = (bf16[4,136,256]{2,1,0:T(8,128)(2,1)S(1)}, bf16[4,136,256]{2,1,0:T(8,128)(2,1)S(1)}, u32[]{:S(2)}, u32[]{:S(2)}) collective-permute-start(bf16[4,136,256]{2,1,0:T(8,128)(2,1)S(1)} %collective-permute-done.3), channel_id=1, source_target_pairs={{0,32},{8,40},{16,48},{24,56},{32,64},{40,72},{48,80},{56,88},{64,... | collective-permute-start | bytes 835592 | tf_op jit(solution)/shard_map/ppermute | solution.py:148
  35.8 9.6 %collective-permute-start.5 = (bf16[4,136,256]{2,1,0:T(8,128)(2,1)S(1)}, bf16[4,136,256]{2,1,0:T(8,128)(2,1)S(1)}, u32[]{:S(2)}, u32[]{:S(2)}) collective-permute-start(bf16[4,136,256]{2,1,0:T(8,128)(2,1)S(1)} %collective-permute-done.4), channel_id=1, source_target_pairs={{0,32},{8,40},{16,48},{24,56},{32,64},{40,72},{48,80},{56,88},{64,... | collective-permute-start | bytes 835592 | tf_op jit(solution)/shard_map/ppermute | solution.py:148
  39.0 16.8 %copy-start.1 = (bf16[136,512]{1,0:T(8,128)(2,1)}, bf16[136,512]{1,0:T(8,128)(2,1)S(1)}, u32[]{:S(2)}) copy-start(bf16[136,512]{1,0:T(8,128)(2,1)S(1)} %collective-permute-done.7.query_ref) | copy-start | bytes 417796
  45.5 9.6 %collective-permute-start.6 = (bf16[4,136,256]{2,1,0:T(8,128)(2,1)S(1)}, bf16[4,136,256]{2,1,0:T(8,128)(2,1)S(1)}, u32[]{:S(2)}, u32[]{:S(2)}) collective-permute-start(bf16[4,136,256]{2,1,0:T(8,128)(2,1)S(1)} %collective-permute-done.5), channel_id=1, source_target_pairs={{0,32},{8,40},{16,48},{24,56},{32,64},{40,72},{48,80},{56,88},{64,... | collective-permute-start | bytes 835592 | tf_op jit(solution)/shard_map/ppermute | solution.py:148
  55.1 1.1 copy-start
  63.9 29.7 %collective-permute-start.8 = (bf16[152,512]{0,1:T(8,128)(2,1)S(1)}, bf16[152,512]{0,1:T(8,128)(2,1)S(1)}, u32[]{:S(2)}, u32[]{:S(2)}) collective-permute-start(bf16[152,512]{0,1:T(8,128)(2,1)S(1)} %pad_maximum_fusion.1), channel_id=1, source_target_pairs={{0,160},{8,168},{16,176},{24,184},{32,192},{40,200},{48,208},{56,2... | collective-permute-start | bytes 466952 | tf_op jit(solution)/shard_map/ppermute | solution.py:175

commit v7 on v4

v7 whole, which is shorter than its diff:
```python
import math

import jax
import jax.numpy as jnp
from jax import lax
from jax.experimental import pallas as pl
from jax.experimental.pallas import tpu as pltpu
from jax.sharding import PartitionSpec as P

HEAD_DIM = 128
MAX_DOC = 4224
PLANE = 4
DOC_ROWS = 8
neg_large = -1e30


def partial_kernel(*refs):
    block_ref, key_pos_ref, key_doc_ref = refs[:3]
    sets = len(refs[3:]) // 5
    query_refs = refs[3:3 + sets]
    pos_refs = refs[3 + sets:3 + 2 * sets]
    doc_refs = refs[3 + 2 * sets:3 + 3 * sets]
    out_refs = refs[3 + 3 * sets:3 + 4 * sets]
    stats_refs = refs[3 + 4 * sets:]
    rows = pos_refs[0].shape[0]
    width = out_refs[0].shape[1]
    count, _, packed = block_ref.shape
    head_dim = packed // 2
    heads = width // head_dim
    tokens = count * rows
    key_part = block_ref[:, :rows, :head_dim].reshape(tokens, head_dim)
    value_part = block_ref[:, :rows, head_dim:].reshape(tokens, head_dim)
    key_pos = key_pos_ref[...]
    key_doc = key_doc_ref[...]
    scale = 1.0 / math.sqrt(head_dim)
    for query_ref, pos_ref, doc_ref, out_ref, stats_ref in zip(
        query_refs, pos_refs, doc_refs, out_refs, stats_refs
    ):
        allowed = (key_pos <= pos_ref[...]) & (key_pos >= 0) & (key_doc == doc_ref[...])
        for head in range(heads):
            columns = slice(head * head_dim, (head + 1) * head_dim)
            query = query_ref[:rows, columns]
            scores = lax.dot_general(
                query, key_part, (((1,), (1,)), ((), ())), preferred_element_type=jnp.float32
            )
            scores = scores * scale
            peak = jnp.max(jnp.where(allowed, scores, neg_large), axis=1, keepdims=True)
            weight = jnp.where(allowed, jnp.exp(scores - peak), 0.0)
            total = jnp.sum(weight, axis=1, keepdims=True)
            summed = jnp.dot(
                weight.astype(jnp.bfloat16), value_part, preferred_element_type=jnp.float32
            )
            out_ref[:, columns] = jnp.where(total > 0.0, summed / jnp.maximum(total, 1e-30), 0.0)
            stats_ref[:, head:head + 1] = peak
            stats_ref[:, heads + head:heads + head + 1] = total


def partial(blocks, key_pos, key_doc, queries, positions, docs):
    rows = positions[0].shape[0]
    width = queries[0].shape[1]
    heads = width // HEAD_DIM
    tokens = key_pos.shape[1]
    sets = len(queries)
    vmem = pl.BlockSpec(memory_space=pltpu.VMEM)
    outs = pl.pallas_call(
        partial_kernel,
        out_shape=tuple(
            [jax.ShapeDtypeStruct((rows, width), jnp.float32)] * sets
            + [jax.ShapeDtypeStruct((rows, 2 * heads), jnp.float32)] * sets
        ),
        in_specs=[vmem] * (3 + 3 * sets),
        out_specs=tuple([vmem] * (2 * sets)),
        cost_estimate=pl.CostEstimate(
            flops=4 * sets * rows * tokens * width,
            transcendentals=sets * rows * tokens * heads,
            bytes_accessed=blocks.size * 2 + sets * rows * width * 6,
        ),
    )(blocks, key_pos, key_doc, *queries, *positions, *docs)
    return list(zip(outs[:sets], outs[sets:]))


def combine(first, second):
    out_a, stats_a = first
    out_b, stats_b = second
    rows, width = out_a.shape
    heads = stats_a.shape[1] // 2
    peak = jnp.maximum(stats_a[:, :heads], stats_b[:, :heads])
    share_a = stats_a[:, heads:] * jnp.exp(stats_a[:, :heads] - peak)
    share_b = stats_b[:, heads:] * jnp.exp(stats_b[:, :heads] - peak)
    total = share_a + share_b
    summed = (
        out_a.reshape(rows, heads, -1) * share_a[:, :, None]
        + out_b.astype(jnp.float32).reshape(rows, heads, -1) * share_b[:, :, None]
    )
    out = jnp.where(
        total[:, :, None] > 0.0, summed / jnp.maximum(total, 1e-30)[:, :, None], 0.0
    ).reshape(rows, width)
    return out, jnp.concatenate([peak, total], axis=1)


def pack_rows(out, stats, dtype):
    rows_of = stats.T
    if dtype == jnp.float32:
        parts = rows_of
    else:
        parts = []
        for part in range(3):
            rounded = lax.reduce_precision(rows_of, exponent_bits=8, mantissa_bits=7)
            parts.append(rounded.astype(dtype))
            rows_of = rows_of - rounded
        parts = jnp.concatenate(parts, axis=0)
    parts = jnp.pad(parts.astype(dtype), ((0, 0), (0, out.shape[1] - out.shape[0])))
    return jnp.concatenate([out.astype(dtype), parts], axis=0)


def unpack_rows(packed, rows, split):
    out = packed[:rows]
    parts = packed[rows:, :rows].astype(jnp.float32)
    pieces = parts.shape[0] // split
    stats = parts[:split]
    for piece in range(1, pieces):
        stats = stats + parts[piece * split:(piece + 1) * split]
    return out, stats.T


def merge_kernel(near_ref, near_stats_ref, far_ref, far_stats_ref, weight_ref, out_ref):
    rows, width = near_ref.shape
    heads = near_stats_ref.shape[1] // 2
    head_dim = width // heads
    outputs = []
    for head in range(heads):
        near_peak = near_stats_ref[:, head:head + 1]
        near_total = near_stats_ref[:, heads + head:heads + head + 1]
        far_peak = far_stats_ref[:, head:head + 1]
        far_total = far_stats_ref[:, heads + head:heads + head + 1]
        peak = jnp.maximum(near_peak, far_peak)
        near_share = near_total * jnp.exp(near_peak - peak)
        far_share = far_total * jnp.exp(far_peak - peak)
        columns = slice(head * head_dim, (head + 1) * head_dim)
        summed = (
            near_ref[:, columns].astype(jnp.float32) * near_share
            + far_ref[:, columns].astype(jnp.float32) * far_share
        )
        outputs.append((summed / (near_share + far_share)).astype(jnp.bfloat16))
    attention = jnp.concatenate(outputs, axis=1)
    partial_terms = jnp.dot(attention, weight_ref[...], preferred_element_type=jnp.float32)
    pieces, _, piece_width = out_ref.shape
    for piece in range(pieces):
        out_ref[piece] = partial_terms[:, piece * piece_width:(piece + 1) * piece_width].astype(
            out_ref.dtype
        )


def merge(near, near_stats, far, far_stats, out_weight, pieces):
    rows = near.shape[0]
    width = out_weight.shape[1]
    vmem = pl.BlockSpec(memory_space=pltpu.VMEM)
    return pl.pallas_call(
        merge_kernel,
        out_shape=jax.ShapeDtypeStruct((pieces, rows, width // pieces), jnp.bfloat16),
        in_specs=[vmem] * 5,
        out_specs=vmem,
        cost_estimate=pl.CostEstimate(
            flops=2 * rows * near.shape[1] * width, transcendentals=0,
            bytes_accessed=out_weight.size * 2 + rows * width * 2,
        ),
    )(near, near_stats, far, far_stats, out_weight)


def shards(queries, keys, values, docs, out_weight):
    rows = queries.shape[0]
    head_dim = HEAD_DIM
    heads = queries.shape[1] // head_dim
    ctx = lax.psum(1, "ctx")
    tp = lax.psum(1, "tp")
    my_index = lax.axis_index("ctx")
    plane = my_index // PLANE
    slot = my_index % PLANE
    planes = ctx // PLANE

    shards_back = -(-(MAX_DOC - 1) // rows)
    reach = min(-(-(shards_back + PLANE - 1) // PLANE), planes - 1)
    hops = reach // 2
    far = hops + 1
    step = PLANE * far

    doc_rows = jnp.zeros((DOC_ROWS, 2 * head_dim), jnp.bfloat16)
    doc_rows = doc_rows.at[0, :rows].set(docs.astype(jnp.bfloat16))
    block = jnp.concatenate([jnp.concatenate([keys, values], axis=1), doc_rows], axis=0)

    query_docs = jnp.zeros((DOC_ROWS, queries.shape[1]), jnp.bfloat16)
    query_docs = query_docs.at[0, :rows].set(docs.astype(jnp.bfloat16))
    packed_queries = jnp.concatenate([queries, query_docs], axis=0)
    swap = [(s, s ^ 1) for s in range(ctx)]
    sibling_queries = lax.ppermute(packed_queries, "ctx", swap)
    visit_same = lax.ppermute(packed_queries, "ctx", [(s, s - step) for s in range(step, ctx)])
    visit_other = lax.ppermute(
        packed_queries, "ctx", [(s, (s - step) ^ 1) for s in range(step, ctx)]
    )

    partner = lax.ppermute(block, "ctx", [(s, s ^ 2) for s in range(ctx)])
    current = jnp.stack([block, partner])
    forward = [(s, s + PLANE) for s in range(ctx - PLANE)]
    collected = [current]
    for hop in range(hops):
        current = lax.ppermute(current, "ctx", forward)
        collected.append(current)
    blocks = jnp.stack(collected)

    hop_ids = jnp.arange(hops + 1, dtype=jnp.int32)[:, None, None]
    pair_ids = jnp.arange(2, dtype=jnp.int32)[None, :, None]
    tokens = jnp.arange(rows, dtype=jnp.int32)[None, None, :]
    key_shard = PLANE * (plane - hop_ids) + (slot ^ (2 * pair_ids))
    key_pos = (key_shard * rows + tokens).reshape(1, -1)
    blocks = blocks.reshape(-1, rows + DOC_ROWS, 2 * head_dim)
    key_doc = blocks[:, rows, :rows].astype(jnp.int32).reshape(1, -1)

    offsets_in_shard = jnp.arange(rows, dtype=jnp.int32).reshape(rows, 1)

    def doc_column(packed):
        return packed[rows, :rows].astype(jnp.int32).reshape(rows, 1)

    far_same, far_other = partial(
        blocks, key_pos, key_doc, [visit_same, visit_other],
        [(my_index + step) * rows + offsets_in_shard,
         ((my_index ^ 1) + step) * rows + offsets_in_shard],
        [doc_column(visit_same), doc_column(visit_other)],
    )
    got = lax.ppermute(pack_rows(*far_other, jnp.float32), "ctx", swap)
    far_total = combine(far_same, unpack_rows(got, rows, 2 * heads))
    ahead = [(s, s + step) for s in range(ctx - step)]
    got = lax.ppermute(pack_rows(*far_total, jnp.bfloat16), "ctx", ahead)
    far_out, far_stats = unpack_rows(got, rows, 2 * heads)

    near_own, near_other = partial(
        blocks, key_pos, key_doc, [queries, sibling_queries],
        [my_index * rows + offsets_in_shard, (my_index ^ 1) * rows + offsets_in_shard],
        [docs.reshape(rows, 1), doc_column(sibling_queries)],
    )
    got = lax.ppermute(pack_rows(*near_other, jnp.float32), "ctx", swap)
    near_out, near_stats = combine(near_own, unpack_rows(got, rows, 2 * heads))

    has_far = plane >= far
    lane = jnp.arange(2 * heads, dtype=jnp.int32)[None, :]
    far_stats = jnp.where(has_far, far_stats, jnp.where(lane < heads, neg_large, 0.0))
    chunks = merge(near_out, near_stats, far_out, far_stats, out_weight, tp)

    received = lax.all_to_all(chunks, "tp", 0, 0, tiled=True)
    mixed = jnp.sum(received.astype(jnp.float32), axis=0)
    return mixed.astype(jnp.bfloat16)


def solution(mesh):
    placed = (P("ctx", "tp"), P("ctx", "tp"), P("ctx", "tp"), P("ctx"), P("tp", None))
    return jax.shard_map(
        shards, mesh=mesh, in_specs=placed, out_specs=P("ctx", "tp"), check_vma=False
    )
```

time: 116 us -> 153 us (1.32)
  waiting for transfers between devices: 27.5 us -> 49.4 us
  local copies, waits for them, and re-layouts: 3.32 us -> 10.7 us
  starting transfers between devices: 38.4 us -> 42 us
  other arithmetic: 6.54 us -> 9.58 us
    ppermute x6 -> x7, waiting for transfers between devices: 5.66 us -> 31.5 us  [the longest x1 26.1 us: shards(): got = lax.ppermute(pack_rows(*far_total, jnp.bfloat16), 'ctx', ahead)]
    ppermute x4, starting transfers between devices: 17.6 us -> 24.2 us  [shards(): current = lax.ppermute(current, 'ctx', forward)]
    pallas_call x0 -> x4, local copies, waits for them, and re-layouts: none -> 4.35 us  [partial(): pl.pallas_call(partial_kernel, out_shape=tuple([jax.ShapeDtypeStruct((row...]
    ppermute x4, waiting for transfers between devices: 21.8 us -> 17.9 us  [shards(): current = lax.ppermute(current, 'ctx', forward)]
    ppermute x6 -> x7, starting transfers between devices: 20.8 us -> 17.7 us  [the longest x1 5.49 us: shards(): got = lax.ppermute(pack_rows(*far_total, jnp.bfloat16), 'ctx', ahead)]
    concatenate x0 -> x5, other arithmetic: none -> 2.5 us  [the longest x3 1.79 us: pack_rows(): return jnp.concatenate([out.astype(dtype), parts], axis=0)]
  transfers between devices with their start and end apart: 10 -> 11, of which waited for: 5 -> 6; matrix products, arithmetic and copies ran while one was open for 5% -> 11% of each run, Pallas kernels for 5% -> 8%
where the time goes in v7:
time: 153 us; the launch traced here: 152 us
  waiting for transfers between devices  49.4 us (32%)
  starting transfers between devices  42 us (27%)
  blocking collectives  23.5 us (15%)
  Pallas kernels  16.5 us (11%)
  local copies, waits for them, and re-layouts  10.7 us (7%)
  other arithmetic  9.58 us (6%)
    ppermute x1, waiting for transfers between devices, shards(): got = lax.ppermute(pack_rows(*far_total, jnp.bfloat16), 'ctx', ahead)  26.1 us
    ppermute x4, starting transfers between devices, shards(): current = lax.ppermute(current, 'ctx', forward)  24.2 us
    all_to_all x1, blocking collectives, shards(): received = lax.all_to_all(chunks, 'tp', 0, 0, tiled=True)  23.5 us
    ppermute x4, waiting for transfers between devices, shards(): current = lax.ppermute(current, 'ctx', forward)  17.9 us
    pallas_call x2, Pallas kernels, partial(): pl.pallas_call(partial_kernel, out_shape=tuple([jax.ShapeDtypeStruct((row...  12 us
    ppermute x1, starting transfers between devices, shards(): got = lax.ppermute(pack_rows(*far_total, jnp.bfloat16), 'ctx', ahead)  5.49 us
    pallas_call x1, Pallas kernels, merge(): pl.pallas_call(merge_kernel, out_shape=jax.ShapeDtypeStruct((pieces, rows...  4.5 us
    pallas_call x4, local copies, waits for them, and re-layouts, partial(): pl.pallas_call(partial_kernel, out_shape=tuple([jax.ShapeDtypeStruct((row...  4.35 us
  transfers between devices with their start and end apart: 11, of which 6 were waited for; matrix products, arithmetic and copies ran while one was open for 11% of the time, Pallas kernels for 8%

profile of v7, /device:TPU:128, one launch (start us, length us, event | category | flops | bytes accessed | tf_op | source)
XLA Modules:
  0.0 152.0 jit_solution(8563379489375108174)
XLA Ops:
  1.6 1.3 collective-permute-start.7
  2.9 1.3 collective-permute-start.8
  4.2 1.9 %collective-permute-start.5 = (bf16[136,512]{1,0:T(8,128)(2,1)S(1)}, bf16[136,512]{1,0:T(8,128)(2,1)S(1)}, u32[]{:S(2)}, u32[]{:S(2)}) collective-permute-start(bf16[136,512]{1,0:T(8,128)(2,1)S(1)} %fusion.12), channel_id=1, source_target_pairs={{0,8},{8,0},{16,24},{24,16},{32,40},{40,32},{48,56},{56,48},{64,72... | collective-permute-start | bytes 417800 | tf_op jit(solution)/shard_map/ppermute | solution.py:195
  6.9 3.4 %collective-permute-start = (bf16[136,256]{1,0:T(8,128)(2,1)S(1)}, bf16[136,256]{1,0:T(8,128)(2,1)S(1)}, u32[]{:S(2)}, u32[]{:S(2)}) collective-permute-start(bf16[136,256]{1,0:T(8,128)(2,1)S(1)} %get-tuple-element.56), channel_id=1, source_target_pairs={{0,16},{8,24},{16,0},{24,8},{32,48},{40,56},{48,32},{56,40},{64,80... | collective-permute-start | bytes 208904 | tf_op jit(solution)/shard_map/ppermute | solution.py:201
  11.1 1.4 copy.69.refs_7_
  13.8 8.3 %collective-permute-start.1 = (bf16[2,136,256]{2,1,0:T(8,128)(2,1)S(1)}, bf16[2,136,256]{2,1,0:T(8,128)(2,1)S(1)}, u32[]{:S(2)}, u32[]{:S(2)}) collective-permute-start(bf16[2,136,256]{2,1,0:T(8,128)(2,1)S(1)} %pad_maximum_fusion), channel_id=1, source_target_pairs={{0,32},{8,40},{16,48},{24,56},{32,64},{40,72},{48,80},{56,88},{64,... | collective-permute-start | bytes 417800 | tf_op jit(solution)/shard_map/ppermute | solution.py:206
  22.2 4.1 %collective-permute-done.7.refs_3_ = bf16[136,512]{1,0:T(8,128)(2,1)S(1)} collective-permute-done((bf16[136,512]{1,0:T(8,128)(2,1)S(1)}, bf16[136,512]{1,0:T(8,128)(2,1)S(1)}, u32[]{:S(2)}, u32[]{:S(2)}) %collective-permute-start.7) | collective-permute-done | bytes 139296 | tf_op jit(solution)/shard_map/ppermute | solution.py:196
  27.0 1.3 collective-permute-done.8.refs_4_
  29.0 1.9 %collective-permute-start.2 = (bf16[2,136,256]{2,1,0:T(8,128)(2,1)S(1)}, bf16[2,136,256]{2,1,0:T(8,128)(2,1)S(1)}, u32[]{:S(2)}, u32[]{:S(2)}) collective-permute-start(bf16[2,136,256]{2,1,0:T(8,128)(2,1)S(1)} %collective-permute-done.1), channel_id=1, source_target_pairs={{0,32},{8,40},{16,48},{24,56},{32,64},{40,72},{48,80},{56,88},{64,... | collective-permute-start | bytes 417800 | tf_op jit(solution)/shard_map/ppermute | solution.py:206
  31.0 11.5 %collective-permute-done.2 = bf16[2,136,256]{2,1,0:T(8,128)(2,1)S(1)} collective-permute-done((bf16[2,136,256]{2,1,0:T(8,128)(2,1)S(1)}, bf16[2,136,256]{2,1,0:T(8,128)(2,1)S(1)}, u32[]{:S(2)}, u32[]{:S(2)}) %collective-permute-start.2) | collective-permute-done | bytes 139296 | tf_op jit(solution)/shard_map/ppermute | solution.py:206
  42.5 9.6 %collective-permute-start.3 = (bf16[2,136,256]{2,1,0:T(8,128)(2,1)S(1)}, bf16[2,136,256]{2,1,0:T(8,128)(2,1)S(1)}, u32[]{:S(2)}, u32[]{:S(2)}) collective-permute-start(bf16[2,136,256]{2,1,0:T(8,128)(2,1)S(1)} %collective-permute-done.2), channel_id=1, source_target_pairs={{0,32},{8,40},{16,48},{24,56},{32,64},{40,72},{48,80},{56,88},{64,... | collective-permute-start | bytes 417800 | tf_op jit(solution)/shard_map/ppermute | solution.py:206
  52.2 2.6 %collective-permute-done.3 = bf16[2,136,256]{2,1,0:T(8,128)(2,1)S(1)} collective-permute-done((bf16[2,136,256]{2,1,0:T(8,128)(2,1)S(1)}, bf16[2,136,256]{2,1,0:T(8,128)(2,1)S(1)}, u32[]{:S(2)}, u32[]{:S(2)}) %collective-permute-start.3) | collective-permute-done | bytes 139296 | tf_op jit(solution)/shard_map/ppermute | solution.py:206
  54.8 4.4 %collective-permute-start.4 = (bf16[2,136,256]{2,1,0:T(8,128)(2,1)S(1)}, bf16[2,136,256]{2,1,0:T(8,128)(2,1)S(1)}, u32[]{:S(2)}, u32[]{:S(2)}) collective-permute-start(bf16[2,136,256]{2,1,0:T(8,128)(2,1)S(1)} %collective-permute-done.3), channel_id=1, source_target_pairs={{0,32},{8,40},{16,48},{24,56},{32,64},{40,72},{48,80},{56,88},{64,... | collective-permute-start | bytes 417800 | tf_op jit(solution)/shard_map/ppermute | solution.py:206
  59.2 3.7 %collective-permute-done.4 = bf16[2,136,256]{2,1,0:T(8,128)(2,1)S(1)} collective-permute-done((bf16[2,136,256]{2,1,0:T(8,128)(2,1)S(1)}, bf16[2,136,256]{2,1,0:T(8,128)(2,1)S(1)}, u32[]{:S(2)}, u32[]{:S(2)}) %collective-permute-start.4) | collective-permute-done | bytes 139296 | tf_op jit(solution)/shard_map/ppermute | solution.py:206
  63.8 6.0 %shard_map.56 = (f32[128,512]{1,0:T(8,128)}, f32[128,512]{1,0:T(8,128)}, f32[128,8]{1,0:T(8,128)}, f32[128,8]{1,0:T(8,128)}) custom-call(bf16[10,136,256]{2,1,0:T(8,128)(2,1)} %bitcast.85, s32[1,1280]{1,0:T(1,128)} %bitcast.87, s32[1,1280]{1,0:T(1,128)} %fusion.17.refs_2_, bf16[136,512]{1,0:T(8,128)(2,1)} %copy-done.4, bf16[136,512]{1,0:T(8,128)(2,1)} %copy-done.5, ...), custom_call_target="tpu_custom_call" | custom-call | flops 671088640 | bytes 1482752 | tf_op jit(solution)/shard_map/pallas_call | solution.py:65
  69.8 1.1 copy.79
  71.8 1.9 %collective-permute-start.9 = (f32[136,512]{0,1:T(8,128)S(1)}, f32[136,512]{0,1:T(8,128)S(1)}, u32[]{:S(2)}, u32[]{:S(2)}) collective-permute-start(f32[136,512]{0,1:T(8,128)S(1)} %select_maximum_fusion), channel_id=1, source_target_pairs={{0,8},{8,0},{16,24},{24,16},{32,40},{40,32},{48,56},{56,48},{64,72... | collective-permute-start | bytes 835592 | tf_op jit(solution)/shard_map/ppermute | solution.py:229
  75.6 6.0 %shard_map.55 = (f32[128,512]{1,0:T(8,128)}, f32[128,512]{1,0:T(8,128)}, f32[128,8]{1,0:T(8,128)}, f32[128,8]{1,0:T(8,128)}) custom-call(bf16[10,136,256]{2,1,0:T(8,128)(2,1)} %bitcast.86, s32[1,1280]{1,0:T(1,128)} %bitcast.88, s32[1,1280]{1,0:T(1,128)} %fusion.17.refs_2_, bf16[128,512]{1,0:T(8,128)(2,1)} %refs_3_.1, bf16[136,512]{1,0:T(8,128)(2,1)} %copy-done.3, ...), custom_call_target="tpu_custom_call" | custom-call | flops 671088640 | bytes 1482752 | tf_op jit(solution)/shard_map/pallas_call | solution.py:65
  81.6 1.1 copy.71
  83.6 2.4 %collective-permute-start.6 = (f32[136,512]{0,1:T(8,128)S(1)}, f32[136,512]{0,1:T(8,128)S(1)}, u32[]{:S(2)}, u32[]{:S(2)}) collective-permute-start(f32[136,512]{0,1:T(8,128)S(1)} %fusion.1), channel_id=1, source_target_pairs={{0,8},{8,0},{16,24},{24,16},{32,40},{40,32},{48,56},{56,48},{64,72... | collective-permute-start | bytes 835592 | tf_op jit(solution)/shard_map/ppermute | solution.py:240
  88.0 5.5 %collective-permute-start.10 = (bf16[152,512]{0,1:T(8,128)(2,1)S(1)}, bf16[152,512]{0,1:T(8,128)(2,1)S(1)}, u32[]{:S(2)}, u32[]{:S(2)}) collective-permute-start(bf16[152,512]{0,1:T(8,128)(2,1)S(1)} %fusion.4), channel_id=1, source_target_pairs={{0,160},{8,168},{16,176},{24,184},{32,192},{40,200},{48,208},{56,2... | collective-permute-start | bytes 466952 | tf_op jit(solution)/shard_map/ppermute | solution.py:232
  95.6 26.1 %collective-permute-done.10 = bf16[152,512]{0,1:T(8,128)(2,1)S(1)} collective-permute-done((bf16[152,512]{0,1:T(8,128)(2,1)S(1)}, bf16[152,512]{0,1:T(8,128)(2,1)S(1)}, u32[]{:S(2)}, u32[]{:S(2)}) %collective-permute-start.10) | collective-permute-done | bytes 155680 | tf_op jit(solution)/shard_map/ppermute | solution.py:232
  123.2 4.5 %shard_map.57 = bf16[8,128,512]{2,1,0:T(8,128)(2,1)} custom-call(f32[128,512]{1,0:T(8,128)} %copy.88.near_ref, f32[128,8]{1,0:T(8,128)} %pad_maximum_fusion.1.near_stats_ref, bf16[128,512]{1,0:T(8,128)(2,1)} %copy.89.far_ref, f32[128,8]{1,0:T(8,128)} %fusion.16.far_stats_ref, bf16[512,4096]{1,0:T(8,128)(2,1)} %weight_ref.1), custom_call_target="tpu_custom_call" | custom-call | flops 536870912 | bytes 5242880 | tf_op jit(solution)/shard_map/pallas_call | solution.py:158
  127.7 23.5 %all_to_all.5 = bf16[8,128,512]{2,1,0:T(8,128)(2,1)S(1)} all-to-all(bf16[8,128,512]{2,1,0:T(8,128)(2,1)} %shard_map.57), channel_id=1, replica_groups=mesh['ctx'=64,'tp'=8] {'tp'}, dimensions={0} | all-to-all | bytes 2097152 | tf_op jit(solution)/shard_map/all_to_all | solution.py:248
  (73 shorter events, 16.7 us)
Async XLA Ops:
  1.6 24.7 %collective-permute-start.7 = (bf16[136,512]{1,0:T(8,128)(2,1)S(1)}, bf16[136,512]{1,0:T(8,128)(2,1)S(1)}, u32[]{:S(2)}, u32[]{:S(2)}) collective-permute-start(bf16[136,512]{1,0:T(8,128)(2,1)S(1)} %fusion.12), channel_id=1, source_target_pairs={{160,0},{168,8},{176,16},{184,24},{192,32},{200,40},{208,48},{216,... | collective-permute-start | bytes 417800 | tf_op jit(solution)/shard_map/ppermute | solution.py:196
  2.9 25.4 %collective-permute-start.8 = (bf16[136,512]{1,0:T(8,128)(2,1)S(1)}, bf16[136,512]{1,0:T(8,128)(2,1)S(1)}, u32[]{:S(2)}, u32[]{:S(2)}) collective-permute-start(bf16[136,512]{1,0:T(8,128)(2,1)S(1)} %fusion.12), channel_id=1, source_target_pairs={{160,8},{168,0},{176,24},{184,16},{192,40},{200,32},{208,56},{216,... | collective-permute-start | bytes 417800 | tf_op jit(solution)/shard_map/ppermute | solution.py:197
  4.2 69.5 %collective-permute-start.5 = (bf16[136,512]{1,0:T(8,128)(2,1)S(1)}, bf16[136,512]{1,0:T(8,128)(2,1)S(1)}, u32[]{:S(2)}, u32[]{:S(2)}) collective-permute-start(bf16[136,512]{1,0:T(8,128)(2,1)S(1)} %fusion.12), channel_id=1, source_target_pairs={{0,8},{8,0},{16,24},{24,16},{32,40},{40,32},{48,56},{56,48},{64,72... | collective-permute-start | bytes 417800 | tf_op jit(solution)/shard_map/ppermute | solution.py:195
  6.9 6.9 %collective-permute-start = (bf16[136,256]{1,0:T(8,128)(2,1)S(1)}, bf16[136,256]{1,0:T(8,128)(2,1)S(1)}, u32[]{:S(2)}, u32[]{:S(2)}) collective-permute-start(bf16[136,256]{1,0:T(8,128)(2,1)S(1)} %get-tuple-element.56), channel_id=1, source_target_pairs={{0,16},{8,24},{16,0},{24,8},{32,48},{40,56},{48,32},{56,40},{64,80... | collective-permute-start | bytes 208904 | tf_op jit(solution)/shard_map/ppermute | solution.py:201
  13.8 15.2 %collective-permute-start.1 = (bf16[2,136,256]{2,1,0:T(8,128)(2,1)S(1)}, bf16[2,136,256]{2,1,0:T(8,128)(2,1)S(1)}, u32[]{:S(2)}, u32[]{:S(2)}) collective-permute-start(bf16[2,136,256]{2,1,0:T(8,128)(2,1)S(1)} %pad_maximum_fusion), channel_id=1, source_target_pairs={{0,32},{8,40},{16,48},{24,56},{32,64},{40,72},{48,80},{56,88},{64,... | collective-permute-start | bytes 417800 | tf_op jit(solution)/shard_map/ppermute | solution.py:206
  26.3 37.3 %copy-start.4 = (bf16[136,512]{1,0:T(8,128)(2,1)}, bf16[136,512]{1,0:T(8,128)(2,1)S(1)}, u32[]{:S(2)}) copy-start(bf16[136,512]{1,0:T(8,128)(2,1)S(1)} %collective-permute-done.7.refs_3_) | copy-start | bytes 417796
  28.3 35.3 %copy-start.5 = (bf16[136,512]{1,0:T(8,128)(2,1)}, bf16[136,512]{1,0:T(8,128)(2,1)S(1)}, u32[]{:S(2)}) copy-start(bf16[136,512]{1,0:T(8,128)(2,1)S(1)} %collective-permute-done.8.refs_4_) | copy-start | bytes 417796
  29.0 13.5 %collective-permute-start.2 = (bf16[2,136,256]{2,1,0:T(8,128)(2,1)S(1)}, bf16[2,136,256]{2,1,0:T(8,128)(2,1)S(1)}, u32[]{:S(2)}, u32[]{:S(2)}) collective-permute-start(bf16[2,136,256]{2,1,0:T(8,128)(2,1)S(1)} %collective-permute-done.1), channel_id=1, source_target_pairs={{0,32},{8,40},{16,48},{24,56},{32,64},{40,72},{48,80},{56,88},{64,... | collective-permute-start | bytes 417800 | tf_op jit(solution)/shard_map/ppermute | solution.py:206
  42.5 12.3 %collective-permute-start.3 = (bf16[2,136,256]{2,1,0:T(8,128)(2,1)S(1)}, bf16[2,136,256]{2,1,0:T(8,128)(2,1)S(1)}, u32[]{:S(2)}, u32[]{:S(2)}) collective-permute-start(bf16[2,136,256]{2,1,0:T(8,128)(2,1)S(1)} %collective-permute-done.2), channel_id=1, source_target_pairs={{0,32},{8,40},{16,48},{24,56},{32,64},{40,72},{48,80},{56,88},{64,... | collective-permute-start | bytes 417800 | tf_op jit(solution)/shard_map/ppermute | solution.py:206
  54.8 8.1 %collective-permute-start.4 = (bf16[2,136,256]{2,1,0:T(8,128)(2,1)S(1)}, bf16[2,136,256]{2,1,0:T(8,128)(2,1)S(1)}, u32[]{:S(2)}, u32[]{:S(2)}) collective-permute-start(bf16[2,136,256]{2,1,0:T(8,128)(2,1)S(1)} %collective-permute-done.3), channel_id=1, source_target_pairs={{0,32},{8,40},{16,48},{24,56},{32,64},{40,72},{48,80},{56,88},{64,... | collective-permute-start | bytes 417800 | tf_op jit(solution)/shard_map/ppermute | solution.py:206
  62.9 0.9 copy-start.2
  69.8 17.3 %copy-start.1 = (f32[128,8]{1,0:T(8,128)S(1)}, f32[128,8]{1,0:T(8,128)}, u32[]{:S(2)}) copy-start(f32[128,8]{1,0:T(8,128)} %get-tuple-element.41) | copy-start | bytes 12292
  71.8 15.3 %collective-permute-start.9 = (f32[136,512]{0,1:T(8,128)S(1)}, f32[136,512]{0,1:T(8,128)S(1)}, u32[]{:S(2)}, u32[]{:S(2)}) collective-permute-start(f32[136,512]{0,1:T(8,128)S(1)} %select_maximum_fusion), channel_id=1, source_target_pairs={{0,8},{8,0},{16,24},{24,16},{32,40},{40,32},{48,56},{56,48},{64,72... | collective-permute-start | bytes 835592 | tf_op jit(solution)/shard_map/ppermute | solution.py:229
  73.7 1.8 %copy-start.3 = (bf16[136,512]{1,0:T(8,128)(2,1)}, bf16[136,512]{1,0:T(8,128)(2,1)S(1)}, u32[]{:S(2)}) copy-start(bf16[136,512]{1,0:T(8,128)(2,1)S(1)} %collective-permute-done.5.refs_4_) | copy-start | bytes 417796
  81.6 11.9 %copy-start = (f32[128,8]{1,0:T(8,128)S(1)}, f32[128,8]{1,0:T(8,128)}, u32[]{:S(2)}) copy-start(f32[128,8]{1,0:T(8,128)} %get-tuple-element.37) | copy-start | bytes 12292
  83.6 9.9 %collective-permute-start.6 = (f32[136,512]{0,1:T(8,128)S(1)}, f32[136,512]{0,1:T(8,128)S(1)}, u32[]{:S(2)}, u32[]{:S(2)}) collective-permute-start(f32[136,512]{0,1:T(8,128)S(1)} %fusion.1), channel_id=1, source_target_pairs={{0,8},{8,0},{16,24},{24,16},{32,40},{40,32},{48,56},{56,48},{64,72... | collective-permute-start | bytes 835592 | tf_op jit(solution)/shard_map/ppermute | solution.py:240
  88.0 33.7 %collective-permute-start.10 = (bf16[152,512]{0,1:T(8,128)(2,1)S(1)}, bf16[152,512]{0,1:T(8,128)(2,1)S(1)}, u32[]{:S(2)}, u32[]{:S(2)}) collective-permute-start(bf16[152,512]{0,1:T(8,128)(2,1)S(1)} %fusion.4), channel_id=1, source_target_pairs={{0,160},{8,168},{16,176},{24,184},{32,192},{40,200},{48,208},{56,2... | collective-permute-start | bytes 466952 | tf_op jit(solution)/shard_map/ppermute | solution.py:232

commit v8 on v4

--- a/solution.py
+++ b/solution.py
@@ -136,7 +136,6 @@
     query_docs = query_docs.at[0, :rows].set(docs.astype(jnp.bfloat16))
     packed_queries = jnp.concatenate([queries, query_docs], axis=0)
     back = [(s, s - PLANE * far) for s in range(PLANE * far, ctx)]
-    visiting = lax.ppermute(packed_queries, "ctx", back)
 
     plane_blocks = [block]
     for offset in range(1, PLANE):
@@ -146,6 +145,9 @@
     collected = [current]
     for hop in range(hops):
         current = lax.ppermute(current, "ctx", forward)
+        if hop == 0:
+            packed_queries, current = lax.optimization_barrier((packed_queries, current))
+            visiting = lax.ppermute(packed_queries, "ctx", back)
         collected.append(current)
     blocks = jnp.stack(collected)
 

time: 116 us -> 124 us (1.069)
  waiting for transfers between devices: 27.5 us -> 48.5 us
  starting transfers between devices: 38.4 us -> 25.8 us
    ppermute x1, waiting for transfers between devices: 0.01 us -> 12.9 us  [shards(): far_out = lax.ppermute(visit_out, 'ctx', ahead)]
    ppermute x1, waiting for transfers between devices: 0.01 us -> 9.18 us  [shards(): visiting = lax.ppermute(packed_queries, 'ctx', back)]
    ppermute x4, starting transfers between devices: 17.6 us -> 10.2 us  [shards(): current = lax.ppermute(current, 'ctx', forward)]
    ppermute x1, waiting for transfers between devices: 5.65 us -> 0.01 us  [shards(): far_stats = lax.ppermute(visit_stats, 'ctx', ahead)]
    ppermute x1, starting transfers between devices: 6.77 us -> 1.92 us  [shards(): far_out = lax.ppermute(visit_out, 'ctx', ahead)]
    ppermute x3, waiting for transfers between devices: 0.01 us -> 2.73 us  [shards(): lax.ppermute(block, 'ctx', [(s, s ^ offset) for s in range(ctx)])]
    ppermute x4, waiting for transfers between devices: 21.8 us -> 23.7 us  [shards(): current = lax.ppermute(current, 'ctx', forward)]
  transfers between devices with their start and end apart: 10 -> 10, of which waited for: 5 -> 6; matrix products, arithmetic and copies ran while one was open for 5% -> 5% of each run, Pallas kernels for 5% -> 5%
where the time goes in v8:
time: 124 us; the launch traced here: 123 us
  waiting for transfers between devices  48.5 us (39%)
  starting transfers between devices  25.8 us (21%)
  blocking collectives  23.2 us (19%)
  Pallas kernels  15.7 us (13%)
  other arithmetic  6.53 us (5%)
  local copies, waits for them, and re-layouts  3.33 us (3%)
    ppermute x4, waiting for transfers between devices, shards(): current = lax.ppermute(current, 'ctx', forward)  23.7 us
    all_to_all x1, blocking collectives, shards(): received = lax.all_to_all(chunks, 'tp', 0, 0, tiled=True)  23.2 us
    ppermute x1, waiting for transfers between devices, shards(): far_out = lax.ppermute(visit_out, 'ctx', ahead)  12.9 us
    pallas_call x2, Pallas kernels, partial(): pl.pallas_call(partial_kernel, out_shape=(jax.ShapeDtypeStruct((rows, wid...  11.2 us
    ppermute x4, starting transfers between devices, shards(): current = lax.ppermute(current, 'ctx', forward)  10.2 us
    ppermute x1, waiting for transfers between devices, shards(): visiting = lax.ppermute(packed_queries, 'ctx', back)  9.18 us
    ppermute x3, starting transfers between devices, shards(): lax.ppermute(block, 'ctx', [(s, s ^ offset) for s in range(ctx)])  7.59 us
    ppermute x1, starting transfers between devices, shards(): far_stats = lax.ppermute(visit_stats, 'ctx', ahead)  4.74 us
  transfers between devices with their start and end apart: 10, of which 6 were waited for; matrix products, arithmetic and copies ran while one was open for 5% of the time, Pallas kernels for 5%

profile of v8, /device:TPU:128, one launch (start us, length us, event | category | flops | bytes accessed | tf_op | source)
XLA Modules:
  0.0 123.2 jit_solution(5884975570222246593)
XLA Ops:
  0.7 0.8 fusion.6
  1.4 1.9 %collective-permute-start = (bf16[136,256]{1,0:T(8,128)(2,1)S(1)}, bf16[136,256]{1,0:T(8,128)(2,1)S(1)}, u32[]{:S(2)}, u32[]{:S(2)}) collective-permute-start(bf16[136,256]{1,0:T(8,128)(2,1)S(1)} %get-tuple-element.42), channel_id=1, source_target_pairs={{0,8},{8,0},{16,24},{24,16},{32,40},{40,32},{48,56},{56,48},{64,72... | collective-permute-start | bytes 208904 | tf_op jit(solution)/shard_map/ppermute | solution.py:142
  3.4 3.4 %collective-permute-start.1 = (bf16[136,256]{1,0:T(8,128)(2,1)S(1)}, bf16[136,256]{1,0:T(8,128)(2,1)S(1)}, u32[]{:S(2)}, u32[]{:S(2)}) collective-permute-start(bf16[136,256]{1,0:T(8,128)(2,1)S(1)} %get-tuple-element.42), channel_id=1, source_target_pairs={{0,16},{8,24},{16,0},{24,8},{32,48},{40,56},{48,32},{56,40},{64,80... | collective-permute-start | bytes 208904 | tf_op jit(solution)/shard_map/ppermute | solution.py:142
  6.8 2.3 %collective-permute-start.2 = (bf16[136,256]{1,0:T(8,128)(2,1)S(1)}, bf16[136,256]{1,0:T(8,128)(2,1)S(1)}, u32[]{:S(2)}, u32[]{:S(2)}) collective-permute-start(bf16[136,256]{1,0:T(8,128)(2,1)S(1)} %get-tuple-element.42), channel_id=1, source_target_pairs={{0,24},{8,16},{16,8},{24,0},{32,56},{40,48},{48,40},{56,32},{64,88... | collective-permute-start | bytes 208904 | tf_op jit(solution)/shard_map/ppermute | solution.py:142
  9.2 0.9 fusion.1
  10.1 2.7 %collective-permute-done.2 = bf16[136,256]{1,0:T(8,128)(2,1)S(1)} collective-permute-done((bf16[136,256]{1,0:T(8,128)(2,1)S(1)}, bf16[136,256]{1,0:T(8,128)(2,1)S(1)}, u32[]{:S(2)}, u32[]{:S(2)}) %collective-permute-start.2) | collective-permute-done | bytes 69664 | tf_op jit(solution)/shard_map/ppermute | solution.py:142
  12.9 3.8 %collective-permute-start.3 = (bf16[4,136,256]{2,1,0:T(8,128)(2,1)S(1)}, bf16[4,136,256]{2,1,0:T(8,128)(2,1)S(1)}, u32[]{:S(2)}, u32[]{:S(2)}) collective-permute-start(bf16[4,136,256]{2,1,0:T(8,128)(2,1)S(1)} %pad_maximum_fusion), channel_id=1, source_target_pairs={{0,32},{8,40},{16,48},{24,56},{32,64},{40,72},{48,80},{56,88},{64,... | collective-permute-start | bytes 835592 | tf_op jit(solution)/shard_map/ppermute | solution.py:147
  18.0 6.7 %collective-permute-done.3 = bf16[4,136,256]{2,1,0:T(8,128)(2,1)S(1)} collective-permute-done((bf16[4,136,256]{2,1,0:T(8,128)(2,1)S(1)}, bf16[4,136,256]{2,1,0:T(8,128)(2,1)S(1)}, u32[]{:S(2)}, u32[]{:S(2)}) %collective-permute-start.3) | collective-permute-done | bytes 278560 | tf_op jit(solution)/shard_map/ppermute | solution.py:147
  24.7 2.6 %collective-permute-start.4 = (bf16[4,136,256]{2,1,0:T(8,128)(2,1)S(1)}, bf16[4,136,256]{2,1,0:T(8,128)(2,1)S(1)}, u32[]{:S(2)}, u32[]{:S(2)}) collective-permute-start(bf16[4,136,256]{2,1,0:T(8,128)(2,1)S(1)} %collective-permute-done.3), channel_id=1, source_target_pairs={{0,32},{8,40},{16,48},{24,56},{32,64},{40,72},{48,80},{56,88},{64,... | collective-permute-start | bytes 835592 | tf_op jit(solution)/shard_map/ppermute | solution.py:147
  27.3 1.4 %copy.6.query_doc_ref = s32[128,1]{1,0:T(8,128)} copy(s32[128,1]{0,1:T(1,128)} %bitcast.41) | data formatting | bytes 1024 | tf_op jit(solution)/shard_map/reshape | solution.py:174
  29.4 1.3 %collective-permute-start.7 = (bf16[136,512]{1,0:T(8,128)(2,1)S(1)}, bf16[136,512]{1,0:T(8,128)(2,1)S(1)}, u32[]{:S(2)}, u32[]{:S(2)}) collective-permute-start(bf16[136,512]{1,0:T(8,128)(2,1)S(1)} %fusion.1), channel_id=1, source_target_pairs={{160,0},{168,8},{176,16},{184,24},{192,32},{200,40},{208,48},{216,... | collective-permute-start | bytes 417800 | tf_op jit(solution)/shard_map/ppermute | solution.py:150
  30.7 5.0 %collective-permute-done.4 = bf16[4,136,256]{2,1,0:T(8,128)(2,1)S(1)} collective-permute-done((bf16[4,136,256]{2,1,0:T(8,128)(2,1)S(1)}, bf16[4,136,256]{2,1,0:T(8,128)(2,1)S(1)}, u32[]{:S(2)}, u32[]{:S(2)}) %collective-permute-start.4) | collective-permute-done | bytes 278560 | tf_op jit(solution)/shard_map/ppermute | solution.py:147
  35.6 1.9 %collective-permute-start.5 = (bf16[4,136,256]{2,1,0:T(8,128)(2,1)S(1)}, bf16[4,136,256]{2,1,0:T(8,128)(2,1)S(1)}, u32[]{:S(2)}, u32[]{:S(2)}) collective-permute-start(bf16[4,136,256]{2,1,0:T(8,128)(2,1)S(1)} %collective-permute-done.4), channel_id=1, source_target_pairs={{0,32},{8,40},{16,48},{24,56},{32,64},{40,72},{48,80},{56,88},{64,... | collective-permute-start | bytes 835592 | tf_op jit(solution)/shard_map/ppermute | solution.py:147
  37.6 9.2 %collective-permute-done.7.query_ref = bf16[136,512]{1,0:T(8,128)(2,1)S(1)} collective-permute-done((bf16[136,512]{1,0:T(8,128)(2,1)S(1)}, bf16[136,512]{1,0:T(8,128)(2,1)S(1)}, u32[]{:S(2)}, u32[]{:S(2)}) %collective-permute-start.7) | collective-permute-done | bytes 139296 | tf_op jit(solution)/shard_map/ppermute | solution.py:150
  47.5 1.9 %collective-permute-start.6 = (bf16[4,136,256]{2,1,0:T(8,128)(2,1)S(1)}, bf16[4,136,256]{2,1,0:T(8,128)(2,1)S(1)}, u32[]{:S(2)}, u32[]{:S(2)}) collective-permute-start(bf16[4,136,256]{2,1,0:T(8,128)(2,1)S(1)} %collective-permute-done.5), channel_id=1, source_target_pairs={{0,32},{8,40},{16,48},{24,56},{32,64},{40,72},{48,80},{56,88},{64,... | collective-permute-start | bytes 835592 | tf_op jit(solution)/shard_map/ppermute | solution.py:147
  49.5 12.1 %collective-permute-done.6 = bf16[4,136,256]{2,1,0:T(8,128)(2,1)S(1)} collective-permute-done((bf16[4,136,256]{2,1,0:T(8,128)(2,1)S(1)}, bf16[4,136,256]{2,1,0:T(8,128)(2,1)S(1)}, u32[]{:S(2)}, u32[]{:S(2)}) %collective-permute-start.6) | collective-permute-done | bytes 278560 | tf_op jit(solution)/shard_map/ppermute | solution.py:147
  62.7 5.6 %shard_map.56 = (bf16[128,512]{1,0:T(8,128)(2,1)}, f32[128,8]{1,0:T(8,128)}) custom-call(bf16[136,512]{1,0:T(8,128)(2,1)} %copy-done.2, bf16[20,136,256]{2,1,0:T(8,128)(2,1)} %bitcast.37, s32[1,2560]{1,0:T(1,128)} %bitcast.39, s32[1,2560]{1,0:T(1,128)} %fusion.4.key_doc_ref, s32[128,1]{1,0:T(8,128)} %iota_add_fusion.query_pos_ref, s32[128,1]{1,0:T(8,128)} %copy.7.query_doc_ref), custom_call_target="tpu_custom_call" | custom-call | flops 671088640 | bytes 1794048 | tf_op jit(solution)/shard_map/pallas_call | solution.py:57
  68.3 4.7 %collective-permute-start.9 = (f32[128,8]{1,0:T(8,128)}, f32[128,8]{1,0:T(8,128)S(1)}, u32[]{:S(2)}, u32[]{:S(2)}) collective-permute-start(f32[128,8]{1,0:T(8,128)} %get-tuple-element.40), channel_id=1, source_target_pairs={{0,160},{8,168},{16,176},{24,184},{32,192},{40,200},{48,208},{56,2... | collective-permute-start | bytes 12296 | tf_op jit(solution)/shard_map/ppermute | solution.py:170
  73.0 1.9 %collective-permute-start.8 = (bf16[128,512]{1,0:T(8,128)(2,1)}, bf16[128,512]{1,0:T(8,128)(2,1)S(1)}, u32[]{:S(2)}, u32[]{:S(2)}) collective-permute-start(bf16[128,512]{1,0:T(8,128)(2,1)} %get-tuple-element.39), channel_id=1, source_target_pairs={{0,160},{8,168},{16,176},{24,184},{32,192},{40,200},{48,208},{56,2... | collective-permute-start | bytes 393224 | tf_op jit(solution)/shard_map/ppermute | solution.py:169
  75.0 5.6 %shard_map.55 = (f32[128,512]{1,0:T(8,128)}, f32[128,8]{1,0:T(8,128)}) custom-call(bf16[128,512]{1,0:T(8,128)(2,1)} %query_ref.1, bf16[20,136,256]{2,1,0:T(8,128)(2,1)} %bitcast.38, s32[1,2560]{1,0:T(1,128)} %bitcast.40, s32[1,2560]{1,0:T(1,128)} %fusion.4.key_doc_ref, s32[128,1]{1,0:T(8,128)} %iota_add_fusion.1.query_pos_ref, s32[128,1]{1,0:T(8,128)} %copy.6.query_doc_ref), custom_call_target="tpu_custom_call" | custom-call | flops 671088640 | bytes 1785856 | tf_op jit(solution)/shard_map/pallas_call | solution.py:57
  81.2 12.9 %collective-permute-done.8.far_ref = bf16[128,512]{1,0:T(8,128)(2,1)S(1)} collective-permute-done((bf16[128,512]{1,0:T(8,128)(2,1)}, bf16[128,512]{1,0:T(8,128)(2,1)S(1)}, u32[]{:S(2)}, u32[]{:S(2)}) %collective-permute-start.8) | collective-permute-done | bytes 131104 | tf_op jit(solution)/shard_map/ppermute | solution.py:169
  94.7 4.5 %shard_map.57 = bf16[8,128,512]{2,1,0:T(8,128)(2,1)} custom-call(f32[128,512]{1,0:T(8,128)} %get-tuple-element.36.near_ref, f32[128,8]{1,0:T(8,128)} %get-tuple-element.37.near_stats_ref, bf16[128,512]{1,0:T(8,128)(2,1)} %copy-done, f32[128,8]{1,0:T(8,128)} %broadcast_select_fusion.far_stats_ref, bf16[512,4096]{1,0:T(8,128)(2,1)} %weight_ref.1), custom_call_target="tpu_custom_call" | custom-call | flops 536870912 | bytes 5242880 | tf_op jit(solution)/shard_map/pallas_call | solution.py:104
  99.2 23.2 %all_to_all.5 = bf16[8,128,512]{2,1,0:T(8,128)(2,1)S(1)} all-to-all(bf16[8,128,512]{2,1,0:T(8,128)(2,1)} %shard_map.57), channel_id=1, replica_groups=mesh['ctx'=64,'tp'=8] {'tp'}, dimensions={0} | all-to-all | bytes 2097152 | tf_op jit(solution)/shard_map/all_to_all | solution.py:182
  122.4 0.8 reduce_sum.12
  (28 shorter events, 6.0 us)
Async XLA Ops:
  1.4 8.7 %collective-permute-start = (bf16[136,256]{1,0:T(8,128)(2,1)S(1)}, bf16[136,256]{1,0:T(8,128)(2,1)S(1)}, u32[]{:S(2)}, u32[]{:S(2)}) collective-permute-start(bf16[136,256]{1,0:T(8,128)(2,1)S(1)} %get-tuple-element.42), channel_id=1, source_target_pairs={{0,8},{8,0},{16,24},{24,16},{32,40},{40,32},{48,56},{56,48},{64,72... | collective-permute-start | bytes 208904 | tf_op jit(solution)/shard_map/ppermute | solution.py:142
  3.4 6.7 %collective-permute-start.1 = (bf16[136,256]{1,0:T(8,128)(2,1)S(1)}, bf16[136,256]{1,0:T(8,128)(2,1)S(1)}, u32[]{:S(2)}, u32[]{:S(2)}) collective-permute-start(bf16[136,256]{1,0:T(8,128)(2,1)S(1)} %get-tuple-element.42), channel_id=1, source_target_pairs={{0,16},{8,24},{16,0},{24,8},{32,48},{40,56},{48,32},{56,40},{64,80... | collective-permute-start | bytes 208904 | tf_op jit(solution)/shard_map/ppermute | solution.py:142
  6.8 6.1 %collective-permute-start.2 = (bf16[136,256]{1,0:T(8,128)(2,1)S(1)}, bf16[136,256]{1,0:T(8,128)(2,1)S(1)}, u32[]{:S(2)}, u32[]{:S(2)}) collective-permute-start(bf16[136,256]{1,0:T(8,128)(2,1)S(1)} %get-tuple-element.42), channel_id=1, source_target_pairs={{0,24},{8,16},{16,8},{24,0},{32,56},{40,48},{48,40},{56,32},{64,88... | collective-permute-start | bytes 208904 | tf_op jit(solution)/shard_map/ppermute | solution.py:142
  12.9 11.8 %collective-permute-start.3 = (bf16[4,136,256]{2,1,0:T(8,128)(2,1)S(1)}, bf16[4,136,256]{2,1,0:T(8,128)(2,1)S(1)}, u32[]{:S(2)}, u32[]{:S(2)}) collective-permute-start(bf16[4,136,256]{2,1,0:T(8,128)(2,1)S(1)} %pad_maximum_fusion), channel_id=1, source_target_pairs={{0,32},{8,40},{16,48},{24,56},{32,64},{40,72},{48,80},{56,88},{64,... | collective-permute-start | bytes 835592 | tf_op jit(solution)/shard_map/ppermute | solution.py:147
  24.7 11.0 %collective-permute-start.4 = (bf16[4,136,256]{2,1,0:T(8,128)(2,1)S(1)}, bf16[4,136,256]{2,1,0:T(8,128)(2,1)S(1)}, u32[]{:S(2)}, u32[]{:S(2)}) collective-permute-start(bf16[4,136,256]{2,1,0:T(8,128)(2,1)S(1)} %collective-permute-done.3), channel_id=1, source_target_pairs={{0,32},{8,40},{16,48},{24,56},{32,64},{40,72},{48,80},{56,88},{64,... | collective-permute-start | bytes 835592 | tf_op jit(solution)/shard_map/ppermute | solution.py:147
  29.4 17.4 %collective-permute-start.7 = (bf16[136,512]{1,0:T(8,128)(2,1)S(1)}, bf16[136,512]{1,0:T(8,128)(2,1)S(1)}, u32[]{:S(2)}, u32[]{:S(2)}) collective-permute-start(bf16[136,512]{1,0:T(8,128)(2,1)S(1)} %fusion.1), channel_id=1, source_target_pairs={{160,0},{168,8},{176,16},{184,24},{192,32},{200,40},{208,48},{216,... | collective-permute-start | bytes 417800 | tf_op jit(solution)/shard_map/ppermute | solution.py:150
  35.6 11.9 %collective-permute-start.5 = (bf16[4,136,256]{2,1,0:T(8,128)(2,1)S(1)}, bf16[4,136,256]{2,1,0:T(8,128)(2,1)S(1)}, u32[]{:S(2)}, u32[]{:S(2)}) collective-permute-start(bf16[4,136,256]{2,1,0:T(8,128)(2,1)S(1)} %collective-permute-done.4), channel_id=1, source_target_pairs={{0,32},{8,40},{16,48},{24,56},{32,64},{40,72},{48,80},{56,88},{64,... | collective-permute-start | bytes 835592 | tf_op jit(solution)/shard_map/ppermute | solution.py:147
  46.8 15.5 %copy-start.2 = (bf16[136,512]{1,0:T(8,128)(2,1)}, bf16[136,512]{1,0:T(8,128)(2,1)S(1)}, u32[]{:S(2)}) copy-start(bf16[136,512]{1,0:T(8,128)(2,1)S(1)} %collective-permute-done.7.query_ref) | copy-start | bytes 417796
  47.5 14.1 %collective-permute-start.6 = (bf16[4,136,256]{2,1,0:T(8,128)(2,1)S(1)}, bf16[4,136,256]{2,1,0:T(8,128)(2,1)S(1)}, u32[]{:S(2)}, u32[]{:S(2)}) collective-permute-start(bf16[4,136,256]{2,1,0:T(8,128)(2,1)S(1)} %collective-permute-done.5), channel_id=1, source_target_pairs={{0,32},{8,40},{16,48},{24,56},{32,64},{40,72},{48,80},{56,88},{64,... | collective-permute-start | bytes 835592 | tf_op jit(solution)/shard_map/ppermute | solution.py:147
  61.6 1.1 copy-start.1
  68.3 12.3 %collective-permute-start.9 = (f32[128,8]{1,0:T(8,128)}, f32[128,8]{1,0:T(8,128)S(1)}, u32[]{:S(2)}, u32[]{:S(2)}) collective-permute-start(f32[128,8]{1,0:T(8,128)} %get-tuple-element.40), channel_id=1, source_target_pairs={{0,160},{8,168},{16,176},{24,184},{32,192},{40,200},{48,208},{56,2... | collective-permute-start | bytes 12296 | tf_op jit(solution)/shard_map/ppermute | solution.py:170
  73.0 21.0 %collective-permute-start.8 = (bf16[128,512]{1,0:T(8,128)(2,1)}, bf16[128,512]{1,0:T(8,128)(2,1)S(1)}, u32[]{:S(2)}, u32[]{:S(2)}) collective-permute-start(bf16[128,512]{1,0:T(8,128)(2,1)} %get-tuple-element.39), channel_id=1, source_target_pairs={{0,160},{8,168},{16,176},{24,184},{32,192},{40,200},{48,208},{56,2... | collective-permute-start | bytes 393224 | tf_op jit(solution)/shard_map/ppermute | solution.py:169
  94.1 0.7 copy-start

commit v9 on v4

--- a/solution.py
+++ b/solution.py
@@ -14,37 +14,45 @@
 neg_large = -1e30
 
 
-def partial_kernel(query_ref, block_ref, key_pos_ref, key_doc_ref, query_pos_ref,
-                   query_doc_ref, out_ref, stats_ref):
+def partial_kernel(*refs):
+    query_ref = refs[0]
+    block_refs = refs[1:-6]
+    key_pos_ref, key_doc_ref, query_pos_ref, query_doc_ref, out_ref, stats_ref = refs[-6:]
     rows = query_pos_ref.shape[0]
     width = query_ref.shape[1]
-    count, _, packed = block_ref.shape
-    head_dim = packed // 2
+    head_dim = block_refs[0].shape[-1] // 2
     heads = width // head_dim
-    tokens = count * rows
-    key_part = block_ref[:, :rows, :head_dim].reshape(tokens, head_dim)
-    value_part = block_ref[:, :rows, head_dim:].reshape(tokens, head_dim)
+    key_part = jnp.concatenate(
+        [ref[:, :rows, :head_dim].reshape(ref.shape[0] * rows, head_dim) for ref in block_refs],
+        axis=0,
+    )
+    value_part = jnp.concatenate(
+        [ref[:, :rows, head_dim:].reshape(ref.shape[0] * rows, head_dim) for ref in block_refs],
+        axis=0,
+    )
     allowed = (
         (key_pos_ref[...] <= query_pos_ref[...])
         & (key_pos_ref[...] >= 0)
         & (key_doc_ref[...] == query_doc_ref[...])
     )
+    bias = jnp.where(allowed, 0.0, neg_large)
+    seen = jnp.max(jnp.where(allowed, 1.0, 0.0), axis=1, keepdims=True) > 0.0
     scale = 1.0 / math.sqrt(head_dim)
     for head in range(heads):
         query = query_ref[:rows, head * head_dim:(head + 1) * head_dim]
         scores = lax.dot_general(
             query, key_part, (((1,), (1,)), ((), ())), preferred_element_type=jnp.float32
         )
-        scores = scores * scale
-        peak = jnp.max(jnp.where(allowed, scores, neg_large), axis=1, keepdims=True)
-        weight = jnp.where(allowed, jnp.exp(scores - peak), 0.0)
-        total = jnp.sum(weight, axis=1, keepdims=True)
+        scores = scores * scale + bias
+        peak = jnp.max(scores, axis=1, keepdims=True)
+        weight = jnp.exp(scores - peak)
+        total = jnp.where(seen, jnp.sum(weight, axis=1, keepdims=True), 0.0)
         summed = jnp.dot(
             weight.astype(jnp.bfloat16), value_part, preferred_element_type=jnp.float32
         )
-        normed = jnp.where(total > 0.0, summed / jnp.maximum(total, 1e-30), 0.0)
+        normed = jnp.where(seen, summed / jnp.maximum(total, 1e-30), 0.0)
         out_ref[:, head * head_dim:(head + 1) * head_dim] = normed.astype(out_ref.dtype)
-        stats_ref[:, head:head + 1] = peak
+        stats_ref[:, head:head + 1] = jnp.where(seen, peak, neg_large)
         stats_ref[:, heads + head:heads + head + 1] = total
 
 
@@ -60,13 +68,13 @@
             jax.ShapeDtypeStruct((rows, width), out_dtype),
             jax.ShapeDtypeStruct((rows, 2 * heads), jnp.float32),
         ),
-        in_specs=[vmem] * 6,
+        in_specs=[vmem] * (5 + len(blocks)),
         out_specs=(vmem, vmem),
         cost_estimate=pl.CostEstimate(
             flops=4 * rows * tokens * width, transcendentals=rows * tokens * heads,
-            bytes_accessed=blocks.size * 2 + query.size * 2 + rows * width * 4,
+            bytes_accessed=sum(b.size for b in blocks) * 2 + query.size * 2 + rows * width * 4,
         ),
-    )(query, blocks, key_pos, key_doc, query_pos, query_doc)
+    )(query, *blocks, key_pos, key_doc, query_pos, query_doc)
 
 
 def merge_kernel(near_ref, near_stats_ref, far_ref, far_stats_ref, weight_ref, out_ref):
@@ -147,15 +155,16 @@
     for hop in range(hops):
         current = lax.ppermute(current, "ctx", forward)
         collected.append(current)
-    blocks = jnp.stack(collected)
+    blocks = collected
 
     hop_ids = jnp.arange(hops + 1, dtype=jnp.int32)[:, None, None]
     offsets = jnp.arange(PLANE, dtype=jnp.int32)[None, :, None]
     tokens = jnp.arange(rows, dtype=jnp.int32)[None, None, :]
     key_shard = PLANE * (plane - hop_ids) + (slot ^ offsets)
     key_pos = (key_shard * rows + tokens).reshape(1, -1)
-    blocks = blocks.reshape(-1, rows + DOC_ROWS, 2 * head_dim)
-    key_doc = blocks[:, rows, :rows].astype(jnp.int32).reshape(1, -1)
+    key_doc = jnp.concatenate(
+        [b[:, rows, :rows].astype(jnp.int32).reshape(1, -1) for b in blocks], axis=1
+    )
 
     offsets_in_shard = jnp.arange(rows, dtype=jnp.int32).reshape(rows, 1)
     visit_pos = (my_index + PLANE * far) * rows + offsets_in_shard

time: 116 us -> 117 us (level)
  waiting for transfers between devices: 27.5 us -> 30.5 us
    ppermute x1, starting transfers between devices: 6.77 us -> 5.23 us  [shards(): far_out = lax.ppermute(visit_out, 'ctx', ahead)]
    ppermute x1, waiting for transfers between devices: 0.01 us -> 1.48 us  [shards(): far_out = lax.ppermute(visit_out, 'ctx', ahead)]
  transfers between devices with their start and end apart: 10 -> 10, of which waited for: 5 -> 7; matrix products, arithmetic and copies ran while one was open for 5% -> 5% of each run, Pallas kernels for 5% -> 4%
where the time goes in v9:
time: 117 us; the launch traced here: 116 us
  starting transfers between devices  38.1 us (33%)
  waiting for transfers between devices  30.5 us (26%)
  blocking collectives  23.3 us (20%)
  Pallas kernels  14.6 us (12%)
  other arithmetic  6.54 us (6%)
  local copies, waits for them, and re-layouts  2.87 us (2%)
    all_to_all x1, blocking collectives, shards(): received = lax.all_to_all(chunks, 'tp', 0, 0, tiled=True)  23.3 us
    ppermute x4, waiting for transfers between devices, shards(): current = lax.ppermute(current, 'ctx', forward)  22.5 us
    ppermute x4, starting transfers between devices, shards(): current = lax.ppermute(current, 'ctx', forward)  17.4 us
    pallas_call x2, Pallas kernels, partial(): pl.pallas_call(partial_kernel, out_shape=(jax.ShapeDtypeStruct((rows, wid...  10.1 us
    ppermute x3, starting transfers between devices, shards(): lax.ppermute(block, 'ctx', [(s, s ^ offset) for s in range(ctx)])  7.87 us
    ppermute x1, waiting for transfers between devices, shards(): far_stats = lax.ppermute(visit_stats, 'ctx', ahead)  6.33 us
    ppermute x1, starting transfers between devices, shards(): far_stats = lax.ppermute(visit_stats, 'ctx', ahead)  6.31 us
    ppermute x1, starting transfers between devices, shards(): far_out = lax.ppermute(visit_out, 'ctx', ahead)  5.23 us
  transfers between devices with their start and end apart: 10, of which 7 were waited for; matrix products, arithmetic and copies ran while one was open for 5% of the time, Pallas kernels for 4%

profile of v9, /device:TPU:128, one launch (start us, length us, event | category | flops | bytes accessed | tf_op | source)
XLA Modules:
  0.0 116.2 jit_solution(14376299148082674699)
XLA Ops:
  0.7 0.8 fusion.5
  1.4 3.4 %collective-permute-start.1 = (bf16[136,256]{1,0:T(8,128)(2,1)S(1)}, bf16[136,256]{1,0:T(8,128)(2,1)S(1)}, u32[]{:S(2)}, u32[]{:S(2)}) collective-permute-start(bf16[136,256]{1,0:T(8,128)(2,1)S(1)} %get-tuple-element.38), channel_id=1, source_target_pairs={{0,16},{8,24},{16,0},{24,8},{32,48},{40,56},{48,32},{56,40},{64,80... | collective-permute-start | bytes 208904 | tf_op jit(solution)/shard_map/ppermute | solution.py:151
  4.9 1.9 %collective-permute-start = (bf16[136,256]{1,0:T(8,128)(2,1)S(1)}, bf16[136,256]{1,0:T(8,128)(2,1)S(1)}, u32[]{:S(2)}, u32[]{:S(2)}) collective-permute-start(bf16[136,256]{1,0:T(8,128)(2,1)S(1)} %get-tuple-element.38), channel_id=1, source_target_pairs={{0,8},{8,0},{16,24},{24,16},{32,40},{40,32},{48,56},{56,48},{64,72... | collective-permute-start | bytes 208904 | tf_op jit(solution)/shard_map/ppermute | solution.py:151
  6.8 2.5 %collective-permute-start.2 = (bf16[136,256]{1,0:T(8,128)(2,1)S(1)}, bf16[136,256]{1,0:T(8,128)(2,1)S(1)}, u32[]{:S(2)}, u32[]{:S(2)}) collective-permute-start(bf16[136,256]{1,0:T(8,128)(2,1)S(1)} %get-tuple-element.38), channel_id=1, source_target_pairs={{0,24},{8,16},{16,8},{24,0},{32,56},{40,48},{48,40},{56,32},{64,88... | collective-permute-start | bytes 208904 | tf_op jit(solution)/shard_map/ppermute | solution.py:151
  9.3 0.9 fusion.1
  10.3 1.3 %collective-permute-start.7 = (bf16[136,512]{1,0:T(8,128)(2,1)S(1)}, bf16[136,512]{1,0:T(8,128)(2,1)S(1)}, u32[]{:S(2)}, u32[]{:S(2)}) collective-permute-start(bf16[136,512]{1,0:T(8,128)(2,1)S(1)} %fusion.1), channel_id=1, source_target_pairs={{160,0},{168,8},{176,16},{184,24},{192,32},{200,40},{208,48},{216,... | collective-permute-start | bytes 417800 | tf_op jit(solution)/shard_map/ppermute | solution.py:147
  12.6 7.9 %collective-permute-start.3 = (bf16[4,136,256]{2,1,0:T(8,128)(2,1)S(1)}, bf16[4,136,256]{2,1,0:T(8,128)(2,1)S(1)}, u32[]{:S(2)}, u32[]{:S(2)}) collective-permute-start(bf16[4,136,256]{2,1,0:T(8,128)(2,1)S(1)} %pad_maximum_fusion.refs_1_), channel_id=1, source_target_pairs={{0,32},{8,40},{16,48},{24,56},{32,64},{40,72},{48,80},{56,88},{64,... | collective-permute-start | bytes 835592 | tf_op jit(solution)/shard_map/ppermute | solution.py:156
  21.8 4.5 %collective-permute-done.3.refs_2_ = bf16[4,136,256]{2,1,0:T(8,128)(2,1)S(1)} collective-permute-done((bf16[4,136,256]{2,1,0:T(8,128)(2,1)S(1)}, bf16[4,136,256]{2,1,0:T(8,128)(2,1)S(1)}, u32[]{:S(2)}, u32[]{:S(2)}) %collective-permute-start.3) | collective-permute-done | bytes 278560 | tf_op jit(solution)/shard_map/ppermute | solution.py:156
  26.3 4.4 %collective-permute-start.4 = (bf16[4,136,256]{2,1,0:T(8,128)(2,1)S(1)}, bf16[4,136,256]{2,1,0:T(8,128)(2,1)S(1)}, u32[]{:S(2)}, u32[]{:S(2)}) collective-permute-start(bf16[4,136,256]{2,1,0:T(8,128)(2,1)S(1)} %collective-permute-done.3.refs_2_), channel_id=1, source_target_pairs={{0,32},{8,40},{16,48},{24,56},{32,64},{40,72},{48,80},{56,88},{64,... | collective-permute-start | bytes 835592 | tf_op jit(solution)/shard_map/ppermute | solution.py:156
  30.7 1.4 %copy.6.refs_9_ = s32[128,1]{1,0:T(8,128)} copy(s32[128,1]{0,1:T(1,128)} %bitcast.39) | data formatting | bytes 1024 | tf_op jit(solution)/shard_map/reshape | solution.py:181
  32.1 4.7 %collective-permute-done.4.refs_3_ = bf16[4,136,256]{2,1,0:T(8,128)(2,1)S(1)} collective-permute-done((bf16[4,136,256]{2,1,0:T(8,128)(2,1)S(1)}, bf16[4,136,256]{2,1,0:T(8,128)(2,1)S(1)}, u32[]{:S(2)}, u32[]{:S(2)}) %collective-permute-start.4) | collective-permute-done | bytes 278560 | tf_op jit(solution)/shard_map/ppermute | solution.py:156
  36.8 3.2 %collective-permute-start.5 = (bf16[4,136,256]{2,1,0:T(8,128)(2,1)S(1)}, bf16[4,136,256]{2,1,0:T(8,128)(2,1)S(1)}, u32[]{:S(2)}, u32[]{:S(2)}) collective-permute-start(bf16[4,136,256]{2,1,0:T(8,128)(2,1)S(1)} %collective-permute-done.4.refs_3_), channel_id=1, source_target_pairs={{0,32},{8,40},{16,48},{24,56},{32,64},{40,72},{48,80},{56,88},{64,... | collective-permute-start | bytes 835592 | tf_op jit(solution)/shard_map/ppermute | solution.py:156
  40.8 5.7 %collective-permute-done.5.refs_4_ = bf16[4,136,256]{2,1,0:T(8,128)(2,1)S(1)} collective-permute-done((bf16[4,136,256]{2,1,0:T(8,128)(2,1)S(1)}, bf16[4,136,256]{2,1,0:T(8,128)(2,1)S(1)}, u32[]{:S(2)}, u32[]{:S(2)}) %collective-permute-start.5) | collective-permute-done | bytes 278560 | tf_op jit(solution)/shard_map/ppermute | solution.py:156
  46.4 2.0 %collective-permute-start.6 = (bf16[4,136,256]{2,1,0:T(8,128)(2,1)S(1)}, bf16[4,136,256]{2,1,0:T(8,128)(2,1)S(1)}, u32[]{:S(2)}, u32[]{:S(2)}) collective-permute-start(bf16[4,136,256]{2,1,0:T(8,128)(2,1)S(1)} %collective-permute-done.5.refs_4_), channel_id=1, source_target_pairs={{0,32},{8,40},{16,48},{24,56},{32,64},{40,72},{48,80},{56,88},{64,... | collective-permute-start | bytes 835592 | tf_op jit(solution)/shard_map/ppermute | solution.py:156
  48.4 7.6 %collective-permute-done.6.refs_5_ = bf16[4,136,256]{2,1,0:T(8,128)(2,1)S(1)} collective-permute-done((bf16[4,136,256]{2,1,0:T(8,128)(2,1)S(1)}, bf16[4,136,256]{2,1,0:T(8,128)(2,1)S(1)}, u32[]{:S(2)}, u32[]{:S(2)}) %collective-permute-start.6) | collective-permute-done | bytes 278560 | tf_op jit(solution)/shard_map/ppermute | solution.py:156
  56.8 5.0 %shard_map.56 = (bf16[128,512]{1,0:T(8,128)(2,1)}, f32[128,8]{1,0:T(8,128)}) custom-call(bf16[136,512]{1,0:T(8,128)(2,1)} %copy-done.6, bf16[4,136,256]{2,1,0:T(8,128)(2,1)} %copy-done, bf16[4,136,256]{2,1,0:T(8,128)(2,1)} %copy-done.2, bf16[4,136,256]{2,1,0:T(8,128)(2,1)} %copy-done.3, bf16[4,136,256]{2,1,0:T(8,128)(2,1)} %copy-done.4, ...), custom_call_target="tpu_custom_call" | custom-call | flops 671088640 | bytes 1794048 | tf_op jit(solution)/shard_map/pallas_call | solution.py:65
  61.8 6.3 %collective-permute-start.9 = (f32[128,8]{1,0:T(8,128)}, f32[128,8]{1,0:T(8,128)S(1)}, u32[]{:S(2)}, u32[]{:S(2)}) collective-permute-start(f32[128,8]{1,0:T(8,128)} %get-tuple-element.36), channel_id=1, source_target_pairs={{0,160},{8,168},{16,176},{24,184},{32,192},{40,200},{48,208},{56,2... | collective-permute-start | bytes 12296 | tf_op jit(solution)/shard_map/ppermute | solution.py:177
  68.1 5.2 %collective-permute-start.8 = (bf16[128,512]{1,0:T(8,128)(2,1)}, bf16[128,512]{1,0:T(8,128)(2,1)S(1)}, u32[]{:S(2)}, u32[]{:S(2)}) collective-permute-start(bf16[128,512]{1,0:T(8,128)(2,1)} %get-tuple-element.35), channel_id=1, source_target_pairs={{0,160},{8,168},{16,176},{24,184},{32,192},{40,200},{48,208},{56,2... | collective-permute-start | bytes 393224 | tf_op jit(solution)/shard_map/ppermute | solution.py:176
  73.4 5.1 %shard_map.55 = (f32[128,512]{1,0:T(8,128)}, f32[128,8]{1,0:T(8,128)}) custom-call(bf16[128,512]{1,0:T(8,128)(2,1)} %refs_0_.1, bf16[4,136,256]{2,1,0:T(8,128)(2,1)} %copy-done, bf16[4,136,256]{2,1,0:T(8,128)(2,1)} %copy-done.2, bf16[4,136,256]{2,1,0:T(8,128)(2,1)} %copy-done.3, bf16[4,136,256]{2,1,0:T(8,128)(2,1)} %copy-done.4, ...), custom_call_target="tpu_custom_call" | custom-call | flops 671088640 | bytes 1785856 | tf_op jit(solution)/shard_map/pallas_call | solution.py:65
  78.4 6.3 %collective-permute-done.9 = f32[128,8]{1,0:T(8,128)S(1)} collective-permute-done((f32[128,8]{1,0:T(8,128)}, f32[128,8]{1,0:T(8,128)S(1)}, u32[]{:S(2)}, u32[]{:S(2)}) %collective-permute-start.9) | collective-permute-done | bytes 4128 | tf_op jit(solution)/shard_map/ppermute | solution.py:177
  85.4 1.5 %collective-permute-done.8.far_ref = bf16[128,512]{1,0:T(8,128)(2,1)S(1)} collective-permute-done((bf16[128,512]{1,0:T(8,128)(2,1)}, bf16[128,512]{1,0:T(8,128)(2,1)S(1)}, u32[]{:S(2)}, u32[]{:S(2)}) %collective-permute-start.8) | collective-permute-done | bytes 131104 | tf_op jit(solution)/shard_map/ppermute | solution.py:176
  87.5 4.5 %shard_map.57 = bf16[8,128,512]{2,1,0:T(8,128)(2,1)} custom-call(f32[128,512]{1,0:T(8,128)} %get-tuple-element.33.near_ref, f32[128,8]{1,0:T(8,128)} %get-tuple-element.34.near_stats_ref, bf16[128,512]{1,0:T(8,128)(2,1)} %copy-done.1, f32[128,8]{1,0:T(8,128)} %broadcast_select_fusion.far_stats_ref, bf16[512,4096]{1,0:T(8,128)(2,1)} %weight_ref.1), custom_call_target="tpu_custom_call" | custom-call | flops 536870912 | bytes 5242880 | tf_op jit(solution)/shard_map/pallas_call | solution.py:112
  92.0 23.3 %all_to_all.5 = bf16[8,128,512]{2,1,0:T(8,128)(2,1)S(1)} all-to-all(bf16[8,128,512]{2,1,0:T(8,128)(2,1)} %shard_map.57), channel_id=1, replica_groups=mesh['ctx'=64,'tp'=8] {'tp'}, dimensions={0} | all-to-all | bytes 2097152 | tf_op jit(solution)/shard_map/all_to_all | solution.py:189
  115.3 0.8 reduce_sum.12
  (36 shorter events, 5.7 us)
Async XLA Ops:
  1.4 10.9 %collective-permute-start.1 = (bf16[136,256]{1,0:T(8,128)(2,1)S(1)}, bf16[136,256]{1,0:T(8,128)(2,1)S(1)}, u32[]{:S(2)}, u32[]{:S(2)}) collective-permute-start(bf16[136,256]{1,0:T(8,128)(2,1)S(1)} %get-tuple-element.38), channel_id=1, source_target_pairs={{0,16},{8,24},{16,0},{24,8},{32,48},{40,56},{48,32},{56,40},{64,80... | collective-permute-start | bytes 208904 | tf_op jit(solution)/shard_map/ppermute | solution.py:151
  4.9 7.5 %collective-permute-start = (bf16[136,256]{1,0:T(8,128)(2,1)S(1)}, bf16[136,256]{1,0:T(8,128)(2,1)S(1)}, u32[]{:S(2)}, u32[]{:S(2)}) collective-permute-start(bf16[136,256]{1,0:T(8,128)(2,1)S(1)} %get-tuple-element.38), channel_id=1, source_target_pairs={{0,8},{8,0},{16,24},{24,16},{32,40},{40,32},{48,56},{56,48},{64,72... | collective-permute-start | bytes 208904 | tf_op jit(solution)/shard_map/ppermute | solution.py:151
  6.8 5.7 %collective-permute-start.2 = (bf16[136,256]{1,0:T(8,128)(2,1)S(1)}, bf16[136,256]{1,0:T(8,128)(2,1)S(1)}, u32[]{:S(2)}, u32[]{:S(2)}) collective-permute-start(bf16[136,256]{1,0:T(8,128)(2,1)S(1)} %get-tuple-element.38), channel_id=1, source_target_pairs={{0,24},{8,16},{16,8},{24,0},{32,56},{40,48},{48,40},{56,32},{64,88... | collective-permute-start | bytes 208904 | tf_op jit(solution)/shard_map/ppermute | solution.py:151
  10.3 29.7 %collective-permute-start.7 = (bf16[136,512]{1,0:T(8,128)(2,1)S(1)}, bf16[136,512]{1,0:T(8,128)(2,1)S(1)}, u32[]{:S(2)}, u32[]{:S(2)}) collective-permute-start(bf16[136,512]{1,0:T(8,128)(2,1)S(1)} %fusion.1), channel_id=1, source_target_pairs={{160,0},{168,8},{176,16},{184,24},{192,32},{200,40},{208,48},{216,... | collective-permute-start | bytes 417800 | tf_op jit(solution)/shard_map/ppermute | solution.py:147
  12.6 44.2 %copy-start = (bf16[4,136,256]{2,1,0:T(8,128)(2,1)}, bf16[4,136,256]{2,1,0:T(8,128)(2,1)S(1)}, u32[]{:S(2)}) copy-start(bf16[4,136,256]{2,1,0:T(8,128)(2,1)S(1)} %pad_maximum_fusion.refs_1_) | copy-start | bytes 835588
  12.6 13.7 %collective-permute-start.3 = (bf16[4,136,256]{2,1,0:T(8,128)(2,1)S(1)}, bf16[4,136,256]{2,1,0:T(8,128)(2,1)S(1)}, u32[]{:S(2)}, u32[]{:S(2)}) collective-permute-start(bf16[4,136,256]{2,1,0:T(8,128)(2,1)S(1)} %pad_maximum_fusion.refs_1_), channel_id=1, source_target_pairs={{0,32},{8,40},{16,48},{24,56},{32,64},{40,72},{48,80},{56,88},{64,... | collective-permute-start | bytes 835592 | tf_op jit(solution)/shard_map/ppermute | solution.py:156
  26.3 30.5 %copy-start.2 = (bf16[4,136,256]{2,1,0:T(8,128)(2,1)}, bf16[4,136,256]{2,1,0:T(8,128)(2,1)S(1)}, u32[]{:S(2)}) copy-start(bf16[4,136,256]{2,1,0:T(8,128)(2,1)S(1)} %collective-permute-done.3.refs_2_) | copy-start | bytes 835588
  26.3 10.5 %collective-permute-start.4 = (bf16[4,136,256]{2,1,0:T(8,128)(2,1)S(1)}, bf16[4,136,256]{2,1,0:T(8,128)(2,1)S(1)}, u32[]{:S(2)}, u32[]{:S(2)}) collective-permute-start(bf16[4,136,256]{2,1,0:T(8,128)(2,1)S(1)} %collective-permute-done.3.refs_2_), channel_id=1, source_target_pairs={{0,32},{8,40},{16,48},{24,56},{32,64},{40,72},{48,80},{56,88},{64,... | collective-permute-start | bytes 835592 | tf_op jit(solution)/shard_map/ppermute | solution.py:156
  36.8 20.0 %copy-start.3 = (bf16[4,136,256]{2,1,0:T(8,128)(2,1)}, bf16[4,136,256]{2,1,0:T(8,128)(2,1)S(1)}, u32[]{:S(2)}) copy-start(bf16[4,136,256]{2,1,0:T(8,128)(2,1)S(1)} %collective-permute-done.4.refs_3_) | copy-start | bytes 835588
  36.8 9.6 %collective-permute-start.5 = (bf16[4,136,256]{2,1,0:T(8,128)(2,1)S(1)}, bf16[4,136,256]{2,1,0:T(8,128)(2,1)S(1)}, u32[]{:S(2)}, u32[]{:S(2)}) collective-permute-start(bf16[4,136,256]{2,1,0:T(8,128)(2,1)S(1)} %collective-permute-done.4.refs_3_), channel_id=1, source_target_pairs={{0,32},{8,40},{16,48},{24,56},{32,64},{40,72},{48,80},{56,88},{64,... | collective-permute-start | bytes 835592 | tf_op jit(solution)/shard_map/ppermute | solution.py:156
  40.0 16.8 %copy-start.6 = (bf16[136,512]{1,0:T(8,128)(2,1)}, bf16[136,512]{1,0:T(8,128)(2,1)S(1)}, u32[]{:S(2)}) copy-start(bf16[136,512]{1,0:T(8,128)(2,1)S(1)} %collective-permute-done.7.refs_0_) | copy-start | bytes 417796
  46.4 10.3 %copy-start.4 = (bf16[4,136,256]{2,1,0:T(8,128)(2,1)}, bf16[4,136,256]{2,1,0:T(8,128)(2,1)S(1)}, u32[]{:S(2)}) copy-start(bf16[4,136,256]{2,1,0:T(8,128)(2,1)S(1)} %collective-permute-done.5.refs_4_) | copy-start | bytes 835588
  46.4 9.6 %collective-permute-start.6 = (bf16[4,136,256]{2,1,0:T(8,128)(2,1)S(1)}, bf16[4,136,256]{2,1,0:T(8,128)(2,1)S(1)}, u32[]{:S(2)}, u32[]{:S(2)}) collective-permute-start(bf16[4,136,256]{2,1,0:T(8,128)(2,1)S(1)} %collective-permute-done.5.refs_4_), channel_id=1, source_target_pairs={{0,32},{8,40},{16,48},{24,56},{32,64},{40,72},{48,80},{56,88},{64,... | collective-permute-start | bytes 835592 | tf_op jit(solution)/shard_map/ppermute | solution.py:156
  56.1 0.7 copy-start.5
  61.8 22.9 %collective-permute-start.9 = (f32[128,8]{1,0:T(8,128)}, f32[128,8]{1,0:T(8,128)S(1)}, u32[]{:S(2)}, u32[]{:S(2)}) collective-permute-start(f32[128,8]{1,0:T(8,128)} %get-tuple-element.36), channel_id=1, source_target_pairs={{0,160},{8,168},{16,176},{24,184},{32,192},{40,200},{48,208},{56,2... | collective-permute-start | bytes 12296 | tf_op jit(solution)/shard_map/ppermute | solution.py:177
  68.1 18.7 %collective-permute-start.8 = (bf16[128,512]{1,0:T(8,128)(2,1)}, bf16[128,512]{1,0:T(8,128)(2,1)S(1)}, u32[]{:S(2)}, u32[]{:S(2)}) collective-permute-start(bf16[128,512]{1,0:T(8,128)(2,1)} %get-tuple-element.35), channel_id=1, source_target_pairs={{0,160},{8,168},{16,176},{24,184},{32,192},{40,200},{48,208},{56,2... | collective-permute-start | bytes 393224 | tf_op jit(solution)/shard_map/ppermute | solution.py:176
  86.9 0.7 copy-start.1

commit v10 on v9

--- a/solution.py
+++ b/solution.py
@@ -16,8 +16,9 @@
 
 def partial_kernel(*refs):
     query_ref = refs[0]
-    block_refs = refs[1:-6]
-    key_pos_ref, key_doc_ref, query_pos_ref, query_doc_ref, out_ref, stats_ref = refs[-6:]
+    block_refs = refs[1:-8]
+    (key_pos_ref, key_doc_ref, query_pos_ref, query_doc_ref, out_ref, stats_ref,
+     rows_ref, square_ref) = refs[-8:]
     rows = query_pos_ref.shape[0]
     width = query_ref.shape[1]
     head_dim = block_refs[0].shape[-1] // 2
@@ -54,6 +55,9 @@
         out_ref[:, head * head_dim:(head + 1) * head_dim] = normed.astype(out_ref.dtype)
         stats_ref[:, head:head + 1] = jnp.where(seen, peak, neg_large)
         stats_ref[:, heads + head:heads + head + 1] = total
+    square_ref[...] = jnp.zeros_like(square_ref)
+    square_ref[:, :2 * heads] = stats_ref[...]
+    rows_ref[...] = jnp.transpose(square_ref[...])[:2 * heads]
 
 
 def partial(query, blocks, key_pos, key_doc, query_pos, query_doc, out_dtype):
@@ -67,9 +71,11 @@
         out_shape=(
             jax.ShapeDtypeStruct((rows, width), out_dtype),
             jax.ShapeDtypeStruct((rows, 2 * heads), jnp.float32),
+            jax.ShapeDtypeStruct((2 * heads, rows), jnp.float32),
         ),
         in_specs=[vmem] * (5 + len(blocks)),
-        out_specs=(vmem, vmem),
+        out_specs=(vmem, vmem, vmem),
+        scratch_shapes=[pltpu.VMEM((rows, rows), jnp.float32)],
         cost_estimate=pl.CostEstimate(
             flops=4 * rows * tokens * width, transcendentals=rows * tokens * heads,
             bytes_accessed=sum(b.size for b in blocks) * 2 + query.size * 2 + rows * width * 4,
@@ -77,16 +83,20 @@
     )(query, *blocks, key_pos, key_doc, query_pos, query_doc)
 
 
-def merge_kernel(near_ref, near_stats_ref, far_ref, far_stats_ref, weight_ref, out_ref):
+def merge_kernel(near_ref, near_stats_ref, far_ref, far_rows_ref, weight_ref, out_ref,
+                 square_ref):
     rows, width = near_ref.shape
     heads = near_stats_ref.shape[1] // 2
     head_dim = width // heads
+    square_ref[...] = jnp.zeros_like(square_ref)
+    square_ref[:2 * heads, :] = far_rows_ref[...]
+    far_stats = jnp.transpose(square_ref[...])
     outputs = []
     for head in range(heads):
         near_peak = near_stats_ref[:, head:head + 1]
         near_total = near_stats_ref[:, heads + head:heads + head + 1]
-        far_peak = far_stats_ref[:, head:head + 1]
-        far_total = far_stats_ref[:, heads + head:heads + head + 1]
+        far_peak = far_stats[:, head:head + 1]
+        far_total = far_stats[:, heads + head:heads + head + 1]
         peak = jnp.maximum(near_peak, far_peak)
         near_share = near_total * jnp.exp(near_peak - peak)
         far_share = far_total * jnp.exp(far_peak - peak)
@@ -114,6 +124,7 @@
         out_shape=jax.ShapeDtypeStruct((pieces, rows, width // pieces), jnp.bfloat16),
         in_specs=[vmem] * 5,
         out_specs=vmem,
+        scratch_shapes=[pltpu.VMEM((rows, rows), jnp.float32)],
         cost_estimate=pl.CostEstimate(
             flops=2 * rows * near.shape[1] * width, transcendentals=0,
             bytes_accessed=out_weight.size * 2 + rows * width * 2,
@@ -169,22 +180,22 @@
     offsets_in_shard = jnp.arange(rows, dtype=jnp.int32).reshape(rows, 1)
     visit_pos = (my_index + PLANE * far) * rows + offsets_in_shard
     visit_doc = visiting[rows, :rows].astype(jnp.int32).reshape(rows, 1)
-    visit_out, visit_stats = partial(
+    visit_out, visit_stats, visit_rows = partial(
         visiting, blocks, key_pos, key_doc, visit_pos, visit_doc, jnp.bfloat16
     )
     ahead = [(s, s + PLANE * far) for s in range(ctx - PLANE * far)]
     far_out = lax.ppermute(visit_out, "ctx", ahead)
-    far_stats = lax.ppermute(visit_stats, "ctx", ahead)
+    far_rows = lax.ppermute(visit_rows, "ctx", ahead)
 
     query_pos = my_index * rows + offsets_in_shard
-    near_out, near_stats = partial(
+    near_out, near_stats, _ = partial(
         queries, blocks, key_pos, key_doc, query_pos, docs.reshape(rows, 1), jnp.float32
     )
     has_far = plane >= far
     heads = near_stats.shape[1] // 2
-    lane = jnp.arange(2 * heads, dtype=jnp.int32)[None, :]
-    far_stats = jnp.where(has_far, far_stats, jnp.where(lane < heads, neg_large, 0.0))
-    chunks = merge(near_out, near_stats, far_out, far_stats, out_weight, tp)
+    kind = jnp.arange(2 * heads, dtype=jnp.int32)[:, None]
+    far_rows = jnp.where(has_far, far_rows, jnp.where(kind < heads, neg_large, 0.0))
+    chunks = merge(near_out, near_stats, far_out, far_rows, out_weight, tp)
 
     received = lax.all_to_all(chunks, "tp", 0, 0, tiled=True)
     mixed = jnp.sum(received.astype(jnp.float32), axis=0)

time: 117 us -> 113 us (0.966)
  the two profiles are of different devices: /device:TPU:128 before, /device:TPU:64 now
where the time goes in v10:
time: 113 us; the launch traced here: 112 us
  starting transfers between devices  49.6 us (44%)
  blocking collectives  19.9 us (18%)
  waiting for transfers between devices  18.2 us (16%)
  Pallas kernels  14.6 us (13%)
  other arithmetic  6.52 us (6%)
  local copies, waits for them, and re-layouts  2.88 us (3%)
    all_to_all x1, blocking collectives, shards(): received = lax.all_to_all(chunks, 'tp', 0, 0, tiled=True)  19.9 us
    ppermute x4, starting transfers between devices, shards(): current = lax.ppermute(current, 'ctx', forward)  19.6 us
    ppermute x4, waiting for transfers between devices, shards(): current = lax.ppermute(current, 'ctx', forward)  18 us
    ppermute x1, starting transfers between devices, shards(): far_rows = lax.ppermute(visit_rows, 'ctx', ahead)  11.2 us
    pallas_call x2, Pallas kernels, partial(): pl.pallas_call(partial_kernel, out_shape=(jax.ShapeDtypeStruct((rows, wid...  10.1 us
    ppermute x1, starting transfers between devices, shards(): far_out = lax.ppermute(visit_out, 'ctx', ahead)  9.63 us
    ppermute x3, starting transfers between devices, shards(): lax.ppermute(block, 'ctx', [(s, s ^ offset) for s in range(ctx)])  7.87 us
    pallas_call x1, Pallas kernels, merge(): pl.pallas_call(merge_kernel, out_shape=jax.ShapeDtypeStruct((pieces, rows...  4.52 us
  transfers between devices with their start and end apart: 10, of which 5 were waited for; matrix products, arithmetic and copies ran while one was open for 5% of the time, Pallas kernels for 5%

profile of v10, /device:TPU:64, one launch (start us, length us, event | category | flops | bytes accessed | tf_op | source)
XLA Modules:
  0.0 112.0 jit_solution(8796382674159091066)
XLA Ops:
  0.7 0.8 fusion.5
  1.4 3.4 %collective-permute-start.1 = (bf16[136,256]{1,0:T(8,128)(2,1)S(1)}, bf16[136,256]{1,0:T(8,128)(2,1)S(1)}, u32[]{:S(2)}, u32[]{:S(2)}) collective-permute-start(bf16[136,256]{1,0:T(8,128)(2,1)S(1)} %get-tuple-element.38), channel_id=1, source_target_pairs={{0,16},{8,24},{16,0},{24,8},{32,48},{40,56},{48,32},{56,40},{64,80... | collective-permute-start | bytes 208904 | tf_op jit(solution)/shard_map/ppermute | solution.py:162
  4.9 1.9 %collective-permute-start = (bf16[136,256]{1,0:T(8,128)(2,1)S(1)}, bf16[136,256]{1,0:T(8,128)(2,1)S(1)}, u32[]{:S(2)}, u32[]{:S(2)}) collective-permute-start(bf16[136,256]{1,0:T(8,128)(2,1)S(1)} %get-tuple-element.38), channel_id=1, source_target_pairs={{0,8},{8,0},{16,24},{24,16},{32,40},{40,32},{48,56},{56,48},{64,72... | collective-permute-start | bytes 208904 | tf_op jit(solution)/shard_map/ppermute | solution.py:162
  6.8 2.5 %collective-permute-start.2 = (bf16[136,256]{1,0:T(8,128)(2,1)S(1)}, bf16[136,256]{1,0:T(8,128)(2,1)S(1)}, u32[]{:S(2)}, u32[]{:S(2)}) collective-permute-start(bf16[136,256]{1,0:T(8,128)(2,1)S(1)} %get-tuple-element.38), channel_id=1, source_target_pairs={{0,24},{8,16},{16,8},{24,0},{32,56},{40,48},{48,40},{56,32},{64,88... | collective-permute-start | bytes 208904 | tf_op jit(solution)/shard_map/ppermute | solution.py:162
  9.3 0.9 fusion.1
  10.3 1.3 %collective-permute-start.7 = (bf16[136,512]{1,0:T(8,128)(2,1)S(1)}, bf16[136,512]{1,0:T(8,128)(2,1)S(1)}, u32[]{:S(2)}, u32[]{:S(2)}) collective-permute-start(bf16[136,512]{1,0:T(8,128)(2,1)S(1)} %fusion.1), channel_id=1, source_target_pairs={{160,0},{168,8},{176,16},{184,24},{192,32},{200,40},{208,48},{216,... | collective-permute-start | bytes 417800 | tf_op jit(solution)/shard_map/ppermute | solution.py:158
  12.6 3.8 %collective-permute-start.3 = (bf16[4,136,256]{2,1,0:T(8,128)(2,1)S(1)}, bf16[4,136,256]{2,1,0:T(8,128)(2,1)S(1)}, u32[]{:S(2)}, u32[]{:S(2)}) collective-permute-start(bf16[4,136,256]{2,1,0:T(8,128)(2,1)S(1)} %pad_maximum_fusion.refs_1_), channel_id=1, source_target_pairs={{0,32},{8,40},{16,48},{24,56},{32,64},{40,72},{48,80},{56,88},{64,... | collective-permute-start | bytes 835592 | tf_op jit(solution)/shard_map/ppermute | solution.py:167
  17.0 0.7 iota_add_fusion.2
  17.7 5.8 %collective-permute-done.3.refs_2_ = bf16[4,136,256]{2,1,0:T(8,128)(2,1)S(1)} collective-permute-done((bf16[4,136,256]{2,1,0:T(8,128)(2,1)S(1)}, bf16[4,136,256]{2,1,0:T(8,128)(2,1)S(1)}, u32[]{:S(2)}, u32[]{:S(2)}) %collective-permute-start.3) | collective-permute-done | bytes 278560 | tf_op jit(solution)/shard_map/ppermute | solution.py:167
  23.5 4.5 %collective-permute-start.4 = (bf16[4,136,256]{2,1,0:T(8,128)(2,1)S(1)}, bf16[4,136,256]{2,1,0:T(8,128)(2,1)S(1)}, u32[]{:S(2)}, u32[]{:S(2)}) collective-permute-start(bf16[4,136,256]{2,1,0:T(8,128)(2,1)S(1)} %collective-permute-done.3.refs_2_), channel_id=1, source_target_pairs={{0,32},{8,40},{16,48},{24,56},{32,64},{40,72},{48,80},{56,88},{64,... | collective-permute-start | bytes 835592 | tf_op jit(solution)/shard_map/ppermute | solution.py:167
  28.0 1.4 %copy.6.refs_9_ = s32[128,1]{1,0:T(8,128)} copy(s32[128,1]{0,1:T(1,128)} %bitcast.39) | data formatting | bytes 1024 | tf_op jit(solution)/shard_map/reshape | solution.py:192
  29.4 4.9 %collective-permute-done.4.refs_3_ = bf16[4,136,256]{2,1,0:T(8,128)(2,1)S(1)} collective-permute-done((bf16[4,136,256]{2,1,0:T(8,128)(2,1)S(1)}, bf16[4,136,256]{2,1,0:T(8,128)(2,1)S(1)}, u32[]{:S(2)}, u32[]{:S(2)}) %collective-permute-start.4) | collective-permute-done | bytes 278560 | tf_op jit(solution)/shard_map/ppermute | solution.py:167
  34.3 5.8 %collective-permute-start.5 = (bf16[4,136,256]{2,1,0:T(8,128)(2,1)S(1)}, bf16[4,136,256]{2,1,0:T(8,128)(2,1)S(1)}, u32[]{:S(2)}, u32[]{:S(2)}) collective-permute-start(bf16[4,136,256]{2,1,0:T(8,128)(2,1)S(1)} %collective-permute-done.4.refs_3_), channel_id=1, source_target_pairs={{0,32},{8,40},{16,48},{24,56},{32,64},{40,72},{48,80},{56,88},{64,... | collective-permute-start | bytes 835592 | tf_op jit(solution)/shard_map/ppermute | solution.py:167
  40.1 0.7 copy.7.refs_9_
  40.8 3.3 %collective-permute-done.5.refs_4_ = bf16[4,136,256]{2,1,0:T(8,128)(2,1)S(1)} collective-permute-done((bf16[4,136,256]{2,1,0:T(8,128)(2,1)S(1)}, bf16[4,136,256]{2,1,0:T(8,128)(2,1)S(1)}, u32[]{:S(2)}, u32[]{:S(2)}) %collective-permute-start.5) | collective-permute-done | bytes 278560 | tf_op jit(solution)/shard_map/ppermute | solution.py:167
  44.1 5.6 %collective-permute-start.6 = (bf16[4,136,256]{2,1,0:T(8,128)(2,1)S(1)}, bf16[4,136,256]{2,1,0:T(8,128)(2,1)S(1)}, u32[]{:S(2)}, u32[]{:S(2)}) collective-permute-start(bf16[4,136,256]{2,1,0:T(8,128)(2,1)S(1)} %collective-permute-done.5.refs_4_), channel_id=1, source_target_pairs={{0,32},{8,40},{16,48},{24,56},{32,64},{40,72},{48,80},{56,88},{64,... | collective-permute-start | bytes 835592 | tf_op jit(solution)/shard_map/ppermute | solution.py:167
  49.7 4.0 %collective-permute-done.6.refs_5_ = bf16[4,136,256]{2,1,0:T(8,128)(2,1)S(1)} collective-permute-done((bf16[4,136,256]{2,1,0:T(8,128)(2,1)S(1)}, bf16[4,136,256]{2,1,0:T(8,128)(2,1)S(1)}, u32[]{:S(2)}, u32[]{:S(2)}) %collective-permute-start.6) | collective-permute-done | bytes 278560 | tf_op jit(solution)/shard_map/ppermute | solution.py:167
  54.5 5.0 %shard_map.56 = (bf16[128,512]{1,0:T(8,128)(2,1)}, f32[128,8]{1,0:T(8,128)}, f32[8,128]{1,0:T(8,128)}) custom-call(bf16[136,512]{1,0:T(8,128)(2,1)} %copy-done.6, bf16[4,136,256]{2,1,0:T(8,128)(2,1)} %copy-done, bf16[4,136,256]{2,1,0:T(8,128)(2,1)} %copy-done.2, bf16[4,136,256]{2,1,0:T(8,128)(2,1)} %copy-done.3, bf16[4,136,256]{2,1,0:T(8,128)(2,1)} %copy-done.4, ...), custom_call_target="tpu_custom_call" | custom-call | flops 671088640 | bytes 1794048 | tf_op jit(solution)/shard_map/pallas_call | solution.py:69
  59.5 11.2 %collective-permute-start.9 = (f32[8,128]{1,0:T(8,128)}, f32[8,128]{1,0:T(8,128)S(1)}, u32[]{:S(2)}, u32[]{:S(2)}) collective-permute-start(f32[8,128]{1,0:T(8,128)} %get-tuple-element.36), channel_id=1, source_target_pairs={{0,160},{8,168},{16,176},{24,184},{32,192},{40,200},{48,208},{56,2... | collective-permute-start | bytes 12296 | tf_op jit(solution)/shard_map/ppermute | solution.py:188
  70.7 9.6 %collective-permute-start.8 = (bf16[128,512]{1,0:T(8,128)(2,1)}, bf16[128,512]{1,0:T(8,128)(2,1)S(1)}, u32[]{:S(2)}, u32[]{:S(2)}) collective-permute-start(bf16[128,512]{1,0:T(8,128)(2,1)} %get-tuple-element.35), channel_id=1, source_target_pairs={{0,160},{8,168},{16,176},{24,184},{32,192},{40,200},{48,208},{56,2... | collective-permute-start | bytes 393224 | tf_op jit(solution)/shard_map/ppermute | solution.py:187
  80.3 5.1 %shard_map.55 = (f32[128,512]{1,0:T(8,128)}, f32[128,8]{1,0:T(8,128)}, f32[8,128]{1,0:T(8,128)}) custom-call(bf16[128,512]{1,0:T(8,128)(2,1)} %refs_0_.1, bf16[4,136,256]{2,1,0:T(8,128)(2,1)} %copy-done, bf16[4,136,256]{2,1,0:T(8,128)(2,1)} %copy-done.2, bf16[4,136,256]{2,1,0:T(8,128)(2,1)} %copy-done.3, bf16[4,136,256]{2,1,0:T(8,128)(2,1)} %copy-done.4, ...), custom_call_target="tpu_custom_call" | custom-call | flops 671088640 | bytes 1785856 | tf_op jit(solution)/shard_map/pallas_call | solution.py:69
  86.7 4.5 %shard_map.57 = bf16[8,128,512]{2,1,0:T(8,128)(2,1)} custom-call(f32[128,512]{1,0:T(8,128)} %get-tuple-element.33.near_ref, f32[128,8]{1,0:T(8,128)} %get-tuple-element.34.near_stats_ref, bf16[128,512]{1,0:T(8,128)(2,1)} %copy-done.1, f32[8,128]{1,0:T(8,128)} %broadcast_select_fusion.far_rows_ref, bf16[512,4096]{1,0:T(8,128)(2,1)} %weight_ref.1), custom_call_target="tpu_custom_call" | custom-call | flops 536870912 | bytes 5242880 | tf_op jit(solution)/shard_map/pallas_call | solution.py:122
  91.2 19.9 %all_to_all.5 = bf16[8,128,512]{2,1,0:T(8,128)(2,1)S(1)} all-to-all(bf16[8,128,512]{2,1,0:T(8,128)(2,1)} %shard_map.57), channel_id=1, replica_groups=mesh['ctx'=64,'tp'=8] {'tp'}, dimensions={0} | all-to-all | bytes 2097152 | tf_op jit(solution)/shard_map/all_to_all | solution.py:200
  111.2 0.8 reduce_sum.12
  (36 shorter events, 4.3 us)
Async XLA Ops:
  1.4 10.9 %collective-permute-start.1 = (bf16[136,256]{1,0:T(8,128)(2,1)S(1)}, bf16[136,256]{1,0:T(8,128)(2,1)S(1)}, u32[]{:S(2)}, u32[]{:S(2)}) collective-permute-start(bf16[136,256]{1,0:T(8,128)(2,1)S(1)} %get-tuple-element.38), channel_id=1, source_target_pairs={{0,16},{8,24},{16,0},{24,8},{32,48},{40,56},{48,32},{56,40},{64,80... | collective-permute-start | bytes 208904 | tf_op jit(solution)/shard_map/ppermute | solution.py:162
  4.9 7.5 %collective-permute-start = (bf16[136,256]{1,0:T(8,128)(2,1)S(1)}, bf16[136,256]{1,0:T(8,128)(2,1)S(1)}, u32[]{:S(2)}, u32[]{:S(2)}) collective-permute-start(bf16[136,256]{1,0:T(8,128)(2,1)S(1)} %get-tuple-element.38), channel_id=1, source_target_pairs={{0,8},{8,0},{16,24},{24,16},{32,40},{40,32},{48,56},{56,48},{64,72... | collective-permute-start | bytes 208904 | tf_op jit(solution)/shard_map/ppermute | solution.py:162
  6.8 5.7 %collective-permute-start.2 = (bf16[136,256]{1,0:T(8,128)(2,1)S(1)}, bf16[136,256]{1,0:T(8,128)(2,1)S(1)}, u32[]{:S(2)}, u32[]{:S(2)}) collective-permute-start(bf16[136,256]{1,0:T(8,128)(2,1)S(1)} %get-tuple-element.38), channel_id=1, source_target_pairs={{0,24},{8,16},{16,8},{24,0},{32,56},{40,48},{48,40},{56,32},{64,88... | collective-permute-start | bytes 208904 | tf_op jit(solution)/shard_map/ppermute | solution.py:162
  10.3 29.8 %collective-permute-start.7 = (bf16[136,512]{1,0:T(8,128)(2,1)S(1)}, bf16[136,512]{1,0:T(8,128)(2,1)S(1)}, u32[]{:S(2)}, u32[]{:S(2)}) collective-permute-start(bf16[136,512]{1,0:T(8,128)(2,1)S(1)} %fusion.1), channel_id=1, source_target_pairs={{160,0},{168,8},{176,16},{184,24},{192,32},{200,40},{208,48},{216,... | collective-permute-start | bytes 417800 | tf_op jit(solution)/shard_map/ppermute | solution.py:158
  12.6 41.8 %copy-start = (bf16[4,136,256]{2,1,0:T(8,128)(2,1)}, bf16[4,136,256]{2,1,0:T(8,128)(2,1)S(1)}, u32[]{:S(2)}) copy-start(bf16[4,136,256]{2,1,0:T(8,128)(2,1)S(1)} %pad_maximum_fusion.refs_1_) | copy-start | bytes 835588
  12.6 10.9 %collective-permute-start.3 = (bf16[4,136,256]{2,1,0:T(8,128)(2,1)S(1)}, bf16[4,136,256]{2,1,0:T(8,128)(2,1)S(1)}, u32[]{:S(2)}, u32[]{:S(2)}) collective-permute-start(bf16[4,136,256]{2,1,0:T(8,128)(2,1)S(1)} %pad_maximum_fusion.refs_1_), channel_id=1, source_target_pairs={{0,32},{8,40},{16,48},{24,56},{32,64},{40,72},{48,80},{56,88},{64,... | collective-permute-start | bytes 835592 | tf_op jit(solution)/shard_map/ppermute | solution.py:167
  23.5 30.9 %copy-start.2 = (bf16[4,136,256]{2,1,0:T(8,128)(2,1)}, bf16[4,136,256]{2,1,0:T(8,128)(2,1)S(1)}, u32[]{:S(2)}) copy-start(bf16[4,136,256]{2,1,0:T(8,128)(2,1)S(1)} %collective-permute-done.3.refs_2_) | copy-start | bytes 835588
  23.5 10.8 %collective-permute-start.4 = (bf16[4,136,256]{2,1,0:T(8,128)(2,1)S(1)}, bf16[4,136,256]{2,1,0:T(8,128)(2,1)S(1)}, u32[]{:S(2)}, u32[]{:S(2)}) collective-permute-start(bf16[4,136,256]{2,1,0:T(8,128)(2,1)S(1)} %collective-permute-done.3.refs_2_), channel_id=1, source_target_pairs={{0,32},{8,40},{16,48},{24,56},{32,64},{40,72},{48,80},{56,88},{64,... | collective-permute-start | bytes 835592 | tf_op jit(solution)/shard_map/ppermute | solution.py:167
  34.3 20.1 %copy-start.3 = (bf16[4,136,256]{2,1,0:T(8,128)(2,1)}, bf16[4,136,256]{2,1,0:T(8,128)(2,1)S(1)}, u32[]{:S(2)}) copy-start(bf16[4,136,256]{2,1,0:T(8,128)(2,1)S(1)} %collective-permute-done.4.refs_3_) | copy-start | bytes 835588
  34.3 9.8 %collective-permute-start.5 = (bf16[4,136,256]{2,1,0:T(8,128)(2,1)S(1)}, bf16[4,136,256]{2,1,0:T(8,128)(2,1)S(1)}, u32[]{:S(2)}, u32[]{:S(2)}) collective-permute-start(bf16[4,136,256]{2,1,0:T(8,128)(2,1)S(1)} %collective-permute-done.4.refs_3_), channel_id=1, source_target_pairs={{0,32},{8,40},{16,48},{24,56},{32,64},{40,72},{48,80},{56,88},{64,... | collective-permute-start | bytes 835592 | tf_op jit(solution)/shard_map/ppermute | solution.py:167
  40.1 14.3 %copy-start.6 = (bf16[136,512]{1,0:T(8,128)(2,1)}, bf16[136,512]{1,0:T(8,128)(2,1)S(1)}, u32[]{:S(2)}) copy-start(bf16[136,512]{1,0:T(8,128)(2,1)S(1)} %collective-permute-done.7.refs_0_) | copy-start | bytes 417796
  44.1 10.3 %copy-start.4 = (bf16[4,136,256]{2,1,0:T(8,128)(2,1)}, bf16[4,136,256]{2,1,0:T(8,128)(2,1)S(1)}, u32[]{:S(2)}) copy-start(bf16[4,136,256]{2,1,0:T(8,128)(2,1)S(1)} %collective-permute-done.5.refs_4_) | copy-start | bytes 835588
  44.1 9.6 %collective-permute-start.6 = (bf16[4,136,256]{2,1,0:T(8,128)(2,1)S(1)}, bf16[4,136,256]{2,1,0:T(8,128)(2,1)S(1)}, u32[]{:S(2)}, u32[]{:S(2)}) collective-permute-start(bf16[4,136,256]{2,1,0:T(8,128)(2,1)S(1)} %collective-permute-done.5.refs_4_), channel_id=1, source_target_pairs={{0,32},{8,40},{16,48},{24,56},{32,64},{40,72},{48,80},{56,88},{64,... | collective-permute-start | bytes 835592 | tf_op jit(solution)/shard_map/ppermute | solution.py:167
  53.7 0.7 copy-start.5
  59.5 25.9 %collective-permute-start.9 = (f32[8,128]{1,0:T(8,128)}, f32[8,128]{1,0:T(8,128)S(1)}, u32[]{:S(2)}, u32[]{:S(2)}) collective-permute-start(f32[8,128]{1,0:T(8,128)} %get-tuple-element.36), channel_id=1, source_target_pairs={{0,160},{8,168},{16,176},{24,184},{32,192},{40,200},{48,208},{56,2... | collective-permute-start | bytes 12296 | tf_op jit(solution)/shard_map/ppermute | solution.py:188
  70.7 15.4 %collective-permute-start.8 = (bf16[128,512]{1,0:T(8,128)(2,1)}, bf16[128,512]{1,0:T(8,128)(2,1)S(1)}, u32[]{:S(2)}, u32[]{:S(2)}) collective-permute-start(bf16[128,512]{1,0:T(8,128)(2,1)} %get-tuple-element.35), channel_id=1, source_target_pairs={{0,160},{8,168},{16,176},{24,184},{32,192},{40,200},{48,208},{56,2... | collective-permute-start | bytes 393224 | tf_op jit(solution)/shard_map/ppermute | solution.py:187
  86.1 0.7 copy-start.1

commit v11 on v10

--- a/solution.py
+++ b/solution.py
@@ -11,6 +11,7 @@
 MAX_DOC = 4224
 PLANE = 4
 DOC_ROWS = 8
+STAT_ROWS = 32
 neg_large = -1e30
 
 
@@ -52,15 +53,26 @@
             weight.astype(jnp.bfloat16), value_part, preferred_element_type=jnp.float32
         )
         normed = jnp.where(seen, summed / jnp.maximum(total, 1e-30), 0.0)
-        out_ref[:, head * head_dim:(head + 1) * head_dim] = normed.astype(out_ref.dtype)
+        out_ref[:rows, head * head_dim:(head + 1) * head_dim] = normed.astype(out_ref.dtype)
         stats_ref[:, head:head + 1] = jnp.where(seen, peak, neg_large)
         stats_ref[:, heads + head:heads + head + 1] = total
     square_ref[...] = jnp.zeros_like(square_ref)
     square_ref[:, :2 * heads] = stats_ref[...]
-    rows_ref[...] = jnp.transpose(square_ref[...])[:2 * heads]
-
-
-def partial(query, blocks, key_pos, key_doc, query_pos, query_doc, out_dtype):
+    stat_rows = jnp.transpose(square_ref[...])[:2 * heads]
+    rows_ref[...] = stat_rows
+    if out_ref.shape[0] > rows:
+        parts = []
+        for part in range(3):
+            rounded = stat_rows.astype(jnp.bfloat16).astype(jnp.float32)
+            parts.append(rounded)
+            stat_rows = stat_rows - rounded
+        extra = out_ref.shape[0] - rows
+        parts.append(jnp.zeros((extra - 6 * heads, rows), jnp.float32))
+        out_ref[rows:, :] = jnp.zeros((extra, width), out_ref.dtype)
+        out_ref[rows:, :rows] = jnp.concatenate(parts, axis=0).astype(out_ref.dtype)
+
+
+def partial(query, blocks, key_pos, key_doc, query_pos, query_doc, out_dtype, extra=0):
     rows = query_pos.shape[0]
     width = query.shape[1]
     heads = width // HEAD_DIM
@@ -69,7 +81,7 @@
     return pl.pallas_call(
         partial_kernel,
         out_shape=(
-            jax.ShapeDtypeStruct((rows, width), out_dtype),
+            jax.ShapeDtypeStruct((rows + extra, width), out_dtype),
             jax.ShapeDtypeStruct((rows, 2 * heads), jnp.float32),
             jax.ShapeDtypeStruct((2 * heads, rows), jnp.float32),
         ),
@@ -83,13 +95,18 @@
     )(query, *blocks, key_pos, key_doc, query_pos, query_doc)
 
 
-def merge_kernel(near_ref, near_stats_ref, far_ref, far_rows_ref, weight_ref, out_ref,
+def merge_kernel(near_ref, near_stats_ref, far_ref, valid_ref, weight_ref, out_ref,
                  square_ref):
     rows, width = near_ref.shape
     heads = near_stats_ref.shape[1] // 2
     head_dim = width // heads
+    parts = far_ref[rows:rows + 6 * heads, :rows].astype(jnp.float32)
+    stat_rows = parts[:2 * heads] + parts[2 * heads:4 * heads] + parts[4 * heads:]
+    kind = lax.broadcasted_iota(jnp.int32, stat_rows.shape, 0)
+    valid = valid_ref[...] > 0.0
+    fallback = jnp.where(kind < heads, neg_large, 0.0)
     square_ref[...] = jnp.zeros_like(square_ref)
-    square_ref[:2 * heads, :] = far_rows_ref[...]
+    square_ref[:2 * heads, :] = jnp.where(valid, stat_rows, fallback)
     far_stats = jnp.transpose(square_ref[...])
     outputs = []
     for head in range(heads):
@@ -101,10 +118,8 @@
         near_share = near_total * jnp.exp(near_peak - peak)
         far_share = far_total * jnp.exp(far_peak - peak)
         columns = slice(head * head_dim, (head + 1) * head_dim)
-        summed = (
-            near_ref[:, columns].astype(jnp.float32) * near_share
-            + far_ref[:, columns].astype(jnp.float32) * far_share
-        )
+        far_part = jnp.where(valid[:, :1], far_ref[:rows, columns].astype(jnp.float32), 0.0)
+        summed = near_ref[:, columns].astype(jnp.float32) * near_share + far_part * far_share
         outputs.append((summed / (near_share + far_share)).astype(jnp.bfloat16))
     attention = jnp.concatenate(outputs, axis=1)
     partial_terms = jnp.dot(attention, weight_ref[...], preferred_element_type=jnp.float32)
@@ -181,11 +196,10 @@
     visit_pos = (my_index + PLANE * far) * rows + offsets_in_shard
     visit_doc = visiting[rows, :rows].astype(jnp.int32).reshape(rows, 1)
     visit_out, visit_stats, visit_rows = partial(
-        visiting, blocks, key_pos, key_doc, visit_pos, visit_doc, jnp.bfloat16
+        visiting, blocks, key_pos, key_doc, visit_pos, visit_doc, jnp.bfloat16, STAT_ROWS
     )
     ahead = [(s, s + PLANE * far) for s in range(ctx - PLANE * far)]
     far_out = lax.ppermute(visit_out, "ctx", ahead)
-    far_rows = lax.ppermute(visit_rows, "ctx", ahead)
 
     query_pos = my_index * rows + offsets_in_shard
     near_out, near_stats, _ = partial(
@@ -193,9 +207,8 @@
     )
     has_far = plane >= far
     heads = near_stats.shape[1] // 2
-    kind = jnp.arange(2 * heads, dtype=jnp.int32)[:, None]
-    far_rows = jnp.where(has_far, far_rows, jnp.where(kind < heads, neg_large, 0.0))
-    chunks = merge(near_out, near_stats, far_out, far_rows, out_weight, tp)
+    valid = jnp.where(has_far, 1.0, 0.0) * jnp.ones((1, rows), jnp.float32)
+    chunks = merge(near_out, near_stats, far_out, valid, out_weight, tp)
 
     received = lax.all_to_all(chunks, "tp", 0, 0, tiled=True)
     mixed = jnp.sum(received.astype(jnp.float32), axis=0)

time: 113 us -> 113 us (level)
  the two profiles are of different devices: /device:TPU:64 before, /device:TPU:128 now
where the time goes in v11:
time: 113 us
  starting transfers between devices  34.1 us (30%)
  waiting for transfers between devices  30.2 us (27%)
  blocking collectives  24.8 us (22%)
  Pallas kernels  14.6 us (13%)
  other arithmetic  5.92 us (5%)
  local copies, waits for them, and re-layouts  2.89 us (3%)
    all_to_all x1, blocking collectives, shards(): received = lax.all_to_all(chunks, 'tp', 0, 0, tiled=True)  24.8 us
    ppermute x4, waiting for transfers between devices, shards(): current = lax.ppermute(current, 'ctx', forward)  22.5 us
    ppermute x4, starting transfers between devices, shards(): current = lax.ppermute(current, 'ctx', forward)  16.7 us
    pallas_call x2, Pallas kernels, partial(): pl.pallas_call(partial_kernel, out_shape=(jax.ShapeDtypeStruct((rows + ex...  10.1 us
    ppermute x1, starting transfers between devices, shards(): far_out = lax.ppermute(visit_out, 'ctx', ahead)  8.18 us
    ppermute x3, starting transfers between devices, shards(): lax.ppermute(block, 'ctx', [(s, s ^ offset) for s in range(ctx)])  7.87 us
    ppermute x1, waiting for transfers between devices, shards(): far_out = lax.ppermute(visit_out, 'ctx', ahead)  6.85 us
    pallas_call x1, Pallas kernels, merge(): pl.pallas_call(merge_kernel, out_shape=jax.ShapeDtypeStruct((pieces, rows...  4.52 us
  transfers between devices with their start and end apart: 9, of which 6 were waited for; matrix products, arithmetic and copies ran while one was open for 5% of the time, Pallas kernels for 4%

profile of v11, /device:TPU:128, one launch (start us, length us, event | category | flops | bytes accessed | tf_op | source)
XLA Modules:
  0.0 112.7 jit_solution(9847187855654274087)
XLA Ops:
  0.7 0.8 fusion.5
  1.4 3.4 %collective-permute-start.1 = (bf16[136,256]{1,0:T(8,128)(2,1)S(1)}, bf16[136,256]{1,0:T(8,128)(2,1)S(1)}, u32[]{:S(2)}, u32[]{:S(2)}) collective-permute-start(bf16[136,256]{1,0:T(8,128)(2,1)S(1)} %get-tuple-element.36), channel_id=1, source_target_pairs={{0,16},{8,24},{16,0},{24,8},{32,48},{40,56},{48,32},{56,40},{64,80... | collective-permute-start | bytes 208904 | tf_op jit(solution)/shard_map/ppermute | solution.py:177
  4.9 1.9 %collective-permute-start = (bf16[136,256]{1,0:T(8,128)(2,1)S(1)}, bf16[136,256]{1,0:T(8,128)(2,1)S(1)}, u32[]{:S(2)}, u32[]{:S(2)}) collective-permute-start(bf16[136,256]{1,0:T(8,128)(2,1)S(1)} %get-tuple-element.36), channel_id=1, source_target_pairs={{0,8},{8,0},{16,24},{24,16},{32,40},{40,32},{48,56},{56,48},{64,72... | collective-permute-start | bytes 208904 | tf_op jit(solution)/shard_map/ppermute | solution.py:177
  6.8 2.5 %collective-permute-start.2 = (bf16[136,256]{1,0:T(8,128)(2,1)S(1)}, bf16[136,256]{1,0:T(8,128)(2,1)S(1)}, u32[]{:S(2)}, u32[]{:S(2)}) collective-permute-start(bf16[136,256]{1,0:T(8,128)(2,1)S(1)} %get-tuple-element.36), channel_id=1, source_target_pairs={{0,24},{8,16},{16,8},{24,0},{32,56},{40,48},{48,40},{56,32},{64,88... | collective-permute-start | bytes 208904 | tf_op jit(solution)/shard_map/ppermute | solution.py:177
  9.3 0.9 fusion.1
  10.3 1.3 %collective-permute-start.7 = (bf16[136,512]{1,0:T(8,128)(2,1)S(1)}, bf16[136,512]{1,0:T(8,128)(2,1)S(1)}, u32[]{:S(2)}, u32[]{:S(2)}) collective-permute-start(bf16[136,512]{1,0:T(8,128)(2,1)S(1)} %fusion.1), channel_id=1, source_target_pairs={{160,0},{168,8},{176,16},{184,24},{192,32},{200,40},{208,48},{216,... | collective-permute-start | bytes 417800 | tf_op jit(solution)/shard_map/ppermute | solution.py:173
  11.6 0.9 collective-permute-done.2
  12.6 7.2 %collective-permute-start.3 = (bf16[4,136,256]{2,1,0:T(8,128)(2,1)S(1)}, bf16[4,136,256]{2,1,0:T(8,128)(2,1)S(1)}, u32[]{:S(2)}, u32[]{:S(2)}) collective-permute-start(bf16[4,136,256]{2,1,0:T(8,128)(2,1)S(1)} %pad_maximum_fusion.refs_1_), channel_id=1, source_target_pairs={{0,32},{8,40},{16,48},{24,56},{32,64},{40,72},{48,80},{56,88},{64,... | collective-permute-start | bytes 835592 | tf_op jit(solution)/shard_map/ppermute | solution.py:182
  20.6 5.0 %collective-permute-done.3.refs_2_ = bf16[4,136,256]{2,1,0:T(8,128)(2,1)S(1)} collective-permute-done((bf16[4,136,256]{2,1,0:T(8,128)(2,1)S(1)}, bf16[4,136,256]{2,1,0:T(8,128)(2,1)S(1)}, u32[]{:S(2)}, u32[]{:S(2)}) %collective-permute-start.3) | collective-permute-done | bytes 278560 | tf_op jit(solution)/shard_map/ppermute | solution.py:182
  25.6 4.4 %collective-permute-start.4 = (bf16[4,136,256]{2,1,0:T(8,128)(2,1)S(1)}, bf16[4,136,256]{2,1,0:T(8,128)(2,1)S(1)}, u32[]{:S(2)}, u32[]{:S(2)}) collective-permute-start(bf16[4,136,256]{2,1,0:T(8,128)(2,1)S(1)} %collective-permute-done.3.refs_2_), channel_id=1, source_target_pairs={{0,32},{8,40},{16,48},{24,56},{32,64},{40,72},{48,80},{56,88},{64,... | collective-permute-start | bytes 835592 | tf_op jit(solution)/shard_map/ppermute | solution.py:182
  30.6 1.4 %copy.6.refs_9_ = s32[128,1]{1,0:T(8,128)} copy(s32[128,1]{0,1:T(1,128)} %bitcast.39) | data formatting | bytes 1024 | tf_op jit(solution)/shard_map/reshape | solution.py:206
  32.0 4.1 %collective-permute-done.4.refs_3_ = bf16[4,136,256]{2,1,0:T(8,128)(2,1)S(1)} collective-permute-done((bf16[4,136,256]{2,1,0:T(8,128)(2,1)S(1)}, bf16[4,136,256]{2,1,0:T(8,128)(2,1)S(1)}, u32[]{:S(2)}, u32[]{:S(2)}) %collective-permute-start.4) | collective-permute-done | bytes 278560 | tf_op jit(solution)/shard_map/ppermute | solution.py:182
  36.1 3.2 %collective-permute-start.5 = (bf16[4,136,256]{2,1,0:T(8,128)(2,1)S(1)}, bf16[4,136,256]{2,1,0:T(8,128)(2,1)S(1)}, u32[]{:S(2)}, u32[]{:S(2)}) collective-permute-start(bf16[4,136,256]{2,1,0:T(8,128)(2,1)S(1)} %collective-permute-done.4.refs_3_), channel_id=1, source_target_pairs={{0,32},{8,40},{16,48},{24,56},{32,64},{40,72},{48,80},{56,88},{64,... | collective-permute-start | bytes 835592 | tf_op jit(solution)/shard_map/ppermute | solution.py:182
  39.3 0.7 copy.7.refs_9_
  40.1 5.7 %collective-permute-done.5.refs_4_ = bf16[4,136,256]{2,1,0:T(8,128)(2,1)S(1)} collective-permute-done((bf16[4,136,256]{2,1,0:T(8,128)(2,1)S(1)}, bf16[4,136,256]{2,1,0:T(8,128)(2,1)S(1)}, u32[]{:S(2)}, u32[]{:S(2)}) %collective-permute-start.5) | collective-permute-done | bytes 278560 | tf_op jit(solution)/shard_map/ppermute | solution.py:182
  45.7 2.0 %collective-permute-start.6 = (bf16[4,136,256]{2,1,0:T(8,128)(2,1)S(1)}, bf16[4,136,256]{2,1,0:T(8,128)(2,1)S(1)}, u32[]{:S(2)}, u32[]{:S(2)}) collective-permute-start(bf16[4,136,256]{2,1,0:T(8,128)(2,1)S(1)} %collective-permute-done.5.refs_4_), channel_id=1, source_target_pairs={{0,32},{8,40},{16,48},{24,56},{32,64},{40,72},{48,80},{56,88},{64,... | collective-permute-start | bytes 835592 | tf_op jit(solution)/shard_map/ppermute | solution.py:182
  47.7 7.6 %collective-permute-done.6.refs_5_ = bf16[4,136,256]{2,1,0:T(8,128)(2,1)S(1)} collective-permute-done((bf16[4,136,256]{2,1,0:T(8,128)(2,1)S(1)}, bf16[4,136,256]{2,1,0:T(8,128)(2,1)S(1)}, u32[]{:S(2)}, u32[]{:S(2)}) %collective-permute-start.6) | collective-permute-done | bytes 278560 | tf_op jit(solution)/shard_map/ppermute | solution.py:182
  56.1 5.0 %shard_map.56 = (bf16[160,512]{1,0:T(8,128)(2,1)}, f32[128,8]{1,0:T(8,128)}, f32[8,128]{1,0:T(8,128)}) custom-call(bf16[136,512]{1,0:T(8,128)(2,1)} %copy-done.6, bf16[4,136,256]{2,1,0:T(8,128)(2,1)} %copy-done, bf16[4,136,256]{2,1,0:T(8,128)(2,1)} %copy-done.2, bf16[4,136,256]{2,1,0:T(8,128)(2,1)} %copy-done.3, bf16[4,136,256]{2,1,0:T(8,128)(2,1)} %copy-done.4, ...), custom_call_target="tpu_custom_call" | custom-call | flops 671088640 | bytes 1794048 | tf_op jit(solution)/shard_map/pallas_call | solution.py:81
  61.1 8.2 %collective-permute-start.8 = (bf16[160,512]{1,0:T(8,128)(2,1)}, bf16[160,512]{1,0:T(8,128)(2,1)S(1)}, u32[]{:S(2)}, u32[]{:S(2)}) collective-permute-start(bf16[160,512]{1,0:T(8,128)(2,1)} %get-tuple-element.34), channel_id=1, source_target_pairs={{0,160},{8,168},{16,176},{24,184},{32,192},{40,200},{48,208},{56,2... | collective-permute-start | bytes 491528 | tf_op jit(solution)/shard_map/ppermute | solution.py:202
  70.0 5.1 %shard_map.55 = (f32[128,512]{1,0:T(8,128)}, f32[128,8]{1,0:T(8,128)}, f32[8,128]{1,0:T(8,128)}) custom-call(bf16[128,512]{1,0:T(8,128)(2,1)} %refs_0_.1, bf16[4,136,256]{2,1,0:T(8,128)(2,1)} %copy-done, bf16[4,136,256]{2,1,0:T(8,128)(2,1)} %copy-done.2, bf16[4,136,256]{2,1,0:T(8,128)(2,1)} %copy-done.3, bf16[4,136,256]{2,1,0:T(8,128)(2,1)} %copy-done.4, ...), custom_call_target="tpu_custom_call" | custom-call | flops 671088640 | bytes 1785856 | tf_op jit(solution)/shard_map/pallas_call | solution.py:81
  75.0 6.8 %collective-permute-done.8.far_ref = bf16[160,512]{1,0:T(8,128)(2,1)S(1)} collective-permute-done((bf16[160,512]{1,0:T(8,128)(2,1)}, bf16[160,512]{1,0:T(8,128)(2,1)S(1)}, u32[]{:S(2)}, u32[]{:S(2)}) %collective-permute-start.8) | collective-permute-done | bytes 163872 | tf_op jit(solution)/shard_map/ppermute | solution.py:202
  82.6 4.5 %shard_map.57 = bf16[8,128,512]{2,1,0:T(8,128)(2,1)} custom-call(f32[128,512]{1,0:T(8,128)} %get-tuple-element.32.near_ref, f32[128,8]{1,0:T(8,128)} %get-tuple-element.33.near_stats_ref, bf16[160,512]{1,0:T(8,128)(2,1)} %copy-done.1, f32[1,128]{1,0:T(1,128)} %mul.29.valid_ref, bf16[512,4096]{1,0:T(8,128)(2,1)} %weight_ref.1), custom_call_target="tpu_custom_call" | custom-call | flops 536870912 | bytes 5242880 | tf_op jit(solution)/shard_map/pallas_call | solution.py:137
  87.1 24.8 %all_to_all.5 = bf16[8,128,512]{2,1,0:T(8,128)(2,1)S(1)} all-to-all(bf16[8,128,512]{2,1,0:T(8,128)(2,1)} %shard_map.57), channel_id=1, replica_groups=mesh['ctx'=64,'tp'=8] {'tp'}, dimensions={0} | all-to-all | bytes 2097152 | tf_op jit(solution)/shard_map/all_to_all | solution.py:213
  111.9 0.8 reduce_sum.12
  (33 shorter events, 4.2 us)
Async XLA Ops:
  1.4 10.2 %collective-permute-start.1 = (bf16[136,256]{1,0:T(8,128)(2,1)S(1)}, bf16[136,256]{1,0:T(8,128)(2,1)S(1)}, u32[]{:S(2)}, u32[]{:S(2)}) collective-permute-start(bf16[136,256]{1,0:T(8,128)(2,1)S(1)} %get-tuple-element.36), channel_id=1, source_target_pairs={{0,16},{8,24},{16,0},{24,8},{32,48},{40,56},{48,32},{56,40},{64,80... | collective-permute-start | bytes 208904 | tf_op jit(solution)/shard_map/ppermute | solution.py:177
  4.9 6.8 %collective-permute-start = (bf16[136,256]{1,0:T(8,128)(2,1)S(1)}, bf16[136,256]{1,0:T(8,128)(2,1)S(1)}, u32[]{:S(2)}, u32[]{:S(2)}) collective-permute-start(bf16[136,256]{1,0:T(8,128)(2,1)S(1)} %get-tuple-element.36), channel_id=1, source_target_pairs={{0,8},{8,0},{16,24},{24,16},{32,40},{40,32},{48,56},{56,48},{64,72... | collective-permute-start | bytes 208904 | tf_op jit(solution)/shard_map/ppermute | solution.py:177
  6.8 5.7 %collective-permute-start.2 = (bf16[136,256]{1,0:T(8,128)(2,1)S(1)}, bf16[136,256]{1,0:T(8,128)(2,1)S(1)}, u32[]{:S(2)}, u32[]{:S(2)}) collective-permute-start(bf16[136,256]{1,0:T(8,128)(2,1)S(1)} %get-tuple-element.36), channel_id=1, source_target_pairs={{0,24},{8,16},{16,8},{24,0},{32,56},{40,48},{48,40},{56,32},{64,88... | collective-permute-start | bytes 208904 | tf_op jit(solution)/shard_map/ppermute | solution.py:177
  10.3 29.0 %collective-permute-start.7 = (bf16[136,512]{1,0:T(8,128)(2,1)S(1)}, bf16[136,512]{1,0:T(8,128)(2,1)S(1)}, u32[]{:S(2)}, u32[]{:S(2)}) collective-permute-start(bf16[136,512]{1,0:T(8,128)(2,1)S(1)} %fusion.1), channel_id=1, source_target_pairs={{160,0},{168,8},{176,16},{184,24},{192,32},{200,40},{208,48},{216,... | collective-permute-start | bytes 417800 | tf_op jit(solution)/shard_map/ppermute | solution.py:173
  12.6 43.5 %copy-start = (bf16[4,136,256]{2,1,0:T(8,128)(2,1)}, bf16[4,136,256]{2,1,0:T(8,128)(2,1)S(1)}, u32[]{:S(2)}) copy-start(bf16[4,136,256]{2,1,0:T(8,128)(2,1)S(1)} %pad_maximum_fusion.refs_1_) | copy-start | bytes 835588
  12.6 13.0 %collective-permute-start.3 = (bf16[4,136,256]{2,1,0:T(8,128)(2,1)S(1)}, bf16[4,136,256]{2,1,0:T(8,128)(2,1)S(1)}, u32[]{:S(2)}, u32[]{:S(2)}) collective-permute-start(bf16[4,136,256]{2,1,0:T(8,128)(2,1)S(1)} %pad_maximum_fusion.refs_1_), channel_id=1, source_target_pairs={{0,32},{8,40},{16,48},{24,56},{32,64},{40,72},{48,80},{56,88},{64,... | collective-permute-start | bytes 835592 | tf_op jit(solution)/shard_map/ppermute | solution.py:182
  25.6 30.5 %copy-start.2 = (bf16[4,136,256]{2,1,0:T(8,128)(2,1)}, bf16[4,136,256]{2,1,0:T(8,128)(2,1)S(1)}, u32[]{:S(2)}) copy-start(bf16[4,136,256]{2,1,0:T(8,128)(2,1)S(1)} %collective-permute-done.3.refs_2_) | copy-start | bytes 835588
  25.6 10.5 %collective-permute-start.4 = (bf16[4,136,256]{2,1,0:T(8,128)(2,1)S(1)}, bf16[4,136,256]{2,1,0:T(8,128)(2,1)S(1)}, u32[]{:S(2)}, u32[]{:S(2)}) collective-permute-start(bf16[4,136,256]{2,1,0:T(8,128)(2,1)S(1)} %collective-permute-done.3.refs_2_), channel_id=1, source_target_pairs={{0,32},{8,40},{16,48},{24,56},{32,64},{40,72},{48,80},{56,88},{64,... | collective-permute-start | bytes 835592 | tf_op jit(solution)/shard_map/ppermute | solution.py:182
  36.1 20.0 %copy-start.3 = (bf16[4,136,256]{2,1,0:T(8,128)(2,1)}, bf16[4,136,256]{2,1,0:T(8,128)(2,1)S(1)}, u32[]{:S(2)}) copy-start(bf16[4,136,256]{2,1,0:T(8,128)(2,1)S(1)} %collective-permute-done.4.refs_3_) | copy-start | bytes 835588
  36.1 9.6 %collective-permute-start.5 = (bf16[4,136,256]{2,1,0:T(8,128)(2,1)S(1)}, bf16[4,136,256]{2,1,0:T(8,128)(2,1)S(1)}, u32[]{:S(2)}, u32[]{:S(2)}) collective-permute-start(bf16[4,136,256]{2,1,0:T(8,128)(2,1)S(1)} %collective-permute-done.4.refs_3_), channel_id=1, source_target_pairs={{0,32},{8,40},{16,48},{24,56},{32,64},{40,72},{48,80},{56,88},{64,... | collective-permute-start | bytes 835592 | tf_op jit(solution)/shard_map/ppermute | solution.py:182
  39.3 16.8 %copy-start.6 = (bf16[136,512]{1,0:T(8,128)(2,1)}, bf16[136,512]{1,0:T(8,128)(2,1)S(1)}, u32[]{:S(2)}) copy-start(bf16[136,512]{1,0:T(8,128)(2,1)S(1)} %collective-permute-done.7.refs_0_) | copy-start | bytes 417796
  45.7 10.3 %copy-start.4 = (bf16[4,136,256]{2,1,0:T(8,128)(2,1)}, bf16[4,136,256]{2,1,0:T(8,128)(2,1)S(1)}, u32[]{:S(2)}) copy-start(bf16[4,136,256]{2,1,0:T(8,128)(2,1)S(1)} %collective-permute-done.5.refs_4_) | copy-start | bytes 835588
  45.7 9.6 %collective-permute-start.6 = (bf16[4,136,256]{2,1,0:T(8,128)(2,1)S(1)}, bf16[4,136,256]{2,1,0:T(8,128)(2,1)S(1)}, u32[]{:S(2)}, u32[]{:S(2)}) collective-permute-start(bf16[4,136,256]{2,1,0:T(8,128)(2,1)S(1)} %collective-permute-done.5.refs_4_), channel_id=1, source_target_pairs={{0,32},{8,40},{16,48},{24,56},{32,64},{40,72},{48,80},{56,88},{64,... | collective-permute-start | bytes 835592 | tf_op jit(solution)/shard_map/ppermute | solution.py:182
  55.4 0.7 copy-start.5
  61.1 20.7 %collective-permute-start.8 = (bf16[160,512]{1,0:T(8,128)(2,1)}, bf16[160,512]{1,0:T(8,128)(2,1)S(1)}, u32[]{:S(2)}, u32[]{:S(2)}) collective-permute-start(bf16[160,512]{1,0:T(8,128)(2,1)} %get-tuple-element.34), channel_id=1, source_target_pairs={{0,160},{8,168},{16,176},{24,184},{32,192},{40,200},{48,208},{56,2... | collective-permute-start | bytes 491528 | tf_op jit(solution)/shard_map/ppermute | solution.py:202
  81.9 0.7 copy-start.1

commit v12 on v10

--- a/solution.py
+++ b/solution.py
@@ -144,7 +144,8 @@
 
     shards_back = -(-(MAX_DOC - 1) // rows)
     reach = min(-(-(shards_back + PLANE - 1) // PLANE), planes - 1)
-    hops = reach // 2
+    hops = (reach + 1) // 2
+    far_planes = reach - hops
     far = hops + 1
 
     doc_rows = jnp.zeros((DOC_ROWS, 2 * head_dim), jnp.bfloat16)
@@ -172,16 +173,19 @@
     offsets = jnp.arange(PLANE, dtype=jnp.int32)[None, :, None]
     tokens = jnp.arange(rows, dtype=jnp.int32)[None, None, :]
     key_shard = PLANE * (plane - hop_ids) + (slot ^ offsets)
-    key_pos = (key_shard * rows + tokens).reshape(1, -1)
-    key_doc = jnp.concatenate(
-        [b[:, rows, :rows].astype(jnp.int32).reshape(1, -1) for b in blocks], axis=1
-    )
+    key_pos = (key_shard * rows + tokens).reshape(hops + 1, -1)
+    key_doc = [b[:, rows, :rows].astype(jnp.int32).reshape(1, -1) for b in blocks]
+    far_blocks = blocks[:far_planes]
+    far_key_pos = key_pos[:far_planes].reshape(1, -1)
+    far_key_doc = jnp.concatenate(key_doc[:far_planes], axis=1)
+    key_pos = key_pos.reshape(1, -1)
+    key_doc = jnp.concatenate(key_doc, axis=1)
 
     offsets_in_shard = jnp.arange(rows, dtype=jnp.int32).reshape(rows, 1)
     visit_pos = (my_index + PLANE * far) * rows + offsets_in_shard
     visit_doc = visiting[rows, :rows].astype(jnp.int32).reshape(rows, 1)
     visit_out, visit_stats, visit_rows = partial(
-        visiting, blocks, key_pos, key_doc, visit_pos, visit_doc, jnp.bfloat16
+        visiting, far_blocks, far_key_pos, far_key_doc, visit_pos, visit_doc, jnp.bfloat16
     )
     ahead = [(s, s + PLANE * far) for s in range(ctx - PLANE * far)]
     far_out = lax.ppermute(visit_out, "ctx", ahead)

time: 113 us -> 125 us (1.11)
  the two profiles are of different devices: /device:TPU:64 before, /device:TPU:192 now
where the time goes in v12:
time: 125 us; the launch traced here: 124 us
  waiting for transfers between devices  48.6 us (39%)
  starting transfers between devices  27.4 us (22%)
  blocking collectives  22.7 us (18%)
  Pallas kernels  14.8 us (12%)
  other arithmetic  6.69 us (5%)
  local copies, waits for them, and re-layouts  4.06 us (3%)
    ppermute x5, waiting for transfers between devices, shards(): current = lax.ppermute(current, 'ctx', forward)  28.1 us
    all_to_all x1, blocking collectives, shards(): received = lax.all_to_all(chunks, 'tp', 0, 0, tiled=True)  22.7 us
    ppermute x1, waiting for transfers between devices, shards(): visiting = lax.ppermute(packed_queries, 'ctx', back)  13.7 us
    pallas_call x2, Pallas kernels, partial(): pl.pallas_call(partial_kernel, out_shape=(jax.ShapeDtypeStruct((rows, wid...  10.2 us
    ppermute x5, starting transfers between devices, shards(): current = lax.ppermute(current, 'ctx', forward)  10 us
    ppermute x3, starting transfers between devices, shards(): lax.ppermute(block, 'ctx', [(s, s ^ offset) for s in range(ctx)])  7.59 us
    ppermute x1, waiting for transfers between devices, shards(): far_rows = lax.ppermute(visit_rows, 'ctx', ahead)  6.83 us
    ppermute x1, starting transfers between devices, shards(): visiting = lax.ppermute(packed_queries, 'ctx', back)  5.12 us
  transfers between devices with their start and end apart: 11, of which 5 were waited for; matrix products, arithmetic and copies ran while one was open for 6% of the time, Pallas kernels for 8%

profile of v12, /device:TPU:192, one launch (start us, length us, event | category | flops | bytes accessed | tf_op | source)
XLA Modules:
  0.0 124.4 jit_solution(14881208185100525191)
XLA Ops:
  0.7 0.8 fusion.11
  1.4 2.8 %collective-permute-start.2 = (bf16[136,256]{1,0:T(8,128)(2,1)S(1)}, bf16[136,256]{1,0:T(8,128)(2,1)S(1)}, u32[]{:S(2)}, u32[]{:S(2)}) collective-permute-start(bf16[136,256]{1,0:T(8,128)(2,1)S(1)} %get-tuple-element.38), channel_id=1, source_target_pairs={{0,24},{8,16},{16,8},{24,0},{32,56},{40,48},{48,40},{56,32},{64,88... | collective-permute-start | bytes 208904 | tf_op jit(solution)/shard_map/ppermute | solution.py:163
  4.3 2.5 %collective-permute-start.1 = (bf16[136,256]{1,0:T(8,128)(2,1)S(1)}, bf16[136,256]{1,0:T(8,128)(2,1)S(1)}, u32[]{:S(2)}, u32[]{:S(2)}) collective-permute-start(bf16[136,256]{1,0:T(8,128)(2,1)S(1)} %get-tuple-element.38), channel_id=1, source_target_pairs={{0,16},{8,24},{16,0},{24,8},{32,48},{40,56},{48,32},{56,40},{64,80... | collective-permute-start | bytes 208904 | tf_op jit(solution)/shard_map/ppermute | solution.py:163
  6.8 2.3 %collective-permute-start = (bf16[136,256]{1,0:T(8,128)(2,1)S(1)}, bf16[136,256]{1,0:T(8,128)(2,1)S(1)}, u32[]{:S(2)}, u32[]{:S(2)}) collective-permute-start(bf16[136,256]{1,0:T(8,128)(2,1)S(1)} %get-tuple-element.38), channel_id=1, source_target_pairs={{0,8},{8,0},{16,24},{24,16},{32,40},{40,32},{48,56},{56,48},{64,72... | collective-permute-start | bytes 208904 | tf_op jit(solution)/shard_map/ppermute | solution.py:163
  9.1 0.9 fusion.1
  10.0 5.1 %collective-permute-start.8 = (bf16[136,512]{1,0:T(8,128)(2,1)S(1)}, bf16[136,512]{1,0:T(8,128)(2,1)S(1)}, u32[]{:S(2)}, u32[]{:S(2)}) collective-permute-start(bf16[136,512]{1,0:T(8,128)(2,1)S(1)} %fusion.1), channel_id=1, source_target_pairs={{192,0},{200,8},{208,16},{216,24},{224,32},{232,40},{240,48},{248,... | collective-permute-start | bytes 417800 | tf_op jit(solution)/shard_map/ppermute | solution.py:159
  15.9 1.4 %copy.6.refs_10_ = s32[128,1]{1,0:T(8,128)} copy(s32[128,1]{0,1:T(1,128)} %bitcast.62) | data formatting | bytes 1024 | tf_op jit(solution)/shard_map/reshape | solution.py:196
  18.6 1.9 %collective-permute-start.3 = (bf16[4,136,256]{2,1,0:T(8,128)(2,1)S(1)}, bf16[4,136,256]{2,1,0:T(8,128)(2,1)S(1)}, u32[]{:S(2)}, u32[]{:S(2)}) collective-permute-start(bf16[4,136,256]{2,1,0:T(8,128)(2,1)S(1)} %pad_maximum_fusion.refs_1_), channel_id=1, source_target_pairs={{0,32},{8,40},{16,48},{24,56},{32,64},{40,72},{48,80},{56,88},{64,... | collective-permute-start | bytes 835592 | tf_op jit(solution)/shard_map/ppermute | solution.py:168
  20.6 13.7 %collective-permute-done.8.refs_0_ = bf16[136,512]{1,0:T(8,128)(2,1)S(1)} collective-permute-done((bf16[136,512]{1,0:T(8,128)(2,1)S(1)}, bf16[136,512]{1,0:T(8,128)(2,1)S(1)}, u32[]{:S(2)}, u32[]{:S(2)}) %collective-permute-start.8) | collective-permute-done | bytes 139296 | tf_op jit(solution)/shard_map/ppermute | solution.py:159
  35.0 1.9 %collective-permute-start.4 = (bf16[4,136,256]{2,1,0:T(8,128)(2,1)S(1)}, bf16[4,136,256]{2,1,0:T(8,128)(2,1)S(1)}, u32[]{:S(2)}, u32[]{:S(2)}) collective-permute-start(bf16[4,136,256]{2,1,0:T(8,128)(2,1)S(1)} %collective-permute-done.3.refs_2_), channel_id=1, source_target_pairs={{0,32},{8,40},{16,48},{24,56},{32,64},{40,72},{48,80},{56,88},{64,... | collective-permute-start | bytes 835592 | tf_op jit(solution)/shard_map/ppermute | solution.py:168
  36.9 7.7 %collective-permute-done.4.refs_3_ = bf16[4,136,256]{2,1,0:T(8,128)(2,1)S(1)} collective-permute-done((bf16[4,136,256]{2,1,0:T(8,128)(2,1)S(1)}, bf16[4,136,256]{2,1,0:T(8,128)(2,1)S(1)}, u32[]{:S(2)}, u32[]{:S(2)}) %collective-permute-start.4) | collective-permute-done | bytes 278560 | tf_op jit(solution)/shard_map/ppermute | solution.py:168
  44.6 2.2 %collective-permute-start.5 = (bf16[4,136,256]{2,1,0:T(8,128)(2,1)S(1)}, bf16[4,136,256]{2,1,0:T(8,128)(2,1)S(1)}, u32[]{:S(2)}, u32[]{:S(2)}) collective-permute-start(bf16[4,136,256]{2,1,0:T(8,128)(2,1)S(1)} %collective-permute-done.4.refs_3_), channel_id=1, source_target_pairs={{0,32},{8,40},{16,48},{24,56},{32,64},{40,72},{48,80},{56,88},{64,... | collective-permute-start | bytes 835592 | tf_op jit(solution)/shard_map/ppermute | solution.py:168
  46.9 8.6 %collective-permute-done.5.refs_4_ = bf16[4,136,256]{2,1,0:T(8,128)(2,1)S(1)} collective-permute-done((bf16[4,136,256]{2,1,0:T(8,128)(2,1)S(1)}, bf16[4,136,256]{2,1,0:T(8,128)(2,1)S(1)}, u32[]{:S(2)}, u32[]{:S(2)}) %collective-permute-start.5) | collective-permute-done | bytes 278560 | tf_op jit(solution)/shard_map/ppermute | solution.py:168
  55.4 1.9 %collective-permute-start.6 = (bf16[4,136,256]{2,1,0:T(8,128)(2,1)S(1)}, bf16[4,136,256]{2,1,0:T(8,128)(2,1)S(1)}, u32[]{:S(2)}, u32[]{:S(2)}) collective-permute-start(bf16[4,136,256]{2,1,0:T(8,128)(2,1)S(1)} %collective-permute-done.5.refs_4_), channel_id=1, source_target_pairs={{0,32},{8,40},{16,48},{24,56},{32,64},{40,72},{48,80},{56,88},{64,... | collective-permute-start | bytes 835592 | tf_op jit(solution)/shard_map/ppermute | solution.py:168
  58.0 4.6 %shard_map.56 = (bf16[128,512]{1,0:T(8,128)(2,1)}, f32[128,8]{1,0:T(8,128)}, f32[8,128]{1,0:T(8,128)}) custom-call(bf16[136,512]{1,0:T(8,128)(2,1)} %copy-done.9, bf16[4,136,256]{2,1,0:T(8,128)(2,1)} %copy-done, bf16[4,136,256]{2,1,0:T(8,128)(2,1)} %copy-done.4, bf16[4,136,256]{2,1,0:T(8,128)(2,1)} %copy-done.5, bf16[4,136,256]{2,1,0:T(8,128)(2,1)} %copy-done.6, ...), custom_call_target="tpu_custom_call" | custom-call | flops 536870912 | bytes 1515520 | tf_op jit(solution)/shard_map/pallas_call | solution.py:69
  62.6 2.8 %collective-permute-start.9 = (bf16[128,512]{1,0:T(8,128)(2,1)}, bf16[128,512]{1,0:T(8,128)(2,1)S(1)}, u32[]{:S(2)}, u32[]{:S(2)}) collective-permute-start(bf16[128,512]{1,0:T(8,128)(2,1)} %get-tuple-element.35), channel_id=1, source_target_pairs={{0,192},{8,200},{16,208},{24,216},{32,224},{40,232},{48,240},{56,2... | collective-permute-start | bytes 393224 | tf_op jit(solution)/shard_map/ppermute | solution.py:191
  65.4 1.9 %collective-permute-start.10 = (f32[8,128]{1,0:T(8,128)}, f32[8,128]{1,0:T(8,128)S(1)}, u32[]{:S(2)}, u32[]{:S(2)}) collective-permute-start(f32[8,128]{1,0:T(8,128)} %get-tuple-element.36), channel_id=1, source_target_pairs={{0,192},{8,200},{16,208},{24,216},{32,224},{40,232},{48,240},{56,2... | collective-permute-start | bytes 12296 | tf_op jit(solution)/shard_map/ppermute | solution.py:192
  68.0 2.1 %collective-permute-start.7 = (bf16[4,136,256]{2,1,0:T(8,128)(2,1)S(1)}, bf16[4,136,256]{2,1,0:T(8,128)(2,1)S(1)}, u32[]{:S(2)}, u32[]{:S(2)}) collective-permute-start(bf16[4,136,256]{2,1,0:T(8,128)(2,1)S(1)} %collective-permute-done.6.refs_5_), channel_id=1, source_target_pairs={{0,32},{8,40},{16,48},{24,56},{32,64},{40,72},{48,80},{56,88},{64,... | collective-permute-start | bytes 835592 | tf_op jit(solution)/shard_map/ppermute | solution.py:168
  70.1 6.8 %collective-permute-done.10 = f32[8,128]{1,0:T(8,128)S(1)} collective-permute-done((f32[8,128]{1,0:T(8,128)}, f32[8,128]{1,0:T(8,128)S(1)}, u32[]{:S(2)}, u32[]{:S(2)}) %collective-permute-start.10) | collective-permute-done | bytes 4128 | tf_op jit(solution)/shard_map/ppermute | solution.py:192
  77.6 11.8 %collective-permute-done.7.refs_6_ = bf16[4,136,256]{2,1,0:T(8,128)(2,1)S(1)} collective-permute-done((bf16[4,136,256]{2,1,0:T(8,128)(2,1)S(1)}, bf16[4,136,256]{2,1,0:T(8,128)(2,1)S(1)}, u32[]{:S(2)}, u32[]{:S(2)}) %collective-permute-start.7) | collective-permute-done | bytes 278560 | tf_op jit(solution)/shard_map/ppermute | solution.py:168
  90.1 5.6 %shard_map.55 = (f32[128,512]{1,0:T(8,128)}, f32[128,8]{1,0:T(8,128)}, f32[8,128]{1,0:T(8,128)}) custom-call(bf16[128,512]{1,0:T(8,128)(2,1)} %refs_0_.1, bf16[4,136,256]{2,1,0:T(8,128)(2,1)} %copy-done, bf16[4,136,256]{2,1,0:T(8,128)(2,1)} %copy-done.4, bf16[4,136,256]{2,1,0:T(8,128)(2,1)} %copy-done.5, bf16[4,136,256]{2,1,0:T(8,128)(2,1)} %copy-done.6, ...), custom_call_target="tpu_custom_call" | custom-call | flops 805306368 | bytes 2064384 | tf_op jit(solution)/shard_map/pallas_call | solution.py:69
  96.4 4.5 %shard_map.57 = bf16[8,128,512]{2,1,0:T(8,128)(2,1)} custom-call(f32[128,512]{1,0:T(8,128)} %get-tuple-element.33.near_ref, f32[128,8]{1,0:T(8,128)} %get-tuple-element.34.near_stats_ref, bf16[128,512]{1,0:T(8,128)(2,1)} %copy-done.1, f32[8,128]{1,0:T(8,128)} %broadcast_select_fusion.far_rows_ref, bf16[512,4096]{1,0:T(8,128)(2,1)} %weight_ref.1), custom_call_target="tpu_custom_call" | custom-call | flops 536870912 | bytes 5242880 | tf_op jit(solution)/shard_map/pallas_call | solution.py:122
  100.9 22.7 %all_to_all.5 = bf16[8,128,512]{2,1,0:T(8,128)(2,1)S(1)} all-to-all(bf16[8,128,512]{2,1,0:T(8,128)(2,1)} %shard_map.57), channel_id=1, replica_groups=mesh['ctx'=64,'tp'=8] {'tp'}, dimensions={0} | all-to-all | bytes 2097152 | tf_op jit(solution)/shard_map/all_to_all | solution.py:204
  123.6 0.8 reduce_sum.12
  (50 shorter events, 6.9 us)
Async XLA Ops:
  1.4 17.1 %collective-permute-start.2 = (bf16[136,256]{1,0:T(8,128)(2,1)S(1)}, bf16[136,256]{1,0:T(8,128)(2,1)S(1)}, u32[]{:S(2)}, u32[]{:S(2)}) collective-permute-start(bf16[136,256]{1,0:T(8,128)(2,1)S(1)} %get-tuple-element.38), channel_id=1, source_target_pairs={{0,24},{8,16},{16,8},{24,0},{32,56},{40,48},{48,40},{56,32},{64,88... | collective-permute-start | bytes 208904 | tf_op jit(solution)/shard_map/ppermute | solution.py:163
  4.3 14.3 %collective-permute-start.1 = (bf16[136,256]{1,0:T(8,128)(2,1)S(1)}, bf16[136,256]{1,0:T(8,128)(2,1)S(1)}, u32[]{:S(2)}, u32[]{:S(2)}) collective-permute-start(bf16[136,256]{1,0:T(8,128)(2,1)S(1)} %get-tuple-element.38), channel_id=1, source_target_pairs={{0,16},{8,24},{16,0},{24,8},{32,48},{40,56},{48,32},{56,40},{64,80... | collective-permute-start | bytes 208904 | tf_op jit(solution)/shard_map/ppermute | solution.py:163
  6.8 11.8 %collective-permute-start = (bf16[136,256]{1,0:T(8,128)(2,1)S(1)}, bf16[136,256]{1,0:T(8,128)(2,1)S(1)}, u32[]{:S(2)}, u32[]{:S(2)}) collective-permute-start(bf16[136,256]{1,0:T(8,128)(2,1)S(1)} %get-tuple-element.38), channel_id=1, source_target_pairs={{0,8},{8,0},{16,24},{24,16},{32,40},{40,32},{48,56},{56,48},{64,72... | collective-permute-start | bytes 208904 | tf_op jit(solution)/shard_map/ppermute | solution.py:163
  10.0 24.3 %collective-permute-start.8 = (bf16[136,512]{1,0:T(8,128)(2,1)S(1)}, bf16[136,512]{1,0:T(8,128)(2,1)S(1)}, u32[]{:S(2)}, u32[]{:S(2)}) collective-permute-start(bf16[136,512]{1,0:T(8,128)(2,1)S(1)} %fusion.1), channel_id=1, source_target_pairs={{192,0},{200,8},{208,16},{216,24},{224,32},{232,40},{240,48},{248,... | collective-permute-start | bytes 417800 | tf_op jit(solution)/shard_map/ppermute | solution.py:159
  15.3 74.1 %copy-start.2 = (s32[6,4,128]{2,1,0:T(4,128)}, s32[6,4,128]{2,1,0:T(4,128)S(1)}, u32[]{:S(2)}) copy-start(s32[6,4,128]{2,1,0:T(4,128)S(1)} %iota_add_fusion.2) | copy-start | bytes 36868
  18.6 39.4 %copy-start = (bf16[4,136,256]{2,1,0:T(8,128)(2,1)}, bf16[4,136,256]{2,1,0:T(8,128)(2,1)S(1)}, u32[]{:S(2)}) copy-start(bf16[4,136,256]{2,1,0:T(8,128)(2,1)S(1)} %pad_maximum_fusion.refs_1_) | copy-start | bytes 835588
  18.6 16.4 %collective-permute-start.3 = (bf16[4,136,256]{2,1,0:T(8,128)(2,1)S(1)}, bf16[4,136,256]{2,1,0:T(8,128)(2,1)S(1)}, u32[]{:S(2)}, u32[]{:S(2)}) collective-permute-start(bf16[4,136,256]{2,1,0:T(8,128)(2,1)S(1)} %pad_maximum_fusion.refs_1_), channel_id=1, source_target_pairs={{0,32},{8,40},{16,48},{24,56},{32,64},{40,72},{48,80},{56,88},{64,... | collective-permute-start | bytes 835592 | tf_op jit(solution)/shard_map/ppermute | solution.py:168
  34.2 23.7 %copy-start.9 = (bf16[136,512]{1,0:T(8,128)(2,1)}, bf16[136,512]{1,0:T(8,128)(2,1)S(1)}, u32[]{:S(2)}) copy-start(bf16[136,512]{1,0:T(8,128)(2,1)S(1)} %collective-permute-done.8.refs_0_) | copy-start | bytes 417796
  35.0 23.0 %copy-start.4 = (bf16[4,136,256]{2,1,0:T(8,128)(2,1)}, bf16[4,136,256]{2,1,0:T(8,128)(2,1)S(1)}, u32[]{:S(2)}) copy-start(bf16[4,136,256]{2,1,0:T(8,128)(2,1)S(1)} %collective-permute-done.3.refs_2_) | copy-start | bytes 835588
  35.0 9.7 %collective-permute-start.4 = (bf16[4,136,256]{2,1,0:T(8,128)(2,1)S(1)}, bf16[4,136,256]{2,1,0:T(8,128)(2,1)S(1)}, u32[]{:S(2)}, u32[]{:S(2)}) collective-permute-start(bf16[4,136,256]{2,1,0:T(8,128)(2,1)S(1)} %collective-permute-done.3.refs_2_), channel_id=1, source_target_pairs={{0,32},{8,40},{16,48},{24,56},{32,64},{40,72},{48,80},{56,88},{64,... | collective-permute-start | bytes 835592 | tf_op jit(solution)/shard_map/ppermute | solution.py:168
  44.6 13.3 %copy-start.5 = (bf16[4,136,256]{2,1,0:T(8,128)(2,1)}, bf16[4,136,256]{2,1,0:T(8,128)(2,1)S(1)}, u32[]{:S(2)}) copy-start(bf16[4,136,256]{2,1,0:T(8,128)(2,1)S(1)} %collective-permute-done.4.refs_3_) | copy-start | bytes 835588
  44.6 10.8 %collective-permute-start.5 = (bf16[4,136,256]{2,1,0:T(8,128)(2,1)S(1)}, bf16[4,136,256]{2,1,0:T(8,128)(2,1)S(1)}, u32[]{:S(2)}, u32[]{:S(2)}) collective-permute-start(bf16[4,136,256]{2,1,0:T(8,128)(2,1)S(1)} %collective-permute-done.4.refs_3_), channel_id=1, source_target_pairs={{0,32},{8,40},{16,48},{24,56},{32,64},{40,72},{48,80},{56,88},{64,... | collective-permute-start | bytes 835592 | tf_op jit(solution)/shard_map/ppermute | solution.py:168
  55.4 2.5 %copy-start.6 = (bf16[4,136,256]{2,1,0:T(8,128)(2,1)}, bf16[4,136,256]{2,1,0:T(8,128)(2,1)S(1)}, u32[]{:S(2)}) copy-start(bf16[4,136,256]{2,1,0:T(8,128)(2,1)S(1)} %collective-permute-done.5.refs_4_) | copy-start | bytes 835588
  55.4 12.6 %collective-permute-start.6 = (bf16[4,136,256]{2,1,0:T(8,128)(2,1)S(1)}, bf16[4,136,256]{2,1,0:T(8,128)(2,1)S(1)}, u32[]{:S(2)}, u32[]{:S(2)}) collective-permute-start(bf16[4,136,256]{2,1,0:T(8,128)(2,1)S(1)} %collective-permute-done.5.refs_4_), channel_id=1, source_target_pairs={{0,32},{8,40},{16,48},{24,56},{32,64},{40,72},{48,80},{56,88},{64,... | collective-permute-start | bytes 835592 | tf_op jit(solution)/shard_map/ppermute | solution.py:168
  62.6 33.2 %collective-permute-start.9 = (bf16[128,512]{1,0:T(8,128)(2,1)}, bf16[128,512]{1,0:T(8,128)(2,1)S(1)}, u32[]{:S(2)}, u32[]{:S(2)}) collective-permute-start(bf16[128,512]{1,0:T(8,128)(2,1)} %get-tuple-element.35), channel_id=1, source_target_pairs={{0,192},{8,200},{16,208},{24,216},{32,224},{40,232},{48,240},{56,2... | collective-permute-start | bytes 393224 | tf_op jit(solution)/shard_map/ppermute | solution.py:191
  65.4 11.6 %collective-permute-start.10 = (f32[8,128]{1,0:T(8,128)}, f32[8,128]{1,0:T(8,128)S(1)}, u32[]{:S(2)}, u32[]{:S(2)}) collective-permute-start(f32[8,128]{1,0:T(8,128)} %get-tuple-element.36), channel_id=1, source_target_pairs={{0,192},{8,200},{16,208},{24,216},{32,224},{40,232},{48,240},{56,2... | collective-permute-start | bytes 12296 | tf_op jit(solution)/shard_map/ppermute | solution.py:192
  68.0 21.4 %copy-start.7 = (bf16[4,136,256]{2,1,0:T(8,128)(2,1)}, bf16[4,136,256]{2,1,0:T(8,128)(2,1)S(1)}, u32[]{:S(2)}) copy-start(bf16[4,136,256]{2,1,0:T(8,128)(2,1)S(1)} %collective-permute-done.6.refs_5_) | copy-start | bytes 835588
  68.0 21.4 %collective-permute-start.7 = (bf16[4,136,256]{2,1,0:T(8,128)(2,1)S(1)}, bf16[4,136,256]{2,1,0:T(8,128)(2,1)S(1)}, u32[]{:S(2)}, u32[]{:S(2)}) collective-permute-start(bf16[4,136,256]{2,1,0:T(8,128)(2,1)S(1)} %collective-permute-done.6.refs_5_), channel_id=1, source_target_pairs={{0,32},{8,40},{16,48},{24,56},{32,64},{40,72},{48,80},{56,88},{64,... | collective-permute-start | bytes 835592 | tf_op jit(solution)/shard_map/ppermute | solution.py:168
  89.4 0.7 copy-start.8
  89.4 0.7 copy-start.3
  95.8 0.7 copy-start.1

commit v13 on v10

--- a/solution.py
+++ b/solution.py
@@ -183,14 +183,16 @@
     visit_out, visit_stats, visit_rows = partial(
         visiting, blocks, key_pos, key_doc, visit_pos, visit_doc, jnp.bfloat16
     )
+    query_pos = my_index * rows + offsets_in_shard
+    near_out, near_stats, _ = partial(
+        queries, blocks, key_pos, key_doc, query_pos, docs.reshape(rows, 1), jnp.float32
+    )
+    visit_out, visit_rows, near_out, near_stats = lax.optimization_barrier(
+        (visit_out, visit_rows, near_out, near_stats)
+    )
     ahead = [(s, s + PLANE * far) for s in range(ctx - PLANE * far)]
     far_out = lax.ppermute(visit_out, "ctx", ahead)
     far_rows = lax.ppermute(visit_rows, "ctx", ahead)
-
-    query_pos = my_index * rows + offsets_in_shard
-    near_out, near_stats, _ = partial(
-        queries, blocks, key_pos, key_doc, query_pos, docs.reshape(rows, 1), jnp.float32
-    )
     has_far = plane >= far
     heads = near_stats.shape[1] // 2
     kind = jnp.arange(2 * heads, dtype=jnp.int32)[:, None]

time: 113 us -> 120 us (1.062)
  the two profiles are of different devices: /device:TPU:64 before, /device:TPU:96 now
where the time goes in v13:
time: 120 us; the launch traced here: 119 us
  starting transfers between devices  47.9 us (40%)
  blocking collectives  24.2 us (20%)
  waiting for transfers between devices  23 us (19%)
  Pallas kernels  14.6 us (12%)
  other arithmetic  6.52 us (5%)
  local copies, waits for them, and re-layouts  2.87 us (2%)
    all_to_all x1, blocking collectives, shards(): received = lax.all_to_all(chunks, 'tp', 0, 0, tiled=True)  24.2 us
    ppermute x4, starting transfers between devices, shards(): current = lax.ppermute(current, 'ctx', forward)  22.8 us
    ppermute x4, waiting for transfers between devices, shards(): current = lax.ppermute(current, 'ctx', forward)  15.4 us
    ppermute x1, starting transfers between devices, shards(): far_rows = lax.ppermute(visit_rows, 'ctx', ahead)  12.9 us
    pallas_call x2, Pallas kernels, partial(): pl.pallas_call(partial_kernel, out_shape=(jax.ShapeDtypeStruct((rows, wid...  10.1 us
    ppermute x3, starting transfers between devices, shards(): lax.ppermute(block, 'ctx', [(s, s ^ offset) for s in range(ctx)])  7.87 us
    ppermute x1, waiting for transfers between devices, shards(): far_out = lax.ppermute(visit_out, 'ctx', ahead)  6.77 us
    pallas_call x1, Pallas kernels, merge(): pl.pallas_call(merge_kernel, out_shape=jax.ShapeDtypeStruct((pieces, rows...  4.52 us
  transfers between devices with their start and end apart: 10, of which 6 were waited for; matrix products, arithmetic and copies ran while one was open for 5% of the time, Pallas kernels for 0%

profile of v13, /device:TPU:96, one launch (start us, length us, event | category | flops | bytes accessed | tf_op | source)
XLA Modules:
  0.0 119.3 jit_solution(1665570583039461965)
XLA Ops:
  0.7 0.8 fusion.5
  1.4 3.4 %collective-permute-start.2 = (bf16[136,256]{1,0:T(8,128)(2,1)S(1)}, bf16[136,256]{1,0:T(8,128)(2,1)S(1)}, u32[]{:S(2)}, u32[]{:S(2)}) collective-permute-start(bf16[136,256]{1,0:T(8,128)(2,1)S(1)} %get-tuple-element.46), channel_id=1, source_target_pairs={{0,16},{8,24},{16,0},{24,8},{32,48},{40,56},{48,32},{56,40},{64,80... | collective-permute-start | bytes 208904 | tf_op jit(solution)/shard_map/ppermute | solution.py:162
  4.9 1.9 %collective-permute-start.1 = (bf16[136,256]{1,0:T(8,128)(2,1)S(1)}, bf16[136,256]{1,0:T(8,128)(2,1)S(1)}, u32[]{:S(2)}, u32[]{:S(2)}) collective-permute-start(bf16[136,256]{1,0:T(8,128)(2,1)S(1)} %get-tuple-element.46), channel_id=1, source_target_pairs={{0,8},{8,0},{16,24},{24,16},{32,40},{40,32},{48,56},{56,48},{64,72... | collective-permute-start | bytes 208904 | tf_op jit(solution)/shard_map/ppermute | solution.py:162
  6.8 2.5 %collective-permute-start.3 = (bf16[136,256]{1,0:T(8,128)(2,1)S(1)}, bf16[136,256]{1,0:T(8,128)(2,1)S(1)}, u32[]{:S(2)}, u32[]{:S(2)}) collective-permute-start(bf16[136,256]{1,0:T(8,128)(2,1)S(1)} %get-tuple-element.46), channel_id=1, source_target_pairs={{0,24},{8,16},{16,8},{24,0},{32,56},{40,48},{48,40},{56,32},{64,88... | collective-permute-start | bytes 208904 | tf_op jit(solution)/shard_map/ppermute | solution.py:162
  9.3 0.9 fusion.1
  10.3 1.3 %collective-permute-start = (bf16[136,512]{1,0:T(8,128)(2,1)S(1)}, bf16[136,512]{1,0:T(8,128)(2,1)S(1)}, u32[]{:S(2)}, u32[]{:S(2)}) collective-permute-start(bf16[136,512]{1,0:T(8,128)(2,1)S(1)} %fusion.1), channel_id=1, source_target_pairs={{160,0},{168,8},{176,16},{184,24},{192,32},{200,40},{208,48},{216,... | collective-permute-start | bytes 417800 | tf_op jit(solution)/shard_map/ppermute | solution.py:158
  11.7 0.8 collective-permute-done.3
  12.6 5.0 %collective-permute-start.4 = (bf16[4,136,256]{2,1,0:T(8,128)(2,1)S(1)}, bf16[4,136,256]{2,1,0:T(8,128)(2,1)S(1)}, u32[]{:S(2)}, u32[]{:S(2)}) collective-permute-start(bf16[4,136,256]{2,1,0:T(8,128)(2,1)S(1)} %pad_maximum_fusion.refs_1_), channel_id=1, source_target_pairs={{0,32},{8,40},{16,48},{24,56},{32,64},{40,72},{48,80},{56,88},{64,... | collective-permute-start | bytes 835592 | tf_op jit(solution)/shard_map/ppermute | solution.py:167
  18.9 5.2 %collective-permute-done.4.refs_2_ = bf16[4,136,256]{2,1,0:T(8,128)(2,1)S(1)} collective-permute-done((bf16[4,136,256]{2,1,0:T(8,128)(2,1)S(1)}, bf16[4,136,256]{2,1,0:T(8,128)(2,1)S(1)}, u32[]{:S(2)}, u32[]{:S(2)}) %collective-permute-start.4) | collective-permute-done | bytes 278560 | tf_op jit(solution)/shard_map/ppermute | solution.py:167
  24.1 6.5 %collective-permute-start.5 = (bf16[4,136,256]{2,1,0:T(8,128)(2,1)S(1)}, bf16[4,136,256]{2,1,0:T(8,128)(2,1)S(1)}, u32[]{:S(2)}, u32[]{:S(2)}) collective-permute-start(bf16[4,136,256]{2,1,0:T(8,128)(2,1)S(1)} %collective-permute-done.4.refs_2_), channel_id=1, source_target_pairs={{0,32},{8,40},{16,48},{24,56},{32,64},{40,72},{48,80},{56,88},{64,... | collective-permute-start | bytes 835592 | tf_op jit(solution)/shard_map/ppermute | solution.py:167
  31.3 1.4 %copy.7.refs_9_ = s32[128,1]{1,0:T(8,128)} copy(s32[128,1]{0,1:T(1,128)} %bitcast.39) | data formatting | bytes 1024 | tf_op jit(solution)/shard_map/reshape | solution.py:188
  32.7 2.9 %collective-permute-done.5.refs_3_ = bf16[4,136,256]{2,1,0:T(8,128)(2,1)S(1)} collective-permute-done((bf16[4,136,256]{2,1,0:T(8,128)(2,1)S(1)}, bf16[4,136,256]{2,1,0:T(8,128)(2,1)S(1)}, u32[]{:S(2)}, u32[]{:S(2)}) %collective-permute-start.5) | collective-permute-done | bytes 278560 | tf_op jit(solution)/shard_map/ppermute | solution.py:167
  35.6 5.6 %collective-permute-start.6 = (bf16[4,136,256]{2,1,0:T(8,128)(2,1)S(1)}, bf16[4,136,256]{2,1,0:T(8,128)(2,1)S(1)}, u32[]{:S(2)}, u32[]{:S(2)}) collective-permute-start(bf16[4,136,256]{2,1,0:T(8,128)(2,1)S(1)} %collective-permute-done.5.refs_3_), channel_id=1, source_target_pairs={{0,32},{8,40},{16,48},{24,56},{32,64},{40,72},{48,80},{56,88},{64,... | collective-permute-start | bytes 835592 | tf_op jit(solution)/shard_map/ppermute | solution.py:167
  42.0 3.3 %collective-permute-done.6.refs_4_ = bf16[4,136,256]{2,1,0:T(8,128)(2,1)S(1)} collective-permute-done((bf16[4,136,256]{2,1,0:T(8,128)(2,1)S(1)}, bf16[4,136,256]{2,1,0:T(8,128)(2,1)S(1)}, u32[]{:S(2)}, u32[]{:S(2)}) %collective-permute-start.6) | collective-permute-done | bytes 278560 | tf_op jit(solution)/shard_map/ppermute | solution.py:167
  45.2 5.6 %collective-permute-start.7 = (bf16[4,136,256]{2,1,0:T(8,128)(2,1)S(1)}, bf16[4,136,256]{2,1,0:T(8,128)(2,1)S(1)}, u32[]{:S(2)}, u32[]{:S(2)}) collective-permute-start(bf16[4,136,256]{2,1,0:T(8,128)(2,1)S(1)} %collective-permute-done.6.refs_4_), channel_id=1, source_target_pairs={{0,32},{8,40},{16,48},{24,56},{32,64},{40,72},{48,80},{56,88},{64,... | collective-permute-start | bytes 835592 | tf_op jit(solution)/shard_map/ppermute | solution.py:167
  50.9 4.0 %collective-permute-done.7.refs_5_ = bf16[4,136,256]{2,1,0:T(8,128)(2,1)S(1)} collective-permute-done((bf16[4,136,256]{2,1,0:T(8,128)(2,1)S(1)}, bf16[4,136,256]{2,1,0:T(8,128)(2,1)S(1)}, u32[]{:S(2)}, u32[]{:S(2)}) %collective-permute-start.7) | collective-permute-done | bytes 278560 | tf_op jit(solution)/shard_map/ppermute | solution.py:167
  55.6 5.0 %shard_map.55 = (bf16[128,512]{1,0:T(8,128)(2,1)}, f32[128,8]{1,0:T(8,128)}, f32[8,128]{1,0:T(8,128)}) custom-call(bf16[136,512]{1,0:T(8,128)(2,1)} %copy-done.6, bf16[4,136,256]{2,1,0:T(8,128)(2,1)} %copy-done, bf16[4,136,256]{2,1,0:T(8,128)(2,1)} %copy-done.2, bf16[4,136,256]{2,1,0:T(8,128)(2,1)} %copy-done.3, bf16[4,136,256]{2,1,0:T(8,128)(2,1)} %copy-done.4, ...), custom_call_target="tpu_custom_call" | custom-call | flops 671088640 | bytes 1794048 | tf_op jit(solution)/shard_map/pallas_call | solution.py:69
  60.6 5.1 %shard_map.56 = (f32[128,512]{1,0:T(8,128)}, f32[128,8]{1,0:T(8,128)}, f32[8,128]{1,0:T(8,128)}) custom-call(bf16[128,512]{1,0:T(8,128)(2,1)} %refs_0_.1, bf16[4,136,256]{2,1,0:T(8,128)(2,1)} %copy-done, bf16[4,136,256]{2,1,0:T(8,128)(2,1)} %copy-done.2, bf16[4,136,256]{2,1,0:T(8,128)(2,1)} %copy-done.3, bf16[4,136,256]{2,1,0:T(8,128)(2,1)} %copy-done.4, ...), custom_call_target="tpu_custom_call" | custom-call | flops 671088640 | bytes 1785856 | tf_op jit(solution)/shard_map/pallas_call | solution.py:69
  65.7 12.9 %collective-permute-start.9 = (f32[8,128]{1,0:T(8,128)}, f32[8,128]{1,0:T(8,128)S(1)}, u32[]{:S(2)}, u32[]{:S(2)}) collective-permute-start(f32[8,128]{1,0:T(8,128)} %get-tuple-element.44), channel_id=1, source_target_pairs={{0,160},{8,168},{16,176},{24,184},{32,192},{40,200},{48,208},{56,2... | collective-permute-start | bytes 12296 | tf_op jit(solution)/shard_map/ppermute | solution.py:195
  78.6 3.1 %collective-permute-start.8 = (bf16[128,512]{1,0:T(8,128)(2,1)}, bf16[128,512]{1,0:T(8,128)(2,1)S(1)}, u32[]{:S(2)}, u32[]{:S(2)}) collective-permute-start(bf16[128,512]{1,0:T(8,128)(2,1)} %get-tuple-element.43), channel_id=1, source_target_pairs={{0,160},{8,168},{16,176},{24,184},{32,192},{40,200},{48,208},{56,2... | collective-permute-start | bytes 393224 | tf_op jit(solution)/shard_map/ppermute | solution.py:194
  82.3 6.8 %collective-permute-done.8.far_ref = bf16[128,512]{1,0:T(8,128)(2,1)S(1)} collective-permute-done((bf16[128,512]{1,0:T(8,128)(2,1)}, bf16[128,512]{1,0:T(8,128)(2,1)S(1)}, u32[]{:S(2)}, u32[]{:S(2)}) %collective-permute-start.8) | collective-permute-done | bytes 131104 | tf_op jit(solution)/shard_map/ppermute | solution.py:194
  89.8 4.5 %shard_map.57 = bf16[8,128,512]{2,1,0:T(8,128)(2,1)} custom-call(f32[128,512]{1,0:T(8,128)} %get-tuple-element.41.near_ref, f32[128,8]{1,0:T(8,128)} %get-tuple-element.42.near_stats_ref, bf16[128,512]{1,0:T(8,128)(2,1)} %copy-done.1, f32[8,128]{1,0:T(8,128)} %broadcast_select_fusion.far_rows_ref, bf16[512,4096]{1,0:T(8,128)(2,1)} %weight_ref.1), custom_call_target="tpu_custom_call" | custom-call | flops 536870912 | bytes 5242880 | tf_op jit(solution)/shard_map/pallas_call | solution.py:122
  94.3 24.2 %all_to_all.5 = bf16[8,128,512]{2,1,0:T(8,128)(2,1)S(1)} all-to-all(bf16[8,128,512]{2,1,0:T(8,128)(2,1)} %shard_map.57), channel_id=1, replica_groups=mesh['ctx'=64,'tp'=8] {'tp'}, dimensions={0} | all-to-all | bytes 2097152 | tf_op jit(solution)/shard_map/all_to_all | solution.py:202
  118.5 0.8 reduce_sum.12
  (36 shorter events, 5.5 us)
Async XLA Ops:
  1.4 10.2 %collective-permute-start.2 = (bf16[136,256]{1,0:T(8,128)(2,1)S(1)}, bf16[136,256]{1,0:T(8,128)(2,1)S(1)}, u32[]{:S(2)}, u32[]{:S(2)}) collective-permute-start(bf16[136,256]{1,0:T(8,128)(2,1)S(1)} %get-tuple-element.46), channel_id=1, source_target_pairs={{0,16},{8,24},{16,0},{24,8},{32,48},{40,56},{48,32},{56,40},{64,80... | collective-permute-start | bytes 208904 | tf_op jit(solution)/shard_map/ppermute | solution.py:162
  4.9 6.8 %collective-permute-start.1 = (bf16[136,256]{1,0:T(8,128)(2,1)S(1)}, bf16[136,256]{1,0:T(8,128)(2,1)S(1)}, u32[]{:S(2)}, u32[]{:S(2)}) collective-permute-start(bf16[136,256]{1,0:T(8,128)(2,1)S(1)} %get-tuple-element.46), channel_id=1, source_target_pairs={{0,8},{8,0},{16,24},{24,16},{32,40},{40,32},{48,56},{56,48},{64,72... | collective-permute-start | bytes 208904 | tf_op jit(solution)/shard_map/ppermute | solution.py:162
  6.8 5.7 %collective-permute-start.3 = (bf16[136,256]{1,0:T(8,128)(2,1)S(1)}, bf16[136,256]{1,0:T(8,128)(2,1)S(1)}, u32[]{:S(2)}, u32[]{:S(2)}) collective-permute-start(bf16[136,256]{1,0:T(8,128)(2,1)S(1)} %get-tuple-element.46), channel_id=1, source_target_pairs={{0,24},{8,16},{16,8},{24,0},{32,56},{40,48},{48,40},{56,32},{64,88... | collective-permute-start | bytes 208904 | tf_op jit(solution)/shard_map/ppermute | solution.py:162
  10.3 30.9 %collective-permute-start = (bf16[136,512]{1,0:T(8,128)(2,1)S(1)}, bf16[136,512]{1,0:T(8,128)(2,1)S(1)}, u32[]{:S(2)}, u32[]{:S(2)}) collective-permute-start(bf16[136,512]{1,0:T(8,128)(2,1)S(1)} %fusion.1), channel_id=1, source_target_pairs={{160,0},{168,8},{176,16},{184,24},{192,32},{200,40},{208,48},{216,... | collective-permute-start | bytes 417800 | tf_op jit(solution)/shard_map/ppermute | solution.py:158
  12.6 43.0 %copy-start = (bf16[4,136,256]{2,1,0:T(8,128)(2,1)}, bf16[4,136,256]{2,1,0:T(8,128)(2,1)S(1)}, u32[]{:S(2)}) copy-start(bf16[4,136,256]{2,1,0:T(8,128)(2,1)S(1)} %pad_maximum_fusion.refs_1_) | copy-start | bytes 835588
  12.6 11.6 %collective-permute-start.4 = (bf16[4,136,256]{2,1,0:T(8,128)(2,1)S(1)}, bf16[4,136,256]{2,1,0:T(8,128)(2,1)S(1)}, u32[]{:S(2)}, u32[]{:S(2)}) collective-permute-start(bf16[4,136,256]{2,1,0:T(8,128)(2,1)S(1)} %pad_maximum_fusion.refs_1_), channel_id=1, source_target_pairs={{0,32},{8,40},{16,48},{24,56},{32,64},{40,72},{48,80},{56,88},{64,... | collective-permute-start | bytes 835592 | tf_op jit(solution)/shard_map/ppermute | solution.py:167
  24.1 31.4 %copy-start.2 = (bf16[4,136,256]{2,1,0:T(8,128)(2,1)}, bf16[4,136,256]{2,1,0:T(8,128)(2,1)S(1)}, u32[]{:S(2)}) copy-start(bf16[4,136,256]{2,1,0:T(8,128)(2,1)S(1)} %collective-permute-done.4.refs_2_) | copy-start | bytes 835588
  24.1 11.5 %collective-permute-start.5 = (bf16[4,136,256]{2,1,0:T(8,128)(2,1)S(1)}, bf16[4,136,256]{2,1,0:T(8,128)(2,1)S(1)}, u32[]{:S(2)}, u32[]{:S(2)}) collective-permute-start(bf16[4,136,256]{2,1,0:T(8,128)(2,1)S(1)} %collective-permute-done.4.refs_2_), channel_id=1, source_target_pairs={{0,32},{8,40},{16,48},{24,56},{32,64},{40,72},{48,80},{56,88},{64,... | collective-permute-start | bytes 835592 | tf_op jit(solution)/shard_map/ppermute | solution.py:167
  35.6 20.0 %copy-start.3 = (bf16[4,136,256]{2,1,0:T(8,128)(2,1)}, bf16[4,136,256]{2,1,0:T(8,128)(2,1)S(1)}, u32[]{:S(2)}) copy-start(bf16[4,136,256]{2,1,0:T(8,128)(2,1)S(1)} %collective-permute-done.5.refs_3_) | copy-start | bytes 835588
  35.6 9.6 %collective-permute-start.6 = (bf16[4,136,256]{2,1,0:T(8,128)(2,1)S(1)}, bf16[4,136,256]{2,1,0:T(8,128)(2,1)S(1)}, u32[]{:S(2)}, u32[]{:S(2)}) collective-permute-start(bf16[4,136,256]{2,1,0:T(8,128)(2,1)S(1)} %collective-permute-done.5.refs_3_), channel_id=1, source_target_pairs={{0,32},{8,40},{16,48},{24,56},{32,64},{40,72},{48,80},{56,88},{64,... | collective-permute-start | bytes 835592 | tf_op jit(solution)/shard_map/ppermute | solution.py:167
  41.2 14.3 %copy-start.6 = (bf16[136,512]{1,0:T(8,128)(2,1)}, bf16[136,512]{1,0:T(8,128)(2,1)S(1)}, u32[]{:S(2)}) copy-start(bf16[136,512]{1,0:T(8,128)(2,1)S(1)} %collective-permute-done.refs_0_) | copy-start | bytes 417796
  45.2 10.3 %copy-start.4 = (bf16[4,136,256]{2,1,0:T(8,128)(2,1)}, bf16[4,136,256]{2,1,0:T(8,128)(2,1)S(1)}, u32[]{:S(2)}) copy-start(bf16[4,136,256]{2,1,0:T(8,128)(2,1)S(1)} %collective-permute-done.6.refs_4_) | copy-start | bytes 835588
  45.2 9.6 %collective-permute-start.7 = (bf16[4,136,256]{2,1,0:T(8,128)(2,1)S(1)}, bf16[4,136,256]{2,1,0:T(8,128)(2,1)S(1)}, u32[]{:S(2)}, u32[]{:S(2)}) collective-permute-start(bf16[4,136,256]{2,1,0:T(8,128)(2,1)S(1)} %collective-permute-done.6.refs_4_), channel_id=1, source_target_pairs={{0,32},{8,40},{16,48},{24,56},{32,64},{40,72},{48,80},{56,88},{64,... | collective-permute-start | bytes 835592 | tf_op jit(solution)/shard_map/ppermute | solution.py:167
  54.9 0.7 copy-start.5
  65.7 16.0 %collective-permute-start.9 = (f32[8,128]{1,0:T(8,128)}, f32[8,128]{1,0:T(8,128)S(1)}, u32[]{:S(2)}, u32[]{:S(2)}) collective-permute-start(f32[8,128]{1,0:T(8,128)} %get-tuple-element.44), channel_id=1, source_target_pairs={{0,160},{8,168},{16,176},{24,184},{32,192},{40,200},{48,208},{56,2... | collective-permute-start | bytes 12296 | tf_op jit(solution)/shard_map/ppermute | solution.py:195
  78.6 10.5 %collective-permute-start.8 = (bf16[128,512]{1,0:T(8,128)(2,1)}, bf16[128,512]{1,0:T(8,128)(2,1)S(1)}, u32[]{:S(2)}, u32[]{:S(2)}) collective-permute-start(bf16[128,512]{1,0:T(8,128)(2,1)} %get-tuple-element.43), channel_id=1, source_target_pairs={{0,160},{8,168},{16,176},{24,184},{32,192},{40,200},{48,208},{56,2... | collective-permute-start | bytes 393224 | tf_op jit(solution)/shard_map/ppermute | solution.py:194
  89.1 0.7 copy-start.1

commit v14 on v10

--- a/solution.py
+++ b/solution.py
@@ -39,22 +39,26 @@
     bias = jnp.where(allowed, 0.0, neg_large)
     seen = jnp.max(jnp.where(allowed, 1.0, 0.0), axis=1, keepdims=True) > 0.0
     scale = 1.0 / math.sqrt(head_dim)
+    query = jnp.concatenate(
+        [query_ref[:rows, head * head_dim:(head + 1) * head_dim] for head in range(heads)],
+        axis=0,
+    )
+    scores = lax.dot_general(
+        query, key_part, (((1,), (1,)), ((), ())), preferred_element_type=jnp.float32
+    )
+    scores = scores.reshape(heads, rows, -1) * scale + bias[None]
+    peak = jnp.max(scores, axis=2, keepdims=True)
+    weight = jnp.exp(scores - peak)
+    total = jnp.where(seen[None], jnp.sum(weight, axis=2, keepdims=True), 0.0)
+    summed = jnp.dot(
+        weight.reshape(heads * rows, -1).astype(jnp.bfloat16), value_part,
+        preferred_element_type=jnp.float32,
+    ).reshape(heads, rows, head_dim)
     for head in range(heads):
-        query = query_ref[:rows, head * head_dim:(head + 1) * head_dim]
-        scores = lax.dot_general(
-            query, key_part, (((1,), (1,)), ((), ())), preferred_element_type=jnp.float32
-        )
-        scores = scores * scale + bias
-        peak = jnp.max(scores, axis=1, keepdims=True)
-        weight = jnp.exp(scores - peak)
-        total = jnp.where(seen, jnp.sum(weight, axis=1, keepdims=True), 0.0)
-        summed = jnp.dot(
-            weight.astype(jnp.bfloat16), value_part, preferred_element_type=jnp.float32
-        )
-        normed = jnp.where(seen, summed / jnp.maximum(total, 1e-30), 0.0)
+        normed = jnp.where(seen, summed[head] / jnp.maximum(total[head], 1e-30), 0.0)
         out_ref[:, head * head_dim:(head + 1) * head_dim] = normed.astype(out_ref.dtype)
-        stats_ref[:, head:head + 1] = jnp.where(seen, peak, neg_large)
-        stats_ref[:, heads + head:heads + head + 1] = total
+        stats_ref[:, head:head + 1] = jnp.where(seen, peak[head], neg_large)
+        stats_ref[:, heads + head:heads + head + 1] = total[head]
     square_ref[...] = jnp.zeros_like(square_ref)
     square_ref[:, :2 * heads] = stats_ref[...]
     rows_ref[...] = jnp.transpose(square_ref[...])[:2 * heads]

time: 113 us -> 114 us (level)
  Pallas kernels: 14.6 us -> 16.4 us
    pallas_call x2, Pallas kernels: 10.1 us -> 11.9 us  [partial(): pl.pallas_call(partial_kernel, out_shape=(jax.ShapeDtypeStruct((rows, wid...]
where the time goes in v14:
time: 114 us
  starting transfers between devices  49.6 us (44%)
  blocking collectives  19.9 us (17%)
  waiting for transfers between devices  18.2 us (16%)
  Pallas kernels  16.4 us (14%)
  other arithmetic  6.52 us (6%)
  local copies, waits for them, and re-layouts  2.88 us (3%)
    all_to_all x1, blocking collectives, shards(): received = lax.all_to_all(chunks, 'tp', 0, 0, tiled=True)  19.9 us
    ppermute x4, starting transfers between devices, shards(): current = lax.ppermute(current, 'ctx', forward)  19.6 us
    ppermute x4, waiting for transfers between devices, shards(): current = lax.ppermute(current, 'ctx', forward)  18 us
    pallas_call x2, Pallas kernels, partial(): pl.pallas_call(partial_kernel, out_shape=(jax.ShapeDtypeStruct((rows, wid...  11.9 us
    ppermute x1, starting transfers between devices, shards(): far_rows = lax.ppermute(visit_rows, 'ctx', ahead)  11.2 us
    ppermute x1, starting transfers between devices, shards(): far_out = lax.ppermute(visit_out, 'ctx', ahead)  9.64 us
    ppermute x3, starting transfers between devices, shards(): lax.ppermute(block, 'ctx', [(s, s ^ offset) for s in range(ctx)])  7.87 us
    pallas_call x1, Pallas kernels, merge(): pl.pallas_call(merge_kernel, out_shape=jax.ShapeDtypeStruct((pieces, rows...  4.52 us
  transfers between devices with their start and end apart: 10, of which 5 were waited for; matrix products, arithmetic and copies ran while one was open for 5% of the time, Pallas kernels for 5%

profile of v14, /device:TPU:64, one launch (start us, length us, event | category | flops | bytes accessed | tf_op | source)
XLA Modules:
  0.0 113.8 jit_solution(6666515363414210849)
XLA Ops:
  0.7 0.8 fusion.5
  1.4 3.4 %collective-permute-start.1 = (bf16[136,256]{1,0:T(8,128)(2,1)S(1)}, bf16[136,256]{1,0:T(8,128)(2,1)S(1)}, u32[]{:S(2)}, u32[]{:S(2)}) collective-permute-start(bf16[136,256]{1,0:T(8,128)(2,1)S(1)} %get-tuple-element.38), channel_id=1, source_target_pairs={{0,16},{8,24},{16,0},{24,8},{32,48},{40,56},{48,32},{56,40},{64,80... | collective-permute-start | bytes 208904 | tf_op jit(solution)/shard_map/ppermute | solution.py:166
  4.9 1.9 %collective-permute-start = (bf16[136,256]{1,0:T(8,128)(2,1)S(1)}, bf16[136,256]{1,0:T(8,128)(2,1)S(1)}, u32[]{:S(2)}, u32[]{:S(2)}) collective-permute-start(bf16[136,256]{1,0:T(8,128)(2,1)S(1)} %get-tuple-element.38), channel_id=1, source_target_pairs={{0,8},{8,0},{16,24},{24,16},{32,40},{40,32},{48,56},{56,48},{64,72... | collective-permute-start | bytes 208904 | tf_op jit(solution)/shard_map/ppermute | solution.py:166
  6.8 2.5 %collective-permute-start.2 = (bf16[136,256]{1,0:T(8,128)(2,1)S(1)}, bf16[136,256]{1,0:T(8,128)(2,1)S(1)}, u32[]{:S(2)}, u32[]{:S(2)}) collective-permute-start(bf16[136,256]{1,0:T(8,128)(2,1)S(1)} %get-tuple-element.38), channel_id=1, source_target_pairs={{0,24},{8,16},{16,8},{24,0},{32,56},{40,48},{48,40},{56,32},{64,88... | collective-permute-start | bytes 208904 | tf_op jit(solution)/shard_map/ppermute | solution.py:166
  9.3 0.9 fusion.1
  10.3 1.3 %collective-permute-start.7 = (bf16[136,512]{1,0:T(8,128)(2,1)S(1)}, bf16[136,512]{1,0:T(8,128)(2,1)S(1)}, u32[]{:S(2)}, u32[]{:S(2)}) collective-permute-start(bf16[136,512]{1,0:T(8,128)(2,1)S(1)} %fusion.1), channel_id=1, source_target_pairs={{160,0},{168,8},{176,16},{184,24},{192,32},{200,40},{208,48},{216,... | collective-permute-start | bytes 417800 | tf_op jit(solution)/shard_map/ppermute | solution.py:162
  12.6 3.8 %collective-permute-start.3 = (bf16[4,136,256]{2,1,0:T(8,128)(2,1)S(1)}, bf16[4,136,256]{2,1,0:T(8,128)(2,1)S(1)}, u32[]{:S(2)}, u32[]{:S(2)}) collective-permute-start(bf16[4,136,256]{2,1,0:T(8,128)(2,1)S(1)} %pad_maximum_fusion.refs_1_), channel_id=1, source_target_pairs={{0,32},{8,40},{16,48},{24,56},{32,64},{40,72},{48,80},{56,88},{64,... | collective-permute-start | bytes 835592 | tf_op jit(solution)/shard_map/ppermute | solution.py:171
  17.0 0.7 iota_add_fusion.2
  17.7 5.8 %collective-permute-done.3.refs_2_ = bf16[4,136,256]{2,1,0:T(8,128)(2,1)S(1)} collective-permute-done((bf16[4,136,256]{2,1,0:T(8,128)(2,1)S(1)}, bf16[4,136,256]{2,1,0:T(8,128)(2,1)S(1)}, u32[]{:S(2)}, u32[]{:S(2)}) %collective-permute-start.3) | collective-permute-done | bytes 278560 | tf_op jit(solution)/shard_map/ppermute | solution.py:171
  23.5 4.5 %collective-permute-start.4 = (bf16[4,136,256]{2,1,0:T(8,128)(2,1)S(1)}, bf16[4,136,256]{2,1,0:T(8,128)(2,1)S(1)}, u32[]{:S(2)}, u32[]{:S(2)}) collective-permute-start(bf16[4,136,256]{2,1,0:T(8,128)(2,1)S(1)} %collective-permute-done.3.refs_2_), channel_id=1, source_target_pairs={{0,32},{8,40},{16,48},{24,56},{32,64},{40,72},{48,80},{56,88},{64,... | collective-permute-start | bytes 835592 | tf_op jit(solution)/shard_map/ppermute | solution.py:171
  28.0 1.4 %copy.6.refs_9_ = s32[128,1]{1,0:T(8,128)} copy(s32[128,1]{0,1:T(1,128)} %bitcast.39) | data formatting | bytes 1024 | tf_op jit(solution)/shard_map/reshape | solution.py:196
  29.4 4.9 %collective-permute-done.4.refs_3_ = bf16[4,136,256]{2,1,0:T(8,128)(2,1)S(1)} collective-permute-done((bf16[4,136,256]{2,1,0:T(8,128)(2,1)S(1)}, bf16[4,136,256]{2,1,0:T(8,128)(2,1)S(1)}, u32[]{:S(2)}, u32[]{:S(2)}) %collective-permute-start.4) | collective-permute-done | bytes 278560 | tf_op jit(solution)/shard_map/ppermute | solution.py:171
  34.3 5.8 %collective-permute-start.5 = (bf16[4,136,256]{2,1,0:T(8,128)(2,1)S(1)}, bf16[4,136,256]{2,1,0:T(8,128)(2,1)S(1)}, u32[]{:S(2)}, u32[]{:S(2)}) collective-permute-start(bf16[4,136,256]{2,1,0:T(8,128)(2,1)S(1)} %collective-permute-done.4.refs_3_), channel_id=1, source_target_pairs={{0,32},{8,40},{16,48},{24,56},{32,64},{40,72},{48,80},{56,88},{64,... | collective-permute-start | bytes 835592 | tf_op jit(solution)/shard_map/ppermute | solution.py:171
  40.1 0.7 copy.7.refs_9_
  40.8 3.3 %collective-permute-done.5.refs_4_ = bf16[4,136,256]{2,1,0:T(8,128)(2,1)S(1)} collective-permute-done((bf16[4,136,256]{2,1,0:T(8,128)(2,1)S(1)}, bf16[4,136,256]{2,1,0:T(8,128)(2,1)S(1)}, u32[]{:S(2)}, u32[]{:S(2)}) %collective-permute-start.5) | collective-permute-done | bytes 278560 | tf_op jit(solution)/shard_map/ppermute | solution.py:171
  44.1 5.6 %collective-permute-start.6 = (bf16[4,136,256]{2,1,0:T(8,128)(2,1)S(1)}, bf16[4,136,256]{2,1,0:T(8,128)(2,1)S(1)}, u32[]{:S(2)}, u32[]{:S(2)}) collective-permute-start(bf16[4,136,256]{2,1,0:T(8,128)(2,1)S(1)} %collective-permute-done.5.refs_4_), channel_id=1, source_target_pairs={{0,32},{8,40},{16,48},{24,56},{32,64},{40,72},{48,80},{56,88},{64,... | collective-permute-start | bytes 835592 | tf_op jit(solution)/shard_map/ppermute | solution.py:171
  49.7 4.0 %collective-permute-done.6.refs_5_ = bf16[4,136,256]{2,1,0:T(8,128)(2,1)S(1)} collective-permute-done((bf16[4,136,256]{2,1,0:T(8,128)(2,1)S(1)}, bf16[4,136,256]{2,1,0:T(8,128)(2,1)S(1)}, u32[]{:S(2)}, u32[]{:S(2)}) %collective-permute-start.6) | collective-permute-done | bytes 278560 | tf_op jit(solution)/shard_map/ppermute | solution.py:171
  54.5 5.9 %shard_map.56 = (bf16[128,512]{1,0:T(8,128)(2,1)}, f32[128,8]{1,0:T(8,128)}, f32[8,128]{1,0:T(8,128)}) custom-call(bf16[136,512]{1,0:T(8,128)(2,1)} %copy-done.6, bf16[4,136,256]{2,1,0:T(8,128)(2,1)} %copy-done, bf16[4,136,256]{2,1,0:T(8,128)(2,1)} %copy-done.2, bf16[4,136,256]{2,1,0:T(8,128)(2,1)} %copy-done.3, bf16[4,136,256]{2,1,0:T(8,128)(2,1)} %copy-done.4, ...), custom_call_target="tpu_custom_call" | custom-call | flops 671088640 | bytes 1794048 | tf_op jit(solution)/shard_map/pallas_call | solution.py:73
  60.4 11.2 %collective-permute-start.9 = (f32[8,128]{1,0:T(8,128)}, f32[8,128]{1,0:T(8,128)S(1)}, u32[]{:S(2)}, u32[]{:S(2)}) collective-permute-start(f32[8,128]{1,0:T(8,128)} %get-tuple-element.36), channel_id=1, source_target_pairs={{0,160},{8,168},{16,176},{24,184},{32,192},{40,200},{48,208},{56,2... | collective-permute-start | bytes 12296 | tf_op jit(solution)/shard_map/ppermute | solution.py:192
  71.6 9.6 %collective-permute-start.8 = (bf16[128,512]{1,0:T(8,128)(2,1)}, bf16[128,512]{1,0:T(8,128)(2,1)S(1)}, u32[]{:S(2)}, u32[]{:S(2)}) collective-permute-start(bf16[128,512]{1,0:T(8,128)(2,1)} %get-tuple-element.35), channel_id=1, source_target_pairs={{0,160},{8,168},{16,176},{24,184},{32,192},{40,200},{48,208},{56,2... | collective-permute-start | bytes 393224 | tf_op jit(solution)/shard_map/ppermute | solution.py:191
  81.2 6.0 %shard_map.55 = (f32[128,512]{1,0:T(8,128)}, f32[128,8]{1,0:T(8,128)}, f32[8,128]{1,0:T(8,128)}) custom-call(bf16[128,512]{1,0:T(8,128)(2,1)} %refs_0_.1, bf16[4,136,256]{2,1,0:T(8,128)(2,1)} %copy-done, bf16[4,136,256]{2,1,0:T(8,128)(2,1)} %copy-done.2, bf16[4,136,256]{2,1,0:T(8,128)(2,1)} %copy-done.3, bf16[4,136,256]{2,1,0:T(8,128)(2,1)} %copy-done.4, ...), custom_call_target="tpu_custom_call" | custom-call | flops 671088640 | bytes 1785856 | tf_op jit(solution)/shard_map/pallas_call | solution.py:73
  88.5 4.5 %shard_map.57 = bf16[8,128,512]{2,1,0:T(8,128)(2,1)} custom-call(f32[128,512]{1,0:T(8,128)} %get-tuple-element.33.near_ref, f32[128,8]{1,0:T(8,128)} %get-tuple-element.34.near_stats_ref, bf16[128,512]{1,0:T(8,128)(2,1)} %copy-done.1, f32[8,128]{1,0:T(8,128)} %broadcast_select_fusion.far_rows_ref, bf16[512,4096]{1,0:T(8,128)(2,1)} %weight_ref.1), custom_call_target="tpu_custom_call" | custom-call | flops 536870912 | bytes 5242880 | tf_op jit(solution)/shard_map/pallas_call | solution.py:126
  93.0 19.9 %all_to_all.5 = bf16[8,128,512]{2,1,0:T(8,128)(2,1)S(1)} all-to-all(bf16[8,128,512]{2,1,0:T(8,128)(2,1)} %shard_map.57), channel_id=1, replica_groups=mesh['ctx'=64,'tp'=8] {'tp'}, dimensions={0} | all-to-all | bytes 2097152 | tf_op jit(solution)/shard_map/all_to_all | solution.py:204
  113.0 0.8 reduce_sum.12
  (36 shorter events, 4.3 us)
Async XLA Ops:
  1.4 10.9 %collective-permute-start.1 = (bf16[136,256]{1,0:T(8,128)(2,1)S(1)}, bf16[136,256]{1,0:T(8,128)(2,1)S(1)}, u32[]{:S(2)}, u32[]{:S(2)}) collective-permute-start(bf16[136,256]{1,0:T(8,128)(2,1)S(1)} %get-tuple-element.38), channel_id=1, source_target_pairs={{0,16},{8,24},{16,0},{24,8},{32,48},{40,56},{48,32},{56,40},{64,80... | collective-permute-start | bytes 208904 | tf_op jit(solution)/shard_map/ppermute | solution.py:166
  4.9 7.5 %collective-permute-start = (bf16[136,256]{1,0:T(8,128)(2,1)S(1)}, bf16[136,256]{1,0:T(8,128)(2,1)S(1)}, u32[]{:S(2)}, u32[]{:S(2)}) collective-permute-start(bf16[136,256]{1,0:T(8,128)(2,1)S(1)} %get-tuple-element.38), channel_id=1, source_target_pairs={{0,8},{8,0},{16,24},{24,16},{32,40},{40,32},{48,56},{56,48},{64,72... | collective-permute-start | bytes 208904 | tf_op jit(solution)/shard_map/ppermute | solution.py:166
  6.8 5.7 %collective-permute-start.2 = (bf16[136,256]{1,0:T(8,128)(2,1)S(1)}, bf16[136,256]{1,0:T(8,128)(2,1)S(1)}, u32[]{:S(2)}, u32[]{:S(2)}) collective-permute-start(bf16[136,256]{1,0:T(8,128)(2,1)S(1)} %get-tuple-element.38), channel_id=1, source_target_pairs={{0,24},{8,16},{16,8},{24,0},{32,56},{40,48},{48,40},{56,32},{64,88... | collective-permute-start | bytes 208904 | tf_op jit(solution)/shard_map/ppermute | solution.py:166
  10.3 29.8 %collective-permute-start.7 = (bf16[136,512]{1,0:T(8,128)(2,1)S(1)}, bf16[136,512]{1,0:T(8,128)(2,1)S(1)}, u32[]{:S(2)}, u32[]{:S(2)}) collective-permute-start(bf16[136,512]{1,0:T(8,128)(2,1)S(1)} %fusion.1), channel_id=1, source_target_pairs={{160,0},{168,8},{176,16},{184,24},{192,32},{200,40},{208,48},{216,... | collective-permute-start | bytes 417800 | tf_op jit(solution)/shard_map/ppermute | solution.py:162
  12.6 41.8 %copy-start = (bf16[4,136,256]{2,1,0:T(8,128)(2,1)}, bf16[4,136,256]{2,1,0:T(8,128)(2,1)S(1)}, u32[]{:S(2)}) copy-start(bf16[4,136,256]{2,1,0:T(8,128)(2,1)S(1)} %pad_maximum_fusion.refs_1_) | copy-start | bytes 835588
  12.6 10.9 %collective-permute-start.3 = (bf16[4,136,256]{2,1,0:T(8,128)(2,1)S(1)}, bf16[4,136,256]{2,1,0:T(8,128)(2,1)S(1)}, u32[]{:S(2)}, u32[]{:S(2)}) collective-permute-start(bf16[4,136,256]{2,1,0:T(8,128)(2,1)S(1)} %pad_maximum_fusion.refs_1_), channel_id=1, source_target_pairs={{0,32},{8,40},{16,48},{24,56},{32,64},{40,72},{48,80},{56,88},{64,... | collective-permute-start | bytes 835592 | tf_op jit(solution)/shard_map/ppermute | solution.py:171
  23.5 30.9 %copy-start.2 = (bf16[4,136,256]{2,1,0:T(8,128)(2,1)}, bf16[4,136,256]{2,1,0:T(8,128)(2,1)S(1)}, u32[]{:S(2)}) copy-start(bf16[4,136,256]{2,1,0:T(8,128)(2,1)S(1)} %collective-permute-done.3.refs_2_) | copy-start | bytes 835588
  23.5 10.8 %collective-permute-start.4 = (bf16[4,136,256]{2,1,0:T(8,128)(2,1)S(1)}, bf16[4,136,256]{2,1,0:T(8,128)(2,1)S(1)}, u32[]{:S(2)}, u32[]{:S(2)}) collective-permute-start(bf16[4,136,256]{2,1,0:T(8,128)(2,1)S(1)} %collective-permute-done.3.refs_2_), channel_id=1, source_target_pairs={{0,32},{8,40},{16,48},{24,56},{32,64},{40,72},{48,80},{56,88},{64,... | collective-permute-start | bytes 835592 | tf_op jit(solution)/shard_map/ppermute | solution.py:171
  34.3 20.1 %copy-start.3 = (bf16[4,136,256]{2,1,0:T(8,128)(2,1)}, bf16[4,136,256]{2,1,0:T(8,128)(2,1)S(1)}, u32[]{:S(2)}) copy-start(bf16[4,136,256]{2,1,0:T(8,128)(2,1)S(1)} %collective-permute-done.4.refs_3_) | copy-start | bytes 835588
  34.3 9.8 %collective-permute-start.5 = (bf16[4,136,256]{2,1,0:T(8,128)(2,1)S(1)}, bf16[4,136,256]{2,1,0:T(8,128)(2,1)S(1)}, u32[]{:S(2)}, u32[]{:S(2)}) collective-permute-start(bf16[4,136,256]{2,1,0:T(8,128)(2,1)S(1)} %collective-permute-done.4.refs_3_), channel_id=1, source_target_pairs={{0,32},{8,40},{16,48},{24,56},{32,64},{40,72},{48,80},{56,88},{64,... | collective-permute-start | bytes 835592 | tf_op jit(solution)/shard_map/ppermute | solution.py:171
  40.1 14.3 %copy-start.6 = (bf16[136,512]{1,0:T(8,128)(2,1)}, bf16[136,512]{1,0:T(8,128)(2,1)S(1)}, u32[]{:S(2)}) copy-start(bf16[136,512]{1,0:T(8,128)(2,1)S(1)} %collective-permute-done.7.refs_0_) | copy-start | bytes 417796
  44.1 10.3 %copy-start.4 = (bf16[4,136,256]{2,1,0:T(8,128)(2,1)}, bf16[4,136,256]{2,1,0:T(8,128)(2,1)S(1)}, u32[]{:S(2)}) copy-start(bf16[4,136,256]{2,1,0:T(8,128)(2,1)S(1)} %collective-permute-done.5.refs_4_) | copy-start | bytes 835588
  44.1 9.6 %collective-permute-start.6 = (bf16[4,136,256]{2,1,0:T(8,128)(2,1)S(1)}, bf16[4,136,256]{2,1,0:T(8,128)(2,1)S(1)}, u32[]{:S(2)}, u32[]{:S(2)}) collective-permute-start(bf16[4,136,256]{2,1,0:T(8,128)(2,1)S(1)} %collective-permute-done.5.refs_4_), channel_id=1, source_target_pairs={{0,32},{8,40},{16,48},{24,56},{32,64},{40,72},{48,80},{56,88},{64,... | collective-permute-start | bytes 835592 | tf_op jit(solution)/shard_map/ppermute | solution.py:171
  53.7 0.7 copy-start.5
  60.4 26.8 %collective-permute-start.9 = (f32[8,128]{1,0:T(8,128)}, f32[8,128]{1,0:T(8,128)S(1)}, u32[]{:S(2)}, u32[]{:S(2)}) collective-permute-start(f32[8,128]{1,0:T(8,128)} %get-tuple-element.36), channel_id=1, source_target_pairs={{0,160},{8,168},{16,176},{24,184},{32,192},{40,200},{48,208},{56,2... | collective-permute-start | bytes 12296 | tf_op jit(solution)/shard_map/ppermute | solution.py:192
  71.6 16.3 %collective-permute-start.8 = (bf16[128,512]{1,0:T(8,128)(2,1)}, bf16[128,512]{1,0:T(8,128)(2,1)S(1)}, u32[]{:S(2)}, u32[]{:S(2)}) collective-permute-start(bf16[128,512]{1,0:T(8,128)(2,1)} %get-tuple-element.35), channel_id=1, source_target_pairs={{0,160},{8,168},{16,176},{24,184},{32,192},{40,200},{48,208},{56,2... | collective-permute-start | bytes 393224 | tf_op jit(solution)/shard_map/ppermute | solution.py:191
  87.9 0.7 copy-start.1

commit v15 on v10

--- a/solution.py
+++ b/solution.py
@@ -177,11 +177,21 @@
         [b[:, rows, :rows].astype(jnp.int32).reshape(1, -1) for b in blocks], axis=1
     )
 
+    last = PLANE - 1
+    oldest = lax.dynamic_index_in_dim(collected[hops], slot ^ last, 0, keepdims=True)
+    far_blocks = collected[:hops] + [oldest]
+    far_count = hops * PLANE * rows
+    oldest_pos = (PLANE * (plane - hops) + last) * rows + jnp.arange(rows, dtype=jnp.int32)
+    far_key_pos = jnp.concatenate([key_pos[:, :far_count], oldest_pos[None]], axis=1)
+    far_key_doc = jnp.concatenate(
+        [key_doc[:, :far_count], oldest[0, rows, :rows].astype(jnp.int32)[None]], axis=1
+    )
+
     offsets_in_shard = jnp.arange(rows, dtype=jnp.int32).reshape(rows, 1)
     visit_pos = (my_index + PLANE * far) * rows + offsets_in_shard
     visit_doc = visiting[rows, :rows].astype(jnp.int32).reshape(rows, 1)
     visit_out, visit_stats, visit_rows = partial(
-        visiting, blocks, key_pos, key_doc, visit_pos, visit_doc, jnp.bfloat16
+        visiting, far_blocks, far_key_pos, far_key_doc, visit_pos, visit_doc, jnp.bfloat16
     )
     ahead = [(s, s + PLANE * far) for s in range(ctx - PLANE * far)]
     far_out = lax.ppermute(visit_out, "ctx", ahead)

time: 113 us -> 114 us (level)
  local copies, waits for them, and re-layouts: 2.88 us -> 4.64 us
  transfers between devices with their start and end apart: 10 -> 10, of which waited for: 5 -> 4; matrix products, arithmetic and copies ran while one was open for 5% -> 5% of each run, Pallas kernels for 5% -> 4%
where the time goes in v15:
time: 114 us
  starting transfers between devices  49.6 us (44%)
  blocking collectives  19.9 us (17%)
  waiting for transfers between devices  18.9 us (17%)
  Pallas kernels  14.4 us (13%)
  other arithmetic  5.96 us (5%)
  local copies, waits for them, and re-layouts  4.64 us (4%)
    all_to_all x1, blocking collectives, shards(): received = lax.all_to_all(chunks, 'tp', 0, 0, tiled=True)  19.9 us
    ppermute x4, starting transfers between devices, shards(): current = lax.ppermute(current, 'ctx', forward)  19.6 us
    ppermute x4, waiting for transfers between devices, shards(): current = lax.ppermute(current, 'ctx', forward)  18.9 us
    ppermute x1, starting transfers between devices, shards(): far_rows = lax.ppermute(visit_rows, 'ctx', ahead)  11.2 us
    pallas_call x2, Pallas kernels, partial(): pl.pallas_call(partial_kernel, out_shape=(jax.ShapeDtypeStruct((rows, wid...  9.84 us
    ppermute x1, starting transfers between devices, shards(): far_out = lax.ppermute(visit_out, 'ctx', ahead)  9.65 us
    ppermute x3, starting transfers between devices, shards(): lax.ppermute(block, 'ctx', [(s, s ^ offset) for s in range(ctx)])  7.87 us
    pallas_call x1, Pallas kernels, merge(): pl.pallas_call(merge_kernel, out_shape=jax.ShapeDtypeStruct((pieces, rows...  4.52 us
  transfers between devices with their start and end apart: 10, of which 4 were waited for; matrix products, arithmetic and copies ran while one was open for 5% of the time, Pallas kernels for 4%

profile of v15, /device:TPU:64, one launch (start us, length us, event | category | flops | bytes accessed | tf_op | source)
XLA Modules:
  0.0 113.7 jit_solution(16574700439709076028)
XLA Ops:
  0.7 0.8 fusion.11
  1.4 3.4 %collective-permute-start.1 = (bf16[136,256]{1,0:T(8,128)(2,1)S(1)}, bf16[136,256]{1,0:T(8,128)(2,1)S(1)}, u32[]{:S(2)}, u32[]{:S(2)}) collective-permute-start(bf16[136,256]{1,0:T(8,128)(2,1)S(1)} %get-tuple-element.46), channel_id=1, source_target_pairs={{0,16},{8,24},{16,0},{24,8},{32,48},{40,56},{48,32},{56,40},{64,80... | collective-permute-start | bytes 208904 | tf_op jit(solution)/shard_map/ppermute | solution.py:162
  4.9 1.9 %collective-permute-start = (bf16[136,256]{1,0:T(8,128)(2,1)S(1)}, bf16[136,256]{1,0:T(8,128)(2,1)S(1)}, u32[]{:S(2)}, u32[]{:S(2)}) collective-permute-start(bf16[136,256]{1,0:T(8,128)(2,1)S(1)} %get-tuple-element.46), channel_id=1, source_target_pairs={{0,8},{8,0},{16,24},{24,16},{32,40},{40,32},{48,56},{56,48},{64,72... | collective-permute-start | bytes 208904 | tf_op jit(solution)/shard_map/ppermute | solution.py:162
  6.8 2.5 %collective-permute-start.2 = (bf16[136,256]{1,0:T(8,128)(2,1)S(1)}, bf16[136,256]{1,0:T(8,128)(2,1)S(1)}, u32[]{:S(2)}, u32[]{:S(2)}) collective-permute-start(bf16[136,256]{1,0:T(8,128)(2,1)S(1)} %get-tuple-element.46), channel_id=1, source_target_pairs={{0,24},{8,16},{16,8},{24,0},{32,56},{40,48},{48,40},{56,32},{64,88... | collective-permute-start | bytes 208904 | tf_op jit(solution)/shard_map/ppermute | solution.py:162
  9.3 0.9 fusion.1
  10.3 1.3 %collective-permute-start.7 = (bf16[136,512]{1,0:T(8,128)(2,1)S(1)}, bf16[136,512]{1,0:T(8,128)(2,1)S(1)}, u32[]{:S(2)}, u32[]{:S(2)}) collective-permute-start(bf16[136,512]{1,0:T(8,128)(2,1)S(1)} %fusion.1), channel_id=1, source_target_pairs={{160,0},{168,8},{176,16},{184,24},{192,32},{200,40},{208,48},{216,... | collective-permute-start | bytes 417800 | tf_op jit(solution)/shard_map/ppermute | solution.py:158
  13.1 3.8 %collective-permute-start.3 = (bf16[4,136,256]{2,1,0:T(8,128)(2,1)S(1)}, bf16[4,136,256]{2,1,0:T(8,128)(2,1)S(1)}, u32[]{:S(2)}, u32[]{:S(2)}) collective-permute-start(bf16[4,136,256]{2,1,0:T(8,128)(2,1)S(1)} %pad_maximum_fusion.refs_1_), channel_id=1, source_target_pairs={{0,32},{8,40},{16,48},{24,56},{32,64},{40,72},{48,80},{56,88},{64,... | collective-permute-start | bytes 835592 | tf_op jit(solution)/shard_map/ppermute | solution.py:167
  17.5 6.0 %collective-permute-done.3.refs_2_ = bf16[4,136,256]{2,1,0:T(8,128)(2,1)S(1)} collective-permute-done((bf16[4,136,256]{2,1,0:T(8,128)(2,1)S(1)}, bf16[4,136,256]{2,1,0:T(8,128)(2,1)S(1)}, u32[]{:S(2)}, u32[]{:S(2)}) %collective-permute-start.3) | collective-permute-done | bytes 278560 | tf_op jit(solution)/shard_map/ppermute | solution.py:167
  23.6 4.5 %collective-permute-start.4 = (bf16[4,136,256]{2,1,0:T(8,128)(2,1)S(1)}, bf16[4,136,256]{2,1,0:T(8,128)(2,1)S(1)}, u32[]{:S(2)}, u32[]{:S(2)}) collective-permute-start(bf16[4,136,256]{2,1,0:T(8,128)(2,1)S(1)} %collective-permute-done.3.refs_2_), channel_id=1, source_target_pairs={{0,32},{8,40},{16,48},{24,56},{32,64},{40,72},{48,80},{56,88},{64,... | collective-permute-start | bytes 835592 | tf_op jit(solution)/shard_map/ppermute | solution.py:167
  28.1 1.4 %copy.6.refs_9_ = s32[128,1]{1,0:T(8,128)} copy(s32[128,1]{0,1:T(1,128)} %bitcast.69) | data formatting | bytes 1024 | tf_op jit(solution)/shard_map/reshape | solution.py:202
  29.5 5.5 %collective-permute-done.4.refs_3_ = bf16[4,136,256]{2,1,0:T(8,128)(2,1)S(1)} collective-permute-done((bf16[4,136,256]{2,1,0:T(8,128)(2,1)S(1)}, bf16[4,136,256]{2,1,0:T(8,128)(2,1)S(1)}, u32[]{:S(2)}, u32[]{:S(2)}) %collective-permute-start.4) | collective-permute-done | bytes 278560 | tf_op jit(solution)/shard_map/ppermute | solution.py:167
  35.0 5.8 %collective-permute-start.5 = (bf16[4,136,256]{2,1,0:T(8,128)(2,1)S(1)}, bf16[4,136,256]{2,1,0:T(8,128)(2,1)S(1)}, u32[]{:S(2)}, u32[]{:S(2)}) collective-permute-start(bf16[4,136,256]{2,1,0:T(8,128)(2,1)S(1)} %collective-permute-done.4.refs_3_), channel_id=1, source_target_pairs={{0,32},{8,40},{16,48},{24,56},{32,64},{40,72},{48,80},{56,88},{64,... | collective-permute-start | bytes 835592 | tf_op jit(solution)/shard_map/ppermute | solution.py:167
  40.8 0.7 copy.7.refs_9_
  41.5 3.3 %collective-permute-done.5.refs_4_ = bf16[4,136,256]{2,1,0:T(8,128)(2,1)S(1)} collective-permute-done((bf16[4,136,256]{2,1,0:T(8,128)(2,1)S(1)}, bf16[4,136,256]{2,1,0:T(8,128)(2,1)S(1)}, u32[]{:S(2)}, u32[]{:S(2)}) %collective-permute-start.5) | collective-permute-done | bytes 278560 | tf_op jit(solution)/shard_map/ppermute | solution.py:167
  44.8 5.6 %collective-permute-start.6 = (bf16[4,136,256]{2,1,0:T(8,128)(2,1)S(1)}, bf16[4,136,256]{2,1,0:T(8,128)(2,1)S(1)}, u32[]{:S(2)}, u32[]{:S(2)}) collective-permute-start(bf16[4,136,256]{2,1,0:T(8,128)(2,1)S(1)} %collective-permute-done.5.refs_4_), channel_id=1, source_target_pairs={{0,32},{8,40},{16,48},{24,56},{32,64},{40,72},{48,80},{56,88},{64,... | collective-permute-start | bytes 835592 | tf_op jit(solution)/shard_map/ppermute | solution.py:167
  50.4 4.0 %collective-permute-done.6.refs_5_ = bf16[4,136,256]{2,1,0:T(8,128)(2,1)S(1)} collective-permute-done((bf16[4,136,256]{2,1,0:T(8,128)(2,1)S(1)}, bf16[4,136,256]{2,1,0:T(8,128)(2,1)S(1)}, u32[]{:S(2)}, u32[]{:S(2)}) %collective-permute-start.6) | collective-permute-done | bytes 278560 | tf_op jit(solution)/shard_map/ppermute | solution.py:167
  55.8 4.8 %shard_map.56 = (bf16[128,512]{1,0:T(8,128)(2,1)}, f32[128,8]{1,0:T(8,128)}, f32[8,128]{1,0:T(8,128)}) custom-call(bf16[136,512]{1,0:T(8,128)(2,1)} %copy-done.9, bf16[4,136,256]{2,1,0:T(8,128)(2,1)} %copy-done, bf16[4,136,256]{2,1,0:T(8,128)(2,1)} %copy-done.6, bf16[4,136,256]{2,1,0:T(8,128)(2,1)} %copy-done.7, bf16[4,136,256]{2,1,0:T(8,128)(2,1)} %copy-done.8, ...), custom_call_target="tpu_custom_call" | custom-call | flops 570425344 | bytes 1585152 | tf_op jit(solution)/shard_map/pallas_call | solution.py:69
  60.5 11.2 %collective-permute-start.9 = (f32[8,128]{1,0:T(8,128)}, f32[8,128]{1,0:T(8,128)S(1)}, u32[]{:S(2)}, u32[]{:S(2)}) collective-permute-start(f32[8,128]{1,0:T(8,128)} %get-tuple-element.36), channel_id=1, source_target_pairs={{0,160},{8,168},{16,176},{24,184},{32,192},{40,200},{48,208},{56,2... | collective-permute-start | bytes 12296 | tf_op jit(solution)/shard_map/ppermute | solution.py:198
  71.7 9.7 %collective-permute-start.8 = (bf16[128,512]{1,0:T(8,128)(2,1)}, bf16[128,512]{1,0:T(8,128)(2,1)S(1)}, u32[]{:S(2)}, u32[]{:S(2)}) collective-permute-start(bf16[128,512]{1,0:T(8,128)(2,1)} %get-tuple-element.35), channel_id=1, source_target_pairs={{0,160},{8,168},{16,176},{24,184},{32,192},{40,200},{48,208},{56,2... | collective-permute-start | bytes 393224 | tf_op jit(solution)/shard_map/ppermute | solution.py:197
  82.0 5.1 %shard_map.55 = (f32[128,512]{1,0:T(8,128)}, f32[128,8]{1,0:T(8,128)}, f32[8,128]{1,0:T(8,128)}) custom-call(bf16[128,512]{1,0:T(8,128)(2,1)} %refs_0_.1, bf16[4,136,256]{2,1,0:T(8,128)(2,1)} %copy-done, bf16[4,136,256]{2,1,0:T(8,128)(2,1)} %copy-done.6, bf16[4,136,256]{2,1,0:T(8,128)(2,1)} %copy-done.7, bf16[4,136,256]{2,1,0:T(8,128)(2,1)} %copy-done.8, ...), custom_call_target="tpu_custom_call" | custom-call | flops 671088640 | bytes 1785856 | tf_op jit(solution)/shard_map/pallas_call | solution.py:69
  87.1 0.7 broadcast_select_fusion.far_rows_ref
  88.4 4.5 %shard_map.57 = bf16[8,128,512]{2,1,0:T(8,128)(2,1)} custom-call(f32[128,512]{1,0:T(8,128)} %get-tuple-element.33.near_ref, f32[128,8]{1,0:T(8,128)} %get-tuple-element.34.near_stats_ref, bf16[128,512]{1,0:T(8,128)(2,1)} %copy-done.1, f32[8,128]{1,0:T(8,128)} %broadcast_select_fusion.far_rows_ref, bf16[512,4096]{1,0:T(8,128)(2,1)} %weight_ref.1), custom_call_target="tpu_custom_call" | custom-call | flops 536870912 | bytes 5242880 | tf_op jit(solution)/shard_map/pallas_call | solution.py:122
  92.9 19.9 %all_to_all.5 = bf16[8,128,512]{2,1,0:T(8,128)(2,1)S(1)} all-to-all(bf16[8,128,512]{2,1,0:T(8,128)(2,1)} %shard_map.57), channel_id=1, replica_groups=mesh['ctx'=64,'tp'=8] {'tp'}, dimensions={0} | all-to-all | bytes 2097152 | tf_op jit(solution)/shard_map/all_to_all | solution.py:210
  112.9 0.8 reduce_sum.12
  (46 shorter events, 5.3 us)
Async XLA Ops:
  1.4 11.6 %collective-permute-start.1 = (bf16[136,256]{1,0:T(8,128)(2,1)S(1)}, bf16[136,256]{1,0:T(8,128)(2,1)S(1)}, u32[]{:S(2)}, u32[]{:S(2)}) collective-permute-start(bf16[136,256]{1,0:T(8,128)(2,1)S(1)} %get-tuple-element.46), channel_id=1, source_target_pairs={{0,16},{8,24},{16,0},{24,8},{32,48},{40,56},{48,32},{56,40},{64,80... | collective-permute-start | bytes 208904 | tf_op jit(solution)/shard_map/ppermute | solution.py:162
  4.9 8.2 %collective-permute-start = (bf16[136,256]{1,0:T(8,128)(2,1)S(1)}, bf16[136,256]{1,0:T(8,128)(2,1)S(1)}, u32[]{:S(2)}, u32[]{:S(2)}) collective-permute-start(bf16[136,256]{1,0:T(8,128)(2,1)S(1)} %get-tuple-element.46), channel_id=1, source_target_pairs={{0,8},{8,0},{16,24},{24,16},{32,40},{40,32},{48,56},{56,48},{64,72... | collective-permute-start | bytes 208904 | tf_op jit(solution)/shard_map/ppermute | solution.py:162
  6.8 6.3 %collective-permute-start.2 = (bf16[136,256]{1,0:T(8,128)(2,1)S(1)}, bf16[136,256]{1,0:T(8,128)(2,1)S(1)}, u32[]{:S(2)}, u32[]{:S(2)}) collective-permute-start(bf16[136,256]{1,0:T(8,128)(2,1)S(1)} %get-tuple-element.46), channel_id=1, source_target_pairs={{0,24},{8,16},{16,8},{24,0},{32,56},{40,48},{48,40},{56,32},{64,88... | collective-permute-start | bytes 208904 | tf_op jit(solution)/shard_map/ppermute | solution.py:162
  10.3 30.5 %collective-permute-start.7 = (bf16[136,512]{1,0:T(8,128)(2,1)S(1)}, bf16[136,512]{1,0:T(8,128)(2,1)S(1)}, u32[]{:S(2)}, u32[]{:S(2)}) collective-permute-start(bf16[136,512]{1,0:T(8,128)(2,1)S(1)} %fusion.1), channel_id=1, source_target_pairs={{160,0},{168,8},{176,16},{184,24},{192,32},{200,40},{208,48},{216,... | collective-permute-start | bytes 417800 | tf_op jit(solution)/shard_map/ppermute | solution.py:158
  11.8 69.6 %copy-start.2 = (s32[5,4,128]{2,1,0:T(4,128)}, s32[5,4,128]{2,1,0:T(4,128)S(1)}, u32[]{:S(2)}) copy-start(s32[5,4,128]{2,1,0:T(4,128)S(1)} %iota_add_fusion.2) | copy-start | bytes 30724
  13.1 42.0 %copy-start = (bf16[4,136,256]{2,1,0:T(8,128)(2,1)}, bf16[4,136,256]{2,1,0:T(8,128)(2,1)S(1)}, u32[]{:S(2)}) copy-start(bf16[4,136,256]{2,1,0:T(8,128)(2,1)S(1)} %pad_maximum_fusion.refs_1_) | copy-start | bytes 835588
  13.1 10.5 %collective-permute-start.3 = (bf16[4,136,256]{2,1,0:T(8,128)(2,1)S(1)}, bf16[4,136,256]{2,1,0:T(8,128)(2,1)S(1)}, u32[]{:S(2)}, u32[]{:S(2)}) collective-permute-start(bf16[4,136,256]{2,1,0:T(8,128)(2,1)S(1)} %pad_maximum_fusion.refs_1_), channel_id=1, source_target_pairs={{0,32},{8,40},{16,48},{24,56},{32,64},{40,72},{48,80},{56,88},{64,... | collective-permute-start | bytes 835592 | tf_op jit(solution)/shard_map/ppermute | solution.py:167
  23.6 31.6 %copy-start.6 = (bf16[4,136,256]{2,1,0:T(8,128)(2,1)}, bf16[4,136,256]{2,1,0:T(8,128)(2,1)S(1)}, u32[]{:S(2)}) copy-start(bf16[4,136,256]{2,1,0:T(8,128)(2,1)S(1)} %collective-permute-done.3.refs_2_) | copy-start | bytes 835588
  23.6 11.4 %collective-permute-start.4 = (bf16[4,136,256]{2,1,0:T(8,128)(2,1)S(1)}, bf16[4,136,256]{2,1,0:T(8,128)(2,1)S(1)}, u32[]{:S(2)}, u32[]{:S(2)}) collective-permute-start(bf16[4,136,256]{2,1,0:T(8,128)(2,1)S(1)} %collective-permute-done.3.refs_2_), channel_id=1, source_target_pairs={{0,32},{8,40},{16,48},{24,56},{32,64},{40,72},{48,80},{56,88},{64,... | collective-permute-start | bytes 835592 | tf_op jit(solution)/shard_map/ppermute | solution.py:167
  35.0 20.1 %copy-start.7 = (bf16[4,136,256]{2,1,0:T(8,128)(2,1)}, bf16[4,136,256]{2,1,0:T(8,128)(2,1)S(1)}, u32[]{:S(2)}) copy-start(bf16[4,136,256]{2,1,0:T(8,128)(2,1)S(1)} %collective-permute-done.4.refs_3_) | copy-start | bytes 835588
  35.0 9.8 %collective-permute-start.5 = (bf16[4,136,256]{2,1,0:T(8,128)(2,1)S(1)}, bf16[4,136,256]{2,1,0:T(8,128)(2,1)S(1)}, u32[]{:S(2)}, u32[]{:S(2)}) collective-permute-start(bf16[4,136,256]{2,1,0:T(8,128)(2,1)S(1)} %collective-permute-done.4.refs_3_), channel_id=1, source_target_pairs={{0,32},{8,40},{16,48},{24,56},{32,64},{40,72},{48,80},{56,88},{64,... | collective-permute-start | bytes 835592 | tf_op jit(solution)/shard_map/ppermute | solution.py:167
  40.8 14.4 %copy-start.9 = (bf16[136,512]{1,0:T(8,128)(2,1)}, bf16[136,512]{1,0:T(8,128)(2,1)S(1)}, u32[]{:S(2)}) copy-start(bf16[136,512]{1,0:T(8,128)(2,1)S(1)} %collective-permute-done.7.refs_0_) | copy-start | bytes 417796
  44.8 10.3 %copy-start.8 = (bf16[4,136,256]{2,1,0:T(8,128)(2,1)}, bf16[4,136,256]{2,1,0:T(8,128)(2,1)S(1)}, u32[]{:S(2)}) copy-start(bf16[4,136,256]{2,1,0:T(8,128)(2,1)S(1)} %collective-permute-done.5.refs_4_) | copy-start | bytes 835588
  44.8 9.6 %collective-permute-start.6 = (bf16[4,136,256]{2,1,0:T(8,128)(2,1)S(1)}, bf16[4,136,256]{2,1,0:T(8,128)(2,1)S(1)}, u32[]{:S(2)}, u32[]{:S(2)}) collective-permute-start(bf16[4,136,256]{2,1,0:T(8,128)(2,1)S(1)} %collective-permute-done.5.refs_4_), channel_id=1, source_target_pairs={{0,32},{8,40},{16,48},{24,56},{32,64},{40,72},{48,80},{56,88},{64,... | collective-permute-start | bytes 835592 | tf_op jit(solution)/shard_map/ppermute | solution.py:167
  54.5 27.0 %copy-start.3 = (bf16[4,136,256]{2,1,0:T(8,128)(2,1)}, bf16[4,136,256]{2,1,0:T(8,128)(2,1)S(1)}, u32[]{:S(2)}) copy-start(bf16[4,136,256]{2,1,0:T(8,128)(2,1)S(1)} %collective-permute-done.6.refs_5_) | copy-start | bytes 835588
  55.2 0.6 copy-start.4
  60.5 26.6 %collective-permute-start.9 = (f32[8,128]{1,0:T(8,128)}, f32[8,128]{1,0:T(8,128)S(1)}, u32[]{:S(2)}, u32[]{:S(2)}) collective-permute-start(f32[8,128]{1,0:T(8,128)} %get-tuple-element.36), channel_id=1, source_target_pairs={{0,160},{8,168},{16,176},{24,184},{32,192},{40,200},{48,208},{56,2... | collective-permute-start | bytes 12296 | tf_op jit(solution)/shard_map/ppermute | solution.py:198
  71.7 16.0 %collective-permute-start.8 = (bf16[128,512]{1,0:T(8,128)(2,1)}, bf16[128,512]{1,0:T(8,128)(2,1)S(1)}, u32[]{:S(2)}, u32[]{:S(2)}) collective-permute-start(bf16[128,512]{1,0:T(8,128)(2,1)} %get-tuple-element.35), channel_id=1, source_target_pairs={{0,160},{8,168},{16,176},{24,184},{32,192},{40,200},{48,208},{56,2... | collective-permute-start | bytes 393224 | tf_op jit(solution)/shard_map/ppermute | solution.py:197
  81.4 0.6 copy-start.5
  87.8 0.7 copy-start.1

commit v16 on v10

--- a/solution.py
+++ b/solution.py
@@ -16,9 +16,9 @@
 
 def partial_kernel(*refs):
     query_ref = refs[0]
-    block_refs = refs[1:-8]
-    (key_pos_ref, key_doc_ref, query_pos_ref, query_doc_ref, out_ref, stats_ref,
-     rows_ref, square_ref) = refs[-8:]
+    block_refs = refs[1:-7]
+    (key_pos_ref, query_pos_ref, query_doc_ref, out_ref, stats_ref,
+     rows_ref, square_ref) = refs[-7:]
     rows = query_pos_ref.shape[0]
     width = query_ref.shape[1]
     head_dim = block_refs[0].shape[-1] // 2
@@ -31,10 +31,15 @@
         [ref[:, :rows, head_dim:].reshape(ref.shape[0] * rows, head_dim) for ref in block_refs],
         axis=0,
     )
+    key_doc = jnp.concatenate(
+        [ref[shard, rows:rows + 1, :rows].astype(jnp.float32)
+         for ref in block_refs for shard in range(ref.shape[0])],
+        axis=1,
+    )
     allowed = (
         (key_pos_ref[...] <= query_pos_ref[...])
         & (key_pos_ref[...] >= 0)
-        & (key_doc_ref[...] == query_doc_ref[...])
+        & (key_doc == query_doc_ref[...].astype(jnp.float32))
     )
     bias = jnp.where(allowed, 0.0, neg_large)
     seen = jnp.max(jnp.where(allowed, 1.0, 0.0), axis=1, keepdims=True) > 0.0
@@ -60,7 +65,7 @@
     rows_ref[...] = jnp.transpose(square_ref[...])[:2 * heads]
 
 
-def partial(query, blocks, key_pos, key_doc, query_pos, query_doc, out_dtype):
+def partial(query, blocks, key_pos, query_pos, query_doc, out_dtype):
     rows = query_pos.shape[0]
     width = query.shape[1]
     heads = width // HEAD_DIM
@@ -73,14 +78,14 @@
             jax.ShapeDtypeStruct((rows, 2 * heads), jnp.float32),
             jax.ShapeDtypeStruct((2 * heads, rows), jnp.float32),
         ),
-        in_specs=[vmem] * (5 + len(blocks)),
+        in_specs=[vmem] * (4 + len(blocks)),
         out_specs=(vmem, vmem, vmem),
         scratch_shapes=[pltpu.VMEM((rows, rows), jnp.float32)],
         cost_estimate=pl.CostEstimate(
             flops=4 * rows * tokens * width, transcendentals=rows * tokens * heads,
             bytes_accessed=sum(b.size for b in blocks) * 2 + query.size * 2 + rows * width * 4,
         ),
-    )(query, *blocks, key_pos, key_doc, query_pos, query_doc)
+    )(query, *blocks, key_pos, query_pos, query_doc)
 
 
 def merge_kernel(near_ref, near_stats_ref, far_ref, far_rows_ref, weight_ref, out_ref,
@@ -173,15 +178,12 @@
     tokens = jnp.arange(rows, dtype=jnp.int32)[None, None, :]
     key_shard = PLANE * (plane - hop_ids) + (slot ^ offsets)
     key_pos = (key_shard * rows + tokens).reshape(1, -1)
-    key_doc = jnp.concatenate(
-        [b[:, rows, :rows].astype(jnp.int32).reshape(1, -1) for b in blocks], axis=1
-    )
 
     offsets_in_shard = jnp.arange(rows, dtype=jnp.int32).reshape(rows, 1)
     visit_pos = (my_index + PLANE * far) * rows + offsets_in_shard
     visit_doc = visiting[rows, :rows].astype(jnp.int32).reshape(rows, 1)
     visit_out, visit_stats, visit_rows = partial(
-        visiting, blocks, key_pos, key_doc, visit_pos, visit_doc, jnp.bfloat16
+        visiting, blocks, key_pos, visit_pos, visit_doc, jnp.bfloat16
     )
     ahead = [(s, s + PLANE * far) for s in range(ctx - PLANE * far)]
     far_out = lax.ppermute(visit_out, "ctx", ahead)
@@ -189,7 +191,7 @@
 
     query_pos = my_index * rows + offsets_in_shard
     near_out, near_stats, _ = partial(
-        queries, blocks, key_pos, key_doc, query_pos, docs.reshape(rows, 1), jnp.float32
+        queries, blocks, key_pos, query_pos, docs.reshape(rows, 1), jnp.float32
     )
     has_far = plane >= far
     heads = near_stats.shape[1] // 2

time: 113 us -> 115 us (1.018)
  the two profiles are of different devices: /device:TPU:64 before, /device:TPU:96 now
where the time goes in v16:
time: 115 us
  starting transfers between devices  45.9 us (40%)
  blocking collectives  24 us (21%)
  waiting for transfers between devices  20.7 us (18%)
  Pallas kernels  14.6 us (13%)
  other arithmetic  5.88 us (5%)
  local copies, waits for them, and re-layouts  3.48 us (3%)
    all_to_all x1, blocking collectives, shards(): received = lax.all_to_all(chunks, 'tp', 0, 0, tiled=True)  24 us
    ppermute x4, starting transfers between devices, shards(): current = lax.ppermute(current, 'ctx', forward)  21.8 us
    ppermute x4, waiting for transfers between devices, shards(): current = lax.ppermute(current, 'ctx', forward)  14.7 us
    ppermute x1, starting transfers between devices, shards(): far_rows = lax.ppermute(visit_rows, 'ctx', ahead)  12.2 us
    pallas_call x2, Pallas kernels, partial(): pl.pallas_call(partial_kernel, out_shape=(jax.ShapeDtypeStruct((rows, wid...  10.1 us
    ppermute x3, starting transfers between devices, shards(): lax.ppermute(block, 'ctx', [(s, s ^ offset) for s in range(ctx)])  7.87 us
    pallas_call x1, Pallas kernels, merge(): pl.pallas_call(merge_kernel, out_shape=jax.ShapeDtypeStruct((pieces, rows...  4.52 us
    ppermute x3, waiting for transfers between devices, shards(): lax.ppermute(block, 'ctx', [(s, s ^ offset) for s in range(ctx)])  3.17 us
  transfers between devices with their start and end apart: 10, of which 6 were waited for; matrix products, arithmetic and copies ran while one was open for 5% of the time, Pallas kernels for 4%

profile of v16, /device:TPU:96, one launch (start us, length us, event | category | flops | bytes accessed | tf_op | source)
XLA Modules:
  0.0 114.7 jit_solution(7377567237917079238)
XLA Ops:
  0.7 0.8 fusion.5
  1.4 3.4 %collective-permute-start.1 = (bf16[136,256]{1,0:T(8,128)(2,1)S(1)}, bf16[136,256]{1,0:T(8,128)(2,1)S(1)}, u32[]{:S(2)}, u32[]{:S(2)}) collective-permute-start(bf16[136,256]{1,0:T(8,128)(2,1)S(1)} %get-tuple-element.38), channel_id=1, source_target_pairs={{0,16},{8,24},{16,0},{24,8},{32,48},{40,56},{48,32},{56,40},{64,80... | collective-permute-start | bytes 208904 | tf_op jit(solution)/shard_map/ppermute | solution.py:167
  4.9 1.9 %collective-permute-start = (bf16[136,256]{1,0:T(8,128)(2,1)S(1)}, bf16[136,256]{1,0:T(8,128)(2,1)S(1)}, u32[]{:S(2)}, u32[]{:S(2)}) collective-permute-start(bf16[136,256]{1,0:T(8,128)(2,1)S(1)} %get-tuple-element.38), channel_id=1, source_target_pairs={{0,8},{8,0},{16,24},{24,16},{32,40},{40,32},{48,56},{56,48},{64,72... | collective-permute-start | bytes 208904 | tf_op jit(solution)/shard_map/ppermute | solution.py:167
  6.8 2.5 %collective-permute-start.2 = (bf16[136,256]{1,0:T(8,128)(2,1)S(1)}, bf16[136,256]{1,0:T(8,128)(2,1)S(1)}, u32[]{:S(2)}, u32[]{:S(2)}) collective-permute-start(bf16[136,256]{1,0:T(8,128)(2,1)S(1)} %get-tuple-element.38), channel_id=1, source_target_pairs={{0,24},{8,16},{16,8},{24,0},{32,56},{40,48},{48,40},{56,32},{64,88... | collective-permute-start | bytes 208904 | tf_op jit(solution)/shard_map/ppermute | solution.py:167
  9.4 3.2 %collective-permute-done.2 = bf16[136,256]{1,0:T(8,128)(2,1)S(1)} collective-permute-done((bf16[136,256]{1,0:T(8,128)(2,1)S(1)}, bf16[136,256]{1,0:T(8,128)(2,1)S(1)}, u32[]{:S(2)}, u32[]{:S(2)}) %collective-permute-start.2) | collective-permute-done | bytes 69664 | tf_op jit(solution)/shard_map/ppermute | solution.py:167
  12.6 5.0 %collective-permute-start.3 = (bf16[4,136,256]{2,1,0:T(8,128)(2,1)S(1)}, bf16[4,136,256]{2,1,0:T(8,128)(2,1)S(1)}, u32[]{:S(2)}, u32[]{:S(2)}) collective-permute-start(bf16[4,136,256]{2,1,0:T(8,128)(2,1)S(1)} %pad_maximum_fusion.refs_1_), channel_id=1, source_target_pairs={{0,32},{8,40},{16,48},{24,56},{32,64},{40,72},{48,80},{56,88},{64,... | collective-permute-start | bytes 835592 | tf_op jit(solution)/shard_map/ppermute | solution.py:172
  17.6 0.9 fusion.1
  18.5 1.3 %collective-permute-start.7 = (bf16[136,512]{1,0:T(8,128)(2,1)S(1)}, bf16[136,512]{1,0:T(8,128)(2,1)S(1)}, u32[]{:S(2)}, u32[]{:S(2)}) collective-permute-start(bf16[136,512]{1,0:T(8,128)(2,1)S(1)} %fusion.1), channel_id=1, source_target_pairs={{160,0},{168,8},{176,16},{184,24},{192,32},{200,40},{208,48},{216,... | collective-permute-start | bytes 417800 | tf_op jit(solution)/shard_map/ppermute | solution.py:163
  19.9 4.3 %collective-permute-done.3.refs_2_ = bf16[4,136,256]{2,1,0:T(8,128)(2,1)S(1)} collective-permute-done((bf16[4,136,256]{2,1,0:T(8,128)(2,1)S(1)}, bf16[4,136,256]{2,1,0:T(8,128)(2,1)S(1)}, u32[]{:S(2)}, u32[]{:S(2)}) %collective-permute-start.3) | collective-permute-done | bytes 278560 | tf_op jit(solution)/shard_map/ppermute | solution.py:172
  24.1 5.6 %collective-permute-start.4 = (bf16[4,136,256]{2,1,0:T(8,128)(2,1)S(1)}, bf16[4,136,256]{2,1,0:T(8,128)(2,1)S(1)}, u32[]{:S(2)}, u32[]{:S(2)}) collective-permute-start(bf16[4,136,256]{2,1,0:T(8,128)(2,1)S(1)} %collective-permute-done.3.refs_2_), channel_id=1, source_target_pairs={{0,32},{8,40},{16,48},{24,56},{32,64},{40,72},{48,80},{56,88},{64,... | collective-permute-start | bytes 835592 | tf_op jit(solution)/shard_map/ppermute | solution.py:172
  29.8 5.6 %collective-permute-done.4.refs_3_ = bf16[4,136,256]{2,1,0:T(8,128)(2,1)S(1)} collective-permute-done((bf16[4,136,256]{2,1,0:T(8,128)(2,1)S(1)}, bf16[4,136,256]{2,1,0:T(8,128)(2,1)S(1)}, u32[]{:S(2)}, u32[]{:S(2)}) %collective-permute-start.4) | collective-permute-done | bytes 278560 | tf_op jit(solution)/shard_map/ppermute | solution.py:172
  35.5 5.6 %collective-permute-start.5 = (bf16[4,136,256]{2,1,0:T(8,128)(2,1)S(1)}, bf16[4,136,256]{2,1,0:T(8,128)(2,1)S(1)}, u32[]{:S(2)}, u32[]{:S(2)}) collective-permute-start(bf16[4,136,256]{2,1,0:T(8,128)(2,1)S(1)} %collective-permute-done.4.refs_3_), channel_id=1, source_target_pairs={{0,32},{8,40},{16,48},{24,56},{32,64},{40,72},{48,80},{56,88},{64,... | collective-permute-start | bytes 835592 | tf_op jit(solution)/shard_map/ppermute | solution.py:172
  43.0 2.9 %collective-permute-done.5.refs_4_ = bf16[4,136,256]{2,1,0:T(8,128)(2,1)S(1)} collective-permute-done((bf16[4,136,256]{2,1,0:T(8,128)(2,1)S(1)}, bf16[4,136,256]{2,1,0:T(8,128)(2,1)S(1)}, u32[]{:S(2)}, u32[]{:S(2)}) %collective-permute-start.5) | collective-permute-done | bytes 278560 | tf_op jit(solution)/shard_map/ppermute | solution.py:172
  45.9 5.6 %collective-permute-start.6 = (bf16[4,136,256]{2,1,0:T(8,128)(2,1)S(1)}, bf16[4,136,256]{2,1,0:T(8,128)(2,1)S(1)}, u32[]{:S(2)}, u32[]{:S(2)}) collective-permute-start(bf16[4,136,256]{2,1,0:T(8,128)(2,1)S(1)} %collective-permute-done.5.refs_4_), channel_id=1, source_target_pairs={{0,32},{8,40},{16,48},{24,56},{32,64},{40,72},{48,80},{56,88},{64,... | collective-permute-start | bytes 835592 | tf_op jit(solution)/shard_map/ppermute | solution.py:172
  51.5 1.4 %copy.6.refs_8_ = s32[128,1]{1,0:T(8,128)} copy(s32[128,1]{0,1:T(1,128)} %bitcast.19) | data formatting | bytes 1024 | tf_op jit(solution)/shard_map/reshape | solution.py:194
  53.6 1.9 %collective-permute-done.6.refs_5_ = bf16[4,136,256]{2,1,0:T(8,128)(2,1)S(1)} collective-permute-done((bf16[4,136,256]{2,1,0:T(8,128)(2,1)S(1)}, bf16[4,136,256]{2,1,0:T(8,128)(2,1)S(1)}, u32[]{:S(2)}, u32[]{:S(2)}) %collective-permute-start.6) | collective-permute-done | bytes 278560 | tf_op jit(solution)/shard_map/ppermute | solution.py:172
  56.2 5.0 %shard_map.56 = (bf16[128,512]{1,0:T(8,128)(2,1)}, f32[128,8]{1,0:T(8,128)}, f32[8,128]{1,0:T(8,128)}) custom-call(bf16[136,512]{1,0:T(8,128)(2,1)} %copy-done.6, bf16[4,136,256]{2,1,0:T(8,128)(2,1)} %copy-done, bf16[4,136,256]{2,1,0:T(8,128)(2,1)} %copy-done.2, bf16[4,136,256]{2,1,0:T(8,128)(2,1)} %copy-done.3, bf16[4,136,256]{2,1,0:T(8,128)(2,1)} %copy-done.4, ...), custom_call_target="tpu_custom_call" | custom-call | flops 671088640 | bytes 1794048 | tf_op jit(solution)/shard_map/pallas_call | solution.py:74
  61.3 12.2 %collective-permute-start.9 = (f32[8,128]{1,0:T(8,128)}, f32[8,128]{1,0:T(8,128)S(1)}, u32[]{:S(2)}, u32[]{:S(2)}) collective-permute-start(f32[8,128]{1,0:T(8,128)} %get-tuple-element.36), channel_id=1, source_target_pairs={{0,160},{8,168},{16,176},{24,184},{32,192},{40,200},{48,208},{56,2... | collective-permute-start | bytes 12296 | tf_op jit(solution)/shard_map/ppermute | solution.py:190
  73.5 2.7 %collective-permute-start.8 = (bf16[128,512]{1,0:T(8,128)(2,1)}, bf16[128,512]{1,0:T(8,128)(2,1)S(1)}, u32[]{:S(2)}, u32[]{:S(2)}) collective-permute-start(bf16[128,512]{1,0:T(8,128)(2,1)} %get-tuple-element.35), channel_id=1, source_target_pairs={{0,160},{8,168},{16,176},{24,184},{32,192},{40,200},{48,208},{56,2... | collective-permute-start | bytes 393224 | tf_op jit(solution)/shard_map/ppermute | solution.py:189
  76.2 5.1 %shard_map.55 = (f32[128,512]{1,0:T(8,128)}, f32[128,8]{1,0:T(8,128)}, f32[8,128]{1,0:T(8,128)}) custom-call(bf16[128,512]{1,0:T(8,128)(2,1)} %refs_0_.1, bf16[4,136,256]{2,1,0:T(8,128)(2,1)} %copy-done, bf16[4,136,256]{2,1,0:T(8,128)(2,1)} %copy-done.2, bf16[4,136,256]{2,1,0:T(8,128)(2,1)} %copy-done.3, bf16[4,136,256]{2,1,0:T(8,128)(2,1)} %copy-done.4, ...), custom_call_target="tpu_custom_call" | custom-call | flops 671088640 | bytes 1785856 | tf_op jit(solution)/shard_map/pallas_call | solution.py:74
  81.9 2.9 %collective-permute-done.8.far_ref = bf16[128,512]{1,0:T(8,128)(2,1)S(1)} collective-permute-done((bf16[128,512]{1,0:T(8,128)(2,1)}, bf16[128,512]{1,0:T(8,128)(2,1)S(1)}, u32[]{:S(2)}, u32[]{:S(2)}) %collective-permute-start.8) | collective-permute-done | bytes 131104 | tf_op jit(solution)/shard_map/ppermute | solution.py:189
  85.4 4.5 %shard_map.57 = bf16[8,128,512]{2,1,0:T(8,128)(2,1)} custom-call(f32[128,512]{1,0:T(8,128)} %get-tuple-element.33.near_ref, f32[128,8]{1,0:T(8,128)} %get-tuple-element.34.near_stats_ref, bf16[128,512]{1,0:T(8,128)(2,1)} %copy-done.1, f32[8,128]{1,0:T(8,128)} %broadcast_select_fusion.far_rows_ref, bf16[512,4096]{1,0:T(8,128)(2,1)} %weight_ref.1), custom_call_target="tpu_custom_call" | custom-call | flops 536870912 | bytes 5242880 | tf_op jit(solution)/shard_map/pallas_call | solution.py:127
  89.9 24.0 %all_to_all.5 = bf16[8,128,512]{2,1,0:T(8,128)(2,1)S(1)} all-to-all(bf16[8,128,512]{2,1,0:T(8,128)(2,1)} %shard_map.57), channel_id=1, replica_groups=mesh['ctx'=64,'tp'=8] {'tp'}, dimensions={0} | all-to-all | bytes 2097152 | tf_op jit(solution)/shard_map/all_to_all | solution.py:202
  113.9 0.8 reduce_sum.12
  (30 shorter events, 5.5 us)
Async XLA Ops:
  1.4 7.9 %collective-permute-start.1 = (bf16[136,256]{1,0:T(8,128)(2,1)S(1)}, bf16[136,256]{1,0:T(8,128)(2,1)S(1)}, u32[]{:S(2)}, u32[]{:S(2)}) collective-permute-start(bf16[136,256]{1,0:T(8,128)(2,1)S(1)} %get-tuple-element.38), channel_id=1, source_target_pairs={{0,16},{8,24},{16,0},{24,8},{32,48},{40,56},{48,32},{56,40},{64,80... | collective-permute-start | bytes 208904 | tf_op jit(solution)/shard_map/ppermute | solution.py:167
  4.9 4.5 %collective-permute-start = (bf16[136,256]{1,0:T(8,128)(2,1)S(1)}, bf16[136,256]{1,0:T(8,128)(2,1)S(1)}, u32[]{:S(2)}, u32[]{:S(2)}) collective-permute-start(bf16[136,256]{1,0:T(8,128)(2,1)S(1)} %get-tuple-element.38), channel_id=1, source_target_pairs={{0,8},{8,0},{16,24},{24,16},{32,40},{40,32},{48,56},{56,48},{64,72... | collective-permute-start | bytes 208904 | tf_op jit(solution)/shard_map/ppermute | solution.py:167
  6.8 5.7 %collective-permute-start.2 = (bf16[136,256]{1,0:T(8,128)(2,1)S(1)}, bf16[136,256]{1,0:T(8,128)(2,1)S(1)}, u32[]{:S(2)}, u32[]{:S(2)}) collective-permute-start(bf16[136,256]{1,0:T(8,128)(2,1)S(1)} %get-tuple-element.38), channel_id=1, source_target_pairs={{0,24},{8,16},{16,8},{24,0},{32,56},{40,48},{48,40},{56,32},{64,88... | collective-permute-start | bytes 208904 | tf_op jit(solution)/shard_map/ppermute | solution.py:167
  12.6 43.0 %copy-start = (bf16[4,136,256]{2,1,0:T(8,128)(2,1)}, bf16[4,136,256]{2,1,0:T(8,128)(2,1)S(1)}, u32[]{:S(2)}) copy-start(bf16[4,136,256]{2,1,0:T(8,128)(2,1)S(1)} %pad_maximum_fusion.refs_1_) | copy-start | bytes 835588
  12.6 11.6 %collective-permute-start.3 = (bf16[4,136,256]{2,1,0:T(8,128)(2,1)S(1)}, bf16[4,136,256]{2,1,0:T(8,128)(2,1)S(1)}, u32[]{:S(2)}, u32[]{:S(2)}) collective-permute-start(bf16[4,136,256]{2,1,0:T(8,128)(2,1)S(1)} %pad_maximum_fusion.refs_1_), channel_id=1, source_target_pairs={{0,32},{8,40},{16,48},{24,56},{32,64},{40,72},{48,80},{56,88},{64,... | collective-permute-start | bytes 835592 | tf_op jit(solution)/shard_map/ppermute | solution.py:172
  18.5 34.4 %collective-permute-start.7 = (bf16[136,512]{1,0:T(8,128)(2,1)S(1)}, bf16[136,512]{1,0:T(8,128)(2,1)S(1)}, u32[]{:S(2)}, u32[]{:S(2)}) collective-permute-start(bf16[136,512]{1,0:T(8,128)(2,1)S(1)} %fusion.1), channel_id=1, source_target_pairs={{160,0},{168,8},{176,16},{184,24},{192,32},{200,40},{208,48},{216,... | collective-permute-start | bytes 417800 | tf_op jit(solution)/shard_map/ppermute | solution.py:163
  24.1 31.4 %copy-start.2 = (bf16[4,136,256]{2,1,0:T(8,128)(2,1)}, bf16[4,136,256]{2,1,0:T(8,128)(2,1)S(1)}, u32[]{:S(2)}) copy-start(bf16[4,136,256]{2,1,0:T(8,128)(2,1)S(1)} %collective-permute-done.3.refs_2_) | copy-start | bytes 835588
  24.1 11.3 %collective-permute-start.4 = (bf16[4,136,256]{2,1,0:T(8,128)(2,1)S(1)}, bf16[4,136,256]{2,1,0:T(8,128)(2,1)S(1)}, u32[]{:S(2)}, u32[]{:S(2)}) collective-permute-start(bf16[4,136,256]{2,1,0:T(8,128)(2,1)S(1)} %collective-permute-done.3.refs_2_), channel_id=1, source_target_pairs={{0,32},{8,40},{16,48},{24,56},{32,64},{40,72},{48,80},{56,88},{64,... | collective-permute-start | bytes 835592 | tf_op jit(solution)/shard_map/ppermute | solution.py:172
  35.5 20.1 %copy-start.3 = (bf16[4,136,256]{2,1,0:T(8,128)(2,1)}, bf16[4,136,256]{2,1,0:T(8,128)(2,1)S(1)}, u32[]{:S(2)}) copy-start(bf16[4,136,256]{2,1,0:T(8,128)(2,1)S(1)} %collective-permute-done.4.refs_3_) | copy-start | bytes 835588
  35.5 10.4 %collective-permute-start.5 = (bf16[4,136,256]{2,1,0:T(8,128)(2,1)S(1)}, bf16[4,136,256]{2,1,0:T(8,128)(2,1)S(1)}, u32[]{:S(2)}, u32[]{:S(2)}) collective-permute-start(bf16[4,136,256]{2,1,0:T(8,128)(2,1)S(1)} %collective-permute-done.4.refs_3_), channel_id=1, source_target_pairs={{0,32},{8,40},{16,48},{24,56},{32,64},{40,72},{48,80},{56,88},{64,... | collective-permute-start | bytes 835592 | tf_op jit(solution)/shard_map/ppermute | solution.py:172
  45.9 9.7 %copy-start.4 = (bf16[4,136,256]{2,1,0:T(8,128)(2,1)}, bf16[4,136,256]{2,1,0:T(8,128)(2,1)S(1)}, u32[]{:S(2)}) copy-start(bf16[4,136,256]{2,1,0:T(8,128)(2,1)S(1)} %collective-permute-done.5.refs_4_) | copy-start | bytes 835588
  45.9 9.6 %collective-permute-start.6 = (bf16[4,136,256]{2,1,0:T(8,128)(2,1)S(1)}, bf16[4,136,256]{2,1,0:T(8,128)(2,1)S(1)}, u32[]{:S(2)}, u32[]{:S(2)}) collective-permute-start(bf16[4,136,256]{2,1,0:T(8,128)(2,1)S(1)} %collective-permute-done.5.refs_4_), channel_id=1, source_target_pairs={{0,32},{8,40},{16,48},{24,56},{32,64},{40,72},{48,80},{56,88},{64,... | collective-permute-start | bytes 835592 | tf_op jit(solution)/shard_map/ppermute | solution.py:172
  52.9 2.7 %copy-start.6 = (bf16[136,512]{1,0:T(8,128)(2,1)}, bf16[136,512]{1,0:T(8,128)(2,1)S(1)}, u32[]{:S(2)}) copy-start(bf16[136,512]{1,0:T(8,128)(2,1)S(1)} %collective-permute-done.7.refs_0_) | copy-start | bytes 417796
  55.5 0.7 copy-start.5
  61.3 20.0 %collective-permute-start.9 = (f32[8,128]{1,0:T(8,128)}, f32[8,128]{1,0:T(8,128)S(1)}, u32[]{:S(2)}, u32[]{:S(2)}) collective-permute-start(f32[8,128]{1,0:T(8,128)} %get-tuple-element.36), channel_id=1, source_target_pairs={{0,160},{8,168},{16,176},{24,184},{32,192},{40,200},{48,208},{56,2... | collective-permute-start | bytes 12296 | tf_op jit(solution)/shard_map/ppermute | solution.py:190
  73.5 11.3 %collective-permute-start.8 = (bf16[128,512]{1,0:T(8,128)(2,1)}, bf16[128,512]{1,0:T(8,128)(2,1)S(1)}, u32[]{:S(2)}, u32[]{:S(2)}) collective-permute-start(bf16[128,512]{1,0:T(8,128)(2,1)} %get-tuple-element.35), channel_id=1, source_target_pairs={{0,160},{8,168},{16,176},{24,184},{32,192},{40,200},{48,208},{56,2... | collective-permute-start | bytes 393224 | tf_op jit(solution)/shard_map/ppermute | solution.py:189
  84.8 0.7 copy-start.1

commit v17 on v10

--- a/solution.py
+++ b/solution.py
@@ -189,7 +189,7 @@
 
     query_pos = my_index * rows + offsets_in_shard
     near_out, near_stats, _ = partial(
-        queries, blocks, key_pos, key_doc, query_pos, docs.reshape(rows, 1), jnp.float32
+        queries, blocks, key_pos, key_doc, query_pos, docs.reshape(rows, 1), jnp.bfloat16
     )
     has_far = plane >= far
     heads = near_stats.shape[1] // 2

time: 113 us -> 112 us (level)
  transfers between devices with their start and end apart: 10 -> 10, of which waited for: 5 -> 5; matrix products, arithmetic and copies ran while one was open for 5% -> 5% of each run, Pallas kernels for 5% -> 4%
where the time goes in v17:
time: 112 us
  starting transfers between devices  49.6 us (44%)
  blocking collectives  19.9 us (18%)
  waiting for transfers between devices  18.2 us (16%)
  Pallas kernels  14.5 us (13%)
  other arithmetic  6.55 us (6%)
  local copies, waits for them, and re-layouts  2.84 us (3%)
    all_to_all x1, blocking collectives, shards(): received = lax.all_to_all(chunks, 'tp', 0, 0, tiled=True)  19.9 us
    ppermute x4, starting transfers between devices, shards(): current = lax.ppermute(current, 'ctx', forward)  19.6 us
    ppermute x4, waiting for transfers between devices, shards(): current = lax.ppermute(current, 'ctx', forward)  18 us
    ppermute x1, starting transfers between devices, shards(): far_rows = lax.ppermute(visit_rows, 'ctx', ahead)  11.2 us
    pallas_call x2, Pallas kernels, partial(): pl.pallas_call(partial_kernel, out_shape=(jax.ShapeDtypeStruct((rows, wid...  10 us
    ppermute x1, starting transfers between devices, shards(): far_out = lax.ppermute(visit_out, 'ctx', ahead)  9.63 us
    ppermute x3, starting transfers between devices, shards(): lax.ppermute(block, 'ctx', [(s, s ^ offset) for s in range(ctx)])  7.87 us
    pallas_call x1, Pallas kernels, merge(): pl.pallas_call(merge_kernel, out_shape=jax.ShapeDtypeStruct((pieces, rows...  4.51 us
  transfers between devices with their start and end apart: 10, of which 5 were waited for; matrix products, arithmetic and copies ran while one was open for 5% of the time, Pallas kernels for 4%

profile of v17, /device:TPU:64, one launch (start us, length us, event | category | flops | bytes accessed | tf_op | source)
XLA Modules:
  0.0 111.9 jit_solution(11814801838052247001)
XLA Ops:
  0.7 0.8 fusion.5
  1.4 3.4 %collective-permute-start.1 = (bf16[136,256]{1,0:T(8,128)(2,1)S(1)}, bf16[136,256]{1,0:T(8,128)(2,1)S(1)}, u32[]{:S(2)}, u32[]{:S(2)}) collective-permute-start(bf16[136,256]{1,0:T(8,128)(2,1)S(1)} %get-tuple-element.38), channel_id=1, source_target_pairs={{0,16},{8,24},{16,0},{24,8},{32,48},{40,56},{48,32},{56,40},{64,80... | collective-permute-start | bytes 208904 | tf_op jit(solution)/shard_map/ppermute | solution.py:162
  4.9 1.9 %collective-permute-start = (bf16[136,256]{1,0:T(8,128)(2,1)S(1)}, bf16[136,256]{1,0:T(8,128)(2,1)S(1)}, u32[]{:S(2)}, u32[]{:S(2)}) collective-permute-start(bf16[136,256]{1,0:T(8,128)(2,1)S(1)} %get-tuple-element.38), channel_id=1, source_target_pairs={{0,8},{8,0},{16,24},{24,16},{32,40},{40,32},{48,56},{56,48},{64,72... | collective-permute-start | bytes 208904 | tf_op jit(solution)/shard_map/ppermute | solution.py:162
  6.8 2.5 %collective-permute-start.2 = (bf16[136,256]{1,0:T(8,128)(2,1)S(1)}, bf16[136,256]{1,0:T(8,128)(2,1)S(1)}, u32[]{:S(2)}, u32[]{:S(2)}) collective-permute-start(bf16[136,256]{1,0:T(8,128)(2,1)S(1)} %get-tuple-element.38), channel_id=1, source_target_pairs={{0,24},{8,16},{16,8},{24,0},{32,56},{40,48},{48,40},{56,32},{64,88... | collective-permute-start | bytes 208904 | tf_op jit(solution)/shard_map/ppermute | solution.py:162
  9.3 0.9 fusion.1
  10.3 1.3 %collective-permute-start.7 = (bf16[136,512]{1,0:T(8,128)(2,1)S(1)}, bf16[136,512]{1,0:T(8,128)(2,1)S(1)}, u32[]{:S(2)}, u32[]{:S(2)}) collective-permute-start(bf16[136,512]{1,0:T(8,128)(2,1)S(1)} %fusion.1), channel_id=1, source_target_pairs={{160,0},{168,8},{176,16},{184,24},{192,32},{200,40},{208,48},{216,... | collective-permute-start | bytes 417800 | tf_op jit(solution)/shard_map/ppermute | solution.py:158
  12.6 3.8 %collective-permute-start.3 = (bf16[4,136,256]{2,1,0:T(8,128)(2,1)S(1)}, bf16[4,136,256]{2,1,0:T(8,128)(2,1)S(1)}, u32[]{:S(2)}, u32[]{:S(2)}) collective-permute-start(bf16[4,136,256]{2,1,0:T(8,128)(2,1)S(1)} %pad_maximum_fusion.refs_1_), channel_id=1, source_target_pairs={{0,32},{8,40},{16,48},{24,56},{32,64},{40,72},{48,80},{56,88},{64,... | collective-permute-start | bytes 835592 | tf_op jit(solution)/shard_map/ppermute | solution.py:167
  17.1 0.7 iota_add_fusion.2
  17.7 5.8 %collective-permute-done.3.refs_2_ = bf16[4,136,256]{2,1,0:T(8,128)(2,1)S(1)} collective-permute-done((bf16[4,136,256]{2,1,0:T(8,128)(2,1)S(1)}, bf16[4,136,256]{2,1,0:T(8,128)(2,1)S(1)}, u32[]{:S(2)}, u32[]{:S(2)}) %collective-permute-start.3) | collective-permute-done | bytes 278560 | tf_op jit(solution)/shard_map/ppermute | solution.py:167
  23.5 4.5 %collective-permute-start.4 = (bf16[4,136,256]{2,1,0:T(8,128)(2,1)S(1)}, bf16[4,136,256]{2,1,0:T(8,128)(2,1)S(1)}, u32[]{:S(2)}, u32[]{:S(2)}) collective-permute-start(bf16[4,136,256]{2,1,0:T(8,128)(2,1)S(1)} %collective-permute-done.3.refs_2_), channel_id=1, source_target_pairs={{0,32},{8,40},{16,48},{24,56},{32,64},{40,72},{48,80},{56,88},{64,... | collective-permute-start | bytes 835592 | tf_op jit(solution)/shard_map/ppermute | solution.py:167
  28.0 1.4 %copy.6.refs_9_ = s32[128,1]{1,0:T(8,128)} copy(s32[128,1]{0,1:T(1,128)} %bitcast.39) | data formatting | bytes 1024 | tf_op jit(solution)/shard_map/reshape | solution.py:192
  29.4 4.9 %collective-permute-done.4.refs_3_ = bf16[4,136,256]{2,1,0:T(8,128)(2,1)S(1)} collective-permute-done((bf16[4,136,256]{2,1,0:T(8,128)(2,1)S(1)}, bf16[4,136,256]{2,1,0:T(8,128)(2,1)S(1)}, u32[]{:S(2)}, u32[]{:S(2)}) %collective-permute-start.4) | collective-permute-done | bytes 278560 | tf_op jit(solution)/shard_map/ppermute | solution.py:167
  34.3 5.8 %collective-permute-start.5 = (bf16[4,136,256]{2,1,0:T(8,128)(2,1)S(1)}, bf16[4,136,256]{2,1,0:T(8,128)(2,1)S(1)}, u32[]{:S(2)}, u32[]{:S(2)}) collective-permute-start(bf16[4,136,256]{2,1,0:T(8,128)(2,1)S(1)} %collective-permute-done.4.refs_3_), channel_id=1, source_target_pairs={{0,32},{8,40},{16,48},{24,56},{32,64},{40,72},{48,80},{56,88},{64,... | collective-permute-start | bytes 835592 | tf_op jit(solution)/shard_map/ppermute | solution.py:167
  40.1 0.7 copy.7.refs_9_
  40.8 3.3 %collective-permute-done.5.refs_4_ = bf16[4,136,256]{2,1,0:T(8,128)(2,1)S(1)} collective-permute-done((bf16[4,136,256]{2,1,0:T(8,128)(2,1)S(1)}, bf16[4,136,256]{2,1,0:T(8,128)(2,1)S(1)}, u32[]{:S(2)}, u32[]{:S(2)}) %collective-permute-start.5) | collective-permute-done | bytes 278560 | tf_op jit(solution)/shard_map/ppermute | solution.py:167
  44.1 5.6 %collective-permute-start.6 = (bf16[4,136,256]{2,1,0:T(8,128)(2,1)S(1)}, bf16[4,136,256]{2,1,0:T(8,128)(2,1)S(1)}, u32[]{:S(2)}, u32[]{:S(2)}) collective-permute-start(bf16[4,136,256]{2,1,0:T(8,128)(2,1)S(1)} %collective-permute-done.5.refs_4_), channel_id=1, source_target_pairs={{0,32},{8,40},{16,48},{24,56},{32,64},{40,72},{48,80},{56,88},{64,... | collective-permute-start | bytes 835592 | tf_op jit(solution)/shard_map/ppermute | solution.py:167
  49.7 4.0 %collective-permute-done.6.refs_5_ = bf16[4,136,256]{2,1,0:T(8,128)(2,1)S(1)} collective-permute-done((bf16[4,136,256]{2,1,0:T(8,128)(2,1)S(1)}, bf16[4,136,256]{2,1,0:T(8,128)(2,1)S(1)}, u32[]{:S(2)}, u32[]{:S(2)}) %collective-permute-start.6) | collective-permute-done | bytes 278560 | tf_op jit(solution)/shard_map/ppermute | solution.py:167
  54.4 5.0 %shard_map.56 = (bf16[128,512]{1,0:T(8,128)(2,1)}, f32[128,8]{1,0:T(8,128)}, f32[8,128]{1,0:T(8,128)}) custom-call(bf16[136,512]{1,0:T(8,128)(2,1)} %copy-done.6, bf16[4,136,256]{2,1,0:T(8,128)(2,1)} %copy-done, bf16[4,136,256]{2,1,0:T(8,128)(2,1)} %copy-done.2, bf16[4,136,256]{2,1,0:T(8,128)(2,1)} %copy-done.3, bf16[4,136,256]{2,1,0:T(8,128)(2,1)} %copy-done.4, ...), custom_call_target="tpu_custom_call" | custom-call | flops 671088640 | bytes 1794048 | tf_op jit(solution)/shard_map/pallas_call | solution.py:69
  59.5 11.2 %collective-permute-start.9 = (f32[8,128]{1,0:T(8,128)}, f32[8,128]{1,0:T(8,128)S(1)}, u32[]{:S(2)}, u32[]{:S(2)}) collective-permute-start(f32[8,128]{1,0:T(8,128)} %get-tuple-element.36), channel_id=1, source_target_pairs={{0,160},{8,168},{16,176},{24,184},{32,192},{40,200},{48,208},{56,2... | collective-permute-start | bytes 12296 | tf_op jit(solution)/shard_map/ppermute | solution.py:188
  70.7 9.6 %collective-permute-start.8 = (bf16[128,512]{1,0:T(8,128)(2,1)}, bf16[128,512]{1,0:T(8,128)(2,1)S(1)}, u32[]{:S(2)}, u32[]{:S(2)}) collective-permute-start(bf16[128,512]{1,0:T(8,128)(2,1)} %get-tuple-element.35), channel_id=1, source_target_pairs={{0,160},{8,168},{16,176},{24,184},{32,192},{40,200},{48,208},{56,2... | collective-permute-start | bytes 393224 | tf_op jit(solution)/shard_map/ppermute | solution.py:187
  80.3 5.0 %shard_map.55 = (bf16[128,512]{1,0:T(8,128)(2,1)}, f32[128,8]{1,0:T(8,128)}, f32[8,128]{1,0:T(8,128)}) custom-call(bf16[128,512]{1,0:T(8,128)(2,1)} %refs_0_.1, bf16[4,136,256]{2,1,0:T(8,128)(2,1)} %copy-done, bf16[4,136,256]{2,1,0:T(8,128)(2,1)} %copy-done.2, bf16[4,136,256]{2,1,0:T(8,128)(2,1)} %copy-done.3, bf16[4,136,256]{2,1,0:T(8,128)(2,1)} %copy-done.4, ...), custom_call_target="tpu_custom_call" | custom-call | flops 671088640 | bytes 1785856 | tf_op jit(solution)/shard_map/pallas_call | solution.py:69
  86.6 4.5 %shard_map.57 = bf16[8,128,512]{2,1,0:T(8,128)(2,1)} custom-call(bf16[128,512]{1,0:T(8,128)(2,1)} %get-tuple-element.33.near_ref, f32[128,8]{1,0:T(8,128)} %get-tuple-element.34.near_stats_ref, bf16[128,512]{1,0:T(8,128)(2,1)} %copy-done.1, f32[8,128]{1,0:T(8,128)} %broadcast_select_fusion.far_rows_ref, bf16[512,4096]{1,0:T(8,128)(2,1)} %weight_ref.1), custom_call_target="tpu_custom_call" | custom-call | flops 536870912 | bytes 5242880 | tf_op jit(solution)/shard_map/pallas_call | solution.py:122
  91.2 19.9 %all_to_all.5 = bf16[8,128,512]{2,1,0:T(8,128)(2,1)S(1)} all-to-all(bf16[8,128,512]{2,1,0:T(8,128)(2,1)} %shard_map.57), channel_id=1, replica_groups=mesh['ctx'=64,'tp'=8] {'tp'}, dimensions={0} | all-to-all | bytes 2097152 | tf_op jit(solution)/shard_map/all_to_all | solution.py:200
  111.1 0.8 reduce_sum.12
  (36 shorter events, 4.3 us)
Async XLA Ops:
  1.4 10.9 %collective-permute-start.1 = (bf16[136,256]{1,0:T(8,128)(2,1)S(1)}, bf16[136,256]{1,0:T(8,128)(2,1)S(1)}, u32[]{:S(2)}, u32[]{:S(2)}) collective-permute-start(bf16[136,256]{1,0:T(8,128)(2,1)S(1)} %get-tuple-element.38), channel_id=1, source_target_pairs={{0,16},{8,24},{16,0},{24,8},{32,48},{40,56},{48,32},{56,40},{64,80... | collective-permute-start | bytes 208904 | tf_op jit(solution)/shard_map/ppermute | solution.py:162
  4.9 7.5 %collective-permute-start = (bf16[136,256]{1,0:T(8,128)(2,1)S(1)}, bf16[136,256]{1,0:T(8,128)(2,1)S(1)}, u32[]{:S(2)}, u32[]{:S(2)}) collective-permute-start(bf16[136,256]{1,0:T(8,128)(2,1)S(1)} %get-tuple-element.38), channel_id=1, source_target_pairs={{0,8},{8,0},{16,24},{24,16},{32,40},{40,32},{48,56},{56,48},{64,72... | collective-permute-start | bytes 208904 | tf_op jit(solution)/shard_map/ppermute | solution.py:162
  6.8 5.7 %collective-permute-start.2 = (bf16[136,256]{1,0:T(8,128)(2,1)S(1)}, bf16[136,256]{1,0:T(8,128)(2,1)S(1)}, u32[]{:S(2)}, u32[]{:S(2)}) collective-permute-start(bf16[136,256]{1,0:T(8,128)(2,1)S(1)} %get-tuple-element.38), channel_id=1, source_target_pairs={{0,24},{8,16},{16,8},{24,0},{32,56},{40,48},{48,40},{56,32},{64,88... | collective-permute-start | bytes 208904 | tf_op jit(solution)/shard_map/ppermute | solution.py:162
  10.3 29.8 %collective-permute-start.7 = (bf16[136,512]{1,0:T(8,128)(2,1)S(1)}, bf16[136,512]{1,0:T(8,128)(2,1)S(1)}, u32[]{:S(2)}, u32[]{:S(2)}) collective-permute-start(bf16[136,512]{1,0:T(8,128)(2,1)S(1)} %fusion.1), channel_id=1, source_target_pairs={{160,0},{168,8},{176,16},{184,24},{192,32},{200,40},{208,48},{216,... | collective-permute-start | bytes 417800 | tf_op jit(solution)/shard_map/ppermute | solution.py:158
  12.6 41.8 %copy-start = (bf16[4,136,256]{2,1,0:T(8,128)(2,1)}, bf16[4,136,256]{2,1,0:T(8,128)(2,1)S(1)}, u32[]{:S(2)}) copy-start(bf16[4,136,256]{2,1,0:T(8,128)(2,1)S(1)} %pad_maximum_fusion.refs_1_) | copy-start | bytes 835588
  12.6 10.9 %collective-permute-start.3 = (bf16[4,136,256]{2,1,0:T(8,128)(2,1)S(1)}, bf16[4,136,256]{2,1,0:T(8,128)(2,1)S(1)}, u32[]{:S(2)}, u32[]{:S(2)}) collective-permute-start(bf16[4,136,256]{2,1,0:T(8,128)(2,1)S(1)} %pad_maximum_fusion.refs_1_), channel_id=1, source_target_pairs={{0,32},{8,40},{16,48},{24,56},{32,64},{40,72},{48,80},{56,88},{64,... | collective-permute-start | bytes 835592 | tf_op jit(solution)/shard_map/ppermute | solution.py:167
  23.5 30.9 %copy-start.2 = (bf16[4,136,256]{2,1,0:T(8,128)(2,1)}, bf16[4,136,256]{2,1,0:T(8,128)(2,1)S(1)}, u32[]{:S(2)}) copy-start(bf16[4,136,256]{2,1,0:T(8,128)(2,1)S(1)} %collective-permute-done.3.refs_2_) | copy-start | bytes 835588
  23.5 10.8 %collective-permute-start.4 = (bf16[4,136,256]{2,1,0:T(8,128)(2,1)S(1)}, bf16[4,136,256]{2,1,0:T(8,128)(2,1)S(1)}, u32[]{:S(2)}, u32[]{:S(2)}) collective-permute-start(bf16[4,136,256]{2,1,0:T(8,128)(2,1)S(1)} %collective-permute-done.3.refs_2_), channel_id=1, source_target_pairs={{0,32},{8,40},{16,48},{24,56},{32,64},{40,72},{48,80},{56,88},{64,... | collective-permute-start | bytes 835592 | tf_op jit(solution)/shard_map/ppermute | solution.py:167
  34.3 20.1 %copy-start.3 = (bf16[4,136,256]{2,1,0:T(8,128)(2,1)}, bf16[4,136,256]{2,1,0:T(8,128)(2,1)S(1)}, u32[]{:S(2)}) copy-start(bf16[4,136,256]{2,1,0:T(8,128)(2,1)S(1)} %collective-permute-done.4.refs_3_) | copy-start | bytes 835588
  34.3 9.8 %collective-permute-start.5 = (bf16[4,136,256]{2,1,0:T(8,128)(2,1)S(1)}, bf16[4,136,256]{2,1,0:T(8,128)(2,1)S(1)}, u32[]{:S(2)}, u32[]{:S(2)}) collective-permute-start(bf16[4,136,256]{2,1,0:T(8,128)(2,1)S(1)} %collective-permute-done.4.refs_3_), channel_id=1, source_target_pairs={{0,32},{8,40},{16,48},{24,56},{32,64},{40,72},{48,80},{56,88},{64,... | collective-permute-start | bytes 835592 | tf_op jit(solution)/shard_map/ppermute | solution.py:167
  40.1 14.4 %copy-start.6 = (bf16[136,512]{1,0:T(8,128)(2,1)}, bf16[136,512]{1,0:T(8,128)(2,1)S(1)}, u32[]{:S(2)}) copy-start(bf16[136,512]{1,0:T(8,128)(2,1)S(1)} %collective-permute-done.7.refs_0_) | copy-start | bytes 417796
  44.1 10.3 %copy-start.4 = (bf16[4,136,256]{2,1,0:T(8,128)(2,1)}, bf16[4,136,256]{2,1,0:T(8,128)(2,1)S(1)}, u32[]{:S(2)}) copy-start(bf16[4,136,256]{2,1,0:T(8,128)(2,1)S(1)} %collective-permute-done.5.refs_4_) | copy-start | bytes 835588
  44.1 9.6 %collective-permute-start.6 = (bf16[4,136,256]{2,1,0:T(8,128)(2,1)S(1)}, bf16[4,136,256]{2,1,0:T(8,128)(2,1)S(1)}, u32[]{:S(2)}, u32[]{:S(2)}) collective-permute-start(bf16[4,136,256]{2,1,0:T(8,128)(2,1)S(1)} %collective-permute-done.5.refs_4_), channel_id=1, source_target_pairs={{0,32},{8,40},{16,48},{24,56},{32,64},{40,72},{48,80},{56,88},{64,... | collective-permute-start | bytes 835592 | tf_op jit(solution)/shard_map/ppermute | solution.py:167
  53.7 0.7 copy-start.5
  59.5 25.9 %collective-permute-start.9 = (f32[8,128]{1,0:T(8,128)}, f32[8,128]{1,0:T(8,128)S(1)}, u32[]{:S(2)}, u32[]{:S(2)}) collective-permute-start(f32[8,128]{1,0:T(8,128)} %get-tuple-element.36), channel_id=1, source_target_pairs={{0,160},{8,168},{16,176},{24,184},{32,192},{40,200},{48,208},{56,2... | collective-permute-start | bytes 12296 | tf_op jit(solution)/shard_map/ppermute | solution.py:188
  70.7 15.3 %collective-permute-start.8 = (bf16[128,512]{1,0:T(8,128)(2,1)}, bf16[128,512]{1,0:T(8,128)(2,1)S(1)}, u32[]{:S(2)}, u32[]{:S(2)}) collective-permute-start(bf16[128,512]{1,0:T(8,128)(2,1)} %get-tuple-element.35), channel_id=1, source_target_pairs={{0,160},{8,168},{16,176},{24,184},{32,192},{40,200},{48,208},{56,2... | collective-permute-start | bytes 393224 | tf_op jit(solution)/shard_map/ppermute | solution.py:187
  86.0 0.7 copy-start.1

commit v18 on v15

--- a/solution.py
+++ b/solution.py
@@ -199,7 +199,7 @@
 
     query_pos = my_index * rows + offsets_in_shard
     near_out, near_stats, _ = partial(
-        queries, blocks, key_pos, key_doc, query_pos, docs.reshape(rows, 1), jnp.float32
+        queries, blocks, key_pos, key_doc, query_pos, docs.reshape(rows, 1), jnp.bfloat16
     )
     has_far = plane >= far
     heads = near_stats.shape[1] // 2

time: 114 us -> 114 us (level)
  no operation moved by 1% of the time
where the time goes in v18:
time: 114 us
  starting transfers between devices  49.6 us (44%)
  blocking collectives  19.9 us (17%)
  waiting for transfers between devices  18.9 us (17%)
  Pallas kernels  14.3 us (13%)
  other arithmetic  5.97 us (5%)
  local copies, waits for them, and re-layouts  4.67 us (4%)
    all_to_all x1, blocking collectives, shards(): received = lax.all_to_all(chunks, 'tp', 0, 0, tiled=True)  19.9 us
    ppermute x4, starting transfers between devices, shards(): current = lax.ppermute(current, 'ctx', forward)  19.6 us
    ppermute x4, waiting for transfers between devices, shards(): current = lax.ppermute(current, 'ctx', forward)  18.8 us
    ppermute x1, starting transfers between devices, shards(): far_rows = lax.ppermute(visit_rows, 'ctx', ahead)  11.2 us
    pallas_call x2, Pallas kernels, partial(): pl.pallas_call(partial_kernel, out_shape=(jax.ShapeDtypeStruct((rows, wid...  9.81 us
    ppermute x1, starting transfers between devices, shards(): far_out = lax.ppermute(visit_out, 'ctx', ahead)  9.65 us
    ppermute x3, starting transfers between devices, shards(): lax.ppermute(block, 'ctx', [(s, s ^ offset) for s in range(ctx)])  7.87 us
    pallas_call x1, Pallas kernels, merge(): pl.pallas_call(merge_kernel, out_shape=jax.ShapeDtypeStruct((pieces, rows...  4.52 us
  transfers between devices with their start and end apart: 10, of which 4 were waited for; matrix products, arithmetic and copies ran while one was open for 5% of the time, Pallas kernels for 4%

profile of v18, /device:TPU:64, one launch (start us, length us, event | category | flops | bytes accessed | tf_op | source)
XLA Modules:
  0.0 113.7 jit_solution(12885941842865227043)
XLA Ops:
  0.7 0.8 fusion.11
  1.4 3.4 %collective-permute-start.1 = (bf16[136,256]{1,0:T(8,128)(2,1)S(1)}, bf16[136,256]{1,0:T(8,128)(2,1)S(1)}, u32[]{:S(2)}, u32[]{:S(2)}) collective-permute-start(bf16[136,256]{1,0:T(8,128)(2,1)S(1)} %get-tuple-element.46), channel_id=1, source_target_pairs={{0,16},{8,24},{16,0},{24,8},{32,48},{40,56},{48,32},{56,40},{64,80... | collective-permute-start | bytes 208904 | tf_op jit(solution)/shard_map/ppermute | solution.py:162
  4.9 1.9 %collective-permute-start = (bf16[136,256]{1,0:T(8,128)(2,1)S(1)}, bf16[136,256]{1,0:T(8,128)(2,1)S(1)}, u32[]{:S(2)}, u32[]{:S(2)}) collective-permute-start(bf16[136,256]{1,0:T(8,128)(2,1)S(1)} %get-tuple-element.46), channel_id=1, source_target_pairs={{0,8},{8,0},{16,24},{24,16},{32,40},{40,32},{48,56},{56,48},{64,72... | collective-permute-start | bytes 208904 | tf_op jit(solution)/shard_map/ppermute | solution.py:162
  6.8 2.5 %collective-permute-start.2 = (bf16[136,256]{1,0:T(8,128)(2,1)S(1)}, bf16[136,256]{1,0:T(8,128)(2,1)S(1)}, u32[]{:S(2)}, u32[]{:S(2)}) collective-permute-start(bf16[136,256]{1,0:T(8,128)(2,1)S(1)} %get-tuple-element.46), channel_id=1, source_target_pairs={{0,24},{8,16},{16,8},{24,0},{32,56},{40,48},{48,40},{56,32},{64,88... | collective-permute-start | bytes 208904 | tf_op jit(solution)/shard_map/ppermute | solution.py:162
  9.3 0.9 fusion.1
  10.3 1.3 %collective-permute-start.7 = (bf16[136,512]{1,0:T(8,128)(2,1)S(1)}, bf16[136,512]{1,0:T(8,128)(2,1)S(1)}, u32[]{:S(2)}, u32[]{:S(2)}) collective-permute-start(bf16[136,512]{1,0:T(8,128)(2,1)S(1)} %fusion.1), channel_id=1, source_target_pairs={{160,0},{168,8},{176,16},{184,24},{192,32},{200,40},{208,48},{216,... | collective-permute-start | bytes 417800 | tf_op jit(solution)/shard_map/ppermute | solution.py:158
  13.1 3.8 %collective-permute-start.3 = (bf16[4,136,256]{2,1,0:T(8,128)(2,1)S(1)}, bf16[4,136,256]{2,1,0:T(8,128)(2,1)S(1)}, u32[]{:S(2)}, u32[]{:S(2)}) collective-permute-start(bf16[4,136,256]{2,1,0:T(8,128)(2,1)S(1)} %pad_maximum_fusion.refs_1_), channel_id=1, source_target_pairs={{0,32},{8,40},{16,48},{24,56},{32,64},{40,72},{48,80},{56,88},{64,... | collective-permute-start | bytes 835592 | tf_op jit(solution)/shard_map/ppermute | solution.py:167
  17.5 6.0 %collective-permute-done.3.refs_2_ = bf16[4,136,256]{2,1,0:T(8,128)(2,1)S(1)} collective-permute-done((bf16[4,136,256]{2,1,0:T(8,128)(2,1)S(1)}, bf16[4,136,256]{2,1,0:T(8,128)(2,1)S(1)}, u32[]{:S(2)}, u32[]{:S(2)}) %collective-permute-start.3) | collective-permute-done | bytes 278560 | tf_op jit(solution)/shard_map/ppermute | solution.py:167
  23.6 4.5 %collective-permute-start.4 = (bf16[4,136,256]{2,1,0:T(8,128)(2,1)S(1)}, bf16[4,136,256]{2,1,0:T(8,128)(2,1)S(1)}, u32[]{:S(2)}, u32[]{:S(2)}) collective-permute-start(bf16[4,136,256]{2,1,0:T(8,128)(2,1)S(1)} %collective-permute-done.3.refs_2_), channel_id=1, source_target_pairs={{0,32},{8,40},{16,48},{24,56},{32,64},{40,72},{48,80},{56,88},{64,... | collective-permute-start | bytes 835592 | tf_op jit(solution)/shard_map/ppermute | solution.py:167
  28.1 1.4 %copy.6.refs_9_ = s32[128,1]{1,0:T(8,128)} copy(s32[128,1]{0,1:T(1,128)} %bitcast.69) | data formatting | bytes 1024 | tf_op jit(solution)/shard_map/reshape | solution.py:202
  29.5 5.5 %collective-permute-done.4.refs_3_ = bf16[4,136,256]{2,1,0:T(8,128)(2,1)S(1)} collective-permute-done((bf16[4,136,256]{2,1,0:T(8,128)(2,1)S(1)}, bf16[4,136,256]{2,1,0:T(8,128)(2,1)S(1)}, u32[]{:S(2)}, u32[]{:S(2)}) %collective-permute-start.4) | collective-permute-done | bytes 278560 | tf_op jit(solution)/shard_map/ppermute | solution.py:167
  35.0 5.8 %collective-permute-start.5 = (bf16[4,136,256]{2,1,0:T(8,128)(2,1)S(1)}, bf16[4,136,256]{2,1,0:T(8,128)(2,1)S(1)}, u32[]{:S(2)}, u32[]{:S(2)}) collective-permute-start(bf16[4,136,256]{2,1,0:T(8,128)(2,1)S(1)} %collective-permute-done.4.refs_3_), channel_id=1, source_target_pairs={{0,32},{8,40},{16,48},{24,56},{32,64},{40,72},{48,80},{56,88},{64,... | collective-permute-start | bytes 835592 | tf_op jit(solution)/shard_map/ppermute | solution.py:167
  40.8 0.7 copy.7.refs_9_
  41.6 3.3 %collective-permute-done.5.refs_4_ = bf16[4,136,256]{2,1,0:T(8,128)(2,1)S(1)} collective-permute-done((bf16[4,136,256]{2,1,0:T(8,128)(2,1)S(1)}, bf16[4,136,256]{2,1,0:T(8,128)(2,1)S(1)}, u32[]{:S(2)}, u32[]{:S(2)}) %collective-permute-start.5) | collective-permute-done | bytes 278560 | tf_op jit(solution)/shard_map/ppermute | solution.py:167
  44.8 5.6 %collective-permute-start.6 = (bf16[4,136,256]{2,1,0:T(8,128)(2,1)S(1)}, bf16[4,136,256]{2,1,0:T(8,128)(2,1)S(1)}, u32[]{:S(2)}, u32[]{:S(2)}) collective-permute-start(bf16[4,136,256]{2,1,0:T(8,128)(2,1)S(1)} %collective-permute-done.5.refs_4_), channel_id=1, source_target_pairs={{0,32},{8,40},{16,48},{24,56},{32,64},{40,72},{48,80},{56,88},{64,... | collective-permute-start | bytes 835592 | tf_op jit(solution)/shard_map/ppermute | solution.py:167
  50.5 4.0 %collective-permute-done.6.refs_5_ = bf16[4,136,256]{2,1,0:T(8,128)(2,1)S(1)} collective-permute-done((bf16[4,136,256]{2,1,0:T(8,128)(2,1)S(1)}, bf16[4,136,256]{2,1,0:T(8,128)(2,1)S(1)}, u32[]{:S(2)}, u32[]{:S(2)}) %collective-permute-start.6) | collective-permute-done | bytes 278560 | tf_op jit(solution)/shard_map/ppermute | solution.py:167
  54.5 0.7 constant_dynamic-slice_fusion.refs_5_
  55.8 4.8 %shard_map.56 = (bf16[128,512]{1,0:T(8,128)(2,1)}, f32[128,8]{1,0:T(8,128)}, f32[8,128]{1,0:T(8,128)}) custom-call(bf16[136,512]{1,0:T(8,128)(2,1)} %copy-done.9, bf16[4,136,256]{2,1,0:T(8,128)(2,1)} %copy-done, bf16[4,136,256]{2,1,0:T(8,128)(2,1)} %copy-done.6, bf16[4,136,256]{2,1,0:T(8,128)(2,1)} %copy-done.7, bf16[4,136,256]{2,1,0:T(8,128)(2,1)} %copy-done.8, ...), custom_call_target="tpu_custom_call" | custom-call | flops 570425344 | bytes 1585152 | tf_op jit(solution)/shard_map/pallas_call | solution.py:69
  60.6 11.2 %collective-permute-start.9 = (f32[8,128]{1,0:T(8,128)}, f32[8,128]{1,0:T(8,128)S(1)}, u32[]{:S(2)}, u32[]{:S(2)}) collective-permute-start(f32[8,128]{1,0:T(8,128)} %get-tuple-element.36), channel_id=1, source_target_pairs={{0,160},{8,168},{16,176},{24,184},{32,192},{40,200},{48,208},{56,2... | collective-permute-start | bytes 12296 | tf_op jit(solution)/shard_map/ppermute | solution.py:198
  71.8 9.7 %collective-permute-start.8 = (bf16[128,512]{1,0:T(8,128)(2,1)}, bf16[128,512]{1,0:T(8,128)(2,1)S(1)}, u32[]{:S(2)}, u32[]{:S(2)}) collective-permute-start(bf16[128,512]{1,0:T(8,128)(2,1)} %get-tuple-element.35), channel_id=1, source_target_pairs={{0,160},{8,168},{16,176},{24,184},{32,192},{40,200},{48,208},{56,2... | collective-permute-start | bytes 393224 | tf_op jit(solution)/shard_map/ppermute | solution.py:197
  82.1 5.0 %shard_map.55 = (bf16[128,512]{1,0:T(8,128)(2,1)}, f32[128,8]{1,0:T(8,128)}, f32[8,128]{1,0:T(8,128)}) custom-call(bf16[128,512]{1,0:T(8,128)(2,1)} %refs_0_.1, bf16[4,136,256]{2,1,0:T(8,128)(2,1)} %copy-done, bf16[4,136,256]{2,1,0:T(8,128)(2,1)} %copy-done.6, bf16[4,136,256]{2,1,0:T(8,128)(2,1)} %copy-done.7, bf16[4,136,256]{2,1,0:T(8,128)(2,1)} %copy-done.8, ...), custom_call_target="tpu_custom_call" | custom-call | flops 671088640 | bytes 1785856 | tf_op jit(solution)/shard_map/pallas_call | solution.py:69
  88.4 4.5 %shard_map.57 = bf16[8,128,512]{2,1,0:T(8,128)(2,1)} custom-call(bf16[128,512]{1,0:T(8,128)(2,1)} %get-tuple-element.33.near_ref, f32[128,8]{1,0:T(8,128)} %get-tuple-element.34.near_stats_ref, bf16[128,512]{1,0:T(8,128)(2,1)} %copy-done.1, f32[8,128]{1,0:T(8,128)} %broadcast_select_fusion.far_rows_ref, bf16[512,4096]{1,0:T(8,128)(2,1)} %weight_ref.1), custom_call_target="tpu_custom_call" | custom-call | flops 536870912 | bytes 5242880 | tf_op jit(solution)/shard_map/pallas_call | solution.py:122
  92.9 19.9 %all_to_all.5 = bf16[8,128,512]{2,1,0:T(8,128)(2,1)S(1)} all-to-all(bf16[8,128,512]{2,1,0:T(8,128)(2,1)} %shard_map.57), channel_id=1, replica_groups=mesh['ctx'=64,'tp'=8] {'tp'}, dimensions={0} | all-to-all | bytes 2097152 | tf_op jit(solution)/shard_map/all_to_all | solution.py:210
  112.9 0.8 reduce_sum.12
  (46 shorter events, 5.3 us)
Async XLA Ops:
  1.4 11.6 %collective-permute-start.1 = (bf16[136,256]{1,0:T(8,128)(2,1)S(1)}, bf16[136,256]{1,0:T(8,128)(2,1)S(1)}, u32[]{:S(2)}, u32[]{:S(2)}) collective-permute-start(bf16[136,256]{1,0:T(8,128)(2,1)S(1)} %get-tuple-element.46), channel_id=1, source_target_pairs={{0,16},{8,24},{16,0},{24,8},{32,48},{40,56},{48,32},{56,40},{64,80... | collective-permute-start | bytes 208904 | tf_op jit(solution)/shard_map/ppermute | solution.py:162
  4.9 8.2 %collective-permute-start = (bf16[136,256]{1,0:T(8,128)(2,1)S(1)}, bf16[136,256]{1,0:T(8,128)(2,1)S(1)}, u32[]{:S(2)}, u32[]{:S(2)}) collective-permute-start(bf16[136,256]{1,0:T(8,128)(2,1)S(1)} %get-tuple-element.46), channel_id=1, source_target_pairs={{0,8},{8,0},{16,24},{24,16},{32,40},{40,32},{48,56},{56,48},{64,72... | collective-permute-start | bytes 208904 | tf_op jit(solution)/shard_map/ppermute | solution.py:162
  6.8 6.3 %collective-permute-start.2 = (bf16[136,256]{1,0:T(8,128)(2,1)S(1)}, bf16[136,256]{1,0:T(8,128)(2,1)S(1)}, u32[]{:S(2)}, u32[]{:S(2)}) collective-permute-start(bf16[136,256]{1,0:T(8,128)(2,1)S(1)} %get-tuple-element.46), channel_id=1, source_target_pairs={{0,24},{8,16},{16,8},{24,0},{32,56},{40,48},{48,40},{56,32},{64,88... | collective-permute-start | bytes 208904 | tf_op jit(solution)/shard_map/ppermute | solution.py:162
  10.3 30.5 %collective-permute-start.7 = (bf16[136,512]{1,0:T(8,128)(2,1)S(1)}, bf16[136,512]{1,0:T(8,128)(2,1)S(1)}, u32[]{:S(2)}, u32[]{:S(2)}) collective-permute-start(bf16[136,512]{1,0:T(8,128)(2,1)S(1)} %fusion.1), channel_id=1, source_target_pairs={{160,0},{168,8},{176,16},{184,24},{192,32},{200,40},{208,48},{216,... | collective-permute-start | bytes 417800 | tf_op jit(solution)/shard_map/ppermute | solution.py:158
  11.8 69.7 %copy-start.2 = (s32[5,4,128]{2,1,0:T(4,128)}, s32[5,4,128]{2,1,0:T(4,128)S(1)}, u32[]{:S(2)}) copy-start(s32[5,4,128]{2,1,0:T(4,128)S(1)} %iota_add_fusion.2) | copy-start | bytes 30724
  13.1 42.0 %copy-start = (bf16[4,136,256]{2,1,0:T(8,128)(2,1)}, bf16[4,136,256]{2,1,0:T(8,128)(2,1)S(1)}, u32[]{:S(2)}) copy-start(bf16[4,136,256]{2,1,0:T(8,128)(2,1)S(1)} %pad_maximum_fusion.refs_1_) | copy-start | bytes 835588
  13.1 10.5 %collective-permute-start.3 = (bf16[4,136,256]{2,1,0:T(8,128)(2,1)S(1)}, bf16[4,136,256]{2,1,0:T(8,128)(2,1)S(1)}, u32[]{:S(2)}, u32[]{:S(2)}) collective-permute-start(bf16[4,136,256]{2,1,0:T(8,128)(2,1)S(1)} %pad_maximum_fusion.refs_1_), channel_id=1, source_target_pairs={{0,32},{8,40},{16,48},{24,56},{32,64},{40,72},{48,80},{56,88},{64,... | collective-permute-start | bytes 835592 | tf_op jit(solution)/shard_map/ppermute | solution.py:167
  23.6 31.6 %copy-start.6 = (bf16[4,136,256]{2,1,0:T(8,128)(2,1)}, bf16[4,136,256]{2,1,0:T(8,128)(2,1)S(1)}, u32[]{:S(2)}) copy-start(bf16[4,136,256]{2,1,0:T(8,128)(2,1)S(1)} %collective-permute-done.3.refs_2_) | copy-start | bytes 835588
  23.6 11.4 %collective-permute-start.4 = (bf16[4,136,256]{2,1,0:T(8,128)(2,1)S(1)}, bf16[4,136,256]{2,1,0:T(8,128)(2,1)S(1)}, u32[]{:S(2)}, u32[]{:S(2)}) collective-permute-start(bf16[4,136,256]{2,1,0:T(8,128)(2,1)S(1)} %collective-permute-done.3.refs_2_), channel_id=1, source_target_pairs={{0,32},{8,40},{16,48},{24,56},{32,64},{40,72},{48,80},{56,88},{64,... | collective-permute-start | bytes 835592 | tf_op jit(solution)/shard_map/ppermute | solution.py:167
  35.0 20.1 %copy-start.7 = (bf16[4,136,256]{2,1,0:T(8,128)(2,1)}, bf16[4,136,256]{2,1,0:T(8,128)(2,1)S(1)}, u32[]{:S(2)}) copy-start(bf16[4,136,256]{2,1,0:T(8,128)(2,1)S(1)} %collective-permute-done.4.refs_3_) | copy-start | bytes 835588
  35.0 9.8 %collective-permute-start.5 = (bf16[4,136,256]{2,1,0:T(8,128)(2,1)S(1)}, bf16[4,136,256]{2,1,0:T(8,128)(2,1)S(1)}, u32[]{:S(2)}, u32[]{:S(2)}) collective-permute-start(bf16[4,136,256]{2,1,0:T(8,128)(2,1)S(1)} %collective-permute-done.4.refs_3_), channel_id=1, source_target_pairs={{0,32},{8,40},{16,48},{24,56},{32,64},{40,72},{48,80},{56,88},{64,... | collective-permute-start | bytes 835592 | tf_op jit(solution)/shard_map/ppermute | solution.py:167
  40.8 14.4 %copy-start.9 = (bf16[136,512]{1,0:T(8,128)(2,1)}, bf16[136,512]{1,0:T(8,128)(2,1)S(1)}, u32[]{:S(2)}) copy-start(bf16[136,512]{1,0:T(8,128)(2,1)S(1)} %collective-permute-done.7.refs_0_) | copy-start | bytes 417796
  44.8 10.4 %copy-start.8 = (bf16[4,136,256]{2,1,0:T(8,128)(2,1)}, bf16[4,136,256]{2,1,0:T(8,128)(2,1)S(1)}, u32[]{:S(2)}) copy-start(bf16[4,136,256]{2,1,0:T(8,128)(2,1)S(1)} %collective-permute-done.5.refs_4_) | copy-start | bytes 835588
  44.8 9.6 %collective-permute-start.6 = (bf16[4,136,256]{2,1,0:T(8,128)(2,1)S(1)}, bf16[4,136,256]{2,1,0:T(8,128)(2,1)S(1)}, u32[]{:S(2)}, u32[]{:S(2)}) collective-permute-start(bf16[4,136,256]{2,1,0:T(8,128)(2,1)S(1)} %collective-permute-done.5.refs_4_), channel_id=1, source_target_pairs={{0,32},{8,40},{16,48},{24,56},{32,64},{40,72},{48,80},{56,88},{64,... | collective-permute-start | bytes 835592 | tf_op jit(solution)/shard_map/ppermute | solution.py:167
  54.5 27.0 %copy-start.3 = (bf16[4,136,256]{2,1,0:T(8,128)(2,1)}, bf16[4,136,256]{2,1,0:T(8,128)(2,1)S(1)}, u32[]{:S(2)}) copy-start(bf16[4,136,256]{2,1,0:T(8,128)(2,1)S(1)} %collective-permute-done.6.refs_5_) | copy-start | bytes 835588
  55.2 0.6 copy-start.4
  60.6 26.5 %collective-permute-start.9 = (f32[8,128]{1,0:T(8,128)}, f32[8,128]{1,0:T(8,128)S(1)}, u32[]{:S(2)}, u32[]{:S(2)}) collective-permute-start(f32[8,128]{1,0:T(8,128)} %get-tuple-element.36), channel_id=1, source_target_pairs={{0,160},{8,168},{16,176},{24,184},{32,192},{40,200},{48,208},{56,2... | collective-permute-start | bytes 12296 | tf_op jit(solution)/shard_map/ppermute | solution.py:198
  71.8 16.0 %collective-permute-start.8 = (bf16[128,512]{1,0:T(8,128)(2,1)}, bf16[128,512]{1,0:T(8,128)(2,1)S(1)}, u32[]{:S(2)}, u32[]{:S(2)}) collective-permute-start(bf16[128,512]{1,0:T(8,128)(2,1)} %get-tuple-element.35), channel_id=1, source_target_pairs={{0,160},{8,168},{16,176},{24,184},{32,192},{40,200},{48,208},{56,2... | collective-permute-start | bytes 393224 | tf_op jit(solution)/shard_map/ppermute | solution.py:197
  81.5 0.6 copy-start.5
  87.8 0.7 copy-start.1
